TPU v7x, 32 devices: a whole 2x2x4 slice. The times are simulated.
32 devices in a mesh: seq: 8 (over z, x), dp: 4 (over y, core).
Axes of the slice: x: 2, y: 2, z: 4, core: 2. Of those that a mesh axis runs over, the one named last changes fastest.
Arguments:
- encoder_out: bfloat16 [4, 2560, 1536], P('dp', 'seq'), may hold values from -0.59765625 to 0.59765625
- out_grad: bfloat16 [4, 2560, 1536], P('dp', 'seq'), may hold values from -12 to 12
- segment_states: bfloat16 [4, 1024, 1536], P('dp', 'seq'), may hold values from -6 to 6
- segment_starts: int32 [4, 1024], P('dp', 'seq'), may hold values from 0 to 320, as said below
- segment_counts: int32 [4, 8], P('dp', 'seq'), may hold values from 32 to 128, as said below
- segment_probs: int32 [4, 1024], P('dp', 'seq'), may hold values from 0 to 65535, as said below
- query_weight: bfloat16 [1536, 1536], P('dp'), may hold values from -0.15625 to 0.15625
- key_weight: bfloat16 [1536, 1536], P('dp'), may hold values from -0.15625 to 0.15625
Outputs:
- x_grad: bfloat16 [4, 2560, 1536], P('dp', 'seq')
- segment_grad: bfloat16 [4, 1024, 1536], P('dp', 'seq')
Inputs may be any that keep to these rules, and one draw needn't show every extreme that they name: `segment_starts`: for block s of sequence b, the entries s * 128 + j with j < segment_counts[b, s] hold distinct increasing local positions below 320 at which segments start; the other entries hold 320. Byte 0 of every sequence starts a segment. `segment_counts`: every sequence has one block with exactly 128 segments and another with exactly a quarter of 128. `segment_probs`: A slot holds 0 exactly when it is past its block's count; slot 0 of every sequence holds 65535.
All inputs are finite; a program needn't handle non-finite values.
Results may differ from a plain program's by a relative error of at most 0.0049.
Values may be sent and summed in bfloat16 or wider, within the bound.
No kernel may reach another device: no remote copies, remote signals or barrier semaphores. Data moves between devices by JAX's collectives and lax.ppermute only.
A program may use at most 64 MiB of HBM per device.

v0:
```python
import jax
import jax.numpy as jnp
from jax import lax
from jax.sharding import PartitionSpec as P

prob_scale = 65536.0
norm_eps = 1e-06
exact = lax.Precision.HIGHEST
contract_last = (((1,), (1,)), ((), ()))
contract_first = (((0,), (0,)), ((), ()))


def shifted(block, axis, distance):
    devices = range(lax.axis_size(axis))
    route = [(i - distance, i) for i in devices if i - distance in devices]
    return lax.ppermute(block, axis, route)


def normalize_grad(vectors, scales, unit_grad):
    inner_prod = jnp.sum(vectors * unit_grad, axis=-1, keepdims=True)
    return scales * unit_grad - scales * scales * scales * inner_prod * vectors


def carry_from(log_keep, vectors, shard_index, from_lower):
    running_log = jnp.cumsum(log_keep)
    before = running_log - log_keep
    shard_order = jnp.arange(log_keep.shape[0])
    if from_lower:
        own_value = lax.dynamic_index_in_dim(before, shard_index, keepdims=False)
        selected = shard_order < shard_index
        log_gap = own_value - running_log
    else:
        own_value = lax.dynamic_index_in_dim(running_log, shard_index, keepdims=False)
        selected = shard_order > shard_index
        log_gap = before - own_value
    factor = jnp.where(selected, jnp.exp(jnp.where(selected, log_gap, 0.0)), 0.0)
    return jnp.dot(factor[None, :], vectors, precision=exact)


def per_device(
    encoder_out,
    out_grad,
    segment_states,
    segment_starts,
    segment_counts,
    segment_probs,
    query_weight,
    key_weight,
):
    token_rows = encoder_out[0]
    grad_rows = out_grad[0]
    token_count = token_rows.shape[0]
    slot_count = segment_states.shape[1]
    shard_index = lax.axis_index("seq")
    full_query, full_key = (
        lax.all_gather(query_weight, "dp", axis=0, tiled=True),
        lax.all_gather(key_weight, "dp", axis=0, tiled=True),
    )
    key_rows = jnp.dot(token_rows, full_key, preferred_element_type=jnp.float32)
    queries = jnp.dot(token_rows, full_query, preferred_element_type=jnp.float32)
    query_scale = lax.rsqrt(jnp.sum(queries * queries, axis=1, keepdims=True) + norm_eps)
    key_scale = lax.rsqrt(jnp.sum(key_rows * key_rows, axis=1, keepdims=True) + norm_eps)
    query_unit = queries * query_scale
    key_unit = key_rows * key_scale
    position = jnp.arange(token_count)
    later_rows = (shard_index > 0) | (position > 0)
    key_before = shifted(key_unit[token_count - 1 :], "seq", 1)
    key_prior = jnp.concatenate([key_before, key_unit[:-1]], axis=0)
    cosine = jnp.sum(query_unit * key_prior, axis=1)
    segment_total = segment_counts[0, 0]
    slot_index = jnp.arange(slot_count)
    slot_used = slot_index < segment_total
    start_pos = segment_starts[0]
    smoothing = jnp.where(slot_used, segment_probs[0].astype(jnp.float32) / prob_scale, 0.0)
    reached = slot_used[None, :] & (start_pos[None, :] <= position[:, None])
    member_id = jnp.sum(reached.astype(jnp.int32), axis=1) - 1
    membership = (member_id[:, None] == slot_index[None, :]).astype(jnp.float32)
    leading = (member_id < 0).astype(jnp.float32)
    starts = jnp.any(slot_used[None, :] & (start_pos[None, :] == position[:, None]), axis=1)
    running = jnp.cumsum(jnp.log(1.0 - smoothing))
    lower = slot_index[None, :] <= slot_index[:, None]
    decay_table = jnp.where(
        lower, jnp.exp(jnp.where(lower, running[:, None] - running[None, :], 0.0)), 0.0
    )
    weighted_states = smoothing[:, None] * segment_states[0].astype(jnp.float32)
    local_state = jnp.dot(decay_table, weighted_states, precision=exact)
    keep_all = jnp.exp(running)
    boundary_prob = jnp.where(later_rows, 0.5 * (1.0 - cosine), 1.0)
    confidence = jnp.where(starts, boundary_prob, 1.0 - boundary_prob)
    weighted_grad = confidence[:, None] * grad_rows
    slot_grad = lax.dot_general(membership, weighted_grad, contract_first, precision=exact)
    lead_grad = jnp.dot(leading[None, :], weighted_grad, precision=exact)
    back_vector = lead_grad + jnp.dot(keep_all[None, :], slot_grad, precision=exact)
    last_log = running[slot_count - 1 :]
    last_state = local_state[slot_count - 1 :]
    summaries = (
        lax.all_gather(last_log, "seq", axis=0, tiled=True),
        lax.all_gather(last_state, "seq", axis=0, tiled=True),
        lax.all_gather(last_log, "seq", axis=0, tiled=True),
        lax.all_gather(back_vector, "seq", axis=0, tiled=True),
    )
    state_in = carry_from(summaries[0], summaries[1], shard_index, True)
    grad_in = carry_from(summaries[2], summaries[3], shard_index, False)
    smoothed = local_state + keep_all[:, None] * state_in
    picked = jnp.dot(membership, smoothed, precision=exact) + leading[:, None] * state_in
    conf_grad = jnp.sum(grad_rows * picked, axis=1)
    cos_grad = jnp.where(later_rows, jnp.where(starts, -0.5 * conf_grad, 0.5 * conf_grad), 0.0)
    reach_end = jnp.exp(running[slot_count - 1] - running)
    state_grad = (
        lax.dot_general(decay_table, slot_grad, contract_first, precision=exact)
        + reach_end[:, None] * grad_in
    )
    segment_grad = (smoothing[:, None] * state_grad).astype(jnp.bfloat16)
    unit_q_grad = cos_grad[:, None] * key_prior
    prior_grad = cos_grad[:, None] * query_unit
    query_grad = normalize_grad(queries, query_scale, unit_q_grad).astype(jnp.bfloat16)
    from_next = shifted(prior_grad[:1], "seq", -1)
    unit_k_grad = jnp.concatenate([prior_grad[1:], from_next], axis=0)
    key_grad = normalize_grad(key_rows, key_scale, unit_k_grad).astype(jnp.bfloat16)
    x_grad = lax.dot_general(
        query_grad, full_query, contract_last, preferred_element_type=jnp.float32
    )
    x_grad = x_grad + lax.dot_general(
        key_grad, full_key, contract_last, preferred_element_type=jnp.float32
    )
    return (x_grad.astype(jnp.bfloat16)[None], segment_grad[None])


def solution(mesh):
    placed = (
        P("dp", "seq", None),
        P("dp", "seq", None),
        P("dp", "seq", None),
        P("dp", "seq"),
        P("dp", "seq"),
        P("dp", "seq"),
        P("dp", None),
        P("dp", None),
    )
    return jax.shard_map(
        per_device,
        mesh=mesh,
        in_specs=placed,
        out_specs=(P("dp", "seq", None), P("dp", "seq", None)),
        check_vma=False,
    )
```

profile of v0, /device:TPU:0, one launch (start us, length us, event | category | flops | bytes accessed | tf_op | source)
XLA Modules:
  0.0 151.8 jit_solution(7152754689850499982)
XLA Ops:
  7.2 0.0 copy-start
  7.2 0.0 copy-start.7
  7.2 0.0 copy-start.6
  7.2 0.0 copy-start.4
  7.2 0.0 copy-start.5
  7.2 0.0 copy-start.1
  7.2 0.0 all-gather.7.cloned.1.call-start
  7.3 0.7 all-gather.7.cloned.1.call-update
  8.0 0.0 all-gather.9.cloned.1.call-start
  8.0 0.7 all-gather.9.cloned.1.call-update
  9.4 0.0 copy-done.6
  9.4 0.1 copy.13
  9.5 0.2 broadcast_in_dim.32
  9.7 0.6 slice.29
  10.2 0.0 copy-done.7
  10.3 0.6 dynamic-slice.2
  10.8 1.3 bitcast_dynamic-update-slice_fusion
  12.1 23.1 %all-reduce = f32[8]{0:T(128)S(1)} all-reduce(f32[8]{0:T(128)S(1)} %bitcast_dynamic-update-slice_fusion), channel_id=2, replica_groups=mesh['seq'=8,'dp'=4] {'seq'}, use_global_device_ids=true, to_apply=%add | all-reduce | flops 8 | bytes 64
  35.2 0.1 reduce
  35.3 0.2 reduce-window.6
  35.5 0.6 constant_dynamic-slice_fusion
  36.1 0.0 copy-done.4
  36.1 0.9 fusion.24
  37.0 30.7 %all-gather.2 = f32[8,1,1536]{2,1,0:T(1,128)S(1)} all-gather(f32[1,1,1536]{2,1,0:T(1,128)S(1)} %slice_bitcast_fusion), channel_id=1, replica_groups=mesh['seq'=8,'dp'=4] {'seq'}, dimensions={0}, use_global_device_ids=true | all-gather | bytes 55296 | tf_op jit(solution)/shard_map/all_gather | solution.py:98
  67.7 0.8 convolution_reduce_fusion.2
  68.6 0.0 copy-done.5
  68.6 0.1 fusion.32
  68.7 0.2 convert_reduce_fusion
  68.9 0.6 subtract_exponential_fusion
  69.5 0.0 copy-done.1
  69.6 1.5 fusion.8
  71.0 0.0 all-gather.7.cloned.1.call-done
  71.1 0.0 copy-done
  71.1 4.2 %multiply_reduce_fusion.4 = (f32[320]{0:T(512)S(1)}, f32[320,1536]{1,0:T(8,128)S(1)}) fusion(bf16[1536,1536]{1,0:T(8,128)(2,1)} %all-gather.7.cloned.1.call-done, bf16[1,320,1536]{2,1,0:T(8,128)(2,1)S(1)} %copy-done), kind=kOutput, calls=%fused_computation.20 | convolution fusion | flops 1510932224 | bytes 7668992 | tf_op jit(solution)/shard_map/dot_general | solution.py:60
  75.2 0.3 multiply_multiply_fusion
  75.5 1.3 collective-permute-start.1
  76.8 1.4 slice.33
  78.3 10.6 %all-gather.9.cloned.1.call-done = bf16[1536,1536]{1,0:T(8,128)(2,1)} async-done(((bf16[384,1536]{1,0:T(8,128)(2,1)}), bf16[1536,1536]{1,0:T(8,128)(2,1)}) %all-gather.9.cloned.1.call-update) | async-done | bytes 4718608 | tf_op jit(solution)/shard_map/all_gather | solution.py:57
  88.9 0.0 collective-permute-done.1
  88.9 4.8 %multiply_reduce_fusion.1 = (f32[320]{0:T(512)S(1)}, f32[320]{0:T(512)S(1)}, f32[320,1536]{1,0:T(8,128)S(1)}) fusion(f32[1,1536]{1,0:T(1,128)S(1)} %collective-permute-done.1, f32[319,1536]{1,0:T(8,128)} %slice.33, bf16[1536,1536]{1,0:T(8,128)(2,1)} %all-gather.9.cloned.1.call-done, bf16[1,320,1536]{2,1,0:T(8,128)(2,1)S(1)} %copy-done), kind=kOutput, calls=%fused_computation.16 | convolution fusion | flops 1512406528 | bytes 9636352 | tf_op jit(solution)/shard_map/dot_general | solution.py:59
  93.7 0.2 broadcast_multiply_fusion
  93.9 3.4 %collective-permute-start = (f32[1,1536]{1,0:T(1,128)S(1)}, f32[1,1536]{1,0:T(1,128)S(1)}, u32[]{:S(2)}, u32[]{:S(2)}) collective-permute-start(f32[1,1536]{1,0:T(1,128)S(1)} %slice.31), channel_id=1, source_target_pairs={{0,4},{4,8},{8,12},{12,16},{16,20},{20,24},{24,28},{1,5},{5,9},{9,... | collective-permute-start | bytes 18440 | tf_op jit(solution)/shard_map/ppermute | solution.py:16
  97.3 0.6 constant_dynamic-slice_fusion.1
  97.9 0.7 collective-permute-done
  98.7 0.0 copy-start.2
  98.7 0.8 multiply_reduce_fusion
  99.5 0.4 copy-done.2
  99.9 1.2 fusion.7
  101.1 0.9 fusion.9
  102.0 0.5 convolution_reduce_fusion
  102.6 32.6 %all-gather.3 = f32[8,1,1536]{2,1,0:T(1,128)S(1)} all-gather(f32[1,1,1536]{2,1,0:T(1,128)S(1)} %reshape.174), channel_id=3, replica_groups=mesh['seq'=8,'dp'=4] {'seq'}, dimensions={0}, use_global_device_ids=true | all-gather | bytes 55296 | tf_op jit(solution)/shard_map/all_gather | solution.py:100
  135.2 0.8 convolution_reduce_fusion.1
  136.0 0.0 slice-start
  136.0 1.7 %fusion.5 = bf16[1,128,1536]{2,1,0:T(8,128)(2,1)} fusion(f32[128,1536]{1,0:T(8,128)S(1)} %fusion.7, f32[1536]{0:T(1024)S(1)} %convolution_reduce_fusion.1, f32[128]{0:T(128)S(1)} %get-tuple-element.10, f32[128]{0:T(128)S(1)} %bitcast_select_fusion, f32[128]{0:T(128)S(1)} %reduce), kind=kOutput, calls=%fused_computation.9 | convolution fusion | flops 302841856 | bytes 1187328 | tf_op jit(solution)/shard_map/dot_general | solution.py:110
  137.7 0.0 copy-start.3
  137.7 0.0 slice-start.1
  137.7 4.3 %fusion.10 = f32[320,1536]{1,0:T(8,128)S(1)} fusion(bf16[1536,1536]{1,0:T(8,128)(2,1)} %all-gather.7.cloned.1.call-done, f32[320,1536]{1,0:T(8,128)S(1)} %get-tuple-element.13, f32[319,1536]{1,0:T(8,128)S(1)} %bitcast.85, f32[1,1536]{1,0:T(1,128)S(1)} %collective-permute-done, f32[320]{0:T(512)S(1)} %get-tuple-element.16, f32[320]{0:T(512)S(1)} %select_select_fusion, ...), kind=kOutput, calls=%fused_computation.27 | convolution fusion | flops 1512898560 | bytes 10620672 | tf_op jit(solution)/shard_map/dot_general | solution.py:120
  142.1 0.0 slice-done
  142.1 0.0 copy-done.3
  142.1 0.0 slice-done.1
  142.1 2.9 %fusion.2 = bf16[1,320,1536]{2,1,0:T(8,128)(2,1)} fusion(f32[320,1536]{1,0:T(8,128)S(1)} %fusion.10, bf16[1536,1536]{1,0:T(8,128)(2,1)S(1)} %bitcast.89, f32[320,1536]{1,0:T(8,128)S(1)} %get-tuple-element.14, f32[1,1536]{1,0:T(1,128)S(1)} %collective-permute-done.1, f32[319,1536]{1,0:T(8,128)S(1)} %copy-done.3, f32[320]{0:T(512)S(1)} %get-tuple-element.8, ...), kind=kOutput, calls=%fused_computation.4 | convolution fusion | flops 1513390080 | bytes 11602432 | tf_op jit(solution)/shard_map/dot_general | solution.py:123
  (18 shorter events, 0.1 us)
Async XLA Ops:
  7.2 63.9 %copy-start = (bf16[1,320,1536]{2,1,0:T(8,128)(2,1)S(1)}, bf16[1,320,1536]{2,1,0:T(8,128)(2,1)}, u32[]{:S(2)}) copy-start(bf16[1,320,1536]{2,1,0:T(8,128)(2,1)} %param.8) | copy-start | bytes 2949124
  7.2 3.1 %copy-start.7 = (u32[32]{0:T(128)S(1)}, u32[32]{0:T(128)}, u32[]{:S(2)}) copy-start(u32[32]{0:T(128)} %constant.53) | copy-start | bytes 388
  7.2 2.2 %copy-start.6 = (s32[1,128]{1,0:T(1,128)S(1)}, s32[1,128]{1,0:T(1,128)}, u32[]{:S(2)}) copy-start(s32[1,128]{1,0:T(1,128)} %param.13) | copy-start | bytes 1540
  7.2 28.9 %copy-start.4 = (bf16[1,128,1536]{2,1,0:T(8,128)(2,1)S(1)}, bf16[1,128,1536]{2,1,0:T(8,128)(2,1)}, u32[]{:S(2)}) copy-start(bf16[1,128,1536]{2,1,0:T(8,128)(2,1)} %param.10) | copy-start | bytes 1179652
  7.2 61.4 %copy-start.5 = (s32[1,128]{1,0:T(1,128)S(1)}, s32[1,128]{1,0:T(1,128)}, u32[]{:S(2)}) copy-start(s32[1,128]{1,0:T(1,128)} %param.11) | copy-start | bytes 1540
  7.2 62.3 %copy-start.1 = (bf16[1,320,1536]{2,1,0:T(8,128)(2,1)S(1)}, bf16[1,320,1536]{2,1,0:T(8,128)(2,1)}, u32[]{:S(2)}) copy-start(bf16[1,320,1536]{2,1,0:T(8,128)(2,1)} %param.9) | copy-start | bytes 2949124
  7.2 63.8 %all-gather.7.cloned.1.call-start = ((), (), s32[]{:S(2)}) async-start(), calls=%async_computation | async-start | bytes 5898240 | tf_op jit(solution)/shard_map/all_gather | solution.py:56
  8.0 80.9 %all-gather.9.cloned.1.call-start = ((), (), s32[]{:S(2)}) async-start(), calls=%async_computation.1 | async-start | bytes 5898240 | tf_op jit(solution)/shard_map/all_gather | solution.py:57
  75.5 13.4 %collective-permute-start.1 = (f32[1,1536]{1,0:T(1,128)S(1)}, f32[1,1536]{1,0:T(1,128)S(1)}, u32[]{:S(2)}, u32[]{:S(2)}) collective-permute-start(f32[1,1536]{1,0:T(1,128)S(1)} %slice.34), channel_id=1, source_target_pairs={{4,0},{8,4},{12,8},{16,12},{20,16},{24,20},{28,24},{5,1},{9,5},{13... | collective-permute-start | bytes 18440 | tf_op jit(solution)/shard_map/ppermute | solution.py:16
  93.9 4.7 %collective-permute-start = (f32[1,1536]{1,0:T(1,128)S(1)}, f32[1,1536]{1,0:T(1,128)S(1)}, u32[]{:S(2)}, u32[]{:S(2)}) collective-permute-start(f32[1,1536]{1,0:T(1,128)S(1)} %slice.31), channel_id=1, source_target_pairs={{0,4},{4,8},{8,12},{12,16},{16,20},{20,24},{24,28},{1,5},{5,9},{9,... | collective-permute-start | bytes 18440 | tf_op jit(solution)/shard_map/ppermute | solution.py:16
  98.7 1.2 copy-start.2
  136.0 6.0 %slice-start = ((s8[4718592]{0:T(1024)(128)(4,1)}), s8[4194304]{0:T(1024)(128)(4,1)S(1)}, s32[]{:S(2)}) async-start(s8[4718592]{0:T(1024)(128)(4,1)} %bitcast.88), calls=%async_computation.2 | async-start | bytes 8388608
  137.7 4.4 %copy-start.3 = (f32[319,1536]{1,0:T(8,128)S(1)}, f32[319,1536]{1,0:T(8,128)}, u32[]{:S(2)}) copy-start(f32[319,1536]{1,0:T(8,128)} %slice.33) | copy-start | bytes 5879812
  137.7 4.4 %slice-start.1 = ((s8[4718592]{0:T(1024)(128)(4,1)}), s8[524288]{0:T(1024)(128)(4,1)S(1)}, s32[]{:S(2)}) async-start(s8[4718592]{0:T(1024)(128)(4,1)} %bitcast.88), calls=%async_computation.3 | async-start | bytes 1048576
Sparse Core Ops, SparseCore 0:
  9.6 40.1 all-gather.6
  51.4 37.4 all-gather.8
where the time goes:
time: 152 us
  blocking collectives  86.4 us (57%)
  matrix products  24.5 us (16%)
  between operations  15 us (10%)
  waiting for transfers between devices  12.7 us (8%)
  local copies, waits for them, and re-layouts  5.63 us (4%)
  starting transfers between devices  4.76 us (3%)
  other arithmetic  2.75 us (2%)
    all_gather x1, blocking collectives, per_device(): lax.all_gather(back_vector, 'seq', axis=0, tiled=True)  32.6 us
    all_gather x1, blocking collectives, per_device(): lax.all_gather(last_state, 'seq', axis=0, tiled=True)  30.7 us
    unnamed x1, blocking collectives  23.1 us
    all_gather x1, waiting for transfers between devices, per_device(): lax.all_gather(key_weight, 'dp', axis=0, tiled=True)  10.6 us
    dot_general x1, matrix products, per_device(): key_rows = jnp.dot(token_rows, full_key, preferred_element_type=jnp.float32)  4.83 us
    ppermute x2, starting transfers between devices, shifted(): return lax.ppermute(block, axis, route)  4.68 us
    dot_general x1, matrix products, per_device(): lax.dot_general(query_grad, full_query, contract_last, preferred_element_...  4.34 us
    dot_general x1, matrix products, per_device(): jnp.dot(token_rows, full_query, preferred_element_type=jnp.float32)  4.17 us
  transfers between devices with their start and end apart: 4, of which 2 were waited for; matrix products, arithmetic and copies ran while one was open for 9% of the time, Pallas kernels for 0%

commit v1 on v0

--- a/solution.py
+++ b/solution.py
@@ -21,20 +21,23 @@
     return scales * unit_grad - scales * scales * scales * inner_prod * vectors
 
 
-def carry_from(log_keep, vectors, shard_index, from_lower):
-    running_log = jnp.cumsum(log_keep)
-    before = running_log - log_keep
-    shard_order = jnp.arange(log_keep.shape[0])
-    if from_lower:
-        own_value = lax.dynamic_index_in_dim(before, shard_index, keepdims=False)
-        selected = shard_order < shard_index
-        log_gap = own_value - running_log
-    else:
-        own_value = lax.dynamic_index_in_dim(running_log, shard_index, keepdims=False)
-        selected = shard_order > shard_index
-        log_gap = before - own_value
-    factor = jnp.where(selected, jnp.exp(jnp.where(selected, log_gap, 0.0)), 0.0)
-    return jnp.dot(factor[None, :], vectors, precision=exact)
+def seq_scan(log_keep, vectors, axis, from_lower):
+    size = lax.axis_size(axis)
+    step = 1
+    incl_log, incl_vec = log_keep, vectors
+    excl_log = jnp.zeros_like(log_keep)
+    excl_vec = jnp.zeros_like(vectors)
+    while step < size:
+        packed = jnp.concatenate([incl_log, incl_vec], axis=-1)
+        got = shifted(packed, axis, step if from_lower else -step)
+        got_log, got_vec = got[:, :1], got[:, 1:]
+        excl_vec = jnp.exp(excl_log) * got_vec + excl_vec
+        excl_log = excl_log + got_log
+        if 2 * step < size:
+            incl_vec = jnp.exp(incl_log) * got_vec + incl_vec
+            incl_log = incl_log + got_log
+        step *= 2
+    return excl_vec
 
 
 def per_device(
@@ -93,14 +96,8 @@
     back_vector = lead_grad + jnp.dot(keep_all[None, :], slot_grad, precision=exact)
     last_log = running[slot_count - 1 :]
     last_state = local_state[slot_count - 1 :]
-    summaries = (
-        lax.all_gather(last_log, "seq", axis=0, tiled=True),
-        lax.all_gather(last_state, "seq", axis=0, tiled=True),
-        lax.all_gather(last_log, "seq", axis=0, tiled=True),
-        lax.all_gather(back_vector, "seq", axis=0, tiled=True),
-    )
-    state_in = carry_from(summaries[0], summaries[1], shard_index, True)
-    grad_in = carry_from(summaries[2], summaries[3], shard_index, False)
+    state_in = seq_scan(last_log[None], last_state, "seq", True)
+    grad_in = seq_scan(last_log[None], back_vector, "seq", False)
     smoothed = local_state + keep_all[:, None] * state_in
     picked = jnp.dot(membership, smoothed, precision=exact) + leading[:, None] * state_in
     conf_grad = jnp.sum(grad_rows * picked, axis=1)

time: 152 us -> 136 us (0.89)
  blocking collectives: 86.4 us -> 0 us
  waiting for transfers between devices: 12.7 us -> 54.8 us
  starting transfers between devices: 4.76 us -> 23.8 us
  between operations: 15 us -> 23.7 us
  other arithmetic: 2.75 us -> 5.16 us
  matrix products: 24.5 us -> 22.7 us
    all_gather x2 -> x0, blocking collectives: 63.3 us -> none  [the longest x1 32.6 us: per_device(): lax.all_gather(back_vector, 'seq', axis=0, tiled=True)]
    unnamed x1 -> x0, blocking collectives: 23.1 us -> none
    all_gather x1, waiting for transfers between devices: 10.6 us -> 31.9 us  [per_device(): lax.all_gather(key_weight, 'dp', axis=0, tiled=True)]
    ppermute x2 -> x8, starting transfers between devices: 4.68 us -> 23.7 us  [shifted(): return lax.ppermute(block, axis, route)]
    all_gather x1, waiting for transfers between devices: 0.02 us -> 12.8 us  [per_device(): lax.all_gather(query_weight, 'dp', axis=0, tiled=True)]
    ppermute x2 -> x8, waiting for transfers between devices: 0.74 us -> 8.73 us  [shifted(): return lax.ppermute(block, axis, route)]
    slice x0 -> x5, local copies, waits for them, and re-layouts: none -> 2.22 us  [the longest x4 2.21 us: seq_scan(): got_log, got_vec = (got[:, :1], got[:, 1:])]
    concatenate x0 -> x6, other arithmetic: none -> 2.03 us  [seq_scan(): packed = jnp.concatenate([incl_log, incl_vec], axis=-1)]
  transfers between devices with their start and end apart: 4 -> 10, of which waited for: 2 -> 8; matrix products, arithmetic and copies ran while one was open for 9% -> 14% of each run, Pallas kernels for 0% -> 0%
where the time goes in v1:
time: 136 us; the launch traced here: 135 us
  waiting for transfers between devices  54.8 us (40%)
  starting transfers between devices  23.8 us (18%)
  between operations  23.7 us (17%)
  matrix products  22.7 us (17%)
  other arithmetic  5.16 us (4%)
  local copies, waits for them, and re-layouts  4.73 us (3%)
    all_gather x1, waiting for transfers between devices, per_device(): lax.all_gather(key_weight, 'dp', axis=0, tiled=True)  31.9 us
    ppermute x8, starting transfers between devices, shifted(): return lax.ppermute(block, axis, route)  23.7 us
    all_gather x1, waiting for transfers between devices, per_device(): lax.all_gather(query_weight, 'dp', axis=0, tiled=True)  12.8 us
    ppermute x8, waiting for transfers between devices, shifted(): return lax.ppermute(block, axis, route)  8.73 us
    dot_general x1, matrix products, per_device(): key_rows = jnp.dot(token_rows, full_key, preferred_element_type=jnp.float32)  4.83 us
    dot_general x1, matrix products, per_device(): lax.dot_general(query_grad, full_query, contract_last, preferred_element_...  4.34 us
    dot_general x1, matrix products, per_device(): jnp.dot(token_rows, full_query, preferred_element_type=jnp.float32)  4.12 us
    dot_general x1, matrix products, per_device(): lax.dot_general(key_grad, full_key, contract_last, preferred_element_type...  2.73 us
  transfers between devices with their start and end apart: 10, of which 8 were waited for; matrix products, arithmetic and copies ran while one was open for 14% of the time, Pallas kernels for 0%

profile of v1, /device:TPU:0, one launch (start us, length us, event | category | flops | bytes accessed | tf_op | source)
XLA Modules:
  0.0 134.9 jit_solution(11223383162558335644)
XLA Ops:
  7.2 0.0 copy-start
  7.2 0.0 copy-start.1
  7.2 0.0 all-gather.3.cloned.1.call-start
  7.3 0.7 all-gather.3.cloned.1.call-update
  8.0 0.0 all-gather.5.cloned.1.call-start
  8.0 0.7 all-gather.5.cloned.1.call-update
  9.4 0.1 copy.12
  9.5 0.2 broadcast_in_dim.25
  9.7 0.5 slice.66
  10.2 0.1 reduce
  10.3 0.9 fusion.24
  11.2 0.7 pad_maximum_fusion.2
  11.9 4.8 %collective-permute-start = (f32[1,1537]{1,0:T(1,128)S(1)}, f32[1,1537]{1,0:T(1,128)S(1)}, u32[]{:S(2)}, u32[]{:S(2)}) collective-permute-start(f32[1,1537]{1,0:T(1,128)S(1)} %pad_maximum_fusion.2), channel_id=1, source_target_pairs={{0,4},{4,8},{8,12},{12,16},{16,20},{20,24},{24,28},{1,5},{5,9},{9,... | collective-permute-start | bytes 18452 | tf_op jit(solution)/shard_map/ppermute | solution.py:16
  16.8 0.1 convert_reduce_fusion
  17.7 0.5 collective-permute-done
  18.1 0.6 slice.68
  20.0 0.1 multiply_add_fusion.3
  20.1 0.1 pad_maximum_fusion.3
  20.1 5.2 %collective-permute-start.1 = (f32[1,1537]{1,0:T(1,128)S(1)}, f32[1,1537]{1,0:T(1,128)S(1)}, u32[]{:S(2)}, u32[]{:S(2)}) collective-permute-start(f32[1,1537]{1,0:T(1,128)S(1)} %pad_maximum_fusion.3), channel_id=1, source_target_pairs={{0,8},{4,12},{8,16},{12,20},{16,24},{20,28},{1,9},{5,13},{9,17},{1... | collective-permute-start | bytes 18452 | tf_op jit(solution)/shard_map/ppermute | solution.py:16
  25.3 0.7 subtract_exponential_fusion
  26.0 0.6 collective-permute-done.1
  26.6 0.6 slice.70
  27.9 0.1 multiply_add_fusion.2
  28.0 0.1 pad_maximum_fusion.4
  28.1 5.2 %collective-permute-start.2 = (f32[1,1537]{1,0:T(1,128)S(1)}, f32[1,1537]{1,0:T(1,128)S(1)}, u32[]{:S(2)}, u32[]{:S(2)}) collective-permute-start(f32[1,1537]{1,0:T(1,128)S(1)} %pad_maximum_fusion.4), channel_id=1, source_target_pairs={{0,16},{4,20},{8,24},{12,28},{1,17},{5,21},{9,25},{13,29},{2,18},{... | collective-permute-start | bytes 18452 | tf_op jit(solution)/shard_map/ppermute | solution.py:16
  33.3 0.1 fusion.32
  35.4 0.0 collective-permute-done.2
  35.5 0.1 fusion.44
  35.6 1.4 %fusion.8 = f32[320]{0:T(512)S(1)} fusion(bf16[1,320,1536]{2,1,0:T(8,128)(2,1)S(1)} %copy-done.1, f32[1536]{0:T(1024)S(1)} %fusion.44, f32[320]{0:T(512)S(1)} %get-tuple-element.6, f32[128,1536]{1,0:T(8,128)S(1)} %fusion.24, f32[128]{0:T(128)S(1)} %get-tuple-element.11, s32[320]{0:T(512)S(1)} %broadcast_add_fusion), kind=kOutput, calls=%fused_computation.22 | convolution fusion | flops 757866176 | bytes 1779968 | tf_op jit(solution)/shard_map/dot_general | solution.py:102
  37.0 12.8 %all-gather.3.cloned.1.call-done = bf16[1536,1536]{1,0:T(8,128)(2,1)} async-done(((bf16[384,1536]{1,0:T(8,128)(2,1)}), bf16[1536,1536]{1,0:T(8,128)(2,1)}) %all-gather.3.cloned.1.call-update) | async-done | bytes 4718608 | tf_op jit(solution)/shard_map/all_gather | solution.py:59
  49.8 4.1 %multiply_reduce_fusion.4 = (f32[320]{0:T(512)S(1)}, f32[320,1536]{1,0:T(8,128)S(1)}) fusion(bf16[1536,1536]{1,0:T(8,128)(2,1)} %all-gather.3.cloned.1.call-done, bf16[1,320,1536]{2,1,0:T(8,128)(2,1)S(1)} %copy-done), kind=kOutput, calls=%fused_computation.20 | convolution fusion | flops 1510932224 | bytes 7668992 | tf_op jit(solution)/shard_map/dot_general | solution.py:63
  54.0 0.3 multiply_multiply_fusion
  54.3 1.3 collective-permute-start.4
  55.6 1.4 %slice.75 = f32[319,1536]{1,0:T(8,128)} slice(f32[320,1536]{1,0:T(8,128)S(1)} %multiply_multiply_fusion), slice={[1:320], [0:1536]} | slice | bytes 3919872 | tf_op jit(solution)/shard_map/slice | solution.py:115
  57.0 31.9 %all-gather.5.cloned.1.call-done = bf16[1536,1536]{1,0:T(8,128)(2,1)} async-done(((bf16[384,1536]{1,0:T(8,128)(2,1)}), bf16[1536,1536]{1,0:T(8,128)(2,1)}) %all-gather.5.cloned.1.call-update) | async-done | bytes 4718608 | tf_op jit(solution)/shard_map/all_gather | solution.py:60
  88.9 0.0 collective-permute-done.4
  88.9 4.8 %multiply_reduce_fusion.1 = (f32[320]{0:T(512)S(1)}, f32[320]{0:T(512)S(1)}, f32[320,1536]{1,0:T(8,128)S(1)}) fusion(f32[1,1536]{1,0:T(1,128)S(1)} %collective-permute-done.4, f32[319,1536]{1,0:T(8,128)} %slice.75, bf16[1536,1536]{1,0:T(8,128)(2,1)} %all-gather.5.cloned.1.call-done, bf16[1,320,1536]{2,1,0:T(8,128)(2,1)S(1)} %copy-done), kind=kOutput, calls=%fused_computation.16 | convolution fusion | flops 1512406528 | bytes 9636352 | tf_op jit(solution)/shard_map/dot_general | solution.py:62
  93.7 0.2 broadcast_multiply_fusion
  94.0 3.4 %collective-permute-start.3 = (f32[1,1536]{1,0:T(1,128)S(1)}, f32[1,1536]{1,0:T(1,128)S(1)}, u32[]{:S(2)}, u32[]{:S(2)}) collective-permute-start(f32[1,1536]{1,0:T(1,128)S(1)} %slice.73), channel_id=1, source_target_pairs={{0,4},{4,8},{8,12},{12,16},{16,20},{20,24},{24,28},{1,5},{5,9},{9,... | collective-permute-start | bytes 18440 | tf_op jit(solution)/shard_map/ppermute | solution.py:16
  97.4 1.3 collective-permute-done.3
  98.7 0.8 multiply_reduce_fusion
  99.5 0.4 copy-done.2
  99.9 1.2 fusion.7
  101.1 0.9 fusion.9
  102.0 0.0 slice-start
  102.0 0.5 convolution_reduce_fusion
  102.6 1.0 pad_maximum_fusion.5
  103.6 1.3 collective-permute-start.5
  104.9 4.5 %collective-permute-done.5 = f32[1,1537]{1,0:T(1,128)S(1)} collective-permute-done((f32[1,1537]{1,0:T(1,128)S(1)}, f32[1,1537]{1,0:T(1,128)S(1)}, u32[]{:S(2)}, u32[]{:S(2)}) %collective-permute-start.5) | collective-permute-done | bytes 6180 | tf_op jit(solution)/shard_map/ppermute | solution.py:16
  109.4 0.6 slice.77
  111.3 0.1 multiply_add_fusion.1
  111.4 0.1 pad_maximum_fusion.6
  111.4 1.3 collective-permute-start.6
  112.8 0.0 slice-start.1
  112.8 4.3 %fusion.10 = f32[320,1536]{1,0:T(8,128)S(1)} fusion(bf16[1536,1536]{1,0:T(8,128)(2,1)} %all-gather.3.cloned.1.call-done, f32[320,1536]{1,0:T(8,128)S(1)} %get-tuple-element.13, f32[319,1536]{1,0:T(8,128)S(1)} %bitcast.61, f32[1,1536]{1,0:T(1,128)S(1)} %collective-permute-done.3, f32[320]{0:T(512)S(1)} %get-tuple-element.16, f32[320]{0:T(512)S(1)} %select_select_fusion, ...), kind=kOutput, calls=%fused_computation.25 | convolution fusion | flops 1512898560 | bytes 10620672 | tf_op jit(solution)/shard_map/dot_general | solution.py:117
  117.2 0.7 collective-permute-done.6
  117.9 0.5 slice.79
  118.9 0.1 multiply_add_fusion
  119.0 0.1 pad_maximum_fusion.7
  119.1 1.3 collective-permute-start.7
  120.4 2.7 %fusion.2 = bf16[1,320,1536]{2,1,0:T(8,128)(2,1)} fusion(f32[320,1536]{1,0:T(8,128)S(1)} %fusion.10, bf16[1536,1536]{1,0:T(8,128)(2,1)S(1)} %bitcast.65, f32[320,1536]{1,0:T(8,128)S(1)} %get-tuple-element.14, f32[1,1536]{1,0:T(1,128)S(1)} %collective-permute-done.4, f32[319,1536]{1,0:T(8,128)S(1)} %copy-done.3, f32[320]{0:T(512)S(1)} %get-tuple-element.8, ...), kind=kOutput, calls=%fused_computation.4 | convolution fusion | flops 1513390080 | bytes 11602432 | tf_op jit(solution)/shard_map/dot_general | solution.py:120
  125.2 1.1 collective-permute-done.7
  126.3 0.1 fusion.45
  126.4 1.7 %fusion.5 = bf16[1,128,1536]{2,1,0:T(8,128)(2,1)} fusion(f32[128,1536]{1,0:T(8,128)S(1)} %fusion.7, f32[1536]{0:T(1024)S(1)} %fusion.45, f32[128]{0:T(128)S(1)} %get-tuple-element.10, f32[128]{0:T(128)S(1)} %bitcast_select_fusion, f32[128]{0:T(128)S(1)} %reduce), kind=kOutput, calls=%fused_computation.9 | convolution fusion | flops 302841856 | bytes 1187328 | tf_op jit(solution)/shard_map/dot_general | solution.py:107
  (29 shorter events, 0.1 us)
Async XLA Ops:
  7.2 42.7 %copy-start = (bf16[1,320,1536]{2,1,0:T(8,128)(2,1)S(1)}, bf16[1,320,1536]{2,1,0:T(8,128)(2,1)}, u32[]{:S(2)}) copy-start(bf16[1,320,1536]{2,1,0:T(8,128)(2,1)} %param.8) | copy-start | bytes 2949124
  7.2 2.2 %copy-start.6 = (s32[1,128]{1,0:T(1,128)S(1)}, s32[1,128]{1,0:T(1,128)}, u32[]{:S(2)}) copy-start(s32[1,128]{1,0:T(1,128)} %param.13) | copy-start | bytes 1540
  7.2 3.1 %copy-start.4 = (bf16[1,128,1536]{2,1,0:T(8,128)(2,1)S(1)}, bf16[1,128,1536]{2,1,0:T(8,128)(2,1)}, u32[]{:S(2)}) copy-start(bf16[1,128,1536]{2,1,0:T(8,128)(2,1)} %param.10) | copy-start | bytes 1179652
  7.2 9.6 %copy-start.5 = (s32[1,128]{1,0:T(1,128)S(1)}, s32[1,128]{1,0:T(1,128)}, u32[]{:S(2)}) copy-start(s32[1,128]{1,0:T(1,128)} %param.11) | copy-start | bytes 1540
  7.2 28.4 %copy-start.1 = (bf16[1,320,1536]{2,1,0:T(8,128)(2,1)S(1)}, bf16[1,320,1536]{2,1,0:T(8,128)(2,1)}, u32[]{:S(2)}) copy-start(bf16[1,320,1536]{2,1,0:T(8,128)(2,1)} %param.9) | copy-start | bytes 2949124
  7.2 42.6 %all-gather.3.cloned.1.call-start = ((), (), s32[]{:S(2)}) async-start(), calls=%async_computation | async-start | bytes 5898240 | tf_op jit(solution)/shard_map/all_gather | solution.py:59
  8.0 80.9 %all-gather.5.cloned.1.call-start = ((), (), s32[]{:S(2)}) async-start(), calls=%async_computation.1 | async-start | bytes 5898240 | tf_op jit(solution)/shard_map/all_gather | solution.py:60
  11.9 6.2 %collective-permute-start = (f32[1,1537]{1,0:T(1,128)S(1)}, f32[1,1537]{1,0:T(1,128)S(1)}, u32[]{:S(2)}, u32[]{:S(2)}) collective-permute-start(f32[1,1537]{1,0:T(1,128)S(1)} %pad_maximum_fusion.2), channel_id=1, source_target_pairs={{0,4},{4,8},{8,12},{12,16},{16,20},{20,24},{24,28},{1,5},{5,9},{9,... | collective-permute-start | bytes 18452 | tf_op jit(solution)/shard_map/ppermute | solution.py:16
  20.1 6.5 %collective-permute-start.1 = (f32[1,1537]{1,0:T(1,128)S(1)}, f32[1,1537]{1,0:T(1,128)S(1)}, u32[]{:S(2)}, u32[]{:S(2)}) collective-permute-start(f32[1,1537]{1,0:T(1,128)S(1)} %pad_maximum_fusion.3), channel_id=1, source_target_pairs={{0,8},{4,12},{8,16},{12,20},{16,24},{20,28},{1,9},{5,13},{9,17},{1... | collective-permute-start | bytes 18452 | tf_op jit(solution)/shard_map/ppermute | solution.py:16
  28.1 7.4 %collective-permute-start.2 = (f32[1,1537]{1,0:T(1,128)S(1)}, f32[1,1537]{1,0:T(1,128)S(1)}, u32[]{:S(2)}, u32[]{:S(2)}) collective-permute-start(f32[1,1537]{1,0:T(1,128)S(1)} %pad_maximum_fusion.4), channel_id=1, source_target_pairs={{0,16},{4,20},{8,24},{12,28},{1,17},{5,21},{9,25},{13,29},{2,18},{... | collective-permute-start | bytes 18452 | tf_op jit(solution)/shard_map/ppermute | solution.py:16
  54.3 34.6 %collective-permute-start.4 = (f32[1,1536]{1,0:T(1,128)S(1)}, f32[1,1536]{1,0:T(1,128)S(1)}, u32[]{:S(2)}, u32[]{:S(2)}) collective-permute-start(f32[1,1536]{1,0:T(1,128)S(1)} %slice.76), channel_id=1, source_target_pairs={{4,0},{8,4},{12,8},{16,12},{20,16},{24,20},{28,24},{5,1},{9,5},{13... | collective-permute-start | bytes 18440 | tf_op jit(solution)/shard_map/ppermute | solution.py:16
  94.0 4.7 %collective-permute-start.3 = (f32[1,1536]{1,0:T(1,128)S(1)}, f32[1,1536]{1,0:T(1,128)S(1)}, u32[]{:S(2)}, u32[]{:S(2)}) collective-permute-start(f32[1,1536]{1,0:T(1,128)S(1)} %slice.73), channel_id=1, source_target_pairs={{0,4},{4,8},{8,12},{12,16},{16,20},{20,24},{24,28},{1,5},{5,9},{9,... | collective-permute-start | bytes 18440 | tf_op jit(solution)/shard_map/ppermute | solution.py:16
  98.7 1.2 copy-start.2
  102.0 18.3 %slice-start = ((s8[4718592]{0:T(1024)(128)(4,1)}), s8[4194304]{0:T(1024)(128)(4,1)S(1)}, s32[]{:S(2)}) async-start(s8[4718592]{0:T(1024)(128)(4,1)} %bitcast.64), calls=%async_computation.2 | async-start | bytes 8388608
  103.6 5.8 %collective-permute-start.5 = (f32[1,1537]{1,0:T(1,128)S(1)}, f32[1,1537]{1,0:T(1,128)S(1)}, u32[]{:S(2)}, u32[]{:S(2)}) collective-permute-start(f32[1,1537]{1,0:T(1,128)S(1)} %pad_maximum_fusion.5), channel_id=1, source_target_pairs={{4,0},{8,4},{12,8},{16,12},{20,16},{24,20},{28,24},{5,1},{9,5},{13... | collective-permute-start | bytes 18452 | tf_op jit(solution)/shard_map/ppermute | solution.py:16
  111.4 6.4 %collective-permute-start.6 = (f32[1,1537]{1,0:T(1,128)S(1)}, f32[1,1537]{1,0:T(1,128)S(1)}, u32[]{:S(2)}, u32[]{:S(2)}) collective-permute-start(f32[1,1537]{1,0:T(1,128)S(1)} %pad_maximum_fusion.6), channel_id=1, source_target_pairs={{8,0},{12,4},{16,8},{20,12},{24,16},{28,20},{9,1},{13,5},{17,9},{2... | collective-permute-start | bytes 18452 | tf_op jit(solution)/shard_map/ppermute | solution.py:16
  112.7 7.7 %copy-start.3 = (f32[319,1536]{1,0:T(8,128)S(1)}, f32[319,1536]{1,0:T(8,128)}, u32[]{:S(2)}) copy-start(f32[319,1536]{1,0:T(8,128)} %slice.75) | copy-start | bytes 5879812
  112.8 7.7 %slice-start.1 = ((s8[4718592]{0:T(1024)(128)(4,1)}), s8[524288]{0:T(1024)(128)(4,1)S(1)}, s32[]{:S(2)}) async-start(s8[4718592]{0:T(1024)(128)(4,1)} %bitcast.64), calls=%async_computation.3 | async-start | bytes 1048576
  119.1 7.2 %collective-permute-start.7 = (f32[1,1537]{1,0:T(1,128)S(1)}, f32[1,1537]{1,0:T(1,128)S(1)}, u32[]{:S(2)}, u32[]{:S(2)}) collective-permute-start(f32[1,1537]{1,0:T(1,128)S(1)} %pad_maximum_fusion.7), channel_id=1, source_target_pairs={{16,0},{20,4},{24,8},{28,12},{17,1},{21,5},{25,9},{29,13},{18,2},{... | collective-permute-start | bytes 18452 | tf_op jit(solution)/shard_map/ppermute | solution.py:16
Sparse Core Ops, SparseCore 0:
  9.6 40.1 all-gather.2
  51.4 37.4 all-gather.4

commit v2 on v1

--- a/solution.py
+++ b/solution.py
@@ -40,6 +40,31 @@
     return excl_vec
 
 
+def gather_blocks(blocks, axis):
+    size = lax.axis_size(axis)
+    own = lax.axis_index(axis)
+    pairs = [blocks]
+    index = [own]
+    for k in range(1, size // 2):
+        route = [(i, (i + 2 * k) % size) for i in range(size)]
+        pairs.append(lax.ppermute(blocks, axis, route))
+        index.append((own - 2 * k) % size)
+    swap = [(i, i ^ 1) for i in range(size)]
+    partner = lax.ppermute(pairs, axis, swap)
+    pairs = pairs + partner
+    index = index + [i ^ 1 for i in index]
+    return pairs, index
+
+
+def split_dot(rows, blocks, index, width):
+    total = None
+    for block, at in zip(blocks, index):
+        part = lax.dynamic_slice_in_dim(rows, at * width, width, axis=1)
+        term = jnp.dot(part, block, preferred_element_type=jnp.float32)
+        total = term if total is None else total + term
+    return total
+
+
 def per_device(
     encoder_out,
     out_grad,
@@ -55,12 +80,10 @@
     token_count = token_rows.shape[0]
     slot_count = segment_states.shape[1]
     shard_index = lax.axis_index("seq")
-    full_query, full_key = (
-        lax.all_gather(query_weight, "dp", axis=0, tiled=True),
-        lax.all_gather(key_weight, "dp", axis=0, tiled=True),
-    )
-    key_rows = jnp.dot(token_rows, full_key, preferred_element_type=jnp.float32)
-    queries = jnp.dot(token_rows, full_query, preferred_element_type=jnp.float32)
+    pairs, index = gather_blocks((query_weight, key_weight), "dp")
+    width = query_weight.shape[0]
+    key_rows = split_dot(token_rows, [p[1] for p in pairs], index, width)
+    queries = split_dot(token_rows, [p[0] for p in pairs], index, width)
     query_scale = lax.rsqrt(jnp.sum(queries * queries, axis=1, keepdims=True) + norm_eps)
     key_scale = lax.rsqrt(jnp.sum(key_rows * key_rows, axis=1, keepdims=True) + norm_eps)
     query_unit = queries * query_scale
@@ -114,13 +137,15 @@
     from_next = shifted(prior_grad[:1], "seq", -1)
     unit_k_grad = jnp.concatenate([prior_grad[1:], from_next], axis=0)
     key_grad = normalize_grad(key_rows, key_scale, unit_k_grad).astype(jnp.bfloat16)
-    x_grad = lax.dot_general(
-        query_grad, full_query, contract_last, preferred_element_type=jnp.float32
-    )
-    x_grad = x_grad + lax.dot_general(
-        key_grad, full_key, contract_last, preferred_element_type=jnp.float32
-    )
-    return (x_grad.astype(jnp.bfloat16)[None], segment_grad[None])
+    parts = []
+    for (q_block, k_block) in pairs:
+        part = lax.dot_general(query_grad, q_block, contract_last, preferred_element_type=jnp.float32)
+        part = part + lax.dot_general(key_grad, k_block, contract_last, preferred_element_type=jnp.float32)
+        parts.append(part.astype(jnp.bfloat16))
+    order = jnp.zeros((len(index),), jnp.int32).at[jnp.stack(index)].set(jnp.arange(len(index), dtype=jnp.int32))
+    x_grad = jnp.stack(parts)[order]
+    x_grad = jnp.transpose(x_grad, (1, 0, 2)).reshape(token_count, -1)
+    return (x_grad[None], segment_grad[None])
 
 
 def solution(mesh):

time: 136 us -> 112 us (0.82)
  waiting for transfers between devices: 54.8 us -> 22 us
  between operations: 23.7 us -> 10.7 us
  matrix products: 22.7 us -> 33.2 us
  local copies, waits for them, and re-layouts: 4.73 us -> 10.6 us
  other arithmetic: 5.16 us -> 8.75 us
  starting transfers between devices: 23.8 us -> 25.8 us
    all_gather x2 -> x0, waiting for transfers between devices: 44.7 us -> none  [the longest x1 31.9 us: per_device(): lax.all_gather(key_weight, 'dp', axis=0, tiled=True)]
    ppermute x0 -> x6, waiting for transfers between devices: none -> 14.6 us  [the longest x2 14.6 us: gather_blocks(): pairs.append(lax.ppermute(blocks, axis, route))]
    dot_general x4 -> x16, matrix products: 16 us -> 24.1 us  [the longest x8 13.5 us: split_dot(): term = jnp.dot(part, block, preferred_element_type=jnp.float32)]
    ppermute x0 -> x6, starting transfers between devices: none -> 3.62 us  [the longest x2 3.19 us: gather_blocks(): pairs.append(lax.ppermute(blocks, axis, route))]
    transpose x0 -> x1, local copies, waits for them, and re-layouts: none -> 1.96 us  [per_device(): x_grad = jnp.transpose(x_grad, (1, 0, 2)).reshape(token_count, -1)]
    gather x0 -> x1, local copies, waits for them, and re-layouts: none -> 1.63 us  [per_device(): x_grad = jnp.stack(parts)[order]]
    unnamed x18 -> x16, local copies, waits for them, and re-layouts: 0.41 us -> 2.01 us
    ppermute x8, starting transfers between devices: 23.7 us -> 22.1 us  [shifted(): return lax.ppermute(block, axis, route)]
  transfers between devices with their start and end apart: 10 -> 14, of which waited for: 8 -> 4; matrix products, arithmetic and copies ran while one was open for 14% -> 38% of each run, Pallas kernels for 0% -> 0%
where the time goes in v2:
time: 112 us; the launch traced here: 111 us
  matrix products  33.2 us (30%)
  starting transfers between devices  25.8 us (23%)
  waiting for transfers between devices  22 us (20%)
  between operations  10.7 us (10%)
  local copies, waits for them, and re-layouts  10.6 us (9%)
  other arithmetic  8.75 us (8%)
    ppermute x8, starting transfers between devices, shifted(): return lax.ppermute(block, axis, route)  22.1 us
    ppermute x2, waiting for transfers between devices, gather_blocks(): pairs.append(lax.ppermute(blocks, axis, route))  14.6 us
    dot_general x8, matrix products, split_dot(): term = jnp.dot(part, block, preferred_element_type=jnp.float32)  13.5 us
    ppermute x8, waiting for transfers between devices, shifted(): return lax.ppermute(block, axis, route)  7.36 us
    dot_general x4, matrix products, per_device(): lax.dot_general(query_grad, q_block, contract_last, preferred_element_typ...  5.33 us
    dot_general x4, matrix products, per_device(): lax.dot_general(key_grad, k_block, contract_last, preferred_element_type=...  5.29 us
    ppermute x2, starting transfers between devices, gather_blocks(): pairs.append(lax.ppermute(blocks, axis, route))  3.19 us
    dot_general x1, matrix products, per_device(): jnp.dot(membership, smoothed, precision=exact) + leading[:, None] * state_in  2.87 us
  transfers between devices with their start and end apart: 14, of which 4 were waited for; matrix products, arithmetic and copies ran while one was open for 38% of the time, Pallas kernels for 0%

profile of v2, /device:TPU:0, one launch (start us, length us, event | category | flops | bytes accessed | tf_op | source)
XLA Modules:
  0.0 110.9 jit_solution(13292254602666094183)
XLA Ops:
  0.7 3.0 %collective-permute-start = (bf16[384,1536]{1,0:T(8,128)(2,1)}, bf16[384,1536]{1,0:T(8,128)(2,1)}, u32[]{:S(2)}, u32[]{:S(2)}) collective-permute-start(bf16[384,1536]{1,0:T(8,128)(2,1)} %param.14), channel_id=1, source_target_pairs={{0,2},{1,3},{2,0},{3,1},{4,6},{5,7},{6,4},{7,5},{8,10},{9,11},{10,... | collective-permute-start | bytes 3538952 | tf_op jit(solution)/shard_map/ppermute | solution.py:50
  3.7 0.2 collective-permute-start.6
  3.8 0.4 collective-permute-start.7
  4.9 0.7 fusion.74
  5.6 0.2 broadcast_in_dim.25
  5.8 0.6 slice.68
  6.5 0.7 bitcast_select_fusion
  7.2 1.9 %fusion.20 = f32[128,1536]{1,0:T(8,128)S(1)} fusion(bf16[1,128,1536]{2,1,0:T(8,128)(2,1)} %param.10, f32[128]{0:T(128)S(1)} %bitcast_select_fusion, f32[128]{0:T(128)S(1)} %reduce), kind=kOutput, calls=%fused_computation.49 | convolution fusion | flops 302448640 | bytes 1180672 | tf_op jit(solution)/shard_map/dot_general | solution.py:112
  9.1 0.9 copy-done.6
  10.0 0.8 pad_maximum_fusion.3
  10.7 3.6 %collective-permute-start.3 = (f32[1,1537]{1,0:T(1,128)S(1)}, f32[1,1537]{1,0:T(1,128)S(1)}, u32[]{:S(2)}, u32[]{:S(2)}) collective-permute-start(f32[1,1537]{1,0:T(1,128)S(1)} %pad_maximum_fusion.3), channel_id=1, source_target_pairs={{0,4},{4,8},{8,12},{12,16},{16,20},{20,24},{24,28},{1,5},{5,9},{9,... | collective-permute-start | bytes 18452 | tf_op jit(solution)/shard_map/ppermute | solution.py:16
  14.4 0.8 convert_reduce_fusion
  15.2 2.0 %fusion.35 = f32[320,1536]{1,0:T(8,128)} fusion(bf16[384,1536]{1,0:T(8,128)(2,1)S(1)} %copy-done.2, bf16[1,320,1536]{2,1,0:T(8,128)(2,1)S(1)} %copy-done, s32[]{:T(128)S(6)} %select_n.89), kind=kOutput, calls=%fused_computation.64 | convolution fusion | flops 377487360 | bytes 3391492 | tf_op jit(solution)/shard_map/dot_general | solution.py:63
  17.2 1.9 %fusion.33 = f32[320,1536]{1,0:T(8,128)S(1)} fusion(bf16[384,1536]{1,0:T(8,128)(2,1)} %param.15, bf16[1,320,1536]{2,1,0:T(8,128)(2,1)S(1)} %copy-done, s32[]{:T(128)S(6)} %select_n.89), kind=kOutput, calls=%fused_computation.62 | convolution fusion | flops 377487360 | bytes 3391492 | tf_op jit(solution)/shard_map/dot_general | solution.py:63
  19.1 0.7 subtract_exponential_fusion
  19.9 0.6 scatter_custom_fusion
  21.3 0.6 slice.70
  23.2 0.9 multiply_add_fusion.3
  24.1 3.5 %collective-permute-start.4 = (f32[1,1537]{1,0:T(1,128)S(1)}, f32[1,1537]{1,0:T(1,128)S(1)}, u32[]{:S(2)}, u32[]{:S(2)}) collective-permute-start(f32[1,1537]{1,0:T(1,128)S(1)} %pad_maximum_fusion.4), channel_id=1, source_target_pairs={{0,8},{4,12},{8,16},{12,20},{16,24},{20,28},{1,9},{5,13},{9,17},{1... | collective-permute-start | bytes 18452 | tf_op jit(solution)/shard_map/ppermute | solution.py:16
  27.6 0.1 fusion.46
  27.8 1.1 %collective-permute-done.4 = f32[1,1537]{1,0:T(1,128)S(1)} collective-permute-done((f32[1,1537]{1,0:T(1,128)S(1)}, f32[1,1537]{1,0:T(1,128)S(1)}, u32[]{:S(2)}, u32[]{:S(2)}) %collective-permute-start.4) | collective-permute-done | bytes 6180 | tf_op jit(solution)/shard_map/ppermute | solution.py:16
  28.9 0.5 slice.72
  30.2 5.2 %collective-permute-start.5 = (f32[1,1537]{1,0:T(1,128)S(1)}, f32[1,1537]{1,0:T(1,128)S(1)}, u32[]{:S(2)}, u32[]{:S(2)}) collective-permute-start(f32[1,1537]{1,0:T(1,128)S(1)} %pad_maximum_fusion.5), channel_id=1, source_target_pairs={{0,16},{4,20},{8,24},{12,28},{1,17},{5,21},{9,25},{13,29},{2,18},{... | collective-permute-start | bytes 18452 | tf_op jit(solution)/shard_map/ppermute | solution.py:16
  37.7 2.9 %fusion.6 = f32[320]{0:T(512)S(1)} fusion(bf16[1,320,1536]{2,1,0:T(8,128)(2,1)} %param.9, f32[1536]{0:T(1024)S(1)} %fusion.58, f32[320]{0:T(512)S(1)} %get-tuple-element.6, f32[128,1536]{1,0:T(8,128)} %copy-done.6, f32[128]{0:T(128)S(1)} %get-tuple-element.13, s32[320]{0:T(512)S(1)} %broadcast_add_fusion), kind=kOutput, calls=%fused_computation.27 | convolution fusion | flops 757866176 | bytes 1779968 | tf_op jit(solution)/shard_map/dot_general | solution.py:125
  40.6 14.6 %collective-permute-done.6 = bf16[384,1536]{1,0:T(8,128)(2,1)} collective-permute-done((bf16[384,1536]{1,0:T(8,128)(2,1)}, bf16[384,1536]{1,0:T(8,128)(2,1)}, u32[]{:S(2)}, u32[]{:S(2)}) %collective-permute-start.6) | collective-permute-done | bytes 1179680 | tf_op jit(solution)/shard_map/ppermute | solution.py:50
  55.3 2.0 %convolution_add_fusion.6 = f32[320,1536]{1,0:T(8,128)S(1)} fusion(f32[320,1536]{1,0:T(8,128)S(1)} %copy-done.1, bf16[384,1536]{1,0:T(8,128)(2,1)} %collective-permute-done, bf16[1,320,1536]{2,1,0:T(8,128)(2,1)S(1)} %copy-done, s32[]{:T(128)S(6)} %select_n.91), kind=kOutput, calls=%fused_computation.9 | convolution fusion | flops 377978880 | bytes 5357572 | tf_op jit(solution)/shard_map/dot_general | solution.py:63
  57.2 2.0 %convolution_add_fusion.3 = f32[320,1536]{1,0:T(8,128)S(1)} fusion(f32[320,1536]{1,0:T(8,128)S(1)} %fusion.33, bf16[384,1536]{1,0:T(8,128)(2,1)} %collective-permute-done.6, bf16[1,320,1536]{2,1,0:T(8,128)(2,1)S(1)} %copy-done, s32[]{:T(128)S(6)} %select_n.91), kind=kOutput, calls=%fused_computation.6 | convolution fusion | flops 377978880 | bytes 5357572 | tf_op jit(solution)/shard_map/dot_general | solution.py:63
  59.2 2.0 %convolution_add_fusion.5 = f32[320,1536]{1,0:T(8,128)S(1)} fusion(f32[320,1536]{1,0:T(8,128)S(1)} %convolution_add_fusion.6, bf16[384,1536]{1,0:T(8,128)(2,1)} %collective-permute-done.1, bf16[1,320,1536]{2,1,0:T(8,128)(2,1)S(1)} %copy-done, s32[]{:T(128)S(6)} %select_n.92), kind=kOutput, calls=%fused_computation.8 | convolution fusion | flops 377978880 | bytes 5357572 | tf_op jit(solution)/shard_map/dot_general | solution.py:63
  61.2 0.8 multiply_reduce_fusion.4
  62.0 0.3 multiply_multiply_fusion
  62.3 1.3 %collective-permute-start.10 = (f32[1,1536]{1,0:T(1,128)S(1)}, f32[1,1536]{1,0:T(1,128)S(1)}, u32[]{:S(2)}, u32[]{:S(2)}) collective-permute-start(f32[1,1536]{1,0:T(1,128)S(1)} %slice.78), channel_id=1, source_target_pairs={{4,0},{8,4},{12,8},{16,12},{20,16},{24,20},{28,24},{5,1},{9,5},{13... | collective-permute-start | bytes 18440 | tf_op jit(solution)/shard_map/ppermute | solution.py:16
  63.6 2.0 %convolution_add_fusion.2 = f32[320,1536]{1,0:T(8,128)S(1)} fusion(f32[320,1536]{1,0:T(8,128)S(1)} %convolution_add_fusion.3, bf16[384,1536]{1,0:T(8,128)(2,1)} %collective-permute-done.7, bf16[1,320,1536]{2,1,0:T(8,128)(2,1)S(1)} %copy-done, s32[]{:T(128)S(6)} %select_n.92), kind=kOutput, calls=%fused_computation.5 | convolution fusion | flops 377978880 | bytes 5357572 | tf_op jit(solution)/shard_map/dot_general | solution.py:63
  65.6 0.2 slice.77
  65.8 2.0 %collective-permute-done.10 = f32[1,1536]{1,0:T(1,128)S(1)} collective-permute-done((f32[1,1536]{1,0:T(1,128)S(1)}, f32[1,1536]{1,0:T(1,128)S(1)}, u32[]{:S(2)}, u32[]{:S(2)}) %collective-permute-start.10) | collective-permute-done | bytes 6176 | tf_op jit(solution)/shard_map/ppermute | solution.py:16
  67.8 0.9 multiply_reduce_fusion.3
  68.8 0.4 broadcast_multiply_fusion
  69.2 4.7 %collective-permute-start.9 = (f32[1,1536]{1,0:T(1,128)S(1)}, f32[1,1536]{1,0:T(1,128)S(1)}, u32[]{:S(2)}, u32[]{:S(2)}) collective-permute-start(f32[1,1536]{1,0:T(1,128)S(1)} %slice.75), channel_id=1, source_target_pairs={{0,4},{4,8},{8,12},{12,16},{16,20},{20,24},{24,28},{1,5},{5,9},{9,... | collective-permute-start | bytes 18440 | tf_op jit(solution)/shard_map/ppermute | solution.py:16
  73.9 0.7 fusion.81
  74.6 2.0 %fusion.82 = f32[320,384]{1,0:T(8,128)S(1)} fusion(bf16[320,1536]{1,0:T(8,128)(2,1)S(1)} %get-tuple-element.9, bf16[384,1536]{1,0:T(8,128)(2,1)} %collective-permute-done.6), kind=kOutput, calls=%fused_computation.146 | convolution fusion | flops 377487360 | bytes 2654208 | tf_op jit(solution)/shard_map/dot_general | solution.py:143
  76.6 2.0 %fusion.83 = f32[320,384]{1,0:T(8,128)S(1)} fusion(bf16[320,1536]{1,0:T(8,128)(2,1)S(1)} %get-tuple-element.9, bf16[384,1536]{1,0:T(8,128)(2,1)} %collective-permute-done.7), kind=kOutput, calls=%fused_computation.147 | convolution fusion | flops 377487360 | bytes 2654208 | tf_op jit(solution)/shard_map/dot_general | solution.py:143
  78.5 0.7 fusion.84
  79.2 0.9 multiply_reduce_fusion
  80.1 0.3 copy-done.5
  80.4 1.2 %fusion.5 = f32[128,1536]{1,0:T(8,128)S(1)} fusion(bf16[1,320,1536]{2,1,0:T(8,128)(2,1)S(1)} %copy-done.5, f32[320]{0:T(512)S(1)} %get-tuple-element.17, s32[320]{0:T(512)S(1)} %broadcast_add_fusion), kind=kOutput, calls=%fused_computation.16 | convolution fusion | flops 755998720 | bytes 1772032 | tf_op jit(solution)/shard_map/dot_general | solution.py:117
  81.7 0.5 convolution_reduce_fusion
  82.2 0.9 fusion.15
  83.1 0.8 pad_maximum_fusion.6
  83.9 1.3 %collective-permute-start.11 = (f32[1,1537]{1,0:T(1,128)S(1)}, f32[1,1537]{1,0:T(1,128)S(1)}, u32[]{:S(2)}, u32[]{:S(2)}) collective-permute-start(f32[1,1537]{1,0:T(1,128)S(1)} %pad_maximum_fusion.6), channel_id=1, source_target_pairs={{4,0},{8,4},{12,8},{16,12},{20,16},{24,20},{28,24},{5,1},{9,5},{13... | collective-permute-start | bytes 18452 | tf_op jit(solution)/shard_map/ppermute | solution.py:16
  85.2 0.5 subtract_convert_fusion.1
  85.7 0.8 copy-done.3
  86.5 0.7 fusion.14
  87.2 2.0 %fusion.13 = bf16[1,320,384]{2,1,0:T(8,128)(2,1)S(1)} fusion(f32[320,384]{1,0:T(8,128)S(1)} %fusion.82, bf16[320,1536]{1,0:T(8,128)(2,1)S(1)} %subtract_convert_fusion.1, bf16[384,1536]{1,0:T(8,128)(2,1)} %collective-permute-done), kind=kOutput, calls=%fused_computation.38 | convolution fusion | flops 377733120 | bytes 2899968 | tf_op jit(solution)/shard_map/dot_general | solution.py:142
  89.1 2.0 %fusion.12 = bf16[1,320,384]{2,1,0:T(8,128)(2,1)S(1)} fusion(f32[320,384]{1,0:T(8,128)S(1)} %fusion.83, bf16[320,1536]{1,0:T(8,128)(2,1)S(1)} %subtract_convert_fusion.1, bf16[384,1536]{1,0:T(8,128)(2,1)} %collective-permute-done.1), kind=kOutput, calls=%fused_computation.37 | convolution fusion | flops 377733120 | bytes 2899968 | tf_op jit(solution)/shard_map/dot_general | solution.py:142
  91.1 0.6 slice.79
  93.3 1.3 %collective-permute-start.12 = (f32[1,1537]{1,0:T(1,128)S(1)}, f32[1,1537]{1,0:T(1,128)S(1)}, u32[]{:S(2)}, u32[]{:S(2)}) collective-permute-start(f32[1,1537]{1,0:T(1,128)S(1)} %pad_maximum_fusion.7), channel_id=1, source_target_pairs={{8,0},{12,4},{16,8},{20,12},{24,16},{28,20},{9,1},{13,5},{17,9},{2... | collective-permute-start | bytes 18452 | tf_op jit(solution)/shard_map/ppermute | solution.py:16
  94.6 0.7 fusion.11
  95.3 4.2 %collective-permute-done.12 = f32[1,1537]{1,0:T(1,128)S(1)} collective-permute-done((f32[1,1537]{1,0:T(1,128)S(1)}, f32[1,1537]{1,0:T(1,128)S(1)}, u32[]{:S(2)}, u32[]{:S(2)}) %collective-permute-start.12) | collective-permute-done | bytes 6180 | tf_op jit(solution)/shard_map/ppermute | solution.py:16
  99.5 0.5 slice.81
  100.7 1.3 %collective-permute-start.13 = (f32[1,1537]{1,0:T(1,128)S(1)}, f32[1,1537]{1,0:T(1,128)S(1)}, u32[]{:S(2)}, u32[]{:S(2)}) collective-permute-start(f32[1,1537]{1,0:T(1,128)S(1)} %pad_maximum_fusion.8), channel_id=1, source_target_pairs={{16,0},{20,4},{24,8},{28,12},{17,1},{21,5},{25,9},{29,13},{18,2},{... | collective-permute-start | bytes 18452 | tf_op jit(solution)/shard_map/ppermute | solution.py:16
  102.0 0.2 pad_maximum_fusion.2
  102.2 1.6 %gather_fusion = bf16[4,320,384]{2,1,0:T(8,128)(2,1)} fusion(bf16[4,320,384]{2,1,0:T(8,128)(2,1)S(1)} %pad_maximum_fusion.2, s32[1024]{0:T(1024)S(1)} %pad_clamp_fusion), kind=kCustom, calls=%fused_computation | custom fusion | bytes 1966096 | tf_op jit(solution)/shard_map/gather | solution.py:146
  103.8 2.0 %copy.14 = bf16[320,4,384]{2,1,0:T(4,128)(2,1)S(1)} copy(bf16[320,4,384]{2,0,1:T(8,128)(2,1)} %bitcast.110) | data formatting | bytes 1966080 | tf_op jit(solution)/shard_map/transpose | solution.py:147
  105.8 1.3 %broadcast_in_dim_reshape.3 = bf16[1,320,1536]{2,1,0:T(8,128)(2,1)} reshape(bf16[320,4,384]{2,1,0:T(4,128)(2,1)S(1)} %copy.14) | data formatting | bytes 1966080 | tf_op jit(solution)/shard_map/broadcast_in_dim;reshape | solution.py:148
  109.3 1.7 %fusion.3 = bf16[1,128,1536]{2,1,0:T(8,128)(2,1)} fusion(f32[128,1536]{1,0:T(8,128)S(1)} %fusion.5, f32[1536]{0:T(1024)S(1)} %fusion.59, f32[128]{0:T(128)S(1)} %get-tuple-element.12, f32[128]{0:T(128)S(1)} %bitcast_select_fusion, f32[128]{0:T(128)S(1)} %reduce), kind=kOutput, calls=%fused_computation.14 | convolution fusion | flops 302841856 | bytes 1187328 | tf_op jit(solution)/shard_map/dot_general | solution.py:130
  (54 shorter events, 1.3 us)
Async XLA Ops:
  0.6 14.6 %copy-start = (bf16[1,320,1536]{2,1,0:T(8,128)(2,1)S(1)}, bf16[1,320,1536]{2,1,0:T(8,128)(2,1)}, u32[]{:S(2)}) copy-start(bf16[1,320,1536]{2,1,0:T(8,128)(2,1)} %param.8) | copy-start | bytes 2949124
  0.6 14.6 %copy-start.2 = (bf16[384,1536]{1,0:T(8,128)(2,1)S(1)}, bf16[384,1536]{1,0:T(8,128)(2,1)}, u32[]{:S(2)}) copy-start(bf16[384,1536]{1,0:T(8,128)(2,1)} %param.14) | copy-start | bytes 3538948
  0.7 39.9 %collective-permute-start = (bf16[384,1536]{1,0:T(8,128)(2,1)}, bf16[384,1536]{1,0:T(8,128)(2,1)}, u32[]{:S(2)}, u32[]{:S(2)}) collective-permute-start(bf16[384,1536]{1,0:T(8,128)(2,1)} %param.14), channel_id=1, source_target_pairs={{0,2},{1,3},{2,0},{3,1},{4,6},{5,7},{6,4},{7,5},{8,10},{9,11},{10,... | collective-permute-start | bytes 3538952 | tf_op jit(solution)/shard_map/ppermute | solution.py:50
  3.7 55.5 %collective-permute-start.1 = (bf16[384,1536]{1,0:T(8,128)(2,1)}, bf16[384,1536]{1,0:T(8,128)(2,1)}, u32[]{:S(2)}, u32[]{:S(2)}) collective-permute-start(bf16[384,1536]{1,0:T(8,128)(2,1)} %param.14), channel_id=1, source_target_pairs={{0,1},{1,0},{2,3},{3,2},{4,5},{5,4},{6,7},{7,6},{8,9},{9,8},{10,11... | collective-permute-start | bytes 3538952 | tf_op jit(solution)/shard_map/ppermute | solution.py:53
  3.7 51.6 %collective-permute-start.6 = (bf16[384,1536]{1,0:T(8,128)(2,1)}, bf16[384,1536]{1,0:T(8,128)(2,1)}, u32[]{:S(2)}, u32[]{:S(2)}) collective-permute-start(bf16[384,1536]{1,0:T(8,128)(2,1)} %param.15), channel_id=1, source_target_pairs={{0,2},{1,3},{2,0},{3,1},{4,6},{5,7},{6,4},{7,5},{8,10},{9,11},{10,... | collective-permute-start | bytes 3538952 | tf_op jit(solution)/shard_map/ppermute | solution.py:50
  3.8 59.8 %collective-permute-start.7 = (bf16[384,1536]{1,0:T(8,128)(2,1)}, bf16[384,1536]{1,0:T(8,128)(2,1)}, u32[]{:S(2)}, u32[]{:S(2)}) collective-permute-start(bf16[384,1536]{1,0:T(8,128)(2,1)} %param.15), channel_id=1, source_target_pairs={{0,1},{1,0},{2,3},{3,2},{4,5},{5,4},{6,7},{7,6},{8,9},{9,8},{10,11... | collective-permute-start | bytes 3538952 | tf_op jit(solution)/shard_map/ppermute | solution.py:53
  9.1 0.9 copy-start.6
  10.7 10.5 %collective-permute-start.3 = (f32[1,1537]{1,0:T(1,128)S(1)}, f32[1,1537]{1,0:T(1,128)S(1)}, u32[]{:S(2)}, u32[]{:S(2)}) collective-permute-start(f32[1,1537]{1,0:T(1,128)S(1)} %pad_maximum_fusion.3), channel_id=1, source_target_pairs={{0,4},{4,8},{8,12},{12,16},{16,20},{20,24},{24,28},{1,5},{5,9},{9,... | collective-permute-start | bytes 18452 | tf_op jit(solution)/shard_map/ppermute | solution.py:16
  17.2 10.4 %copy-start.7 = (s32[1,128]{1,0:T(1,128)S(1)}, s32[1,128]{1,0:T(1,128)}, u32[]{:S(2)}) copy-start(s32[1,128]{1,0:T(1,128)} %param.11) | copy-start | bytes 1540
  24.1 4.8 %collective-permute-start.4 = (f32[1,1537]{1,0:T(1,128)S(1)}, f32[1,1537]{1,0:T(1,128)S(1)}, u32[]{:S(2)}, u32[]{:S(2)}) collective-permute-start(f32[1,1537]{1,0:T(1,128)S(1)} %pad_maximum_fusion.4), channel_id=1, source_target_pairs={{0,8},{4,12},{8,16},{12,20},{16,24},{20,28},{1,9},{5,13},{9,17},{1... | collective-permute-start | bytes 18452 | tf_op jit(solution)/shard_map/ppermute | solution.py:16
  30.2 7.3 %collective-permute-start.5 = (f32[1,1537]{1,0:T(1,128)S(1)}, f32[1,1537]{1,0:T(1,128)S(1)}, u32[]{:S(2)}, u32[]{:S(2)}) collective-permute-start(f32[1,1537]{1,0:T(1,128)S(1)} %pad_maximum_fusion.5), channel_id=1, source_target_pairs={{0,16},{4,20},{8,24},{12,28},{1,17},{5,21},{9,25},{13,29},{2,18},{... | collective-permute-start | bytes 18452 | tf_op jit(solution)/shard_map/ppermute | solution.py:16
  35.5 19.8 %copy-start.1 = (f32[320,1536]{1,0:T(8,128)S(1)}, f32[320,1536]{1,0:T(8,128)}, u32[]{:S(2)}) copy-start(f32[320,1536]{1,0:T(8,128)} %fusion.35) | copy-start | bytes 5898244
  40.6 20.7 %collective-permute-start.2 = (bf16[384,1536]{1,0:T(8,128)(2,1)}, bf16[384,1536]{1,0:T(8,128)(2,1)S(1)}, u32[]{:S(2)}, u32[]{:S(2)}) collective-permute-start(bf16[384,1536]{1,0:T(8,128)(2,1)} %collective-permute-done), channel_id=1, source_target_pairs={{0,1},{1,0},{2,3},{3,2},{4,5},{5,4},{6,7},{7,6},{8,9},{9,8},{10,11... | collective-permute-start | bytes 3538952 | tf_op jit(solution)/shard_map/ppermute | solution.py:53
  55.3 10.5 %collective-permute-start.8 = (bf16[384,1536]{1,0:T(8,128)(2,1)}, bf16[384,1536]{1,0:T(8,128)(2,1)S(1)}, u32[]{:S(2)}, u32[]{:S(2)}) collective-permute-start(bf16[384,1536]{1,0:T(8,128)(2,1)} %collective-permute-done.6), channel_id=1, source_target_pairs={{0,1},{1,0},{2,3},{3,2},{4,5},{5,4},{6,7},{7,6},{8,9},{9,8},{10,11... | collective-permute-start | bytes 3538952 | tf_op jit(solution)/shard_map/ppermute | solution.py:53
  62.3 5.5 %collective-permute-start.10 = (f32[1,1536]{1,0:T(1,128)S(1)}, f32[1,1536]{1,0:T(1,128)S(1)}, u32[]{:S(2)}, u32[]{:S(2)}) collective-permute-start(f32[1,1536]{1,0:T(1,128)S(1)} %slice.78), channel_id=1, source_target_pairs={{4,0},{8,4},{12,8},{16,12},{20,16},{24,20},{28,24},{5,1},{9,5},{13... | collective-permute-start | bytes 18440 | tf_op jit(solution)/shard_map/ppermute | solution.py:16
  68.8 5.1 %copy-start.4 = (bf16[384,1536]{1,0:T(8,128)(2,1)S(1)}, bf16[384,1536]{1,0:T(8,128)(2,1)}, u32[]{:S(2)}) copy-start(bf16[384,1536]{1,0:T(8,128)(2,1)} %param.15) | copy-start | bytes 3538948
  69.2 10.0 %collective-permute-start.9 = (f32[1,1536]{1,0:T(1,128)S(1)}, f32[1,1536]{1,0:T(1,128)S(1)}, u32[]{:S(2)}, u32[]{:S(2)}) collective-permute-start(f32[1,1536]{1,0:T(1,128)S(1)} %slice.75), channel_id=1, source_target_pairs={{0,4},{4,8},{8,12},{12,16},{16,20},{20,24},{24,28},{1,5},{5,9},{9,... | collective-permute-start | bytes 18440 | tf_op jit(solution)/shard_map/ppermute | solution.py:16
  79.2 1.2 %copy-start.5 = (bf16[1,320,1536]{2,1,0:T(8,128)(2,1)S(1)}, bf16[1,320,1536]{2,1,0:T(8,128)(2,1)}, u32[]{:S(2)}) copy-start(bf16[1,320,1536]{2,1,0:T(8,128)(2,1)} %param.9) | copy-start | bytes 2949124
  83.9 7.2 %collective-permute-start.11 = (f32[1,1537]{1,0:T(1,128)S(1)}, f32[1,1537]{1,0:T(1,128)S(1)}, u32[]{:S(2)}, u32[]{:S(2)}) collective-permute-start(f32[1,1537]{1,0:T(1,128)S(1)} %pad_maximum_fusion.6), channel_id=1, source_target_pairs={{4,0},{8,4},{12,8},{16,12},{20,16},{24,20},{28,24},{5,1},{9,5},{13... | collective-permute-start | bytes 18452 | tf_op jit(solution)/shard_map/ppermute | solution.py:16
  85.2 1.3 %copy-start.3 = (bf16[384,1536]{1,0:T(8,128)(2,1)S(1)}, bf16[384,1536]{1,0:T(8,128)(2,1)}, u32[]{:S(2)}) copy-start(bf16[384,1536]{1,0:T(8,128)(2,1)} %param.14) | copy-start | bytes 3538948
  93.3 6.2 %collective-permute-start.12 = (f32[1,1537]{1,0:T(1,128)S(1)}, f32[1,1537]{1,0:T(1,128)S(1)}, u32[]{:S(2)}, u32[]{:S(2)}) collective-permute-start(f32[1,1537]{1,0:T(1,128)S(1)} %pad_maximum_fusion.7), channel_id=1, source_target_pairs={{8,0},{12,4},{16,8},{20,12},{24,16},{28,20},{9,1},{13,5},{17,9},{2... | collective-permute-start | bytes 18452 | tf_op jit(solution)/shard_map/ppermute | solution.py:16
  100.7 8.4 %collective-permute-start.13 = (f32[1,1537]{1,0:T(1,128)S(1)}, f32[1,1537]{1,0:T(1,128)S(1)}, u32[]{:S(2)}, u32[]{:S(2)}) collective-permute-start(f32[1,1537]{1,0:T(1,128)S(1)} %pad_maximum_fusion.8), channel_id=1, source_target_pairs={{16,0},{20,4},{24,8},{28,12},{17,1},{21,5},{25,9},{29,13},{18,2},{... | collective-permute-start | bytes 18452 | tf_op jit(solution)/shard_map/ppermute | solution.py:16

commit v3 on v2

--- a/solution.py
+++ b/solution.py
@@ -28,9 +28,9 @@
     excl_log = jnp.zeros_like(log_keep)
     excl_vec = jnp.zeros_like(vectors)
     while step < size:
-        packed = jnp.concatenate([incl_log, incl_vec], axis=-1)
+        packed = jnp.concatenate([incl_vec, incl_log], axis=-1)
         got = shifted(packed, axis, step if from_lower else -step)
-        got_log, got_vec = got[:, :1], got[:, 1:]
+        got_log, got_vec = got[:, -1:], got[:, :-1]
         excl_vec = jnp.exp(excl_log) * got_vec + excl_vec
         excl_log = excl_log + got_log
         if 2 * step < size:
@@ -54,6 +54,25 @@
     pairs = pairs + partner
     index = index + [i ^ 1 for i in index]
     return pairs, index
+
+
+def direct_scan(log_keep, vectors, axis):
+    size = lax.axis_size(axis)
+    packed = jnp.concatenate([vectors, log_keep], axis=-1)
+    total = jnp.zeros_like(vectors)
+    gap = jnp.zeros_like(log_keep)
+    for step in range(1, size):
+        got = shifted(packed, axis, -step)
+        total = total + jnp.exp(gap) * got[:, :-1]
+        gap = gap + got[:, -1:]
+    return total
+
+
+def assemble(blocks, index, width):
+    full = jnp.zeros((width * len(blocks),) + blocks[0].shape[1:], blocks[0].dtype)
+    for block, at in zip(blocks, index):
+        full = lax.dynamic_update_slice_in_dim(full, block, at * width, axis=0)
+    return full
 
 
 def split_dot(rows, blocks, index, width):
@@ -82,8 +101,10 @@
     shard_index = lax.axis_index("seq")
     pairs, index = gather_blocks((query_weight, key_weight), "dp")
     width = query_weight.shape[0]
-    key_rows = split_dot(token_rows, [p[1] for p in pairs], index, width)
-    queries = split_dot(token_rows, [p[0] for p in pairs], index, width)
+    full_query = assemble([p[0] for p in pairs], index, width)
+    full_key = assemble([p[1] for p in pairs], index, width)
+    key_rows = jnp.dot(token_rows, full_key, preferred_element_type=jnp.float32)
+    queries = jnp.dot(token_rows, full_query, preferred_element_type=jnp.float32)
     query_scale = lax.rsqrt(jnp.sum(queries * queries, axis=1, keepdims=True) + norm_eps)
     key_scale = lax.rsqrt(jnp.sum(key_rows * key_rows, axis=1, keepdims=True) + norm_eps)
     query_unit = queries * query_scale
@@ -120,7 +141,10 @@
     last_log = running[slot_count - 1 :]
     last_state = local_state[slot_count - 1 :]
     state_in = seq_scan(last_log[None], last_state, "seq", True)
-    grad_in = seq_scan(last_log[None], back_vector, "seq", False)
+    if lax.axis_size("seq") <= 8:
+        grad_in = direct_scan(last_log[None], back_vector, "seq")
+    else:
+        grad_in = seq_scan(last_log[None], back_vector, "seq", False)
     smoothed = local_state + keep_all[:, None] * state_in
     picked = jnp.dot(membership, smoothed, precision=exact) + leading[:, None] * state_in
     conf_grad = jnp.sum(grad_rows * picked, axis=1)
@@ -137,14 +161,13 @@
     from_next = shifted(prior_grad[:1], "seq", -1)
     unit_k_grad = jnp.concatenate([prior_grad[1:], from_next], axis=0)
     key_grad = normalize_grad(key_rows, key_scale, unit_k_grad).astype(jnp.bfloat16)
-    parts = []
-    for (q_block, k_block) in pairs:
-        part = lax.dot_general(query_grad, q_block, contract_last, preferred_element_type=jnp.float32)
-        part = part + lax.dot_general(key_grad, k_block, contract_last, preferred_element_type=jnp.float32)
-        parts.append(part.astype(jnp.bfloat16))
-    order = jnp.zeros((len(index),), jnp.int32).at[jnp.stack(index)].set(jnp.arange(len(index), dtype=jnp.int32))
-    x_grad = jnp.stack(parts)[order]
-    x_grad = jnp.transpose(x_grad, (1, 0, 2)).reshape(token_count, -1)
+    x_grad = lax.dot_general(
+        query_grad, full_query, contract_last, preferred_element_type=jnp.float32
+    )
+    x_grad = x_grad + lax.dot_general(
+        key_grad, full_key, contract_last, preferred_element_type=jnp.float32
+    )
+    x_grad = x_grad.astype(jnp.bfloat16)
     return (x_grad[None], segment_grad[None])
 
 

time: 112 us -> 119 us (1.062)
  the two profiles are of different devices: /device:TPU:0 before, /device:TPU:28 now
where the time goes in v3:
time: 119 us
  waiting for transfers between devices  30.1 us (25%)
  starting transfers between devices  28.8 us (24%)
  local copies, waits for them, and re-layouts  21.8 us (18%)
  matrix products  21.2 us (18%)
  between operations  11.2 us (9%)
  other arithmetic  5.34 us (4%)
    ppermute x12, starting transfers between devices, shifted(): return lax.ppermute(block, axis, route)  25.9 us
    ppermute x2, waiting for transfers between devices, gather_blocks(): pairs.append(lax.ppermute(blocks, axis, route))  18.8 us
    dynamic_update_slice x8, local copies, waits for them, and re-layouts, assemble(): full = lax.dynamic_update_slice_in_dim(full, block, at * width, axis=0)  12 us
    ppermute x12, waiting for transfers between devices, shifted(): return lax.ppermute(block, axis, route)  11.4 us
    dot_general x1, matrix products, per_device(): lax.dot_general(query_grad, full_query, contract_last, preferred_element_...  5.15 us
    dot_general x1, matrix products, per_device(): jnp.dot(token_rows, full_query, preferred_element_type=jnp.float32)  4.7 us
    slice x6, local copies, waits for them, and re-layouts, direct_scan(): gap = gap + got[:, -1:]  3.07 us
    another operation x2, local copies, waits for them, and re-layouts  2.79 us
  transfers between devices with their start and end apart: 18, of which 6 were waited for; matrix products, arithmetic and copies ran while one was open for 32% of the time, Pallas kernels for 0%

profile of v3, /device:TPU:28, one launch (start us, length us, event | category | flops | bytes accessed | tf_op | source)
XLA Modules:
  0.0 118.5 jit_solution(1101550272346620024)
XLA Ops:
  0.6 0.6 collective-permute-start.6
  1.2 1.5 %collective-permute-start = (bf16[384,1536]{1,0:T(8,128)(2,1)}, bf16[384,1536]{1,0:T(8,128)(2,1)}, u32[]{:S(2)}, u32[]{:S(2)}) collective-permute-start(bf16[384,1536]{1,0:T(8,128)(2,1)} %param.14), channel_id=1, source_target_pairs={{0,2},{1,3},{2,0},{3,1},{4,6},{5,7},{6,4},{7,5},{8,10},{9,11},{10,... | collective-permute-start | bytes 3538952 | tf_op jit(solution)/shard_map/ppermute | solution.py:50
  2.7 0.2 collective-permute-start.1
  3.6 0.7 fusion.54
  4.4 0.2 broadcast_in_dim.25
  4.6 0.5 slice.99
  5.1 0.7 bitcast_select_fusion
  5.9 1.9 %fusion.22 = f32[128,1536]{1,0:T(8,128)S(1)} fusion(bf16[1,128,1536]{2,1,0:T(8,128)(2,1)} %param.10, f32[128]{0:T(128)S(1)} %bitcast_select_fusion, f32[128]{0:T(128)S(1)} %reduce), kind=kOutput, calls=%fused_computation.41 | convolution fusion | flops 302448640 | bytes 1180672 | tf_op jit(solution)/shard_map/dot_general | solution.py:133
  7.8 0.7 pad_maximum_fusion.2
  8.4 3.4 %collective-permute-start.3 = (f32[1,1537]{1,0:T(1,128)S(1)}, f32[1,1537]{1,0:T(1,128)S(1)}, u32[]{:S(2)}, u32[]{:S(2)}) collective-permute-start(f32[1,1537]{1,0:T(1,128)S(1)} %pad_maximum_fusion.2), channel_id=1, source_target_pairs={{0,4},{4,8},{8,12},{12,16},{16,20},{20,24},{24,28},{1,5},{5,9},{9,... | collective-permute-start | bytes 18452 | tf_op jit(solution)/shard_map/ppermute | solution.py:16
  11.9 0.3 broadcast.152.clone
  12.2 0.9 copy-done.3
  13.2 2.5 %broadcast.152.clone.1 = bf16[1536,1536]{1,0:T(8,128)(2,1)} broadcast(bf16[]{:T(256)} %constant.19.clone.1), dimensions={} | broadcast | bytes 4718594 | tf_op jit(solution)/shard_map/broadcast.9
  15.7 1.0 copy-done.1
  16.8 1.1 constant_dynamic-update-slice_fusion.7
  17.9 0.1 convert_reduce_fusion
  18.7 0.5 slice.100
  20.6 1.3 %collective-permute-start.4 = (f32[1,1537]{1,0:T(1,128)S(1)}, f32[1,1537]{1,0:T(1,128)S(1)}, u32[]{:S(2)}, u32[]{:S(2)}) collective-permute-start(f32[1,1537]{1,0:T(1,128)S(1)} %pad_maximum_fusion.3), channel_id=1, source_target_pairs={{0,8},{4,12},{8,16},{12,20},{16,24},{20,28},{1,9},{5,13},{9,17},{1... | collective-permute-start | bytes 18452 | tf_op jit(solution)/shard_map/ppermute | solution.py:16
  21.9 0.7 subtract_exponential_fusion
  22.6 3.5 %collective-permute-done.4 = f32[1,1537]{1,0:T(1,128)S(1)} collective-permute-done((f32[1,1537]{1,0:T(1,128)S(1)}, f32[1,1537]{1,0:T(1,128)S(1)}, u32[]{:S(2)}, u32[]{:S(2)}) %collective-permute-start.4) | collective-permute-done | bytes 6180 | tf_op jit(solution)/shard_map/ppermute | solution.py:16
  26.1 0.5 slice.102
  27.3 1.3 %collective-permute-start.5 = (f32[1,1537]{1,0:T(1,128)S(1)}, f32[1,1537]{1,0:T(1,128)S(1)}, u32[]{:S(2)}, u32[]{:S(2)}) collective-permute-start(f32[1,1537]{1,0:T(1,128)S(1)} %pad_maximum_fusion.4), channel_id=1, source_target_pairs={{0,16},{4,20},{8,24},{12,28},{1,17},{5,21},{9,25},{13,29},{2,18},{... | collective-permute-start | bytes 18452 | tf_op jit(solution)/shard_map/ppermute | solution.py:16
  28.6 0.1 fusion.30
  30.9 2.9 %collective-permute-done.5 = f32[1,1537]{1,0:T(1,128)S(1)} collective-permute-done((f32[1,1537]{1,0:T(1,128)S(1)}, f32[1,1537]{1,0:T(1,128)S(1)}, u32[]{:S(2)}, u32[]{:S(2)}) %collective-permute-start.5) | collective-permute-done | bytes 6180 | tf_op jit(solution)/shard_map/ppermute | solution.py:16
  33.8 1.4 %fusion.8 = f32[320]{0:T(512)S(1)} fusion(bf16[1,320,1536]{2,1,0:T(8,128)(2,1)S(1)} %copy-done.2, f32[1536]{0:T(1024)S(1)} %fusion.47, f32[320]{0:T(512)S(1)} %get-tuple-element.6, f32[128,1536]{1,0:T(8,128)S(1)} %fusion.22, f32[128]{0:T(128)S(1)} %get-tuple-element.11, s32[320]{0:T(512)S(1)} %broadcast_add_fusion), kind=kOutput, calls=%fused_computation.24 | convolution fusion | flops 757866176 | bytes 1779968 | tf_op jit(solution)/shard_map/dot_general | solution.py:149
  35.2 18.8 %collective-permute-done = bf16[384,1536]{1,0:T(8,128)(2,1)} collective-permute-done((bf16[384,1536]{1,0:T(8,128)(2,1)}, bf16[384,1536]{1,0:T(8,128)(2,1)}, u32[]{:S(2)}, u32[]{:S(2)}) %collective-permute-start) | collective-permute-done | bytes 1179680 | tf_op jit(solution)/shard_map/ppermute | solution.py:50
  54.0 0.6 collective-permute-start.8
  54.6 2.4 %constant_dynamic-update-slice_fusion.2 = bf16[1536,1536]{1,0:T(8,128)(2,1)} fusion(bf16[1536,1536]{1,0:T(8,128)(2,1)} %copy-done.1, bf16[384,1536]{1,0:T(8,128)(2,1)} %collective-permute-done.6, s32[]{:T(128)S(6)} %select_n.78), kind=kLoop, calls=%fused_computation.98 | loop fusion | bytes 2359300 | tf_op jit(solution)/shard_map/dynamic_update_slice | solution.py:74
  57.0 2.4 %constant_dynamic-update-slice_fusion.6 = bf16[1536,1536]{1,0:T(8,128)(2,1)} fusion(bf16[1536,1536]{1,0:T(8,128)(2,1)} %constant_dynamic-update-slice_fusion.7, bf16[384,1536]{1,0:T(8,128)(2,1)} %collective-permute-done, s32[]{:T(128)S(6)} %select_n.78), kind=kLoop, calls=%fused_computation.102 | loop fusion | bytes 2359300 | tf_op jit(solution)/shard_map/dynamic_update_slice | solution.py:74
  59.4 2.3 %constant_dynamic-update-slice_fusion.1 = bf16[1536,1536]{1,0:T(8,128)(2,1)} fusion(bf16[1536,1536]{1,0:T(8,128)(2,1)} %constant_dynamic-update-slice_fusion.2, bf16[384,1536]{1,0:T(8,128)(2,1)} %collective-permute-done.7, s32[]{:T(128)S(6)} %select_n.79), kind=kLoop, calls=%fused_computation.97 | loop fusion | bytes 2359300 | tf_op jit(solution)/shard_map/dynamic_update_slice | solution.py:74
  61.7 2.5 %constant_dynamic-update-slice_fusion.5 = bf16[1536,1536]{1,0:T(8,128)(2,1)} fusion(bf16[1536,1536]{1,0:T(8,128)(2,1)} %constant_dynamic-update-slice_fusion.6, bf16[384,1536]{1,0:T(8,128)(2,1)} %collective-permute-done.1, s32[]{:T(128)S(6)} %select_n.79), kind=kLoop, calls=%fused_computation.101 | loop fusion | bytes 2359300 | tf_op jit(solution)/shard_map/dynamic_update_slice | solution.py:74
  64.2 1.1 constant_dynamic-update-slice_fusion.4
  65.3 4.7 %multiply_reduce_fusion.4 = (f32[320]{0:T(512)S(1)}, f32[320,1536]{1,0:T(8,128)S(1)}) fusion(bf16[1536,1536]{1,0:T(8,128)(2,1)} %constant_dynamic-update-slice_fusion.4, bf16[1,320,1536]{2,1,0:T(8,128)(2,1)S(1)} %copy-done), kind=kOutput, calls=%fused_computation.22 | convolution fusion | flops 1510932224 | bytes 7668992 | tf_op jit(solution)/shard_map/dot_general | solution.py:107
  70.0 0.3 multiply_multiply_fusion
  70.3 3.3 %collective-permute-start.10 = (f32[1,1536]{1,0:T(1,128)S(1)}, f32[1,1536]{1,0:T(1,128)S(1)}, u32[]{:S(2)}, u32[]{:S(2)}) collective-permute-start(f32[1,1536]{1,0:T(1,128)S(1)} %slice.108), channel_id=1, source_target_pairs={{4,0},{8,4},{12,8},{16,12},{20,16},{24,20},{28,24},{5,1},{9,5},{13... | collective-permute-start | bytes 18440 | tf_op jit(solution)/shard_map/ppermute | solution.py:16
  73.6 0.1 constant_dynamic-update-slice_fusion
  73.7 0.2 slice.107
  73.9 1.9 %collective-permute-done.10 = f32[1,1536]{1,0:T(1,128)S(1)} collective-permute-done((f32[1,1536]{1,0:T(1,128)S(1)}, f32[1,1536]{1,0:T(1,128)S(1)}, u32[]{:S(2)}, u32[]{:S(2)}) %collective-permute-start.10) | collective-permute-done | bytes 6176 | tf_op jit(solution)/shard_map/ppermute | solution.py:16
  75.8 1.9 %multiply_reduce_fusion.3 = (f32[320]{0:T(512)S(1)}, f32[320]{0:T(512)S(1)}, f32[320,1536]{1,0:T(8,128)S(1)}) fusion(f32[1,1536]{1,0:T(1,128)S(1)} %collective-permute-done.10, f32[319,1536]{1,0:T(8,128)S(1)} %slice.107, bf16[1536,1536]{1,0:T(8,128)(2,1)S(1)} %constant_dynamic-update-slice_fusion, bf16[1,320,1536]{2,1,0:T(8,128)(2,1)S(1)} %copy-done), kind=kOutput, calls=%fused_computation.21 | convolution fusion | flops 1512406528 | bytes 9636352 | tf_op jit(solution)/shard_map/dot_general | solution.py:106
  77.7 0.2 broadcast_multiply_fusion
  77.9 2.1 %collective-permute-start.9 = (f32[1,1536]{1,0:T(1,128)S(1)}, f32[1,1536]{1,0:T(1,128)S(1)}, u32[]{:S(2)}, u32[]{:S(2)}) collective-permute-start(f32[1,1536]{1,0:T(1,128)S(1)} %slice.105), channel_id=1, source_target_pairs={{0,4},{4,8},{8,12},{12,16},{16,20},{20,24},{24,28},{1,5},{5,9},{9,... | collective-permute-start | bytes 18440 | tf_op jit(solution)/shard_map/ppermute | solution.py:16
  80.0 1.8 %fusion.10 = f32[320,1536]{1,0:T(8,128)S(1)} fusion(bf16[1536,1536]{1,0:T(8,128)(2,1)S(1)} %constant_dynamic-update-slice_fusion, f32[320,1536]{1,0:T(8,128)S(1)} %get-tuple-element.14, f32[1,1536]{1,0:T(1,128)S(1)} %collective-permute-done.10, f32[319,1536]{1,0:T(8,128)S(1)} %slice.107, f32[320]{0:T(512)S(1)} %get-tuple-element.9, f32[320]{0:T(512)S(1)} %get-tuple-element.8), kind=kOutput, calls=%fused_computation.27 | convolution fusion | flops 1512407040 | bytes 10619392 | tf_op jit(solution)/shard_map/dot_general | solution.py:167
  81.9 2.5 %collective-permute-done.9 = f32[1,1536]{1,0:T(1,128)S(1)} collective-permute-done((f32[1,1536]{1,0:T(1,128)S(1)}, f32[1,1536]{1,0:T(1,128)S(1)}, u32[]{:S(2)}, u32[]{:S(2)}) %collective-permute-start.9) | collective-permute-done | bytes 6176 | tf_op jit(solution)/shard_map/ppermute | solution.py:16
  84.3 0.8 multiply_reduce_fusion
  85.2 1.2 %fusion.7 = f32[128,1536]{1,0:T(8,128)S(1)} fusion(bf16[1,320,1536]{2,1,0:T(8,128)(2,1)S(1)} %copy-done.2, f32[320]{0:T(512)S(1)} %subtract_select_fusion, s32[320]{0:T(512)S(1)} %broadcast_add_fusion), kind=kOutput, calls=%fused_computation.13 | convolution fusion | flops 755998720 | bytes 1772032 | tf_op jit(solution)/shard_map/dot_general | solution.py:138
  86.4 0.9 fusion.9
  87.4 0.5 convolution_reduce_fusion
  87.9 0.7 pad_maximum_fusion.5
  88.6 0.7 collective-permute-start.17
  89.2 2.7 %collective-permute-start.16 = (f32[1,1537]{1,0:T(1,128)S(1)}, f32[1,1537]{1,0:T(1,128)S(1)}, u32[]{:S(2)}, u32[]{:S(2)}) collective-permute-start(f32[1,1537]{1,0:T(1,128)S(1)} %pad_maximum_fusion.5), channel_id=1, source_target_pairs={{24,0},{28,4},{25,1},{29,5},{26,2},{30,6},{27,3},{31,7}} | collective-permute-start | bytes 18452 | tf_op jit(solution)/shard_map/ppermute | solution.py:16
  91.9 1.7 %collective-permute-start.15 = (f32[1,1537]{1,0:T(1,128)S(1)}, f32[1,1537]{1,0:T(1,128)S(1)}, u32[]{:S(2)}, u32[]{:S(2)}) collective-permute-start(f32[1,1537]{1,0:T(1,128)S(1)} %pad_maximum_fusion.5), channel_id=1, source_target_pairs={{20,0},{24,4},{28,8},{21,1},{25,5},{29,9},{22,2},{26,6},{30,10},{2... | collective-permute-start | bytes 18452 | tf_op jit(solution)/shard_map/ppermute | solution.py:16
  93.6 1.3 %collective-permute-start.12 = (f32[1,1537]{1,0:T(1,128)S(1)}, f32[1,1537]{1,0:T(1,128)S(1)}, u32[]{:S(2)}, u32[]{:S(2)}) collective-permute-start(f32[1,1537]{1,0:T(1,128)S(1)} %pad_maximum_fusion.5), channel_id=1, source_target_pairs={{8,0},{12,4},{16,8},{20,12},{24,16},{28,20},{9,1},{13,5},{17,9},{2... | collective-permute-start | bytes 18452 | tf_op jit(solution)/shard_map/ppermute | solution.py:16
  94.9 3.6 %collective-permute-start.11 = (f32[1,1537]{1,0:T(1,128)S(1)}, f32[1,1537]{1,0:T(1,128)S(1)}, u32[]{:S(2)}, u32[]{:S(2)}) collective-permute-start(f32[1,1537]{1,0:T(1,128)S(1)} %pad_maximum_fusion.5), channel_id=1, source_target_pairs={{4,0},{8,4},{12,8},{16,12},{20,16},{24,20},{28,24},{5,1},{9,5},{13... | collective-permute-start | bytes 18452 | tf_op jit(solution)/shard_map/ppermute | solution.py:16
  98.6 1.3 %collective-permute-start.14 = (f32[1,1537]{1,0:T(1,128)S(1)}, f32[1,1537]{1,0:T(1,128)S(1)}, u32[]{:S(2)}, u32[]{:S(2)}) collective-permute-start(f32[1,1537]{1,0:T(1,128)S(1)} %pad_maximum_fusion.5), channel_id=1, source_target_pairs={{16,0},{20,4},{24,8},{28,12},{17,1},{21,5},{25,9},{29,13},{18,2},{... | collective-permute-start | bytes 18452 | tf_op jit(solution)/shard_map/ppermute | solution.py:16
  99.8 0.6 collective-permute-done.11
  100.4 3.4 %collective-permute-start.13 = (f32[1,1537]{1,0:T(1,128)S(1)}, f32[1,1537]{1,0:T(1,128)S(1)}, u32[]{:S(2)}, u32[]{:S(2)}) collective-permute-start(f32[1,1537]{1,0:T(1,128)S(1)} %pad_maximum_fusion.5), channel_id=1, source_target_pairs={{12,0},{16,4},{20,8},{24,12},{28,16},{13,1},{17,5},{21,9},{25,13},... | collective-permute-start | bytes 18452 | tf_op jit(solution)/shard_map/ppermute | solution.py:16
  103.8 5.2 %fusion.2 = bf16[1,320,1536]{2,1,0:T(8,128)(2,1)} fusion(f32[320,1536]{1,0:T(8,128)S(1)} %fusion.10, bf16[1536,1536]{1,0:T(8,128)(2,1)} %constant_dynamic-update-slice_fusion.4, f32[320,1536]{1,0:T(8,128)S(1)} %get-tuple-element.13, f32[319,1536]{1,0:T(8,128)S(1)} %bitcast.68, f32[1,1536]{1,0:T(1,128)S(1)} %collective-permute-done.9, f32[320]{0:T(512)S(1)} %fusion.49, ...), kind=kOutput, calls=%fused_computation.6 | convolution fusion | flops 1513881600 | bytes 11603712 | tf_op jit(solution)/shard_map/dot_general | solution.py:164
  108.9 0.5 slice.110
  110.1 0.5 slice.112
  111.9 0.5 slice.114
  113.1 0.5 slice.116
  114.3 0.5 slice.118
  115.6 0.5 slice.120
  116.8 1.7 %fusion.5 = bf16[1,128,1536]{2,1,0:T(8,128)(2,1)} fusion(f32[128,1536]{1,0:T(8,128)S(1)} %fusion.7, f32[1536]{0:T(1024)S(1)} %fusion.48, f32[128]{0:T(128)S(1)} %get-tuple-element.10, f32[128]{0:T(128)S(1)} %bitcast_select_fusion, f32[128]{0:T(128)S(1)} %reduce), kind=kOutput, calls=%fused_computation.11 | convolution fusion | flops 302841856 | bytes 1187328 | tf_op jit(solution)/shard_map/dot_general | solution.py:154
  (52 shorter events, 0.6 us)
Async XLA Ops:
  0.6 64.6 %copy-start = (bf16[1,320,1536]{2,1,0:T(8,128)(2,1)S(1)}, bf16[1,320,1536]{2,1,0:T(8,128)(2,1)}, u32[]{:S(2)}) copy-start(bf16[1,320,1536]{2,1,0:T(8,128)(2,1)} %param.8) | copy-start | bytes 2949124
  0.6 53.4 %collective-permute-start.6 = (bf16[384,1536]{1,0:T(8,128)(2,1)}, bf16[384,1536]{1,0:T(8,128)(2,1)}, u32[]{:S(2)}, u32[]{:S(2)}) collective-permute-start(bf16[384,1536]{1,0:T(8,128)(2,1)} %param.15), channel_id=1, source_target_pairs={{0,2},{1,3},{2,0},{3,1},{4,6},{5,7},{6,4},{7,5},{8,10},{9,11},{10,... | collective-permute-start | bytes 3538952 | tf_op jit(solution)/shard_map/ppermute | solution.py:50
  1.2 58.1 %collective-permute-start.7 = (bf16[384,1536]{1,0:T(8,128)(2,1)}, bf16[384,1536]{1,0:T(8,128)(2,1)}, u32[]{:S(2)}, u32[]{:S(2)}) collective-permute-start(bf16[384,1536]{1,0:T(8,128)(2,1)} %param.15), channel_id=1, source_target_pairs={{0,1},{1,0},{2,3},{3,2},{4,5},{5,4},{6,7},{7,6},{8,9},{9,8},{10,11... | collective-permute-start | bytes 3538952 | tf_op jit(solution)/shard_map/ppermute | solution.py:53
  1.2 52.8 %collective-permute-start = (bf16[384,1536]{1,0:T(8,128)(2,1)}, bf16[384,1536]{1,0:T(8,128)(2,1)}, u32[]{:S(2)}, u32[]{:S(2)}) collective-permute-start(bf16[384,1536]{1,0:T(8,128)(2,1)} %param.14), channel_id=1, source_target_pairs={{0,2},{1,3},{2,0},{3,1},{4,6},{5,7},{6,4},{7,5},{8,10},{9,11},{10,... | collective-permute-start | bytes 3538952 | tf_op jit(solution)/shard_map/ppermute | solution.py:50
  2.7 59.0 %collective-permute-start.1 = (bf16[384,1536]{1,0:T(8,128)(2,1)}, bf16[384,1536]{1,0:T(8,128)(2,1)}, u32[]{:S(2)}, u32[]{:S(2)}) collective-permute-start(bf16[384,1536]{1,0:T(8,128)(2,1)} %param.14), channel_id=1, source_target_pairs={{0,1},{1,0},{2,3},{3,2},{4,5},{5,4},{6,7},{7,6},{8,9},{9,8},{10,11... | collective-permute-start | bytes 3538952 | tf_op jit(solution)/shard_map/ppermute | solution.py:53
  8.4 10.3 %collective-permute-start.3 = (f32[1,1537]{1,0:T(1,128)S(1)}, f32[1,1537]{1,0:T(1,128)S(1)}, u32[]{:S(2)}, u32[]{:S(2)}) collective-permute-start(f32[1,1537]{1,0:T(1,128)S(1)} %pad_maximum_fusion.2), channel_id=1, source_target_pairs={{0,4},{4,8},{8,12},{12,16},{16,20},{20,24},{24,28},{1,5},{5,9},{9,... | collective-permute-start | bytes 18452 | tf_op jit(solution)/shard_map/ppermute | solution.py:16
  11.8 1.3 %copy-start.3 = (bf16[384,1536]{1,0:T(8,128)(2,1)S(1)}, bf16[384,1536]{1,0:T(8,128)(2,1)}, u32[]{:S(2)}) copy-start(bf16[384,1536]{1,0:T(8,128)(2,1)} %param.15) | copy-start | bytes 3538948
  13.2 3.5 %copy-start.1 = (bf16[1536,1536]{1,0:T(8,128)(2,1)}, bf16[1536,1536]{1,0:T(8,128)(2,1)S(1)}, u32[]{:S(2)}) copy-start(bf16[1536,1536]{1,0:T(8,128)(2,1)S(1)} %constant_dynamic-update-slice_fusion.3) | copy-start | bytes 14155780
  13.2 3.5 %copy-start.4 = (bf16[384,1536]{1,0:T(8,128)(2,1)S(1)}, bf16[384,1536]{1,0:T(8,128)(2,1)}, u32[]{:S(2)}) copy-start(bf16[384,1536]{1,0:T(8,128)(2,1)} %param.14) | copy-start | bytes 3538948
  16.8 1.1 copy-start.5
  16.8 17.0 %copy-start.2 = (bf16[1,320,1536]{2,1,0:T(8,128)(2,1)S(1)}, bf16[1,320,1536]{2,1,0:T(8,128)(2,1)}, u32[]{:S(2)}) copy-start(bf16[1,320,1536]{2,1,0:T(8,128)(2,1)} %param.9) | copy-start | bytes 2949124
  20.6 5.5 %collective-permute-start.4 = (f32[1,1537]{1,0:T(1,128)S(1)}, f32[1,1537]{1,0:T(1,128)S(1)}, u32[]{:S(2)}, u32[]{:S(2)}) collective-permute-start(f32[1,1537]{1,0:T(1,128)S(1)} %pad_maximum_fusion.3), channel_id=1, source_target_pairs={{0,8},{4,12},{8,16},{12,20},{16,24},{20,28},{1,9},{5,13},{9,17},{1... | collective-permute-start | bytes 18452 | tf_op jit(solution)/shard_map/ppermute | solution.py:16
  27.3 6.4 %collective-permute-start.5 = (f32[1,1537]{1,0:T(1,128)S(1)}, f32[1,1537]{1,0:T(1,128)S(1)}, u32[]{:S(2)}, u32[]{:S(2)}) collective-permute-start(f32[1,1537]{1,0:T(1,128)S(1)} %pad_maximum_fusion.4), channel_id=1, source_target_pairs={{0,16},{4,20},{8,24},{12,28},{1,17},{5,21},{9,25},{13,29},{2,18},{... | collective-permute-start | bytes 18452 | tf_op jit(solution)/shard_map/ppermute | solution.py:16
  54.0 10.2 %collective-permute-start.2 = (bf16[384,1536]{1,0:T(8,128)(2,1)}, bf16[384,1536]{1,0:T(8,128)(2,1)S(1)}, u32[]{:S(2)}, u32[]{:S(2)}) collective-permute-start(bf16[384,1536]{1,0:T(8,128)(2,1)} %collective-permute-done), channel_id=1, source_target_pairs={{0,1},{1,0},{2,3},{3,2},{4,5},{5,4},{6,7},{7,6},{8,9},{9,8},{10,11... | collective-permute-start | bytes 3538952 | tf_op jit(solution)/shard_map/ppermute | solution.py:53
  54.0 19.5 %collective-permute-start.8 = (bf16[384,1536]{1,0:T(8,128)(2,1)}, bf16[384,1536]{1,0:T(8,128)(2,1)S(1)}, u32[]{:S(2)}, u32[]{:S(2)}) collective-permute-start(bf16[384,1536]{1,0:T(8,128)(2,1)} %collective-permute-done.6), channel_id=1, source_target_pairs={{0,1},{1,0},{2,3},{3,2},{4,5},{5,4},{6,7},{7,6},{8,9},{9,8},{10,11... | collective-permute-start | bytes 3538952 | tf_op jit(solution)/shard_map/ppermute | solution.py:53
  64.2 9.4 %slice-start = ((s8[4718592]{0:T(1024)(128)(4,1)}), s8[4194304]{0:T(1024)(128)(4,1)S(1)}, s32[]{:S(2)}) async-start(s8[4718592]{0:T(1024)(128)(4,1)} %bitcast.69), calls=%async_computation | async-start | bytes 8388608
  65.3 8.3 %slice-start.1 = ((s8[4718592]{0:T(1024)(128)(4,1)}), s8[524288]{0:T(1024)(128)(4,1)S(1)}, s32[]{:S(2)}) async-start(s8[4718592]{0:T(1024)(128)(4,1)} %bitcast.69), calls=%async_computation.1 | async-start | bytes 1048576
  70.3 5.5 %collective-permute-start.10 = (f32[1,1536]{1,0:T(1,128)S(1)}, f32[1,1536]{1,0:T(1,128)S(1)}, u32[]{:S(2)}, u32[]{:S(2)}) collective-permute-start(f32[1,1536]{1,0:T(1,128)S(1)} %slice.108), channel_id=1, source_target_pairs={{4,0},{8,4},{12,8},{16,12},{20,16},{24,20},{28,24},{5,1},{9,5},{13... | collective-permute-start | bytes 18440 | tf_op jit(solution)/shard_map/ppermute | solution.py:16
  77.9 6.4 %collective-permute-start.9 = (f32[1,1536]{1,0:T(1,128)S(1)}, f32[1,1536]{1,0:T(1,128)S(1)}, u32[]{:S(2)}, u32[]{:S(2)}) collective-permute-start(f32[1,1536]{1,0:T(1,128)S(1)} %slice.105), channel_id=1, source_target_pairs={{0,4},{4,8},{8,12},{12,16},{16,20},{20,24},{24,28},{1,5},{5,9},{9,... | collective-permute-start | bytes 18440 | tf_op jit(solution)/shard_map/ppermute | solution.py:16
  88.6 28.2 %collective-permute-start.17 = (f32[1,1537]{1,0:T(1,128)S(1)}, f32[1,1537]{1,0:T(1,128)S(1)}, u32[]{:S(2)}, u32[]{:S(2)}) collective-permute-start(f32[1,1537]{1,0:T(1,128)S(1)} %pad_maximum_fusion.5), channel_id=1, source_target_pairs={{28,0},{29,1},{30,2},{31,3}} | collective-permute-start | bytes 18452 | tf_op jit(solution)/shard_map/ppermute | solution.py:16
  89.2 26.3 %collective-permute-start.16 = (f32[1,1537]{1,0:T(1,128)S(1)}, f32[1,1537]{1,0:T(1,128)S(1)}, u32[]{:S(2)}, u32[]{:S(2)}) collective-permute-start(f32[1,1537]{1,0:T(1,128)S(1)} %pad_maximum_fusion.5), channel_id=1, source_target_pairs={{24,0},{28,4},{25,1},{29,5},{26,2},{30,6},{27,3},{31,7}} | collective-permute-start | bytes 18452 | tf_op jit(solution)/shard_map/ppermute | solution.py:16
  91.9 22.4 %collective-permute-start.15 = (f32[1,1537]{1,0:T(1,128)S(1)}, f32[1,1537]{1,0:T(1,128)S(1)}, u32[]{:S(2)}, u32[]{:S(2)}) collective-permute-start(f32[1,1537]{1,0:T(1,128)S(1)} %pad_maximum_fusion.5), channel_id=1, source_target_pairs={{20,0},{24,4},{28,8},{21,1},{25,5},{29,9},{22,2},{26,6},{30,10},{2... | collective-permute-start | bytes 18452 | tf_op jit(solution)/shard_map/ppermute | solution.py:16
  93.6 5.0 %collective-permute-start.12 = (f32[1,1537]{1,0:T(1,128)S(1)}, f32[1,1537]{1,0:T(1,128)S(1)}, u32[]{:S(2)}, u32[]{:S(2)}) collective-permute-start(f32[1,1537]{1,0:T(1,128)S(1)} %pad_maximum_fusion.5), channel_id=1, source_target_pairs={{8,0},{12,4},{16,8},{20,12},{24,16},{28,20},{9,1},{13,5},{17,9},{2... | collective-permute-start | bytes 18452 | tf_op jit(solution)/shard_map/ppermute | solution.py:16
  94.9 5.5 %collective-permute-start.11 = (f32[1,1537]{1,0:T(1,128)S(1)}, f32[1,1537]{1,0:T(1,128)S(1)}, u32[]{:S(2)}, u32[]{:S(2)}) collective-permute-start(f32[1,1537]{1,0:T(1,128)S(1)} %pad_maximum_fusion.5), channel_id=1, source_target_pairs={{4,0},{8,4},{12,8},{16,12},{20,16},{24,20},{28,24},{5,1},{9,5},{13... | collective-permute-start | bytes 18452 | tf_op jit(solution)/shard_map/ppermute | solution.py:16
  98.6 14.6 %collective-permute-start.14 = (f32[1,1537]{1,0:T(1,128)S(1)}, f32[1,1537]{1,0:T(1,128)S(1)}, u32[]{:S(2)}, u32[]{:S(2)}) collective-permute-start(f32[1,1537]{1,0:T(1,128)S(1)} %pad_maximum_fusion.5), channel_id=1, source_target_pairs={{16,0},{20,4},{24,8},{28,12},{17,1},{21,5},{25,9},{29,13},{18,2},{... | collective-permute-start | bytes 18452 | tf_op jit(solution)/shard_map/ppermute | solution.py:16
  100.4 11.5 %collective-permute-start.13 = (f32[1,1537]{1,0:T(1,128)S(1)}, f32[1,1537]{1,0:T(1,128)S(1)}, u32[]{:S(2)}, u32[]{:S(2)}) collective-permute-start(f32[1,1537]{1,0:T(1,128)S(1)} %pad_maximum_fusion.5), channel_id=1, source_target_pairs={{12,0},{16,4},{20,8},{24,12},{28,16},{13,1},{17,5},{21,9},{25,13},... | collective-permute-start | bytes 18452 | tf_op jit(solution)/shard_map/ppermute | solution.py:16

commit v4 on v3

--- a/solution.py
+++ b/solution.py
@@ -68,20 +68,15 @@
     return total
 
 
-def assemble(blocks, index, width):
-    full = jnp.zeros((width * len(blocks),) + blocks[0].shape[1:], blocks[0].dtype)
-    for block, at in zip(blocks, index):
-        full = lax.dynamic_update_slice_in_dim(full, block, at * width, axis=0)
-    return full
+def permute_cols(rows, index, width):
+    return jnp.concatenate(
+        [lax.dynamic_slice_in_dim(rows, at * width, width, axis=1) for at in index], axis=1
+    )
 
 
-def split_dot(rows, blocks, index, width):
-    total = None
-    for block, at in zip(blocks, index):
-        part = lax.dynamic_slice_in_dim(rows, at * width, width, axis=1)
-        term = jnp.dot(part, block, preferred_element_type=jnp.float32)
-        total = term if total is None else total + term
-    return total
+def unit_of(rows):
+    scale = lax.rsqrt(jnp.sum(rows * rows, axis=1, keepdims=True) + norm_eps)
+    return rows * scale, scale
 
 
 def per_device(
@@ -98,22 +93,13 @@
     grad_rows = out_grad[0]
     token_count = token_rows.shape[0]
     slot_count = segment_states.shape[1]
+    width = query_weight.shape[0]
     shard_index = lax.axis_index("seq")
     pairs, index = gather_blocks((query_weight, key_weight), "dp")
-    width = query_weight.shape[0]
-    full_query = assemble([p[0] for p in pairs], index, width)
-    full_key = assemble([p[1] for p in pairs], index, width)
-    key_rows = jnp.dot(token_rows, full_key, preferred_element_type=jnp.float32)
-    queries = jnp.dot(token_rows, full_query, preferred_element_type=jnp.float32)
-    query_scale = lax.rsqrt(jnp.sum(queries * queries, axis=1, keepdims=True) + norm_eps)
-    key_scale = lax.rsqrt(jnp.sum(key_rows * key_rows, axis=1, keepdims=True) + norm_eps)
-    query_unit = queries * query_scale
-    key_unit = key_rows * key_scale
+    full_query = jnp.concatenate([p[0] for p in pairs], axis=0)
+    full_key = jnp.concatenate([p[1] for p in pairs], axis=0)
     position = jnp.arange(token_count)
     later_rows = (shard_index > 0) | (position > 0)
-    key_before = shifted(key_unit[token_count - 1 :], "seq", 1)
-    key_prior = jnp.concatenate([key_before, key_unit[:-1]], axis=0)
-    cosine = jnp.sum(query_unit * key_prior, axis=1)
     segment_total = segment_counts[0, 0]
     slot_index = jnp.arange(slot_count)
     slot_used = slot_index < segment_total
@@ -132,23 +118,39 @@
     weighted_states = smoothing[:, None] * segment_states[0].astype(jnp.float32)
     local_state = jnp.dot(decay_table, weighted_states, precision=exact)
     keep_all = jnp.exp(running)
+    last_log = running[slot_count - 1 :][None]
+    state_in = seq_scan(last_log, local_state[slot_count - 1 :], "seq", True)
+    smoothed = local_state + keep_all[:, None] * state_in
+    picked = jnp.dot(membership, smoothed, precision=exact) + leading[:, None] * state_in
+    conf_grad = jnp.sum(grad_rows * picked, axis=1)
+    cos_grad = jnp.where(later_rows, jnp.where(starts, -0.5 * conf_grad, 0.5 * conf_grad), 0.0)
+    to_prev = jnp.concatenate([token_rows[:1].astype(jnp.float32), cos_grad[:1][None]], axis=1)
+    from_next = shifted(to_prev, "seq", -1)
+    prev_row = shifted(token_rows[token_count - 1 :], "seq", 1)
+    next_row = from_next[:, :-1].astype(token_rows.dtype)
+    next_cos_grad = from_next[:, -1:]
+    rows_ext = jnp.concatenate([token_rows, prev_row, next_row], axis=0)
+    rows_perm = permute_cols(rows_ext, index, width)
+    queries_ext = jnp.dot(rows_perm, full_query, preferred_element_type=jnp.float32)
+    keys_ext = jnp.dot(rows_perm, full_key, preferred_element_type=jnp.float32)
+    queries = queries_ext[:token_count]
+    key_rows = keys_ext[:token_count]
+    query_unit, query_scale = unit_of(queries)
+    key_unit, key_scale = unit_of(key_rows)
+    key_before, _ = unit_of(keys_ext[token_count : token_count + 1])
+    query_next, _ = unit_of(queries_ext[token_count + 1 :])
+    key_prior = jnp.concatenate([key_before, key_unit[:-1]], axis=0)
+    cosine = jnp.sum(query_unit * key_prior, axis=1)
     boundary_prob = jnp.where(later_rows, 0.5 * (1.0 - cosine), 1.0)
     confidence = jnp.where(starts, boundary_prob, 1.0 - boundary_prob)
     weighted_grad = confidence[:, None] * grad_rows
     slot_grad = lax.dot_general(membership, weighted_grad, contract_first, precision=exact)
     lead_grad = jnp.dot(leading[None, :], weighted_grad, precision=exact)
     back_vector = lead_grad + jnp.dot(keep_all[None, :], slot_grad, precision=exact)
-    last_log = running[slot_count - 1 :]
-    last_state = local_state[slot_count - 1 :]
-    state_in = seq_scan(last_log[None], last_state, "seq", True)
     if lax.axis_size("seq") <= 8:
-        grad_in = direct_scan(last_log[None], back_vector, "seq")
+        grad_in = direct_scan(last_log, back_vector, "seq")
     else:
-        grad_in = seq_scan(last_log[None], back_vector, "seq", False)
-    smoothed = local_state + keep_all[:, None] * state_in
-    picked = jnp.dot(membership, smoothed, precision=exact) + leading[:, None] * state_in
-    conf_grad = jnp.sum(grad_rows * picked, axis=1)
-    cos_grad = jnp.where(later_rows, jnp.where(starts, -0.5 * conf_grad, 0.5 * conf_grad), 0.0)
+        grad_in = seq_scan(last_log, back_vector, "seq", False)
     reach_end = jnp.exp(running[slot_count - 1] - running)
     state_grad = (
         lax.dot_general(decay_table, slot_grad, contract_first, precision=exact)
@@ -158,8 +160,7 @@
     unit_q_grad = cos_grad[:, None] * key_prior
     prior_grad = cos_grad[:, None] * query_unit
     query_grad = normalize_grad(queries, query_scale, unit_q_grad).astype(jnp.bfloat16)
-    from_next = shifted(prior_grad[:1], "seq", -1)
-    unit_k_grad = jnp.concatenate([prior_grad[1:], from_next], axis=0)
+    unit_k_grad = jnp.concatenate([prior_grad[1:], next_cos_grad * query_next], axis=0)
     key_grad = normalize_grad(key_rows, key_scale, unit_k_grad).astype(jnp.bfloat16)
     x_grad = lax.dot_general(
         query_grad, full_query, contract_last, preferred_element_type=jnp.float32
@@ -168,6 +169,9 @@
         key_grad, full_key, contract_last, preferred_element_type=jnp.float32
     )
     x_grad = x_grad.astype(jnp.bfloat16)
+    slots = jnp.arange(len(index), dtype=jnp.int32)
+    order = jnp.sum(jnp.where(jnp.stack(index)[None, :] == slots[:, None], slots[None, :], 0), axis=1)
+    x_grad = permute_cols(x_grad, [order[j] for j in range(len(index))], width)
     return (x_grad[None], segment_grad[None])
 
 

time: 119 us -> 117 us (0.983)
  the two profiles are of different devices: /device:TPU:28 before, /device:TPU:0 now
where the time goes in v4:
time: 117 us; the launch traced here: 115 us
  starting transfers between devices  30.3 us (26%)
  matrix products  21.7 us (19%)
  local copies, waits for them, and re-layouts  19.3 us (16%)
  other arithmetic  18 us (15%)
  between operations  14.8 us (13%)
  waiting for transfers between devices  11.2 us (10%)
    ppermute x12, starting transfers between devices, shifted(): return lax.ppermute(block, axis, route)  26.5 us
    unnamed x36, local copies, waits for them, and re-layouts  10.7 us
    ppermute x2, waiting for transfers between devices, gather_blocks(): pairs.append(lax.ppermute(blocks, axis, route))  6.03 us
    ppermute x12, waiting for transfers between devices, shifted(): return lax.ppermute(block, axis, route)  5.17 us
    dot_general x1, matrix products, per_device(): lax.dot_general(key_grad, full_key, contract_last, preferred_element_type...  4.33 us
    dot_general x1, matrix products, per_device(): keys_ext = jnp.dot(rows_perm, full_key, preferred_element_type=jnp.float32)  4.05 us
    ppermute x2, starting transfers between devices, gather_blocks(): pairs.append(lax.ppermute(blocks, axis, route))  3.19 us
    slice x6, local copies, waits for them, and re-layouts, direct_scan(): gap = gap + got[:, -1:]  3.07 us
  transfers between devices with their start and end apart: 18, of which 4 were waited for; matrix products, arithmetic and copies ran while one was open for 39% of the time, Pallas kernels for 0%

profile of v4, /device:TPU:0, one launch (start us, length us, event | category | flops | bytes accessed | tf_op | source)
XLA Modules:
  0.0 115.4 jit_solution(609191391237050751)
XLA Ops:
  0.7 3.0 %collective-permute-start.8 = (bf16[384,1536]{1,0:T(8,128)(2,1)}, bf16[384,1536]{1,0:T(8,128)(2,1)}, u32[]{:S(2)}, u32[]{:S(2)}) collective-permute-start(bf16[384,1536]{1,0:T(8,128)(2,1)} %param.15), channel_id=1, source_target_pairs={{0,2},{1,3},{2,0},{3,1},{4,6},{5,7},{6,4},{7,5},{8,10},{9,11},{10,... | collective-permute-start | bytes 3538952 | tf_op jit(solution)/shard_map/ppermute | solution.py:50
  4.5 0.7 fusion.53
  5.4 0.5 slice.149
  6.0 0.7 bitcast_select_fusion
  6.7 2.8 %fusion.19 = f32[128,1536]{1,0:T(8,128)} fusion(bf16[1,128,1536]{2,1,0:T(8,128)(2,1)} %param.10, f32[128]{0:T(128)S(1)} %bitcast_select_fusion, f32[128]{0:T(128)S(1)} %reduce.2), kind=kOutput, calls=%fused_computation.40 | convolution fusion | flops 302448640 | bytes 1180672 | tf_op jit(solution)/shard_map/dot_general | solution.py:119
  9.5 0.8 slice.148
  10.3 0.6 pad_maximum_fusion.6
  10.9 3.7 %collective-permute-start.1 = (f32[1,1537]{1,0:T(1,128)S(1)}, f32[1,1537]{1,0:T(1,128)S(1)}, u32[]{:S(2)}, u32[]{:S(2)}) collective-permute-start(f32[1,1537]{1,0:T(1,128)S(1)} %pad_maximum_fusion.6), channel_id=1, source_target_pairs={{0,4},{4,8},{8,12},{12,16},{16,20},{20,24},{24,28},{1,5},{5,9},{9,... | collective-permute-start | bytes 18452 | tf_op jit(solution)/shard_map/ppermute | solution.py:16
  14.6 0.8 slice_bitcast_fusion
  15.4 3.6 %collective-permute-start = (bf16[1,1536]{1,0:T(2,128)(2,1)S(1)}, bf16[1,1536]{1,0:T(2,128)(2,1)S(1)}, u32[]{:S(2)}, u32[]{:S(2)}) collective-permute-start(bf16[1,1536]{1,0:T(2,128)(2,1)S(1)} %get-tuple-element.18), channel_id=1, source_target_pairs={{0,4},{4,8},{8,12},{12,16},{16,20},{20,24},{24,28},{1,5},{5,9},{9,... | collective-permute-start | bytes 9224 | tf_op jit(solution)/shard_map/ppermute | solution.py:16
  19.0 1.1 constant_dynamic-update-slice_fusion.7
  20.1 1.1 constant_dynamic-update-slice_fusion.3
  21.4 0.7 subtract_exponential_fusion
  22.9 0.5 slice.150
  24.6 0.8 multiply_add_fusion.1
  25.4 3.5 %collective-permute-start.2 = (f32[1,1537]{1,0:T(1,128)S(1)}, f32[1,1537]{1,0:T(1,128)S(1)}, u32[]{:S(2)}, u32[]{:S(2)}) collective-permute-start(f32[1,1537]{1,0:T(1,128)S(1)} %pad_maximum_fusion.7), channel_id=1, source_target_pairs={{0,8},{4,12},{8,16},{12,20},{16,24},{20,28},{1,9},{5,13},{9,17},{1... | collective-permute-start | bytes 18452 | tf_op jit(solution)/shard_map/ppermute | solution.py:16
  29.1 1.2 %collective-permute-done.2 = f32[1,1537]{1,0:T(1,128)S(1)} collective-permute-done((f32[1,1537]{1,0:T(1,128)S(1)}, f32[1,1537]{1,0:T(1,128)S(1)}, u32[]{:S(2)}, u32[]{:S(2)}) %collective-permute-start.2) | collective-permute-done | bytes 6180 | tf_op jit(solution)/shard_map/ppermute | solution.py:16
  31.3 5.2 %collective-permute-start.3 = (f32[1,1537]{1,0:T(1,128)S(1)}, f32[1,1537]{1,0:T(1,128)S(1)}, u32[]{:S(2)}, u32[]{:S(2)}) collective-permute-start(f32[1,1537]{1,0:T(1,128)S(1)} %pad_maximum_fusion.8), channel_id=1, source_target_pairs={{0,16},{4,20},{8,24},{12,28},{1,17},{5,21},{9,25},{13,29},{2,18},{... | collective-permute-start | bytes 18452 | tf_op jit(solution)/shard_map/ppermute | solution.py:16
  38.6 2.6 %fusion.7 = f32[320]{0:T(512)S(1)} fusion(bf16[1,320,1536]{2,1,0:T(8,128)(2,1)S(1)} %copy-done.5, f32[1536]{0:T(1024)S(1)} %fusion.46, f32[320]{0:T(512)S(1)} %get-tuple-element.6, f32[128,1536]{1,0:T(8,128)} %fusion.19, f32[128]{0:T(128)S(1)} %get-tuple-element.23, s32[320]{0:T(512)S(1)} %broadcast_add_fusion), kind=kOutput, calls=%fused_computation.23 | convolution fusion | flops 757866176 | bytes 1779968 | tf_op jit(solution)/shard_map/dot_general | solution.py:124
  41.2 0.5 slice.122
  41.7 0.7 pad_maximum_fusion.9
  42.4 1.3 %collective-permute-start.4 = (f32[1,1537]{1,0:T(1,128)S(1)}, f32[1,1537]{1,0:T(1,128)S(1)}, u32[]{:S(2)}, u32[]{:S(2)}) collective-permute-start(f32[1,1537]{1,0:T(1,128)S(1)} %pad_maximum_fusion.9), channel_id=1, source_target_pairs={{4,0},{8,4},{12,8},{16,12},{20,16},{24,20},{28,24},{5,1},{9,5},{13... | collective-permute-start | bytes 18452 | tf_op jit(solution)/shard_map/ppermute | solution.py:16
  43.7 0.6 fusion.63
  46.9 1.0 collective-permute-done.4
  47.9 0.5 slice.163
  48.6 0.6 collective-permute-start.10
  49.2 6.0 %collective-permute-done.5 = bf16[384,1536]{1,0:T(8,128)(2,1)} collective-permute-done((bf16[384,1536]{1,0:T(8,128)(2,1)}, bf16[384,1536]{1,0:T(8,128)(2,1)}, u32[]{:S(2)}, u32[]{:S(2)}) %collective-permute-start.5) | collective-permute-done | bytes 1179680 | tf_op jit(solution)/shard_map/ppermute | solution.py:50
  55.2 2.4 %constant_dynamic-update-slice_fusion.6 = bf16[1536,1536]{1,0:T(8,128)(2,1)} fusion(bf16[1536,1536]{1,0:T(8,128)(2,1)} %constant_dynamic-update-slice_fusion.7, bf16[384,1536]{1,0:T(8,128)(2,1)} %collective-permute-done.8), kind=kLoop, calls=%fused_computation.72 | loop fusion | bytes 2359296
  57.6 1.3 %constant_dynamic-update-slice_fusion.2 = bf16[1536,1536]{1,0:T(8,128)(2,1)S(1)} fusion(bf16[1536,1536]{1,0:T(8,128)(2,1)S(1)} %copy-done.10, bf16[384,1536]{1,0:T(8,128)(2,1)} %collective-permute-done.5), kind=kLoop, calls=%fused_computation.68 | loop fusion | bytes 2359296
  59.0 2.4 %constant_dynamic-update-slice_fusion.5 = bf16[1536,1536]{1,0:T(8,128)(2,1)} fusion(bf16[1536,1536]{1,0:T(8,128)(2,1)} %constant_dynamic-update-slice_fusion.6, bf16[384,1536]{1,0:T(8,128)(2,1)} %collective-permute-done.9), kind=kLoop, calls=%fused_computation.71 | loop fusion | bytes 2359296
  61.5 1.1 constant_dynamic-update-slice_fusion.4
  62.5 4.1 %fusion.26 = f32[322,1536]{1,0:T(8,128)S(1)} fusion(bf16[1536,1536]{1,0:T(8,128)(2,1)} %constant_dynamic-update-slice_fusion.4, bf16[322,384]{1,0:T(8,128)(2,1)S(1)} %get-tuple-element.11, bf16[322,384]{1,0:T(8,128)(2,1)S(1)} %get-tuple-element.12, bf16[322,384]{1,0:T(8,128)(2,1)S(1)} %get-tuple-element.13, bf16[322,384]{1,0:T(8,128)(2,1)S(1)} %get-tuple-element.10), kind=kOutput, calls=%fused_computation.47 | convolution fusion | flops 1523343360 | bytes 7686144 | tf_op jit(solution)/shard_map/dot_general | solution.py:135
  66.6 0.7 multiply_reduce_fusion.6
  67.3 1.4 %multiply_reduce_fusion.3 = (f32[320]{0:T(512)S(1)}, f32[320,1536]{1,0:T(8,128)}) fusion(f32[322,1536]{1,0:T(8,128)S(1)} %fusion.26), kind=kLoop, calls=%fused_computation.20 | loop fusion | flops 982720 | bytes 3933440 | tf_op jit(solution)/shard_map/reduce_sum | solution.py:78
  68.9 1.7 %fusion.27 = f32[322,1536]{1,0:T(8,128)S(1)} fusion(bf16[1536,1536]{1,0:T(8,128)(2,1)S(1)} %constant_dynamic-update-slice_fusion, bf16[322,384]{1,0:T(8,128)(2,1)S(1)} %get-tuple-element.11, bf16[322,384]{1,0:T(8,128)(2,1)S(1)} %get-tuple-element.12, bf16[322,384]{1,0:T(8,128)(2,1)S(1)} %get-tuple-element.13, bf16[322,384]{1,0:T(8,128)(2,1)S(1)} %get-tuple-element.10), kind=kOutput, calls=%fused_computation.48 | convolution fusion | flops 1523343360 | bytes 7686144 | tf_op jit(solution)/shard_map/dot_general | solution.py:134
  71.0 1.4 %copy-done.2 = f32[322,1536]{1,0:T(8,128)} copy-done((f32[322,1536]{1,0:T(8,128)}, f32[322,1536]{1,0:T(8,128)S(1)}, u32[]{:S(2)}) %copy-start.2) | copy-done | bytes 1978392
  72.4 0.6 multiply_reduce_fusion.5
  73.7 1.9 %slice_multiply_fusion.1 = f32[319,1536]{1,0:T(8,128)S(1)} fusion(f32[320,1536]{1,0:T(8,128)} %get-tuple-element.9, f32[319]{0:T(512)S(1)} %bitcast.73), kind=kLoop, calls=%fused_computation.12 | loop fusion | flops 489984 | bytes 3921148 | tf_op jit(solution)/shard_map/mul | solution.py:79
  75.9 0.7 multiply_reduce_fusion.2
  76.6 1.7 %multiply_reduce_fusion = (f32[320]{0:T(512)S(1)}, f32[320,1536]{1,0:T(8,128)}) fusion(f32[319,1536]{1,0:T(8,128)S(1)} %slice_multiply_fusion.1, f32[1,1536]{1,0:T(1,128)S(1)} %slice_multiply_fusion.10, f32[320]{0:T(512)S(1)} %get-tuple-element.21, f32[322,1536]{1,0:T(8,128)S(1)} %copy-done.3), kind=kLoop, calls=%fused_computation.15 | loop fusion | flops 1965760 | bytes 5900800 | tf_op jit(solution)/shard_map/reduce_sum | solution.py:143
  78.3 1.2 %fusion.6 = f32[128,1536]{1,0:T(8,128)S(1)} fusion(bf16[1,320,1536]{2,1,0:T(8,128)(2,1)S(1)} %copy-done.6, f32[320]{0:T(512)S(1)} %subtract_select_fusion, s32[320]{0:T(512)S(1)} %broadcast_add_fusion), kind=kOutput, calls=%fused_computation.10 | convolution fusion | flops 755998720 | bytes 1772032 | tf_op jit(solution)/shard_map/dot_general | solution.py:147
  79.5 0.9 fusion.8
  80.4 0.5 convolution_reduce_fusion
  81.0 0.6 pad_maximum_fusion.10
  81.5 1.3 %collective-permute-start.17 = (f32[1,1537]{1,0:T(1,128)S(1)}, f32[1,1537]{1,0:T(1,128)S(1)}, u32[]{:S(2)}, u32[]{:S(2)}) collective-permute-start(f32[1,1537]{1,0:T(1,128)S(1)} %pad_maximum_fusion.10), channel_id=1, source_target_pairs={{28,0},{29,1},{30,2},{31,3}} | collective-permute-start | bytes 18452 | tf_op jit(solution)/shard_map/ppermute | solution.py:16
  82.8 1.3 %collective-permute-start.16 = (f32[1,1537]{1,0:T(1,128)S(1)}, f32[1,1537]{1,0:T(1,128)S(1)}, u32[]{:S(2)}, u32[]{:S(2)}) collective-permute-start(f32[1,1537]{1,0:T(1,128)S(1)} %pad_maximum_fusion.10), channel_id=1, source_target_pairs={{24,0},{28,4},{25,1},{29,5},{26,2},{30,6},{27,3},{31,7}} | collective-permute-start | bytes 18452 | tf_op jit(solution)/shard_map/ppermute | solution.py:16
  84.1 1.3 %collective-permute-start.15 = (f32[1,1537]{1,0:T(1,128)S(1)}, f32[1,1537]{1,0:T(1,128)S(1)}, u32[]{:S(2)}, u32[]{:S(2)}) collective-permute-start(f32[1,1537]{1,0:T(1,128)S(1)} %pad_maximum_fusion.10), channel_id=1, source_target_pairs={{20,0},{24,4},{28,8},{21,1},{25,5},{29,9},{22,2},{26,6},{30,10},{2... | collective-permute-start | bytes 18452 | tf_op jit(solution)/shard_map/ppermute | solution.py:16
  85.4 1.3 %collective-permute-start.12 = (f32[1,1537]{1,0:T(1,128)S(1)}, f32[1,1537]{1,0:T(1,128)S(1)}, u32[]{:S(2)}, u32[]{:S(2)}) collective-permute-start(f32[1,1537]{1,0:T(1,128)S(1)} %pad_maximum_fusion.10), channel_id=1, source_target_pairs={{8,0},{12,4},{16,8},{20,12},{24,16},{28,20},{9,1},{13,5},{17,9},{2... | collective-permute-start | bytes 18452 | tf_op jit(solution)/shard_map/ppermute | solution.py:16
  86.7 1.5 %collective-permute-start.11 = (f32[1,1537]{1,0:T(1,128)S(1)}, f32[1,1537]{1,0:T(1,128)S(1)}, u32[]{:S(2)}, u32[]{:S(2)}) collective-permute-start(f32[1,1537]{1,0:T(1,128)S(1)} %pad_maximum_fusion.10), channel_id=1, source_target_pairs={{4,0},{8,4},{12,8},{16,12},{20,16},{24,20},{28,24},{5,1},{9,5},{13... | collective-permute-start | bytes 18452 | tf_op jit(solution)/shard_map/ppermute | solution.py:16
  88.9 1.5 %multiply_multiply_fusion = f32[1,1536]{1,0:T(1,128)S(1)} fusion(f32[322,1536]{1,0:T(8,128)} %copy-done.2, f32[]{:T(128)S(6)} %rsqrt.33, f32[]{:T(128)} %bitcast.14), kind=kLoop, calls=%fused_computation.95 | loop fusion | flops 3072 | bytes 12296 | tf_op jit(solution)/shard_map/mul | solution.py:163
  90.4 1.9 %slice_multiply_fusion = f32[319,1536]{1,0:T(8,128)S(1)} fusion(f32[320,1536]{1,0:T(8,128)} %get-tuple-element.5, f32[319]{0:T(512)S(1)} %slice.161), kind=kLoop, calls=%fused_computation.11 | loop fusion | flops 489984 | bytes 3921148 | tf_op jit(solution)/shard_map/mul | solution.py:161
  92.8 4.3 %fusion.9 = f32[320,1536]{1,0:T(8,128)S(1)} fusion(bf16[1536,1536]{1,0:T(8,128)(2,1)} %constant_dynamic-update-slice_fusion.4, f32[1,1536]{1,0:T(1,128)S(1)} %multiply_multiply_fusion, f32[319,1536]{1,0:T(8,128)S(1)} %slice_multiply_fusion, f32[320]{0:T(512)S(1)} %fusion.49, f32[320]{0:T(512)S(1)} %add_rsqrt_fusion, f32[322,1536]{1,0:T(8,128)S(1)} %copy-done.1), kind=kOutput, calls=%fused_computation.28 | convolution fusion | flops 1512407040 | bytes 10627072 | tf_op jit(solution)/shard_map/dot_general | solution.py:168
  97.2 1.9 %fusion.1 = bf16[320,1536]{1,0:T(8,128)(2,1)S(1)} fusion(f32[320,1536]{1,0:T(8,128)S(1)} %fusion.9, bf16[1536,1536]{1,0:T(8,128)(2,1)S(1)} %bitcast.72, f32[322,1536]{1,0:T(8,128)S(1)} %copy-done.4, f32[319,1536]{1,0:T(8,128)S(1)} %slice_multiply_fusion.1, f32[1,1536]{1,0:T(1,128)S(1)} %slice_multiply_fusion.10, f32[320]{0:T(512)S(1)} %get-tuple-element.20, ...), kind=kOutput, calls=%fused_computation.3 | convolution fusion | flops 1513881600 | bytes 11612160 | tf_op jit(solution)/shard_map/dot_general | solution.py:165
  99.3 1.3 %collective-permute-start.14 = (f32[1,1537]{1,0:T(1,128)S(1)}, f32[1,1537]{1,0:T(1,128)S(1)}, u32[]{:S(2)}, u32[]{:S(2)}) collective-permute-start(f32[1,1537]{1,0:T(1,128)S(1)} %pad_maximum_fusion.10), channel_id=1, source_target_pairs={{16,0},{20,4},{24,8},{28,12},{17,1},{21,5},{25,9},{29,13},{18,2},{... | collective-permute-start | bytes 18452 | tf_op jit(solution)/shard_map/ppermute | solution.py:16
  100.6 1.3 %collective-permute-start.13 = (f32[1,1537]{1,0:T(1,128)S(1)}, f32[1,1537]{1,0:T(1,128)S(1)}, u32[]{:S(2)}, u32[]{:S(2)}) collective-permute-start(f32[1,1537]{1,0:T(1,128)S(1)} %pad_maximum_fusion.10), channel_id=1, source_target_pairs={{12,0},{16,4},{20,8},{24,12},{28,16},{13,1},{17,5},{21,9},{25,13},... | collective-permute-start | bytes 18452 | tf_op jit(solution)/shard_map/ppermute | solution.py:16
  101.9 1.0 maximum_bitcast_fusion
  102.9 0.5 slice.166
  104.1 0.5 slice.168
  105.9 2.9 %collective-permute-done.13 = f32[1,1537]{1,0:T(1,128)S(1)} collective-permute-done((f32[1,1537]{1,0:T(1,128)S(1)}, f32[1,1537]{1,0:T(1,128)S(1)}, u32[]{:S(2)}, u32[]{:S(2)}) %collective-permute-start.13) | collective-permute-done | bytes 6180 | tf_op jit(solution)/shard_map/ppermute | solution.py:16
  108.8 0.5 slice.170
  110.0 0.5 slice.172
  111.2 0.5 slice.174
  112.5 0.5 slice.176
  113.7 1.7 %fusion.4 = bf16[1,128,1536]{2,1,0:T(8,128)(2,1)} fusion(f32[128,1536]{1,0:T(8,128)S(1)} %fusion.6, f32[1536]{0:T(1024)S(1)} %fusion.47, f32[128]{0:T(128)S(1)} %get-tuple-element.22, f32[128]{0:T(128)S(1)} %bitcast_select_fusion, f32[128]{0:T(128)S(1)} %reduce.2), kind=kOutput, calls=%fused_computation.8 | convolution fusion | flops 302841856 | bytes 1187328 | tf_op jit(solution)/shard_map/dot_general | solution.py:156
  (81 shorter events, 3.5 us)
Async XLA Ops:
  0.6 18.4 %copy-start.7 = (bf16[384,1536]{1,0:T(8,128)(2,1)S(1)}, bf16[384,1536]{1,0:T(8,128)(2,1)}, u32[]{:S(2)}) copy-start(bf16[384,1536]{1,0:T(8,128)(2,1)} %param.15) | copy-start | bytes 3538948
  0.6 19.5 %copy-start.8 = (bf16[384,1536]{1,0:T(8,128)(2,1)S(1)}, bf16[384,1536]{1,0:T(8,128)(2,1)}, u32[]{:S(2)}) copy-start(bf16[384,1536]{1,0:T(8,128)(2,1)} %param.14) | copy-start | bytes 3538948
  0.7 47.9 %collective-permute-start.8 = (bf16[384,1536]{1,0:T(8,128)(2,1)}, bf16[384,1536]{1,0:T(8,128)(2,1)}, u32[]{:S(2)}, u32[]{:S(2)}) collective-permute-start(bf16[384,1536]{1,0:T(8,128)(2,1)} %param.15), channel_id=1, source_target_pairs={{0,2},{1,3},{2,0},{3,1},{4,6},{5,7},{6,4},{7,5},{8,10},{9,11},{10,... | collective-permute-start | bytes 3538952 | tf_op jit(solution)/shard_map/ppermute | solution.py:50
  3.7 55.3 %collective-permute-start.9 = (bf16[384,1536]{1,0:T(8,128)(2,1)}, bf16[384,1536]{1,0:T(8,128)(2,1)}, u32[]{:S(2)}, u32[]{:S(2)}) collective-permute-start(bf16[384,1536]{1,0:T(8,128)(2,1)} %param.15), channel_id=1, source_target_pairs={{0,1},{1,0},{2,3},{3,2},{4,5},{5,4},{6,7},{7,6},{8,9},{9,8},{10,11... | collective-permute-start | bytes 3538952 | tf_op jit(solution)/shard_map/ppermute | solution.py:53
  3.7 51.6 %collective-permute-start.5 = (bf16[384,1536]{1,0:T(8,128)(2,1)}, bf16[384,1536]{1,0:T(8,128)(2,1)}, u32[]{:S(2)}, u32[]{:S(2)}) collective-permute-start(bf16[384,1536]{1,0:T(8,128)(2,1)} %param.14), channel_id=1, source_target_pairs={{0,2},{1,3},{2,0},{3,1},{4,6},{5,7},{6,4},{7,5},{8,10},{9,11},{10,... | collective-permute-start | bytes 3538952 | tf_op jit(solution)/shard_map/ppermute | solution.py:50
  10.9 12.0 %collective-permute-start.1 = (f32[1,1537]{1,0:T(1,128)S(1)}, f32[1,1537]{1,0:T(1,128)S(1)}, u32[]{:S(2)}, u32[]{:S(2)}) collective-permute-start(f32[1,1537]{1,0:T(1,128)S(1)} %pad_maximum_fusion.6), channel_id=1, source_target_pairs={{0,4},{4,8},{8,12},{12,16},{16,20},{20,24},{24,28},{1,5},{5,9},{9,... | collective-permute-start | bytes 18452 | tf_op jit(solution)/shard_map/ppermute | solution.py:16
  15.4 5.9 %copy-start.12 = (s32[1,128]{1,0:T(1,128)S(1)}, s32[1,128]{1,0:T(1,128)}, u32[]{:S(2)}) copy-start(s32[1,128]{1,0:T(1,128)} %param.11) | copy-start | bytes 1540
  15.4 23.2 %copy-start.5 = (bf16[1,320,1536]{2,1,0:T(8,128)(2,1)S(1)}, bf16[1,320,1536]{2,1,0:T(8,128)(2,1)}, u32[]{:S(2)}) copy-start(bf16[1,320,1536]{2,1,0:T(8,128)(2,1)} %param.9) | copy-start | bytes 2949124
  15.4 33.0 %collective-permute-start = (bf16[1,1536]{1,0:T(2,128)(2,1)S(1)}, bf16[1,1536]{1,0:T(2,128)(2,1)S(1)}, u32[]{:S(2)}, u32[]{:S(2)}) collective-permute-start(bf16[1,1536]{1,0:T(2,128)(2,1)S(1)} %get-tuple-element.18), channel_id=1, source_target_pairs={{0,4},{4,8},{8,12},{12,16},{16,20},{20,24},{24,28},{1,5},{5,9},{9,... | collective-permute-start | bytes 9224 | tf_op jit(solution)/shard_map/ppermute | solution.py:16
  21.2 27.2 %copy-start.9 = (bf16[1,320,1536]{2,1,0:T(8,128)(2,1)S(1)}, bf16[1,320,1536]{2,1,0:T(8,128)(2,1)}, u32[]{:S(2)}) copy-start(bf16[1,320,1536]{2,1,0:T(8,128)(2,1)} %param.8) | copy-start | bytes 2949124
  25.4 4.8 %collective-permute-start.2 = (f32[1,1537]{1,0:T(1,128)S(1)}, f32[1,1537]{1,0:T(1,128)S(1)}, u32[]{:S(2)}, u32[]{:S(2)}) collective-permute-start(f32[1,1537]{1,0:T(1,128)S(1)} %pad_maximum_fusion.7), channel_id=1, source_target_pairs={{0,8},{4,12},{8,16},{12,20},{16,24},{20,28},{1,9},{5,13},{9,17},{1... | collective-permute-start | bytes 18452 | tf_op jit(solution)/shard_map/ppermute | solution.py:16
  31.3 7.2 %collective-permute-start.3 = (f32[1,1537]{1,0:T(1,128)S(1)}, f32[1,1537]{1,0:T(1,128)S(1)}, u32[]{:S(2)}, u32[]{:S(2)}) collective-permute-start(f32[1,1537]{1,0:T(1,128)S(1)} %pad_maximum_fusion.8), channel_id=1, source_target_pairs={{0,16},{4,20},{8,24},{12,28},{1,17},{5,21},{9,25},{13,29},{2,18},{... | collective-permute-start | bytes 18452 | tf_op jit(solution)/shard_map/ppermute | solution.py:16
  42.4 5.5 %collective-permute-start.4 = (f32[1,1537]{1,0:T(1,128)S(1)}, f32[1,1537]{1,0:T(1,128)S(1)}, u32[]{:S(2)}, u32[]{:S(2)}) collective-permute-start(f32[1,1537]{1,0:T(1,128)S(1)} %pad_maximum_fusion.9), channel_id=1, source_target_pairs={{4,0},{8,4},{12,8},{16,12},{20,16},{24,20},{28,24},{5,1},{9,5},{13... | collective-permute-start | bytes 18452 | tf_op jit(solution)/shard_map/ppermute | solution.py:16
  47.9 13.5 %collective-permute-start.6 = (bf16[384,1536]{1,0:T(8,128)(2,1)S(1)}, bf16[384,1536]{1,0:T(8,128)(2,1)S(1)}, u32[]{:S(2)}, u32[]{:S(2)}) collective-permute-start(bf16[384,1536]{1,0:T(8,128)(2,1)S(1)} %copy-done.8), channel_id=1, source_target_pairs={{0,1},{1,0},{2,3},{3,2},{4,5},{5,4},{6,7},{7,6},{8,9},{9,8},{10,11... | collective-permute-start | bytes 3538952 | tf_op jit(solution)/shard_map/ppermute | solution.py:53
  48.5 9.2 %copy-start.10 = (bf16[1536,1536]{1,0:T(8,128)(2,1)S(1)}, bf16[1536,1536]{1,0:T(8,128)(2,1)}, u32[]{:S(2)}) copy-start(bf16[1536,1536]{1,0:T(8,128)(2,1)} %constant_dynamic-update-slice_fusion.3) | copy-start | bytes 14155780
  48.6 12.9 %collective-permute-start.10 = (bf16[384,1536]{1,0:T(8,128)(2,1)}, bf16[384,1536]{1,0:T(8,128)(2,1)S(1)}, u32[]{:S(2)}, u32[]{:S(2)}) collective-permute-start(bf16[384,1536]{1,0:T(8,128)(2,1)} %collective-permute-done.8), channel_id=1, source_target_pairs={{0,1},{1,0},{2,3},{3,2},{4,5},{5,4},{6,7},{7,6},{8,9},{9,8},{10,11... | collective-permute-start | bytes 3538952 | tf_op jit(solution)/shard_map/ppermute | solution.py:53
  55.2 13.5 %collective-permute-start.7 = (bf16[384,1536]{1,0:T(8,128)(2,1)}, bf16[384,1536]{1,0:T(8,128)(2,1)S(1)}, u32[]{:S(2)}, u32[]{:S(2)}) collective-permute-start(bf16[384,1536]{1,0:T(8,128)(2,1)} %collective-permute-done.5), channel_id=1, source_target_pairs={{0,1},{1,0},{2,3},{3,2},{4,5},{5,4},{6,7},{7,6},{8,9},{9,8},{10,11... | collective-permute-start | bytes 3538952 | tf_op jit(solution)/shard_map/ppermute | solution.py:53
  66.6 7.1 %copy-start = (f32[322,1536]{1,0:T(8,128)}, f32[322,1536]{1,0:T(8,128)S(1)}, u32[]{:S(2)}) copy-start(f32[322,1536]{1,0:T(8,128)S(1)} %fusion.26) | copy-start | bytes 5935108
  68.8 2.2 %copy-start.11 = (bf16[1536,1536]{1,0:T(8,128)(2,1)}, bf16[1536,1536]{1,0:T(8,128)(2,1)S(1)}, u32[]{:S(2)}) copy-start(bf16[1536,1536]{1,0:T(8,128)(2,1)S(1)} %constant_dynamic-update-slice_fusion) | copy-start | bytes 14155780
  71.0 1.4 %copy-start.2 = (f32[322,1536]{1,0:T(8,128)}, f32[322,1536]{1,0:T(8,128)S(1)}, u32[]{:S(2)}) copy-start(f32[322,1536]{1,0:T(8,128)S(1)} %fusion.27) | copy-start | bytes 5935108
  73.7 2.2 %copy-start.3 = (f32[322,1536]{1,0:T(8,128)S(1)}, f32[322,1536]{1,0:T(8,128)}, u32[]{:S(2)}) copy-start(f32[322,1536]{1,0:T(8,128)} %copy-done.2) | copy-start | bytes 5935108
  76.6 1.7 %copy-start.6 = (bf16[1,320,1536]{2,1,0:T(8,128)(2,1)S(1)}, bf16[1,320,1536]{2,1,0:T(8,128)(2,1)}, u32[]{:S(2)}) copy-start(bf16[1,320,1536]{2,1,0:T(8,128)(2,1)} %param.9) | copy-start | bytes 2949124
  81.5 32.1 %collective-permute-start.17 = (f32[1,1537]{1,0:T(1,128)S(1)}, f32[1,1537]{1,0:T(1,128)S(1)}, u32[]{:S(2)}, u32[]{:S(2)}) collective-permute-start(f32[1,1537]{1,0:T(1,128)S(1)} %pad_maximum_fusion.10), channel_id=1, source_target_pairs={{28,0},{29,1},{30,2},{31,3}} | collective-permute-start | bytes 18452 | tf_op jit(solution)/shard_map/ppermute | solution.py:16
  82.8 29.6 %collective-permute-start.16 = (f32[1,1537]{1,0:T(1,128)S(1)}, f32[1,1537]{1,0:T(1,128)S(1)}, u32[]{:S(2)}, u32[]{:S(2)}) collective-permute-start(f32[1,1537]{1,0:T(1,128)S(1)} %pad_maximum_fusion.10), channel_id=1, source_target_pairs={{24,0},{28,4},{25,1},{29,5},{26,2},{30,6},{27,3},{31,7}} | collective-permute-start | bytes 18452 | tf_op jit(solution)/shard_map/ppermute | solution.py:16
  84.1 27.1 %collective-permute-start.15 = (f32[1,1537]{1,0:T(1,128)S(1)}, f32[1,1537]{1,0:T(1,128)S(1)}, u32[]{:S(2)}, u32[]{:S(2)}) collective-permute-start(f32[1,1537]{1,0:T(1,128)S(1)} %pad_maximum_fusion.10), channel_id=1, source_target_pairs={{20,0},{24,4},{28,8},{21,1},{25,5},{29,9},{22,2},{26,6},{30,10},{2... | collective-permute-start | bytes 18452 | tf_op jit(solution)/shard_map/ppermute | solution.py:16
  85.4 13.8 %collective-permute-start.12 = (f32[1,1537]{1,0:T(1,128)S(1)}, f32[1,1537]{1,0:T(1,128)S(1)}, u32[]{:S(2)}, u32[]{:S(2)}) collective-permute-start(f32[1,1537]{1,0:T(1,128)S(1)} %pad_maximum_fusion.10), channel_id=1, source_target_pairs={{8,0},{12,4},{16,8},{20,12},{24,16},{28,20},{9,1},{13,5},{17,9},{2... | collective-permute-start | bytes 18452 | tf_op jit(solution)/shard_map/ppermute | solution.py:16
  86.7 13.8 %collective-permute-start.11 = (f32[1,1537]{1,0:T(1,128)S(1)}, f32[1,1537]{1,0:T(1,128)S(1)}, u32[]{:S(2)}, u32[]{:S(2)}) collective-permute-start(f32[1,1537]{1,0:T(1,128)S(1)} %pad_maximum_fusion.10), channel_id=1, source_target_pairs={{4,0},{8,4},{12,8},{16,12},{20,16},{24,20},{28,24},{5,1},{9,5},{13... | collective-permute-start | bytes 18452 | tf_op jit(solution)/shard_map/ppermute | solution.py:16
  90.4 2.2 %copy-start.1 = (f32[322,1536]{1,0:T(8,128)S(1)}, f32[322,1536]{1,0:T(8,128)}, u32[]{:S(2)}) copy-start(f32[322,1536]{1,0:T(8,128)} %copy-done) | copy-start | bytes 5935108
  92.5 4.7 %slice-start = ((s8[4718592]{0:T(1024)(128)(4,1)}), s8[4194304]{0:T(1024)(128)(4,1)S(1)}, s32[]{:S(2)}) async-start(s8[4718592]{0:T(1024)(128)(4,1)} %bitcast.71), calls=%async_computation | async-start | bytes 8388608
  92.8 4.4 %copy-start.4 = (f32[322,1536]{1,0:T(8,128)S(1)}, f32[322,1536]{1,0:T(8,128)}, u32[]{:S(2)}) copy-start(f32[322,1536]{1,0:T(8,128)} %copy-done.2) | copy-start | bytes 5935108
  92.8 4.4 %slice-start.1 = ((s8[4718592]{0:T(1024)(128)(4,1)}), s8[524288]{0:T(1024)(128)(4,1)S(1)}, s32[]{:S(2)}) async-start(s8[4718592]{0:T(1024)(128)(4,1)} %bitcast.71), calls=%async_computation.1 | async-start | bytes 1048576
  99.3 10.8 %collective-permute-start.14 = (f32[1,1537]{1,0:T(1,128)S(1)}, f32[1,1537]{1,0:T(1,128)S(1)}, u32[]{:S(2)}, u32[]{:S(2)}) collective-permute-start(f32[1,1537]{1,0:T(1,128)S(1)} %pad_maximum_fusion.10), channel_id=1, source_target_pairs={{16,0},{20,4},{24,8},{28,12},{17,1},{21,5},{25,9},{29,13},{18,2},{... | collective-permute-start | bytes 18452 | tf_op jit(solution)/shard_map/ppermute | solution.py:16
  100.6 8.2 %collective-permute-start.13 = (f32[1,1537]{1,0:T(1,128)S(1)}, f32[1,1537]{1,0:T(1,128)S(1)}, u32[]{:S(2)}, u32[]{:S(2)}) collective-permute-start(f32[1,1537]{1,0:T(1,128)S(1)} %pad_maximum_fusion.10), channel_id=1, source_target_pairs={{12,0},{16,4},{20,8},{24,12},{28,16},{13,1},{17,5},{21,9},{25,13},... | collective-permute-start | bytes 18452 | tf_op jit(solution)/shard_map/ppermute | solution.py:16

commit v5 on v4

--- a/solution.py
+++ b/solution.py
@@ -40,14 +40,24 @@
     return excl_vec
 
 
-def gather_blocks(blocks, axis):
+def gather_blocks(blocks, axis, pair_axis):
     size = lax.axis_size(axis)
     own = lax.axis_index(axis)
+    side = lax.axis_index(pair_axis) % 2
+    cols = blocks[0].shape[1] // 2
+    halves = tuple(lax.dynamic_slice_in_dim(b, side * cols, cols, axis=1) for b in blocks)
+    swap_pair = [(i, i ^ 1) for i in range(lax.axis_size(pair_axis))]
     pairs = [blocks]
     index = [own]
     for k in range(1, size // 2):
         route = [(i, (i + 2 * k) % size) for i in range(size)]
-        pairs.append(lax.ppermute(blocks, axis, route))
+        fetched = lax.ppermute(halves, axis, route)
+        other = lax.ppermute(fetched, pair_axis, swap_pair)
+        whole = tuple(
+            jnp.where(side == 0, jnp.concatenate([a, b], axis=1), jnp.concatenate([b, a], axis=1))
+            for a, b in zip(fetched, other)
+        )
+        pairs.append(whole)
         index.append((own - 2 * k) % size)
     swap = [(i, i ^ 1) for i in range(size)]
     partner = lax.ppermute(pairs, axis, swap)
@@ -95,7 +105,7 @@
     slot_count = segment_states.shape[1]
     width = query_weight.shape[0]
     shard_index = lax.axis_index("seq")
-    pairs, index = gather_blocks((query_weight, key_weight), "dp")
+    pairs, index = gather_blocks((query_weight, key_weight), "dp", "seq")
     full_query = jnp.concatenate([p[0] for p in pairs], axis=0)
     full_key = jnp.concatenate([p[1] for p in pairs], axis=0)
     position = jnp.arange(token_count)

time: 117 us -> 126 us (1.077)
  waiting for transfers between devices: 11.2 us -> 24.7 us
  local copies, waits for them, and re-layouts: 19.3 us -> 14.2 us
  matrix products: 21.7 us -> 18.3 us
  starting transfers between devices: 30.3 us -> 32.6 us
  other arithmetic: 18 us -> 20.1 us
    ppermute x12, waiting for transfers between devices: 5.17 us -> 13.1 us  [shifted(): return lax.ppermute(block, axis, route)]
    unnamed x36 -> x44, local copies, waits for them, and re-layouts: 10.7 us -> 3.32 us
    ppermute x2 -> x4, waiting for transfers between devices: 6.03 us -> 11.6 us  [the longest x2 6.09 us: gather_blocks(): fetched = lax.ppermute(halves, axis, route)]
    dynamic_slice x0 -> x2, local copies, waits for them, and re-layouts: none -> 3.97 us  [gather_blocks(): lax.dynamic_slice_in_dim(b, side * cols, cols, axis=1)]
    select_n x0 -> x2, other arithmetic: none -> 3.52 us  [gather_blocks(): jnp.where(side == 0, jnp.concatenate([a, b], axis=1), jnp.concatenate([b,...]
    ppermute x2 -> x4, starting transfers between devices: 3.19 us -> 6.49 us  [the longest x2 3.47 us: gather_blocks(): fetched = lax.ppermute(halves, axis, route)]
  transfers between devices with their start and end apart: 18 -> 20, of which waited for: 4 -> 5; matrix products, arithmetic and copies ran while one was open for 39% -> 28% of each run, Pallas kernels for 0% -> 0%
where the time goes in v5:
time: 126 us; the launch traced here: 125 us
  starting transfers between devices  32.6 us (26%)
  waiting for transfers between devices  24.7 us (20%)
  other arithmetic  20.1 us (16%)
  matrix products  18.3 us (15%)
  between operations  15.2 us (12%)
  local copies, waits for them, and re-layouts  14.2 us (11%)
    ppermute x12, starting transfers between devices, shifted(): return lax.ppermute(block, axis, route)  25.3 us
    ppermute x12, waiting for transfers between devices, shifted(): return lax.ppermute(block, axis, route)  13.1 us
    ppermute x2, waiting for transfers between devices, gather_blocks(): fetched = lax.ppermute(halves, axis, route)  6.09 us
    ppermute x2, waiting for transfers between devices, gather_blocks(): other = lax.ppermute(fetched, pair_axis, swap_pair)  5.48 us
    dynamic_slice x2, local copies, waits for them, and re-layouts, gather_blocks(): lax.dynamic_slice_in_dim(b, side * cols, cols, axis=1)  3.97 us
    dot_general x1, matrix products, per_device(): lax.dot_general(key_grad, full_key, contract_last, preferred_element_type...  3.57 us
    select_n x2, other arithmetic, gather_blocks(): jnp.where(side == 0, jnp.concatenate([a, b], axis=1), jnp.concatenate([b,...  3.52 us
    ppermute x2, starting transfers between devices, gather_blocks(): fetched = lax.ppermute(halves, axis, route)  3.47 us
  transfers between devices with their start and end apart: 20, of which 5 were waited for; matrix products, arithmetic and copies ran while one was open for 28% of the time, Pallas kernels for 0%

profile of v5, /device:TPU:0, one launch (start us, length us, event | category | flops | bytes accessed | tf_op | source)
XLA Modules:
  0.0 125.1 jit_solution(12119831250439657841)
XLA Ops:
  0.7 2.1 %constant_dynamic-slice_fusion.5 = bf16[384,768]{1,0:T(8,128)(2,1)} fusion(bf16[384,1536]{1,0:T(8,128)(2,1)} %param.14, s32[]{:T(128)S(6)} %select_n.121), kind=kLoop, calls=%fused_computation.108 | loop fusion | bytes 1179652 | tf_op jit(solution)/shard_map/dynamic_slice | solution.py:48
  2.7 3.0 %collective-permute-start.5 = (bf16[384,768]{1,0:T(8,128)(2,1)}, bf16[384,768]{1,0:T(8,128)(2,1)}, u32[]{:S(2)}, u32[]{:S(2)}) collective-permute-start(bf16[384,768]{1,0:T(8,128)(2,1)} %constant_dynamic-slice_fusion.5), channel_id=1, source_target_pairs={{0,2},{1,3},{2,0},{3,1},{4,6},{5,7},{6,4},{7,5},{8,10},{9,11},{10,... | collective-permute-start | bytes 1769480 | tf_op jit(solution)/shard_map/ppermute | solution.py:54
  6.4 0.7 fusion.53
  7.3 0.6 slice.149
  7.9 0.7 bitcast_select_fusion
  8.6 1.9 %fusion.21 = f32[128,1536]{1,0:T(8,128)S(1)} fusion(bf16[1,128,1536]{2,1,0:T(8,128)(2,1)} %param.10, f32[128]{0:T(128)S(1)} %bitcast_select_fusion, f32[128]{0:T(128)S(1)} %reduce.2), kind=kOutput, calls=%fused_computation.46 | convolution fusion | flops 302448640 | bytes 1180672 | tf_op jit(solution)/shard_map/dot_general | solution.py:129
  10.5 0.6 pad_maximum_fusion.12
  11.2 3.4 %collective-permute-start.1 = (f32[1,1537]{1,0:T(1,128)S(1)}, f32[1,1537]{1,0:T(1,128)S(1)}, u32[]{:S(2)}, u32[]{:S(2)}) collective-permute-start(f32[1,1537]{1,0:T(1,128)S(1)} %pad_maximum_fusion.12), channel_id=1, source_target_pairs={{0,4},{4,8},{8,12},{12,16},{16,20},{20,24},{24,28},{1,5},{5,9},{9,... | collective-permute-start | bytes 18452 | tf_op jit(solution)/shard_map/ppermute | solution.py:16
  14.6 3.5 %collective-permute-start = (bf16[1,1536]{1,0:T(2,128)(2,1)S(1)}, bf16[1,1536]{1,0:T(2,128)(2,1)S(1)}, u32[]{:S(2)}, u32[]{:S(2)}) collective-permute-start(bf16[1,1536]{1,0:T(2,128)(2,1)S(1)} %get-tuple-element.18), channel_id=1, source_target_pairs={{0,4},{4,8},{8,12},{12,16},{16,20},{20,24},{24,28},{1,5},{5,9},{9,... | collective-permute-start | bytes 9224 | tf_op jit(solution)/shard_map/ppermute | solution.py:16
  18.1 1.9 %constant_dynamic-slice_fusion.4 = bf16[384,768]{1,0:T(8,128)(2,1)} fusion(bf16[384,1536]{1,0:T(8,128)(2,1)} %param.15, s32[]{:T(128)S(6)} %select_n.121), kind=kLoop, calls=%fused_computation.107 | loop fusion | bytes 1179652 | tf_op jit(solution)/shard_map/dynamic_slice | solution.py:48
  20.1 0.5 collective-permute-start.9
  20.7 0.6 subtract_exponential_fusion
  22.2 0.5 slice.150
  24.0 3.5 %collective-permute-start.2 = (f32[1,1537]{1,0:T(1,128)S(1)}, f32[1,1537]{1,0:T(1,128)S(1)}, u32[]{:S(2)}, u32[]{:S(2)}) collective-permute-start(f32[1,1537]{1,0:T(1,128)S(1)} %pad_maximum_fusion.13), channel_id=1, source_target_pairs={{0,8},{4,12},{8,16},{12,20},{16,24},{20,28},{1,9},{5,13},{9,17},{1... | collective-permute-start | bytes 18452 | tf_op jit(solution)/shard_map/ppermute | solution.py:16
  27.6 1.2 collective-permute-done.2
  29.9 6.1 %collective-permute-done.9 = bf16[384,768]{1,0:T(8,128)(2,1)S(1)} collective-permute-done((bf16[384,768]{1,0:T(8,128)(2,1)}, bf16[384,768]{1,0:T(8,128)(2,1)S(1)}, u32[]{:S(2)}, u32[]{:S(2)}) %collective-permute-start.9) | collective-permute-done | bytes 589856 | tf_op jit(solution)/shard_map/ppermute | solution.py:54
  36.0 1.5 %collective-permute-start.10 = (bf16[384,768]{1,0:T(8,128)(2,1)S(1)}, bf16[384,768]{1,0:T(8,128)(2,1)}, u32[]{:S(2)}, u32[]{:S(2)}) collective-permute-start(bf16[384,768]{1,0:T(8,128)(2,1)S(1)} %collective-permute-done.9), channel_id=1, source_target_pairs={{0,4},{4,0},{8,12},{12,8},{16,20},{20,16},{24,28},{28,24},{1,5},{5... | collective-permute-start | bytes 1769480 | tf_op jit(solution)/shard_map/ppermute | solution.py:55
  37.5 4.5 %collective-permute-start.3 = (f32[1,1537]{1,0:T(1,128)S(1)}, f32[1,1537]{1,0:T(1,128)S(1)}, u32[]{:S(2)}, u32[]{:S(2)}) collective-permute-start(f32[1,1537]{1,0:T(1,128)S(1)} %pad_maximum_fusion.14), channel_id=1, source_target_pairs={{0,16},{4,20},{8,24},{12,28},{1,17},{5,21},{9,25},{13,29},{2,18},{... | collective-permute-start | bytes 18452 | tf_op jit(solution)/shard_map/ppermute | solution.py:16
  44.1 1.4 %fusion.7 = f32[320]{0:T(512)S(1)} fusion(bf16[1,320,1536]{2,1,0:T(8,128)(2,1)S(1)} %copy-done.5, f32[1536]{0:T(1024)S(1)} %fusion.46, f32[320]{0:T(512)S(1)} %get-tuple-element.6, f32[128,1536]{1,0:T(8,128)S(1)} %fusion.21, f32[128]{0:T(128)S(1)} %get-tuple-element.23, s32[320]{0:T(512)S(1)} %broadcast_add_fusion), kind=kOutput, calls=%fused_computation.25 | convolution fusion | flops 757866176 | bytes 1779968 | tf_op jit(solution)/shard_map/dot_general | solution.py:134
  45.6 5.5 %collective-permute-done.10 = bf16[384,768]{1,0:T(8,128)(2,1)} collective-permute-done((bf16[384,768]{1,0:T(8,128)(2,1)S(1)}, bf16[384,768]{1,0:T(8,128)(2,1)}, u32[]{:S(2)}, u32[]{:S(2)}) %collective-permute-start.10) | collective-permute-done | bytes 589856 | tf_op jit(solution)/shard_map/ppermute | solution.py:55
  51.0 1.9 %maximum_select_fusion.1 = bf16[384,1536]{1,0:T(8,128)(2,1)S(1)} fusion(bf16[384,768]{1,0:T(8,128)(2,1)} %collective-permute-done.10, bf16[384,768]{1,0:T(8,128)(2,1)} %copy-done.12, pred[]{:T(512)S(6)} %eq.58), kind=kLoop, calls=%fused_computation.27 | loop fusion | flops 5308416 | bytes 2359297 | tf_op jit(solution)/shard_map/jit(_where)/select_n | solution.py:57
  53.1 0.6 slice.122
  53.7 1.5 %collective-permute-start.6 = (bf16[384,768]{1,0:T(8,128)(2,1)}, bf16[384,768]{1,0:T(8,128)(2,1)S(1)}, u32[]{:S(2)}, u32[]{:S(2)}) collective-permute-start(bf16[384,768]{1,0:T(8,128)(2,1)} %collective-permute-done.5), channel_id=1, source_target_pairs={{0,4},{4,0},{8,12},{12,8},{16,20},{20,16},{24,28},{28,24},{1,5},{5... | collective-permute-start | bytes 1769480 | tf_op jit(solution)/shard_map/ppermute | solution.py:55
  55.2 0.7 pad_maximum_fusion.15
  55.9 1.3 %collective-permute-start.4 = (f32[1,1537]{1,0:T(1,128)S(1)}, f32[1,1537]{1,0:T(1,128)S(1)}, u32[]{:S(2)}, u32[]{:S(2)}) collective-permute-start(f32[1,1537]{1,0:T(1,128)S(1)} %pad_maximum_fusion.15), channel_id=1, source_target_pairs={{4,0},{8,4},{12,8},{16,12},{20,16},{24,20},{28,24},{5,1},{9,5},{13... | collective-permute-start | bytes 18452 | tf_op jit(solution)/shard_map/ppermute | solution.py:16
  57.2 0.7 fusion.65
  60.5 9.1 %collective-permute-done.4 = f32[1,1537]{1,0:T(1,128)S(1)} collective-permute-done((f32[1,1537]{1,0:T(1,128)S(1)}, f32[1,1537]{1,0:T(1,128)S(1)}, u32[]{:S(2)}, u32[]{:S(2)}) %collective-permute-start.4) | collective-permute-done | bytes 6180 | tf_op jit(solution)/shard_map/ppermute | solution.py:16
  69.7 0.5 slice.163
  70.3 1.6 %maximum_select_fusion = bf16[384,1536]{1,0:T(8,128)(2,1)S(1)} fusion(bf16[384,768]{1,0:T(8,128)(2,1)S(1)} %collective-permute-done.6, bf16[384,768]{1,0:T(8,128)(2,1)} %collective-permute-done.5, pred[]{:T(512)S(6)} %eq.58), kind=kLoop, calls=%fused_computation.26 | loop fusion | flops 5308416 | bytes 2359297 | tf_op jit(solution)/shard_map/jit(_where)/select_n | solution.py:57
  71.9 0.6 collective-permute-start.8
  72.6 3.4 %fusion.19 = f32[322,1536]{1,0:T(8,128)S(1)} fusion(bf16[384,1536]{1,0:T(8,128)(2,1)} %collective-permute-done.12, bf16[384,1536]{1,0:T(8,128)(2,1)} %collective-permute-done.11, bf16[384,1536]{1,0:T(8,128)(2,1)S(1)} %maximum_select_fusion.1, bf16[384,1536]{1,0:T(8,128)(2,1)S(1)} %copy-done.13, bf16[322,384]{1,0:T(8,128)(2,1)S(1)} %get-tuple-element.11, ...), kind=kOutput, calls=%fused_computation.43 | convolution fusion | flops 1542217728 | bytes 7686144 | tf_op jit(solution)/shard_map/dot_general | solution.py:145
  76.0 0.7 multiply_reduce_fusion.6
  76.7 1.5 %multiply_reduce_fusion.3 = (f32[320]{0:T(512)S(1)}, f32[320,1536]{1,0:T(8,128)}) fusion(f32[322,1536]{1,0:T(8,128)S(1)} %fusion.19), kind=kLoop, calls=%fused_computation.22 | loop fusion | flops 982720 | bytes 3933440 | tf_op jit(solution)/shard_map/reduce_sum | solution.py:88
  78.4 1.7 %fusion.20 = f32[322,1536]{1,0:T(8,128)S(1)} fusion(bf16[384,1536]{1,0:T(8,128)(2,1)S(1)} %collective-permute-done.8, bf16[384,1536]{1,0:T(8,128)(2,1)S(1)} %collective-permute-done.7, bf16[384,1536]{1,0:T(8,128)(2,1)S(1)} %maximum_select_fusion, bf16[384,1536]{1,0:T(8,128)(2,1)S(1)} %copy-done.15, bf16[322,384]{1,0:T(8,128)(2,1)S(1)} %get-tuple-element.11, ...), kind=kOutput, calls=%fused_computation.44 | convolution fusion | flops 1542217728 | bytes 7686144 | tf_op jit(solution)/shard_map/dot_general | solution.py:144
  80.2 1.3 %copy-done.2 = f32[322,1536]{1,0:T(8,128)} copy-done((f32[322,1536]{1,0:T(8,128)}, f32[322,1536]{1,0:T(8,128)S(1)}, u32[]{:S(2)}) %copy-start.2) | copy-done | bytes 1978392
  81.4 0.6 multiply_reduce_fusion.5
  82.7 1.9 %slice_multiply_fusion.1 = f32[319,1536]{1,0:T(8,128)S(1)} fusion(f32[320,1536]{1,0:T(8,128)} %get-tuple-element.9, f32[319]{0:T(512)S(1)} %bitcast.67), kind=kLoop, calls=%fused_computation.14 | loop fusion | flops 489984 | bytes 3921148 | tf_op jit(solution)/shard_map/mul | solution.py:89
  84.9 0.7 multiply_reduce_fusion.2
  85.5 1.7 %multiply_reduce_fusion = (f32[320]{0:T(512)S(1)}, f32[320,1536]{1,0:T(8,128)}) fusion(f32[319,1536]{1,0:T(8,128)S(1)} %slice_multiply_fusion.1, f32[1,1536]{1,0:T(1,128)S(1)} %slice_multiply_fusion.10, f32[320]{0:T(512)S(1)} %get-tuple-element.21, f32[322,1536]{1,0:T(8,128)S(1)} %copy-done.3), kind=kLoop, calls=%fused_computation.17 | loop fusion | flops 1965760 | bytes 5900800 | tf_op jit(solution)/shard_map/reduce_sum | solution.py:153
  87.3 1.2 fusion.6
  88.5 0.9 fusion.8
  89.4 0.5 convolution_reduce_fusion
  90.0 0.6 pad_maximum_fusion.16
  90.6 1.3 %collective-permute-start.19 = (f32[1,1537]{1,0:T(1,128)S(1)}, f32[1,1537]{1,0:T(1,128)S(1)}, u32[]{:S(2)}, u32[]{:S(2)}) collective-permute-start(f32[1,1537]{1,0:T(1,128)S(1)} %pad_maximum_fusion.16), channel_id=1, source_target_pairs={{28,0},{29,1},{30,2},{31,3}} | collective-permute-start | bytes 18452 | tf_op jit(solution)/shard_map/ppermute | solution.py:16
  91.9 1.3 %collective-permute-start.18 = (f32[1,1537]{1,0:T(1,128)S(1)}, f32[1,1537]{1,0:T(1,128)S(1)}, u32[]{:S(2)}, u32[]{:S(2)}) collective-permute-start(f32[1,1537]{1,0:T(1,128)S(1)} %pad_maximum_fusion.16), channel_id=1, source_target_pairs={{24,0},{28,4},{25,1},{29,5},{26,2},{30,6},{27,3},{31,7}} | collective-permute-start | bytes 18452 | tf_op jit(solution)/shard_map/ppermute | solution.py:16
  93.2 1.3 %collective-permute-start.17 = (f32[1,1537]{1,0:T(1,128)S(1)}, f32[1,1537]{1,0:T(1,128)S(1)}, u32[]{:S(2)}, u32[]{:S(2)}) collective-permute-start(f32[1,1537]{1,0:T(1,128)S(1)} %pad_maximum_fusion.16), channel_id=1, source_target_pairs={{20,0},{24,4},{28,8},{21,1},{25,5},{29,9},{22,2},{26,6},{30,10},{2... | collective-permute-start | bytes 18452 | tf_op jit(solution)/shard_map/ppermute | solution.py:16
  94.5 1.3 %collective-permute-start.14 = (f32[1,1537]{1,0:T(1,128)S(1)}, f32[1,1537]{1,0:T(1,128)S(1)}, u32[]{:S(2)}, u32[]{:S(2)}) collective-permute-start(f32[1,1537]{1,0:T(1,128)S(1)} %pad_maximum_fusion.16), channel_id=1, source_target_pairs={{8,0},{12,4},{16,8},{20,12},{24,16},{28,20},{9,1},{13,5},{17,9},{2... | collective-permute-start | bytes 18452 | tf_op jit(solution)/shard_map/ppermute | solution.py:16
  95.8 1.5 %collective-permute-start.13 = (f32[1,1537]{1,0:T(1,128)S(1)}, f32[1,1537]{1,0:T(1,128)S(1)}, u32[]{:S(2)}, u32[]{:S(2)}) collective-permute-start(f32[1,1537]{1,0:T(1,128)S(1)} %pad_maximum_fusion.16), channel_id=1, source_target_pairs={{4,0},{8,4},{12,8},{16,12},{20,16},{24,20},{28,24},{5,1},{9,5},{13... | collective-permute-start | bytes 18452 | tf_op jit(solution)/shard_map/ppermute | solution.py:16
  98.0 1.5 %multiply_multiply_fusion = f32[1,1536]{1,0:T(1,128)S(1)} fusion(f32[322,1536]{1,0:T(8,128)} %copy-done.2, f32[]{:T(128)S(6)} %rsqrt.33, f32[]{:T(128)} %bitcast.14), kind=kLoop, calls=%fused_computation.91 | loop fusion | flops 3072 | bytes 12296 | tf_op jit(solution)/shard_map/mul | solution.py:173
  99.4 1.9 %slice_multiply_fusion = f32[319,1536]{1,0:T(8,128)S(1)} fusion(f32[320,1536]{1,0:T(8,128)} %get-tuple-element.5, f32[319]{0:T(512)S(1)} %slice.161), kind=kLoop, calls=%fused_computation.13 | loop fusion | flops 489984 | bytes 3921148 | tf_op jit(solution)/shard_map/mul | solution.py:171
  101.9 1.0 copy-done.8
  103.2 3.6 %fusion.9 = f32[320,1536]{1,0:T(8,128)S(1)} fusion(f32[1,1536]{1,0:T(1,128)S(1)} %multiply_multiply_fusion, f32[319,1536]{1,0:T(8,128)S(1)} %slice_multiply_fusion, f32[320]{0:T(512)S(1)} %fusion.49, f32[320]{0:T(512)S(1)} %add_rsqrt_fusion, bf16[384,1536]{1,0:T(8,128)(2,1)} %collective-permute-done.12, bf16[384,1536]{1,0:T(8,128)(2,1)} %collective-permute-done.11, ...), kind=kOutput, calls=%fused_computation.32 | convolution fusion | flops 1531281408 | bytes 10627072 | tf_op jit(solution)/shard_map/dot_general | solution.py:178
  106.9 1.9 %fusion.1 = bf16[320,1536]{1,0:T(8,128)(2,1)S(1)} fusion(f32[320,1536]{1,0:T(8,128)S(1)} %fusion.9, f32[322,1536]{1,0:T(8,128)S(1)} %copy-done.4, f32[319,1536]{1,0:T(8,128)S(1)} %slice_multiply_fusion.1, f32[1,1536]{1,0:T(1,128)S(1)} %slice_multiply_fusion.10, f32[320]{0:T(512)S(1)} %get-tuple-element.20, f32[320]{0:T(512)S(1)} %select_select_fusion, ...), kind=kOutput, calls=%fused_computation.5 | convolution fusion | flops 1532755968 | bytes 11612160 | tf_op jit(solution)/shard_map/dot_general | solution.py:175
  108.9 1.3 %collective-permute-start.16 = (f32[1,1537]{1,0:T(1,128)S(1)}, f32[1,1537]{1,0:T(1,128)S(1)}, u32[]{:S(2)}, u32[]{:S(2)}) collective-permute-start(f32[1,1537]{1,0:T(1,128)S(1)} %pad_maximum_fusion.16), channel_id=1, source_target_pairs={{16,0},{20,4},{24,8},{28,12},{17,1},{21,5},{25,9},{29,13},{18,2},{... | collective-permute-start | bytes 18452 | tf_op jit(solution)/shard_map/ppermute | solution.py:16
  110.2 1.3 %collective-permute-start.15 = (f32[1,1537]{1,0:T(1,128)S(1)}, f32[1,1537]{1,0:T(1,128)S(1)}, u32[]{:S(2)}, u32[]{:S(2)}) collective-permute-start(f32[1,1537]{1,0:T(1,128)S(1)} %pad_maximum_fusion.16), channel_id=1, source_target_pairs={{12,0},{16,4},{20,8},{24,12},{28,16},{13,1},{17,5},{21,9},{25,13},... | collective-permute-start | bytes 18452 | tf_op jit(solution)/shard_map/ppermute | solution.py:16
  111.5 1.0 maximum_bitcast_fusion
  112.6 0.5 slice.166
  113.8 0.6 slice.168
  115.7 2.8 %collective-permute-done.15 = f32[1,1537]{1,0:T(1,128)S(1)} collective-permute-done((f32[1,1537]{1,0:T(1,128)S(1)}, f32[1,1537]{1,0:T(1,128)S(1)}, u32[]{:S(2)}, u32[]{:S(2)}) %collective-permute-start.15) | collective-permute-done | bytes 6180 | tf_op jit(solution)/shard_map/ppermute | solution.py:16
  118.5 0.5 slice.170
  119.7 0.5 slice.172
  120.9 0.5 slice.174
  122.1 0.5 slice.176
  123.4 1.7 %fusion.4 = bf16[1,128,1536]{2,1,0:T(8,128)(2,1)} fusion(f32[128,1536]{1,0:T(8,128)S(1)} %fusion.6, f32[1536]{0:T(1024)S(1)} %fusion.47, f32[128]{0:T(128)S(1)} %get-tuple-element.22, f32[128]{0:T(128)S(1)} %bitcast_select_fusion, f32[128]{0:T(128)S(1)} %reduce.2), kind=kOutput, calls=%fused_computation.10 | convolution fusion | flops 302841856 | bytes 1187328 | tf_op jit(solution)/shard_map/dot_general | solution.py:166
  (94 shorter events, 3.5 us)
Async XLA Ops:
  0.6 13.9 %copy-start.11 = (bf16[1,320,1536]{2,1,0:T(8,128)(2,1)S(1)}, bf16[1,320,1536]{2,1,0:T(8,128)(2,1)}, u32[]{:S(2)}) copy-start(bf16[1,320,1536]{2,1,0:T(8,128)(2,1)} %param.8) | copy-start | bytes 2949124
  0.6 19.9 %copy-start.17 = (s32[1,128]{1,0:T(1,128)S(1)}, s32[1,128]{1,0:T(1,128)}, u32[]{:S(2)}) copy-start(s32[1,128]{1,0:T(1,128)} %param.11) | copy-start | bytes 1540
  0.7 43.4 %copy-start.5 = (bf16[1,320,1536]{2,1,0:T(8,128)(2,1)S(1)}, bf16[1,320,1536]{2,1,0:T(8,128)(2,1)}, u32[]{:S(2)}) copy-start(bf16[1,320,1536]{2,1,0:T(8,128)(2,1)} %param.9) | copy-start | bytes 2949124
  2.7 50.9 %collective-permute-start.5 = (bf16[384,768]{1,0:T(8,128)(2,1)}, bf16[384,768]{1,0:T(8,128)(2,1)}, u32[]{:S(2)}, u32[]{:S(2)}) collective-permute-start(bf16[384,768]{1,0:T(8,128)(2,1)} %constant_dynamic-slice_fusion.5), channel_id=1, source_target_pairs={{0,2},{1,3},{2,0},{3,1},{4,6},{5,7},{6,4},{7,5},{8,10},{9,11},{10,... | collective-permute-start | bytes 1769480 | tf_op jit(solution)/shard_map/ppermute | solution.py:54
  11.2 11.0 %collective-permute-start.1 = (f32[1,1537]{1,0:T(1,128)S(1)}, f32[1,1537]{1,0:T(1,128)S(1)}, u32[]{:S(2)}, u32[]{:S(2)}) collective-permute-start(f32[1,1537]{1,0:T(1,128)S(1)} %pad_maximum_fusion.12), channel_id=1, source_target_pairs={{0,4},{4,8},{8,12},{12,16},{16,20},{20,24},{24,28},{1,5},{5,9},{9,... | collective-permute-start | bytes 18452 | tf_op jit(solution)/shard_map/ppermute | solution.py:16
  14.6 55.6 %collective-permute-start = (bf16[1,1536]{1,0:T(2,128)(2,1)S(1)}, bf16[1,1536]{1,0:T(2,128)(2,1)S(1)}, u32[]{:S(2)}, u32[]{:S(2)}) collective-permute-start(bf16[1,1536]{1,0:T(2,128)(2,1)S(1)} %get-tuple-element.18), channel_id=1, source_target_pairs={{0,4},{4,8},{8,12},{12,16},{16,20},{20,24},{24,28},{1,5},{5,9},{9,... | collective-permute-start | bytes 9224 | tf_op jit(solution)/shard_map/ppermute | solution.py:16
  18.1 54.5 %collective-permute-start.11 = (bf16[384,1536]{1,0:T(8,128)(2,1)}, bf16[384,1536]{1,0:T(8,128)(2,1)}, u32[]{:S(2)}, u32[]{:S(2)}) collective-permute-start(bf16[384,1536]{1,0:T(8,128)(2,1)} %param.15), channel_id=1, source_target_pairs={{0,1},{1,0},{2,3},{3,2},{4,5},{5,4},{6,7},{7,6},{8,9},{9,8},{10,11... | collective-permute-start | bytes 3538952 | tf_op jit(solution)/shard_map/ppermute | solution.py:63
  20.1 15.9 %collective-permute-start.9 = (bf16[384,768]{1,0:T(8,128)(2,1)}, bf16[384,768]{1,0:T(8,128)(2,1)S(1)}, u32[]{:S(2)}, u32[]{:S(2)}) collective-permute-start(bf16[384,768]{1,0:T(8,128)(2,1)} %constant_dynamic-slice_fusion.4), channel_id=1, source_target_pairs={{0,2},{1,3},{2,0},{3,1},{4,6},{5,7},{6,4},{7,5},{8,10},{9,11},{10,... | collective-permute-start | bytes 1769480 | tf_op jit(solution)/shard_map/ppermute | solution.py:54
  24.0 4.8 %collective-permute-start.2 = (f32[1,1537]{1,0:T(1,128)S(1)}, f32[1,1537]{1,0:T(1,128)S(1)}, u32[]{:S(2)}, u32[]{:S(2)}) collective-permute-start(f32[1,1537]{1,0:T(1,128)S(1)} %pad_maximum_fusion.13), channel_id=1, source_target_pairs={{0,8},{4,12},{8,16},{12,20},{16,24},{20,28},{1,9},{5,13},{9,17},{1... | collective-permute-start | bytes 18452 | tf_op jit(solution)/shard_map/ppermute | solution.py:16
  36.0 9.6 %copy-start.12 = (bf16[384,768]{1,0:T(8,128)(2,1)}, bf16[384,768]{1,0:T(8,128)(2,1)S(1)}, u32[]{:S(2)}) copy-start(bf16[384,768]{1,0:T(8,128)(2,1)S(1)} %collective-permute-done.9) | copy-start | bytes 1769476
  36.0 15.0 %collective-permute-start.10 = (bf16[384,768]{1,0:T(8,128)(2,1)S(1)}, bf16[384,768]{1,0:T(8,128)(2,1)}, u32[]{:S(2)}, u32[]{:S(2)}) collective-permute-start(bf16[384,768]{1,0:T(8,128)(2,1)S(1)} %collective-permute-done.9), channel_id=1, source_target_pairs={{0,4},{4,0},{8,12},{12,8},{16,20},{20,16},{24,28},{28,24},{1,5},{5... | collective-permute-start | bytes 1769480 | tf_op jit(solution)/shard_map/ppermute | solution.py:55
  37.5 6.5 %collective-permute-start.3 = (f32[1,1537]{1,0:T(1,128)S(1)}, f32[1,1537]{1,0:T(1,128)S(1)}, u32[]{:S(2)}, u32[]{:S(2)}) collective-permute-start(f32[1,1537]{1,0:T(1,128)S(1)} %pad_maximum_fusion.14), channel_id=1, source_target_pairs={{0,16},{4,20},{8,24},{12,28},{1,17},{5,21},{9,25},{13,29},{2,18},{... | collective-permute-start | bytes 18452 | tf_op jit(solution)/shard_map/ppermute | solution.py:16
  53.0 19.6 %copy-start.7 = (bf16[384,1536]{1,0:T(8,128)(2,1)}, bf16[384,1536]{1,0:T(8,128)(2,1)S(1)}, u32[]{:S(2)}) copy-start(bf16[384,1536]{1,0:T(8,128)(2,1)S(1)} %maximum_select_fusion.1) | copy-start | bytes 3538948
  53.0 19.6 %collective-permute-start.12 = (bf16[384,1536]{1,0:T(8,128)(2,1)S(1)}, bf16[384,1536]{1,0:T(8,128)(2,1)}, u32[]{:S(2)}, u32[]{:S(2)}) collective-permute-start(bf16[384,1536]{1,0:T(8,128)(2,1)S(1)} %maximum_select_fusion.1), channel_id=1, source_target_pairs={{0,1},{1,0},{2,3},{3,2},{4,5},{5,4},{6,7},{7,6},{8,9},{9,8},{10,11... | collective-permute-start | bytes 3538952 | tf_op jit(solution)/shard_map/ppermute | solution.py:63
  53.7 16.6 %collective-permute-start.6 = (bf16[384,768]{1,0:T(8,128)(2,1)}, bf16[384,768]{1,0:T(8,128)(2,1)S(1)}, u32[]{:S(2)}, u32[]{:S(2)}) collective-permute-start(bf16[384,768]{1,0:T(8,128)(2,1)} %collective-permute-done.5), channel_id=1, source_target_pairs={{0,4},{4,0},{8,12},{12,8},{16,20},{20,16},{24,28},{28,24},{1,5},{5... | collective-permute-start | bytes 1769480 | tf_op jit(solution)/shard_map/ppermute | solution.py:55
  55.9 13.8 %collective-permute-start.4 = (f32[1,1537]{1,0:T(1,128)S(1)}, f32[1,1537]{1,0:T(1,128)S(1)}, u32[]{:S(2)}, u32[]{:S(2)}) collective-permute-start(f32[1,1537]{1,0:T(1,128)S(1)} %pad_maximum_fusion.15), channel_id=1, source_target_pairs={{4,0},{8,4},{12,8},{16,12},{20,16},{24,20},{28,24},{5,1},{9,5},{13... | collective-permute-start | bytes 18452 | tf_op jit(solution)/shard_map/ppermute | solution.py:16
  69.7 8.5 %collective-permute-start.7 = (bf16[384,1536]{1,0:T(8,128)(2,1)}, bf16[384,1536]{1,0:T(8,128)(2,1)S(1)}, u32[]{:S(2)}, u32[]{:S(2)}) collective-permute-start(bf16[384,1536]{1,0:T(8,128)(2,1)} %param.14), channel_id=1, source_target_pairs={{0,1},{1,0},{2,3},{3,2},{4,5},{5,4},{6,7},{7,6},{8,9},{9,8},{10,11... | collective-permute-start | bytes 3538952 | tf_op jit(solution)/shard_map/ppermute | solution.py:63
  70.3 2.3 %copy-start.13 = (bf16[384,1536]{1,0:T(8,128)(2,1)S(1)}, bf16[384,1536]{1,0:T(8,128)(2,1)}, u32[]{:S(2)}) copy-start(bf16[384,1536]{1,0:T(8,128)(2,1)} %param.15) | copy-start | bytes 3538948
  71.9 6.3 %copy-start.9 = (bf16[384,1536]{1,0:T(8,128)(2,1)}, bf16[384,1536]{1,0:T(8,128)(2,1)S(1)}, u32[]{:S(2)}) copy-start(bf16[384,1536]{1,0:T(8,128)(2,1)S(1)} %maximum_select_fusion) | copy-start | bytes 3538948
  71.9 6.3 %collective-permute-start.8 = (bf16[384,1536]{1,0:T(8,128)(2,1)S(1)}, bf16[384,1536]{1,0:T(8,128)(2,1)S(1)}, u32[]{:S(2)}, u32[]{:S(2)}) collective-permute-start(bf16[384,1536]{1,0:T(8,128)(2,1)S(1)} %maximum_select_fusion), channel_id=1, source_target_pairs={{0,1},{1,0},{2,3},{3,2},{4,5},{5,4},{6,7},{7,6},{8,9},{9,8},{10,11... | collective-permute-start | bytes 3538952 | tf_op jit(solution)/shard_map/ppermute | solution.py:63
  76.0 6.7 %copy-start = (f32[322,1536]{1,0:T(8,128)}, f32[322,1536]{1,0:T(8,128)S(1)}, u32[]{:S(2)}) copy-start(f32[322,1536]{1,0:T(8,128)S(1)} %fusion.19) | copy-start | bytes 5935108
  76.7 1.7 %copy-start.15 = (bf16[384,1536]{1,0:T(8,128)(2,1)S(1)}, bf16[384,1536]{1,0:T(8,128)(2,1)}, u32[]{:S(2)}) copy-start(bf16[384,1536]{1,0:T(8,128)(2,1)} %param.14) | copy-start | bytes 3538948
  78.2 1.9 %copy-start.18 = (bf16[384,1536]{1,0:T(8,128)(2,1)}, bf16[384,1536]{1,0:T(8,128)(2,1)S(1)}, u32[]{:S(2)}) copy-start(bf16[384,1536]{1,0:T(8,128)(2,1)S(1)} %collective-permute-done.7) | copy-start | bytes 3538948
  78.4 1.8 %copy-start.20 = (bf16[384,1536]{1,0:T(8,128)(2,1)}, bf16[384,1536]{1,0:T(8,128)(2,1)S(1)}, u32[]{:S(2)}) copy-start(bf16[384,1536]{1,0:T(8,128)(2,1)S(1)} %collective-permute-done.8) | copy-start | bytes 3538948
  80.2 1.3 %copy-start.2 = (f32[322,1536]{1,0:T(8,128)}, f32[322,1536]{1,0:T(8,128)S(1)}, u32[]{:S(2)}) copy-start(f32[322,1536]{1,0:T(8,128)S(1)} %fusion.20) | copy-start | bytes 5935108
  82.7 2.2 %copy-start.3 = (f32[322,1536]{1,0:T(8,128)S(1)}, f32[322,1536]{1,0:T(8,128)}, u32[]{:S(2)}) copy-start(f32[322,1536]{1,0:T(8,128)} %copy-done.2) | copy-start | bytes 5935108
  85.5 1.8 %copy-start.6 = (bf16[1,320,1536]{2,1,0:T(8,128)(2,1)S(1)}, bf16[1,320,1536]{2,1,0:T(8,128)(2,1)}, u32[]{:S(2)}) copy-start(bf16[1,320,1536]{2,1,0:T(8,128)(2,1)} %param.9) | copy-start | bytes 2949124
  90.6 32.7 %collective-permute-start.19 = (f32[1,1537]{1,0:T(1,128)S(1)}, f32[1,1537]{1,0:T(1,128)S(1)}, u32[]{:S(2)}, u32[]{:S(2)}) collective-permute-start(f32[1,1537]{1,0:T(1,128)S(1)} %pad_maximum_fusion.16), channel_id=1, source_target_pairs={{28,0},{29,1},{30,2},{31,3}} | collective-permute-start | bytes 18452 | tf_op jit(solution)/shard_map/ppermute | solution.py:16
  91.9 30.2 %collective-permute-start.18 = (f32[1,1537]{1,0:T(1,128)S(1)}, f32[1,1537]{1,0:T(1,128)S(1)}, u32[]{:S(2)}, u32[]{:S(2)}) collective-permute-start(f32[1,1537]{1,0:T(1,128)S(1)} %pad_maximum_fusion.16), channel_id=1, source_target_pairs={{24,0},{28,4},{25,1},{29,5},{26,2},{30,6},{27,3},{31,7}} | collective-permute-start | bytes 18452 | tf_op jit(solution)/shard_map/ppermute | solution.py:16
  93.2 27.7 %collective-permute-start.17 = (f32[1,1537]{1,0:T(1,128)S(1)}, f32[1,1537]{1,0:T(1,128)S(1)}, u32[]{:S(2)}, u32[]{:S(2)}) collective-permute-start(f32[1,1537]{1,0:T(1,128)S(1)} %pad_maximum_fusion.16), channel_id=1, source_target_pairs={{20,0},{24,4},{28,8},{21,1},{25,5},{29,9},{22,2},{26,6},{30,10},{2... | collective-permute-start | bytes 18452 | tf_op jit(solution)/shard_map/ppermute | solution.py:16
  94.5 14.4 %collective-permute-start.14 = (f32[1,1537]{1,0:T(1,128)S(1)}, f32[1,1537]{1,0:T(1,128)S(1)}, u32[]{:S(2)}, u32[]{:S(2)}) collective-permute-start(f32[1,1537]{1,0:T(1,128)S(1)} %pad_maximum_fusion.16), channel_id=1, source_target_pairs={{8,0},{12,4},{16,8},{20,12},{24,16},{28,20},{9,1},{13,5},{17,9},{2... | collective-permute-start | bytes 18452 | tf_op jit(solution)/shard_map/ppermute | solution.py:16
  95.8 14.4 %collective-permute-start.13 = (f32[1,1537]{1,0:T(1,128)S(1)}, f32[1,1537]{1,0:T(1,128)S(1)}, u32[]{:S(2)}, u32[]{:S(2)}) collective-permute-start(f32[1,1537]{1,0:T(1,128)S(1)} %pad_maximum_fusion.16), channel_id=1, source_target_pairs={{4,0},{8,4},{12,8},{16,12},{20,16},{24,20},{28,24},{5,1},{9,5},{13... | collective-permute-start | bytes 18452 | tf_op jit(solution)/shard_map/ppermute | solution.py:16
  99.4 2.2 %copy-start.1 = (f32[322,1536]{1,0:T(8,128)S(1)}, f32[322,1536]{1,0:T(8,128)}, u32[]{:S(2)}) copy-start(f32[322,1536]{1,0:T(8,128)} %copy-done) | copy-start | bytes 5935108
  101.6 1.3 %copy-start.8 = (bf16[384,1536]{1,0:T(8,128)(2,1)S(1)}, bf16[384,1536]{1,0:T(8,128)(2,1)}, u32[]{:S(2)}) copy-start(bf16[384,1536]{1,0:T(8,128)(2,1)} %copy-done.7) | copy-start | bytes 3538948
  101.6 1.6 %copy-start.14 = (bf16[384,1536]{1,0:T(8,128)(2,1)S(1)}, bf16[384,1536]{1,0:T(8,128)(2,1)}, u32[]{:S(2)}) copy-start(bf16[384,1536]{1,0:T(8,128)(2,1)} %param.15) | copy-start | bytes 3538948
  103.2 3.6 %copy-start.4 = (f32[322,1536]{1,0:T(8,128)S(1)}, f32[322,1536]{1,0:T(8,128)}, u32[]{:S(2)}) copy-start(f32[322,1536]{1,0:T(8,128)} %copy-done.2) | copy-start | bytes 5935108
  103.2 3.6 %copy-start.10 = (bf16[384,1536]{1,0:T(8,128)(2,1)S(1)}, bf16[384,1536]{1,0:T(8,128)(2,1)}, u32[]{:S(2)}) copy-start(bf16[384,1536]{1,0:T(8,128)(2,1)} %copy-done.9) | copy-start | bytes 3538948
  103.2 3.6 %copy-start.16 = (bf16[384,1536]{1,0:T(8,128)(2,1)S(1)}, bf16[384,1536]{1,0:T(8,128)(2,1)}, u32[]{:S(2)}) copy-start(bf16[384,1536]{1,0:T(8,128)(2,1)} %param.14) | copy-start | bytes 3538948
  103.2 3.6 %copy-start.19 = (bf16[384,1536]{1,0:T(8,128)(2,1)S(1)}, bf16[384,1536]{1,0:T(8,128)(2,1)}, u32[]{:S(2)}) copy-start(bf16[384,1536]{1,0:T(8,128)(2,1)} %copy-done.18) | copy-start | bytes 3538948
  103.2 3.6 %copy-start.21 = (bf16[384,1536]{1,0:T(8,128)(2,1)S(1)}, bf16[384,1536]{1,0:T(8,128)(2,1)}, u32[]{:S(2)}) copy-start(bf16[384,1536]{1,0:T(8,128)(2,1)} %copy-done.20) | copy-start | bytes 3538948
  108.9 10.8 %collective-permute-start.16 = (f32[1,1537]{1,0:T(1,128)S(1)}, f32[1,1537]{1,0:T(1,128)S(1)}, u32[]{:S(2)}, u32[]{:S(2)}) collective-permute-start(f32[1,1537]{1,0:T(1,128)S(1)} %pad_maximum_fusion.16), channel_id=1, source_target_pairs={{16,0},{20,4},{24,8},{28,12},{17,1},{21,5},{25,9},{29,13},{18,2},{... | collective-permute-start | bytes 18452 | tf_op jit(solution)/shard_map/ppermute | solution.py:16
  110.2 8.2 %collective-permute-start.15 = (f32[1,1537]{1,0:T(1,128)S(1)}, f32[1,1537]{1,0:T(1,128)S(1)}, u32[]{:S(2)}, u32[]{:S(2)}) collective-permute-start(f32[1,1537]{1,0:T(1,128)S(1)} %pad_maximum_fusion.16), channel_id=1, source_target_pairs={{12,0},{16,4},{20,8},{24,12},{28,16},{13,1},{17,5},{21,9},{25,13},... | collective-permute-start | bytes 18452 | tf_op jit(solution)/shard_map/ppermute | solution.py:16

commit v6 on v4

--- a/solution.py
+++ b/solution.py
@@ -95,9 +95,14 @@
     slot_count = segment_states.shape[1]
     width = query_weight.shape[0]
     shard_index = lax.axis_index("seq")
-    pairs, index = gather_blocks((query_weight, key_weight), "dp")
-    full_query = jnp.concatenate([p[0] for p in pairs], axis=0)
-    full_key = jnp.concatenate([p[1] for p in pairs], axis=0)
+    seq_count = lax.axis_size("seq")
+    piece = width // seq_count
+    full_query, full_key = (
+        lax.all_gather(
+            lax.dynamic_slice_in_dim(w, shard_index * piece, piece, axis=0), ("dp", "seq"), axis=0, tiled=True
+        )
+        for w in (query_weight, key_weight)
+    )
     position = jnp.arange(token_count)
     later_rows = (shard_index > 0) | (position > 0)
     segment_total = segment_counts[0, 0]
@@ -130,7 +135,7 @@
     next_row = from_next[:, :-1].astype(token_rows.dtype)
     next_cos_grad = from_next[:, -1:]
     rows_ext = jnp.concatenate([token_rows, prev_row, next_row], axis=0)
-    rows_perm = permute_cols(rows_ext, index, width)
+    rows_perm = rows_ext
     queries_ext = jnp.dot(rows_perm, full_query, preferred_element_type=jnp.float32)
     keys_ext = jnp.dot(rows_perm, full_key, preferred_element_type=jnp.float32)
     queries = queries_ext[:token_count]
@@ -169,9 +174,6 @@
         key_grad, full_key, contract_last, preferred_element_type=jnp.float32
     )
     x_grad = x_grad.astype(jnp.bfloat16)
-    slots = jnp.arange(len(index), dtype=jnp.int32)
-    order = jnp.sum(jnp.where(jnp.stack(index)[None, :] == slots[:, None], slots[None, :], 0), axis=1)
-    x_grad = permute_cols(x_grad, [order[j] for j in range(len(index))], width)
     return (x_grad[None], segment_grad[None])
 
 

time: 117 us -> 196 us (1.68)
  waiting for transfers between devices: 11.2 us -> 89.7 us
  between operations: 14.8 us -> 26 us
  local copies, waits for them, and re-layouts: 19.3 us -> 11.5 us
  other arithmetic: 18 us -> 13.5 us
    all_gather x0 -> x2, waiting for transfers between devices: none -> 87.2 us  [per_device(): lax.all_gather(lax.dynamic_slice_in_dim(w, shard_index * piece, piece, ax...]
    unnamed x36 -> x16, local copies, waits for them, and re-layouts: 10.7 us -> 3.09 us
    ppermute x6 -> x0, waiting for transfers between devices: 6.04 us -> none  [the longest x2 6.03 us: gather_blocks(): pairs.append(lax.ppermute(blocks, axis, route))]
    ppermute x6 -> x0, starting transfers between devices: 3.76 us -> none  [the longest x2 3.19 us: gather_blocks(): pairs.append(lax.ppermute(blocks, axis, route))]
    ppermute x12, starting transfers between devices: 26.5 us -> 29.8 us  [shifted(): return lax.ppermute(block, axis, route)]
    ppermute x12, waiting for transfers between devices: 5.17 us -> 2.45 us  [shifted(): return lax.ppermute(block, axis, route)]
    dot_general x1, matrix products: 1.72 us -> 4.37 us  [per_device(): jnp.dot(rows_perm, full_query, preferred_element_type=jnp.float32)]
    dot_general x1, matrix products: 1.92 us -> 4.25 us  [per_device(): lax.dot_general(query_grad, full_query, contract_last, preferred_element_...]
  transfers between devices with their start and end apart: 18 -> 14, of which waited for: 4 -> 5; matrix products, arithmetic and copies ran while one was open for 39% -> 15% of each run, Pallas kernels for 0% -> 0%
where the time goes in v6:
time: 196 us; the launch traced here: 194 us
  waiting for transfers between devices  89.7 us (46%)
  starting transfers between devices  29.9 us (15%)
  between operations  26 us (13%)
  matrix products  23.5 us (12%)
  other arithmetic  13.5 us (7%)
  local copies, waits for them, and re-layouts  11.5 us (6%)
    all_gather x2, waiting for transfers between devices, per_device(): lax.all_gather(lax.dynamic_slice_in_dim(w, shard_index * piece, piece, ax...  87.2 us
    ppermute x12, starting transfers between devices, shifted(): return lax.ppermute(block, axis, route)  29.8 us
    dot_general x1, matrix products, per_device(): jnp.dot(rows_perm, full_query, preferred_element_type=jnp.float32)  4.37 us
    dot_general x1, matrix products, per_device(): keys_ext = jnp.dot(rows_perm, full_key, preferred_element_type=jnp.float32)  4.36 us
    dot_general x1, matrix products, per_device(): lax.dot_general(query_grad, full_query, contract_last, preferred_element_...  4.25 us
  transfers between devices with their start and end apart: 14, of which 5 were waited for; matrix products, arithmetic and copies ran while one was open for 15% of the time, Pallas kernels for 0%

profile of v6, /device:TPU:0, one launch (start us, length us, event | category | flops | bytes accessed | tf_op | source)
XLA Modules:
  0.0 193.9 jit_solution(16538481557426192448)
XLA Ops:
  7.3 1.2 copy-done
  8.4 0.7 constant_dynamic-slice_fusion.1
  9.2 1.6 constant_dynamic-slice_fusion
  11.4 0.7 fusion.54
  12.2 0.2 broadcast_in_dim.27
  12.4 0.6 slice.133
  13.1 0.7 bitcast_select_fusion
  13.7 1.9 fusion.20
  15.6 0.6 pad_maximum_fusion.5
  16.3 4.8 %collective-permute-start.1 = (f32[1,1537]{1,0:T(1,128)S(1)}, f32[1,1537]{1,0:T(1,128)S(1)}, u32[]{:S(2)}, u32[]{:S(2)}) collective-permute-start(f32[1,1537]{1,0:T(1,128)S(1)} %pad_maximum_fusion.5), channel_id=1, source_target_pairs={{0,4},{4,8},{8,12},{12,16},{16,20},{20,24},{24,28},{1,5},{5,9},{9,... | collective-permute-start | bytes 18452 | tf_op jit(solution)/shard_map/ppermute | solution.py:16
  21.2 0.1 convert_reduce_fusion
  21.3 0.8 slice_bitcast_fusion
  22.8 0.6 slice.134
  24.6 4.9 %collective-permute-start.2 = (f32[1,1537]{1,0:T(1,128)S(1)}, f32[1,1537]{1,0:T(1,128)S(1)}, u32[]{:S(2)}, u32[]{:S(2)}) collective-permute-start(f32[1,1537]{1,0:T(1,128)S(1)} %pad_maximum_fusion.6), channel_id=1, source_target_pairs={{0,8},{4,12},{8,16},{12,20},{16,24},{20,28},{1,9},{5,13},{9,17},{1... | collective-permute-start | bytes 18452 | tf_op jit(solution)/shard_map/ppermute | solution.py:16
  29.5 0.6 subtract_exponential_fusion
  30.2 0.6 collective-permute-done.2
  30.8 0.6 slice.136
  32.1 5.2 %collective-permute-start.3 = (f32[1,1537]{1,0:T(1,128)S(1)}, f32[1,1537]{1,0:T(1,128)S(1)}, u32[]{:S(2)}, u32[]{:S(2)}) collective-permute-start(f32[1,1537]{1,0:T(1,128)S(1)} %pad_maximum_fusion.7), channel_id=1, source_target_pairs={{0,16},{4,20},{8,24},{12,28},{1,17},{5,21},{9,25},{13,29},{2,18},{... | collective-permute-start | bytes 18452 | tf_op jit(solution)/shard_map/ppermute | solution.py:16
  37.4 0.2 fusion.30
  39.6 1.5 fusion.8
  41.1 0.6 slice.110
  41.6 0.6 pad_maximum_fusion.8
  42.3 1.3 collective-permute-start.4
  43.6 4.5 %collective-permute-start = (bf16[1,1536]{1,0:T(2,128)(2,1)S(1)}, bf16[1,1536]{1,0:T(2,128)(2,1)S(1)}, u32[]{:S(2)}, u32[]{:S(2)}) collective-permute-start(bf16[1,1536]{1,0:T(2,128)(2,1)S(1)} %get-tuple-element.9), channel_id=1, source_target_pairs={{0,4},{4,8},{8,12},{12,16},{16,20},{20,24},{24,28},{1,5},{5,9},{9,... | collective-permute-start | bytes 9224 | tf_op jit(solution)/shard_map/ppermute | solution.py:16
  48.2 0.5 slice.147
  48.8 0.7 collective-permute-done
  49.4 28.6 %all-gather.3.cloned.1.call-done = bf16[1536,1536]{1,0:T(8,128)(2,1)} async-done(((bf16[48,1536]{1,0:T(8,128)(2,1)}), bf16[1536,1536]{1,0:T(8,128)(2,1)}) %all-gather.3.cloned.1.call-update) | async-done | bytes 4718608 | tf_op jit(solution)/shard_map/all_gather | solution.py:101
  78.1 4.4 %fusion.24 = f32[322,1536]{1,0:T(8,128)S(1)} fusion(bf16[1536,1536]{1,0:T(8,128)(2,1)} %all-gather.3.cloned.1.call-done, bf16[1,1536]{1,0:T(2,128)(2,1)S(1)} %slice.235, bf16[1,1536]{1,0:T(2,128)(2,1)S(1)} %collective-permute-done, bf16[320,1536]{1,0:T(8,128)(2,1)} %bitcast.65), kind=kOutput, calls=%fused_computation.43 | convolution fusion | flops 1522354176 | bytes 7686144 | tf_op jit(solution)/shard_map/dot_general | solution.py:139
  82.4 0.6 multiply_reduce_fusion.5
  83.8 0.2 multiply_reduce_fusion.4
  84.0 1.6 slice_multiply_fusion.2
  85.6 58.6 %all-gather.5.cloned.1.call-done = bf16[1536,1536]{1,0:T(8,128)(2,1)} async-done(((bf16[48,1536]{1,0:T(8,128)(2,1)}), bf16[1536,1536]{1,0:T(8,128)(2,1)}) %all-gather.5.cloned.1.call-update) | async-done | bytes 4718608 | tf_op jit(solution)/shard_map/all_gather | solution.py:101
  144.2 4.4 %fusion.23 = f32[322,1536]{1,0:T(8,128)S(1)} fusion(bf16[1536,1536]{1,0:T(8,128)(2,1)} %all-gather.5.cloned.1.call-done, bf16[1,1536]{1,0:T(2,128)(2,1)S(1)} %slice.235, bf16[1,1536]{1,0:T(2,128)(2,1)S(1)} %collective-permute-done, bf16[320,1536]{1,0:T(8,128)(2,1)} %bitcast.66), kind=kOutput, calls=%fused_computation.42 | convolution fusion | flops 1522354176 | bytes 7686144 | tf_op jit(solution)/shard_map/dot_general | solution.py:140
  148.5 1.3 copy-done.3
  149.8 0.6 multiply_reduce_fusion.6
  151.1 0.8 slice_multiply_fusion.10
  151.9 0.6 multiply_multiply_fusion
  152.6 1.9 slice_multiply_fusion
  154.5 0.2 copy-done.4
  154.7 0.4 multiply_reduce_fusion.1
  155.2 0.2 slice_multiply_fusion.1
  155.4 0.8 multiply_reduce_fusion
  156.2 0.4 copy-done.2
  156.6 1.2 fusion.7
  157.8 0.9 fusion.9
  158.8 0.5 convolution_reduce_fusion
  159.3 0.9 pad_maximum_fusion.9
  160.2 1.3 collective-permute-start.11
  161.5 1.3 collective-permute-start.10
  162.8 1.3 collective-permute-start.9
  164.1 1.3 collective-permute-start.6
  165.4 1.3 collective-permute-start.5
  166.7 4.2 %fusion.10 = f32[320,1536]{1,0:T(8,128)S(1)} fusion(bf16[1536,1536]{1,0:T(8,128)(2,1)} %all-gather.3.cloned.1.call-done, f32[322,1536]{1,0:T(8,128)S(1)} %fusion.24, f32[319,1536]{1,0:T(8,128)S(1)} %slice_multiply_fusion.1, f32[1,1536]{1,0:T(1,128)S(1)} %slice_multiply_fusion.10, f32[320]{0:T(512)S(1)} %get-tuple-element.16, f32[320]{0:T(512)S(1)} %select_select_fusion, ...), kind=kOutput, calls=%fused_computation.28 | convolution fusion | flops 1512898560 | bytes 10629120 | tf_op jit(solution)/shard_map/dot_general | solution.py:170
  171.0 1.3 collective-permute-start.8
  172.3 1.3 collective-permute-start.7
  173.6 2.9 %fusion.2 = bf16[1,320,1536]{2,1,0:T(8,128)(2,1)} fusion(f32[320,1536]{1,0:T(8,128)S(1)} %fusion.10, bf16[1536,1536]{1,0:T(8,128)(2,1)S(1)} %bitcast.68, f32[1,1536]{1,0:T(1,128)S(1)} %multiply_multiply_fusion, f32[319,1536]{1,0:T(8,128)S(1)} %slice_multiply_fusion, f32[320]{0:T(512)S(1)} %get-tuple-element.11, f32[320]{0:T(512)S(1)} %get-tuple-element.12, ...), kind=kOutput, calls=%fused_computation.4 | convolution fusion | flops 1513390080 | bytes 11610112 | tf_op jit(solution)/shard_map/dot_general | solution.py:173
  176.5 0.5 slice.150
  177.7 0.5 slice.152
  179.4 1.1 collective-permute-done.7
  180.5 0.5 slice.154
  181.7 0.5 slice.156
  182.9 0.5 slice.158
  184.2 0.5 slice.160
  185.4 1.7 fusion.5
  (47 shorter events, 0.7 us)
Async XLA Ops:
  7.2 1.3 copy-start
  7.2 14.0 %copy-start.5 = (s32[1,128]{1,0:T(1,128)S(1)}, s32[1,128]{1,0:T(1,128)}, u32[]{:S(2)}) copy-start(s32[1,128]{1,0:T(1,128)} %param.11) | copy-start | bytes 1540
  7.2 32.4 %copy-start.1 = (bf16[1,320,1536]{2,1,0:T(8,128)(2,1)S(1)}, bf16[1,320,1536]{2,1,0:T(8,128)(2,1)}, u32[]{:S(2)}) copy-start(bf16[1,320,1536]{2,1,0:T(8,128)(2,1)} %param.9) | copy-start | bytes 2949124
  7.2 70.9 %all-gather.3.cloned.1.call-start = ((), (), s32[]{:S(2)}) async-start(), calls=%async_computation | async-start | bytes 4866048 | tf_op jit(solution)/shard_map/all_gather | solution.py:101
  9.1 135.0 %all-gather.5.cloned.1.call-start = ((), (), s32[]{:S(2)}) async-start(), calls=%async_computation.1 | async-start | bytes 4866048 | tf_op jit(solution)/shard_map/all_gather | solution.py:101
  16.3 6.5 %collective-permute-start.1 = (f32[1,1537]{1,0:T(1,128)S(1)}, f32[1,1537]{1,0:T(1,128)S(1)}, u32[]{:S(2)}, u32[]{:S(2)}) collective-permute-start(f32[1,1537]{1,0:T(1,128)S(1)} %pad_maximum_fusion.5), channel_id=1, source_target_pairs={{0,4},{4,8},{8,12},{12,16},{16,20},{20,24},{24,28},{1,5},{5,9},{9,... | collective-permute-start | bytes 18452 | tf_op jit(solution)/shard_map/ppermute | solution.py:16
  24.6 6.2 %collective-permute-start.2 = (f32[1,1537]{1,0:T(1,128)S(1)}, f32[1,1537]{1,0:T(1,128)S(1)}, u32[]{:S(2)}, u32[]{:S(2)}) collective-permute-start(f32[1,1537]{1,0:T(1,128)S(1)} %pad_maximum_fusion.6), channel_id=1, source_target_pairs={{0,8},{4,12},{8,16},{12,20},{16,24},{20,28},{1,9},{5,13},{9,17},{1... | collective-permute-start | bytes 18452 | tf_op jit(solution)/shard_map/ppermute | solution.py:16
  32.1 7.4 %collective-permute-start.3 = (f32[1,1537]{1,0:T(1,128)S(1)}, f32[1,1537]{1,0:T(1,128)S(1)}, u32[]{:S(2)}, u32[]{:S(2)}) collective-permute-start(f32[1,1537]{1,0:T(1,128)S(1)} %pad_maximum_fusion.7), channel_id=1, source_target_pairs={{0,16},{4,20},{8,24},{12,28},{1,17},{5,21},{9,25},{13,29},{2,18},{... | collective-permute-start | bytes 18452 | tf_op jit(solution)/shard_map/ppermute | solution.py:16
  42.3 5.9 %collective-permute-start.4 = (f32[1,1537]{1,0:T(1,128)S(1)}, f32[1,1537]{1,0:T(1,128)S(1)}, u32[]{:S(2)}, u32[]{:S(2)}) collective-permute-start(f32[1,1537]{1,0:T(1,128)S(1)} %pad_maximum_fusion.8), channel_id=1, source_target_pairs={{4,0},{8,4},{12,8},{16,12},{20,16},{24,20},{28,24},{5,1},{9,5},{13... | collective-permute-start | bytes 18452 | tf_op jit(solution)/shard_map/ppermute | solution.py:16
  43.6 5.9 %collective-permute-start = (bf16[1,1536]{1,0:T(2,128)(2,1)S(1)}, bf16[1,1536]{1,0:T(2,128)(2,1)S(1)}, u32[]{:S(2)}, u32[]{:S(2)}) collective-permute-start(bf16[1,1536]{1,0:T(2,128)(2,1)S(1)} %get-tuple-element.9), channel_id=1, source_target_pairs={{0,4},{4,8},{8,12},{12,16},{16,20},{20,24},{24,28},{1,5},{5,9},{9,... | collective-permute-start | bytes 9224 | tf_op jit(solution)/shard_map/ppermute | solution.py:16
  148.5 1.3 copy-start.3
  152.6 2.2 %copy-start.4 = (f32[322,1536]{1,0:T(8,128)S(1)}, f32[322,1536]{1,0:T(8,128)}, u32[]{:S(2)}) copy-start(f32[322,1536]{1,0:T(8,128)} %copy-done.3) | copy-start | bytes 5935108
  155.4 1.2 copy-start.2
  158.8 14.8 %slice-start = ((s8[4718592]{0:T(1024)(128)(4,1)}), s8[4194304]{0:T(1024)(128)(4,1)S(1)}, s32[]{:S(2)}) async-start(s8[4718592]{0:T(1024)(128)(4,1)} %bitcast.67), calls=%async_computation.2 | async-start | bytes 8388608
  160.2 25.2 %collective-permute-start.11 = (f32[1,1537]{1,0:T(1,128)S(1)}, f32[1,1537]{1,0:T(1,128)S(1)}, u32[]{:S(2)}, u32[]{:S(2)}) collective-permute-start(f32[1,1537]{1,0:T(1,128)S(1)} %pad_maximum_fusion.9), channel_id=1, source_target_pairs={{28,0},{29,1},{30,2},{31,3}} | collective-permute-start | bytes 18452 | tf_op jit(solution)/shard_map/ppermute | solution.py:16
  161.5 22.7 %collective-permute-start.10 = (f32[1,1537]{1,0:T(1,128)S(1)}, f32[1,1537]{1,0:T(1,128)S(1)}, u32[]{:S(2)}, u32[]{:S(2)}) collective-permute-start(f32[1,1537]{1,0:T(1,128)S(1)} %pad_maximum_fusion.9), channel_id=1, source_target_pairs={{24,0},{28,4},{25,1},{29,5},{26,2},{30,6},{27,3},{31,7}} | collective-permute-start | bytes 18452 | tf_op jit(solution)/shard_map/ppermute | solution.py:16
  162.8 20.1 %collective-permute-start.9 = (f32[1,1537]{1,0:T(1,128)S(1)}, f32[1,1537]{1,0:T(1,128)S(1)}, u32[]{:S(2)}, u32[]{:S(2)}) collective-permute-start(f32[1,1537]{1,0:T(1,128)S(1)} %pad_maximum_fusion.9), channel_id=1, source_target_pairs={{20,0},{24,4},{28,8},{21,1},{25,5},{29,9},{22,2},{26,6},{30,10},{2... | collective-permute-start | bytes 18452 | tf_op jit(solution)/shard_map/ppermute | solution.py:16
  164.1 6.9 %collective-permute-start.6 = (f32[1,1537]{1,0:T(1,128)S(1)}, f32[1,1537]{1,0:T(1,128)S(1)}, u32[]{:S(2)}, u32[]{:S(2)}) collective-permute-start(f32[1,1537]{1,0:T(1,128)S(1)} %pad_maximum_fusion.9), channel_id=1, source_target_pairs={{8,0},{12,4},{16,8},{20,12},{24,16},{28,20},{9,1},{13,5},{17,9},{2... | collective-permute-start | bytes 18452 | tf_op jit(solution)/shard_map/ppermute | solution.py:16
  165.4 6.9 %collective-permute-start.5 = (f32[1,1537]{1,0:T(1,128)S(1)}, f32[1,1537]{1,0:T(1,128)S(1)}, u32[]{:S(2)}, u32[]{:S(2)}) collective-permute-start(f32[1,1537]{1,0:T(1,128)S(1)} %pad_maximum_fusion.9), channel_id=1, source_target_pairs={{4,0},{8,4},{12,8},{16,12},{20,16},{24,20},{28,24},{5,1},{9,5},{13... | collective-permute-start | bytes 18452 | tf_op jit(solution)/shard_map/ppermute | solution.py:16
  166.7 6.9 %slice-start.1 = ((s8[4718592]{0:T(1024)(128)(4,1)}), s8[524288]{0:T(1024)(128)(4,1)S(1)}, s32[]{:S(2)}) async-start(s8[4718592]{0:T(1024)(128)(4,1)} %bitcast.67), calls=%async_computation.3 | async-start | bytes 1048576
  171.0 10.8 %collective-permute-start.8 = (f32[1,1537]{1,0:T(1,128)S(1)}, f32[1,1537]{1,0:T(1,128)S(1)}, u32[]{:S(2)}, u32[]{:S(2)}) collective-permute-start(f32[1,1537]{1,0:T(1,128)S(1)} %pad_maximum_fusion.9), channel_id=1, source_target_pairs={{16,0},{20,4},{24,8},{28,12},{17,1},{21,5},{25,9},{29,13},{18,2},{... | collective-permute-start | bytes 18452 | tf_op jit(solution)/shard_map/ppermute | solution.py:16
  172.3 8.2 %collective-permute-start.7 = (f32[1,1537]{1,0:T(1,128)S(1)}, f32[1,1537]{1,0:T(1,128)S(1)}, u32[]{:S(2)}, u32[]{:S(2)}) collective-permute-start(f32[1,1537]{1,0:T(1,128)S(1)} %pad_maximum_fusion.9), channel_id=1, source_target_pairs={{12,0},{16,4},{20,8},{24,12},{28,16},{13,1},{17,5},{21,9},{25,13},... | collective-permute-start | bytes 18452 | tf_op jit(solution)/shard_map/ppermute | solution.py:16
Sparse Core Ops, SparseCore 0:
  11.6 66.4 all-gather.2
  81.6 62.4 all-gather.4

commit v7 on v4

--- a/solution.py
+++ b/solution.py
@@ -68,6 +68,15 @@
     return total
 
 
+def split_dot(rows, blocks, index, width):
+    total = None
+    for block, at in zip(blocks, index):
+        part = lax.dynamic_slice_in_dim(rows, at * width, width, axis=1)
+        term = jnp.dot(part, block, preferred_element_type=jnp.float32)
+        total = term if total is None else total + term
+    return total
+
+
 def permute_cols(rows, index, width):
     return jnp.concatenate(
         [lax.dynamic_slice_in_dim(rows, at * width, width, axis=1) for at in index], axis=1
@@ -96,8 +105,8 @@
     width = query_weight.shape[0]
     shard_index = lax.axis_index("seq")
     pairs, index = gather_blocks((query_weight, key_weight), "dp")
-    full_query = jnp.concatenate([p[0] for p in pairs], axis=0)
-    full_key = jnp.concatenate([p[1] for p in pairs], axis=0)
+    query_blocks = [p[0] for p in pairs]
+    key_blocks = [p[1] for p in pairs]
     position = jnp.arange(token_count)
     later_rows = (shard_index > 0) | (position > 0)
     segment_total = segment_counts[0, 0]
@@ -130,9 +139,8 @@
     next_row = from_next[:, :-1].astype(token_rows.dtype)
     next_cos_grad = from_next[:, -1:]
     rows_ext = jnp.concatenate([token_rows, prev_row, next_row], axis=0)
-    rows_perm = permute_cols(rows_ext, index, width)
-    queries_ext = jnp.dot(rows_perm, full_query, preferred_element_type=jnp.float32)
-    keys_ext = jnp.dot(rows_perm, full_key, preferred_element_type=jnp.float32)
+    queries_ext = split_dot(rows_ext, query_blocks, index, width)
+    keys_ext = split_dot(rows_ext, key_blocks, index, width)
     queries = queries_ext[:token_count]
     key_rows = keys_ext[:token_count]
     query_unit, query_scale = unit_of(queries)
@@ -162,13 +170,12 @@
     query_grad = normalize_grad(queries, query_scale, unit_q_grad).astype(jnp.bfloat16)
     unit_k_grad = jnp.concatenate([prior_grad[1:], next_cos_grad * query_next], axis=0)
     key_grad = normalize_grad(key_rows, key_scale, unit_k_grad).astype(jnp.bfloat16)
-    x_grad = lax.dot_general(
-        query_grad, full_query, contract_last, preferred_element_type=jnp.float32
-    )
-    x_grad = x_grad + lax.dot_general(
-        key_grad, full_key, contract_last, preferred_element_type=jnp.float32
-    )
-    x_grad = x_grad.astype(jnp.bfloat16)
+    parts = []
+    for q_block, k_block in zip(query_blocks, key_blocks):
+        part = lax.dot_general(query_grad, q_block, contract_last, preferred_element_type=jnp.float32)
+        part = part + lax.dot_general(key_grad, k_block, contract_last, preferred_element_type=jnp.float32)
+        parts.append(part.astype(jnp.bfloat16))
+    x_grad = jnp.concatenate(parts, axis=1)
     slots = jnp.arange(len(index), dtype=jnp.int32)
     order = jnp.sum(jnp.where(jnp.stack(index)[None, :] == slots[:, None], slots[None, :], 0), axis=1)
     x_grad = permute_cols(x_grad, [order[j] for j in range(len(index))], width)

time: 117 us -> 115 us (0.983)
  local copies, waits for them, and re-layouts: 19.3 us -> 13.3 us
  matrix products: 21.7 us -> 25.5 us
  other arithmetic: 18 us -> 19.8 us
  waiting for transfers between devices: 11.2 us -> 9.88 us
    dot_general x4 -> x16, matrix products: 12 us -> 16.3 us  [the longest x8 8.06 us: split_dot(): term = jnp.dot(part, block, preferred_element_type=jnp.float32)]
    unnamed x36 -> x38, local copies, waits for them, and re-layouts: 10.7 us -> 6.68 us
  transfers between devices with their start and end apart: 18 -> 18, of which waited for: 4 -> 4; matrix products, arithmetic and copies ran while one was open for 39% -> 36% of each run, Pallas kernels for 0% -> 0%
where the time goes in v7:
time: 115 us; the launch traced here: 114 us
  starting transfers between devices  30.6 us (27%)
  matrix products  25.5 us (22%)
  other arithmetic  19.8 us (17%)
  between operations  15.1 us (13%)
  local copies, waits for them, and re-layouts  13.3 us (12%)
  waiting for transfers between devices  9.88 us (9%)
    ppermute x12, starting transfers between devices, shifted(): return lax.ppermute(block, axis, route)  26.4 us
    dot_general x8, matrix products, split_dot(): term = jnp.dot(part, block, preferred_element_type=jnp.float32)  8.06 us
    unnamed x38, local copies, waits for them, and re-layouts  6.68 us
    ppermute x12, waiting for transfers between devices, shifted(): return lax.ppermute(block, axis, route)  4.95 us
    ppermute x2, waiting for transfers between devices, gather_blocks(): pairs.append(lax.ppermute(blocks, axis, route))  4.92 us
    dot_general x4, matrix products, per_device(): lax.dot_general(query_grad, q_block, contract_last, preferred_element_typ...  4.13 us
    dot_general x4, matrix products, per_device(): lax.dot_general(key_grad, k_block, contract_last, preferred_element_type=...  4.11 us
    ppermute x2, starting transfers between devices, gather_blocks(): pairs.append(lax.ppermute(blocks, axis, route))  3.6 us
  transfers between devices with their start and end apart: 18, of which 4 were waited for; matrix products, arithmetic and copies ran while one was open for 36% of the time, Pallas kernels for 0%

profile of v7, /device:TPU:0, one launch (start us, length us, event | category | flops | bytes accessed | tf_op | source)
XLA Modules:
  0.0 114.2 jit_solution(14856653500903422069)
XLA Ops:
  0.6 3.0 %collective-permute-start.5 = (bf16[384,1536]{1,0:T(8,128)(2,1)}, bf16[384,1536]{1,0:T(8,128)(2,1)S(1)}, u32[]{:S(2)}, u32[]{:S(2)}) collective-permute-start(bf16[384,1536]{1,0:T(8,128)(2,1)} %param.14), channel_id=1, source_target_pairs={{0,2},{1,3},{2,0},{3,1},{4,6},{5,7},{6,4},{7,5},{8,10},{9,11},{10,... | collective-permute-start | bytes 3538952 | tf_op jit(solution)/shard_map/ppermute | solution.py:50
  4.3 0.7 fusion.66
  5.8 0.7 bitcast_select_fusion
  6.6 2.0 %fusion.16 = f32[128,1536]{1,0:T(8,128)S(1)} fusion(bf16[1,128,1536]{2,1,0:T(8,128)(2,1)} %param.10, f32[128]{0:T(128)S(1)} %bitcast_select_fusion, f32[128]{0:T(128)S(1)} %reduce.2), kind=kOutput, calls=%fused_computation.46 | convolution fusion | flops 302448640 | bytes 1180672 | tf_op jit(solution)/shard_map/dot_general | solution.py:128
  8.6 0.9 copy-done.18
  9.5 0.6 pad_maximum_fusion.4
  10.1 3.4 %collective-permute-start.1 = (f32[1,1537]{1,0:T(1,128)S(1)}, f32[1,1537]{1,0:T(1,128)S(1)}, u32[]{:S(2)}, u32[]{:S(2)}) collective-permute-start(f32[1,1537]{1,0:T(1,128)S(1)} %pad_maximum_fusion.4), channel_id=1, source_target_pairs={{0,4},{4,8},{8,12},{12,16},{16,20},{20,24},{24,28},{1,5},{5,9},{9,... | collective-permute-start | bytes 18452 | tf_op jit(solution)/shard_map/ppermute | solution.py:16
  13.5 0.8 slice_bitcast_fusion
  14.3 3.5 %collective-permute-start = (bf16[1,1536]{1,0:T(2,128)(2,1)S(1)}, bf16[1,1536]{1,0:T(2,128)(2,1)S(1)}, u32[]{:S(2)}, u32[]{:S(2)}) collective-permute-start(bf16[1,1536]{1,0:T(2,128)(2,1)S(1)} %get-tuple-element.15), channel_id=1, source_target_pairs={{0,4},{4,8},{8,12},{12,16},{16,20},{20,24},{24,28},{1,5},{5,9},{9,... | collective-permute-start | bytes 9224 | tf_op jit(solution)/shard_map/ppermute | solution.py:16
  18.3 0.8 convert_reduce_fusion
  19.1 0.6 subtract_exponential_fusion
  19.7 0.8 fusion.34
  22.9 0.8 multiply_add_fusion.1
  23.7 3.5 %collective-permute-start.2 = (f32[1,1537]{1,0:T(1,128)S(1)}, f32[1,1537]{1,0:T(1,128)S(1)}, u32[]{:S(2)}, u32[]{:S(2)}) collective-permute-start(f32[1,1537]{1,0:T(1,128)S(1)} %pad_maximum_fusion.5), channel_id=1, source_target_pairs={{0,8},{4,12},{8,16},{12,20},{16,24},{20,28},{1,9},{5,13},{9,17},{1... | collective-permute-start | bytes 18452 | tf_op jit(solution)/shard_map/ppermute | solution.py:16
  27.4 1.2 %collective-permute-done.2 = f32[1,1537]{1,0:T(1,128)S(1)} collective-permute-done((f32[1,1537]{1,0:T(1,128)S(1)}, f32[1,1537]{1,0:T(1,128)S(1)}, u32[]{:S(2)}, u32[]{:S(2)}) %collective-permute-start.2) | collective-permute-done | bytes 6180 | tf_op jit(solution)/shard_map/ppermute | solution.py:16
  29.8 5.2 %collective-permute-start.3 = (f32[1,1537]{1,0:T(1,128)S(1)}, f32[1,1537]{1,0:T(1,128)S(1)}, u32[]{:S(2)}, u32[]{:S(2)}) collective-permute-start(f32[1,1537]{1,0:T(1,128)S(1)} %pad_maximum_fusion.6), channel_id=1, source_target_pairs={{0,16},{4,20},{8,24},{12,28},{1,17},{5,21},{9,25},{13,29},{2,18},{... | collective-permute-start | bytes 18452 | tf_op jit(solution)/shard_map/ppermute | solution.py:16
  37.1 2.9 %fusion.6 = f32[320]{0:T(512)S(1)} fusion(bf16[1,320,1536]{2,1,0:T(8,128)(2,1)} %param.9, f32[1536]{0:T(1024)S(1)} %fusion.51, f32[320]{0:T(512)S(1)} %get-tuple-element.6, f32[128,1536]{1,0:T(8,128)} %copy-done.18, f32[128]{0:T(128)S(1)} %get-tuple-element.20, s32[320]{0:T(512)S(1)} %broadcast_add_fusion), kind=kOutput, calls=%fused_computation.27 | convolution fusion | flops 757866176 | bytes 1779968 | tf_op jit(solution)/shard_map/dot_general | solution.py:133
  40.5 0.7 pad_maximum_fusion.7
  41.2 1.5 %collective-permute-start.4 = (f32[1,1537]{1,0:T(1,128)S(1)}, f32[1,1537]{1,0:T(1,128)S(1)}, u32[]{:S(2)}, u32[]{:S(2)}) collective-permute-start(f32[1,1537]{1,0:T(1,128)S(1)} %pad_maximum_fusion.7), channel_id=1, source_target_pairs={{4,0},{8,4},{12,8},{16,12},{20,16},{24,20},{28,24},{5,1},{9,5},{13... | collective-permute-start | bytes 18452 | tf_op jit(solution)/shard_map/ppermute | solution.py:16
  42.7 0.6 fusion.71
  45.9 0.8 collective-permute-done.4
  47.4 0.7 fusion.29
  48.1 1.0 copy-done.10
  49.0 0.7 convolution_add_fusion.5
  49.7 0.6 collective-permute-start.7
  50.3 4.9 %collective-permute-done.8 = bf16[384,1536]{1,0:T(8,128)(2,1)} collective-permute-done((bf16[384,1536]{1,0:T(8,128)(2,1)}, bf16[384,1536]{1,0:T(8,128)(2,1)}, u32[]{:S(2)}, u32[]{:S(2)}) %collective-permute-start.8) | collective-permute-done | bytes 1179680 | tf_op jit(solution)/shard_map/ppermute | solution.py:50
  55.2 1.9 %fusion.27 = f32[322,1536]{1,0:T(8,128)S(1)} fusion(bf16[384,1536]{1,0:T(8,128)(2,1)} %collective-permute-done.8, bf16[322,1536]{1,0:T(8,128)(2,1)S(1)} %pad_maximum_fusion.2, s32[]{:T(128)S(6)} %select_n.100), kind=kOutput, calls=%fused_computation.57 | convolution fusion | flops 379846656 | bytes 3409924 | tf_op jit(solution)/shard_map/dot_general | solution.py:75
  57.2 0.7 convolution_add_fusion.2
  57.9 2.0 %convolution_add_fusion.4 = f32[322,1536]{1,0:T(8,128)S(1)} fusion(f32[322,1536]{1,0:T(8,128)S(1)} %convolution_add_fusion.5, bf16[384,1536]{1,0:T(8,128)(2,1)} %collective-permute-done.6, bf16[322,1536]{1,0:T(8,128)(2,1)S(1)} %pad_maximum_fusion.2, s32[]{:T(128)S(6)} %select_n.101), kind=kOutput, calls=%fused_computation.4 | convolution fusion | flops 380341248 | bytes 5425156 | tf_op jit(solution)/shard_map/dot_general | solution.py:75
  59.9 0.7 convolution_add_fusion.1
  61.0 0.7 convolution_add_fusion
  62.1 0.6 multiply_reduce_fusion.6
  62.7 1.4 %multiply_reduce_fusion.3 = (f32[320]{0:T(512)S(1)}, f32[320,1536]{1,0:T(8,128)}) fusion(f32[322,1536]{1,0:T(8,128)S(1)} %convolution_add_fusion), kind=kLoop, calls=%fused_computation.24 | loop fusion | flops 982720 | bytes 3933440 | tf_op jit(solution)/shard_map/reduce_sum | solution.py:87
  64.2 0.7 convolution_add_fusion.3
  65.2 1.3 %copy-done = f32[322,1536]{1,0:T(8,128)} copy-done((f32[322,1536]{1,0:T(8,128)}, f32[322,1536]{1,0:T(8,128)S(1)}, u32[]{:S(2)}) %copy-start) | copy-done | bytes 1978392
  66.6 0.6 multiply_reduce_fusion.5
  67.9 1.9 %slice_multiply_fusion.1 = f32[319,1536]{1,0:T(8,128)S(1)} fusion(f32[320,1536]{1,0:T(8,128)} %get-tuple-element.10, f32[319]{0:T(512)S(1)} %bitcast.91), kind=kLoop, calls=%fused_computation.16 | loop fusion | flops 489984 | bytes 3921148 | tf_op jit(solution)/shard_map/mul | solution.py:88
  70.0 0.6 multiply_reduce_fusion.2
  70.6 2.0 %multiply_reduce_fusion = (f32[320]{0:T(512)S(1)}, f32[320,1536]{1,0:T(8,128)}, bf16[320,1536]{1,0:T(8,128)(2,1)S(1)}) fusion(f32[319,1536]{1,0:T(8,128)S(1)} %slice_multiply_fusion.1, f32[1,1536]{1,0:T(1,128)S(1)} %slice_multiply_fusion.10, f32[320]{0:T(512)S(1)} %get-tuple-element.18, f32[322,1536]{1,0:T(8,128)S(1)} %copy-done.1, ...), kind=kLoop, calls=%fused_computation.19 | loop fusion | flops 4423360 | bytes 6886400 | tf_op jit(solution)/shard_map/reduce_sum | solution.py:151
  72.6 1.2 %fusion.5 = f32[128,1536]{1,0:T(8,128)S(1)} fusion(bf16[1,320,1536]{2,1,0:T(8,128)(2,1)S(1)} %copy-done.16, f32[320]{0:T(512)S(1)} %subtract_select_fusion, s32[320]{0:T(512)S(1)} %broadcast_add_fusion), kind=kOutput, calls=%fused_computation.14 | convolution fusion | flops 755998720 | bytes 1772032 | tf_op jit(solution)/shard_map/dot_general | solution.py:155
  73.9 0.9 fusion.11
  75.4 0.6 pad_maximum_fusion.8
  75.9 1.3 %collective-permute-start.17 = (f32[1,1537]{1,0:T(1,128)S(1)}, f32[1,1537]{1,0:T(1,128)S(1)}, u32[]{:S(2)}, u32[]{:S(2)}) collective-permute-start(f32[1,1537]{1,0:T(1,128)S(1)} %pad_maximum_fusion.8), channel_id=1, source_target_pairs={{28,0},{29,1},{30,2},{31,3}} | collective-permute-start | bytes 18452 | tf_op jit(solution)/shard_map/ppermute | solution.py:16
  77.2 1.3 %collective-permute-start.16 = (f32[1,1537]{1,0:T(1,128)S(1)}, f32[1,1537]{1,0:T(1,128)S(1)}, u32[]{:S(2)}, u32[]{:S(2)}) collective-permute-start(f32[1,1537]{1,0:T(1,128)S(1)} %pad_maximum_fusion.8), channel_id=1, source_target_pairs={{24,0},{28,4},{25,1},{29,5},{26,2},{30,6},{27,3},{31,7}} | collective-permute-start | bytes 18452 | tf_op jit(solution)/shard_map/ppermute | solution.py:16
  78.5 1.3 %collective-permute-start.15 = (f32[1,1537]{1,0:T(1,128)S(1)}, f32[1,1537]{1,0:T(1,128)S(1)}, u32[]{:S(2)}, u32[]{:S(2)}) collective-permute-start(f32[1,1537]{1,0:T(1,128)S(1)} %pad_maximum_fusion.8), channel_id=1, source_target_pairs={{20,0},{24,4},{28,8},{21,1},{25,5},{29,9},{22,2},{26,6},{30,10},{2... | collective-permute-start | bytes 18452 | tf_op jit(solution)/shard_map/ppermute | solution.py:16
  79.8 1.3 %collective-permute-start.12 = (f32[1,1537]{1,0:T(1,128)S(1)}, f32[1,1537]{1,0:T(1,128)S(1)}, u32[]{:S(2)}, u32[]{:S(2)}) collective-permute-start(f32[1,1537]{1,0:T(1,128)S(1)} %pad_maximum_fusion.8), channel_id=1, source_target_pairs={{8,0},{12,4},{16,8},{20,12},{24,16},{28,20},{9,1},{13,5},{17,9},{2... | collective-permute-start | bytes 18452 | tf_op jit(solution)/shard_map/ppermute | solution.py:16
  81.1 1.5 %collective-permute-start.11 = (f32[1,1537]{1,0:T(1,128)S(1)}, f32[1,1537]{1,0:T(1,128)S(1)}, u32[]{:S(2)}, u32[]{:S(2)}) collective-permute-start(f32[1,1537]{1,0:T(1,128)S(1)} %pad_maximum_fusion.8), channel_id=1, source_target_pairs={{4,0},{8,4},{12,8},{16,12},{20,16},{24,20},{28,24},{5,1},{9,5},{13... | collective-permute-start | bytes 18452 | tf_op jit(solution)/shard_map/ppermute | solution.py:16
  83.3 1.5 %multiply_multiply_fusion = f32[1,1536]{1,0:T(1,128)S(1)} fusion(f32[322,1536]{1,0:T(8,128)} %copy-done, f32[]{:T(128)S(6)} %rsqrt.33, f32[]{:T(128)} %bitcast.14), kind=kLoop, calls=%fused_computation.101 | loop fusion | flops 3072 | bytes 12296 | tf_op jit(solution)/shard_map/mul | solution.py:171
  84.8 1.8 %slice_multiply_fusion = f32[319,1536]{1,0:T(8,128)S(1)} fusion(f32[320,1536]{1,0:T(8,128)} %get-tuple-element.5, f32[319]{0:T(512)S(1)} %slice.161), kind=kLoop, calls=%fused_computation.15 | loop fusion | flops 489984 | bytes 3921148 | tf_op jit(solution)/shard_map/mul | solution.py:169
  87.2 0.9 copy-done.11
  88.2 0.7 fusion.72
  88.9 0.7 fusion.7
  90.1 0.7 fusion.75
  90.8 0.6 copy-done.13
  91.4 0.7 fusion.74
  92.1 2.0 %fusion.73 = f32[320,384]{1,0:T(8,128)S(1)} fusion(bf16[320,1536]{1,0:T(8,128)(2,1)S(1)} %subtract_convert_fusion, bf16[384,1536]{1,0:T(8,128)(2,1)} %collective-permute-done.8), kind=kOutput, calls=%fused_computation.151 | convolution fusion | flops 377487360 | bytes 2654208 | tf_op jit(solution)/shard_map/dot_general | solution.py:176
  94.2 0.7 fusion.10
  94.9 2.1 %fusion.9 = bf16[320,384]{1,0:T(8,128)(2,1)S(1)} fusion(f32[320,384]{1,0:T(8,128)S(1)} %fusion.74, bf16[320,1536]{1,0:T(8,128)(2,1)S(1)} %get-tuple-element.8, bf16[384,1536]{1,0:T(8,128)(2,1)} %collective-permute-done.6), kind=kOutput, calls=%fused_computation.34 | convolution fusion | flops 377733120 | bytes 2899968 | tf_op jit(solution)/shard_map/dot_general | solution.py:175
  96.9 0.7 fusion.8
  97.9 1.4 %collective-permute-start.14 = (f32[1,1537]{1,0:T(1,128)S(1)}, f32[1,1537]{1,0:T(1,128)S(1)}, u32[]{:S(2)}, u32[]{:S(2)}) collective-permute-start(f32[1,1537]{1,0:T(1,128)S(1)} %pad_maximum_fusion.8), channel_id=1, source_target_pairs={{16,0},{20,4},{24,8},{28,12},{17,1},{21,5},{25,9},{29,13},{18,2},{... | collective-permute-start | bytes 18452 | tf_op jit(solution)/shard_map/ppermute | solution.py:16
  99.3 1.3 %collective-permute-start.13 = (f32[1,1537]{1,0:T(1,128)S(1)}, f32[1,1537]{1,0:T(1,128)S(1)}, u32[]{:S(2)}, u32[]{:S(2)}) collective-permute-start(f32[1,1537]{1,0:T(1,128)S(1)} %pad_maximum_fusion.8), channel_id=1, source_target_pairs={{12,0},{16,4},{20,8},{24,12},{28,16},{13,1},{17,5},{21,9},{25,13},... | collective-permute-start | bytes 18452 | tf_op jit(solution)/shard_map/ppermute | solution.py:16
  100.6 1.0 maximum_bitcast_fusion
  104.6 3.0 %collective-permute-done.13 = f32[1,1537]{1,0:T(1,128)S(1)} collective-permute-done((f32[1,1537]{1,0:T(1,128)S(1)}, f32[1,1537]{1,0:T(1,128)S(1)}, u32[]{:S(2)}, u32[]{:S(2)}) %collective-permute-start.13) | collective-permute-done | bytes 6180 | tf_op jit(solution)/shard_map/ppermute | solution.py:16
  112.5 1.7 %fusion.3 = bf16[1,128,1536]{2,1,0:T(8,128)(2,1)} fusion(f32[128,1536]{1,0:T(8,128)S(1)} %copy-done.3, f32[1536]{0:T(1024)S(1)} %fusion.52, f32[128]{0:T(128)S(1)} %get-tuple-element.19, f32[128]{0:T(128)S(1)} %bitcast_select_fusion, f32[128]{0:T(128)S(1)} %reduce.2), kind=kOutput, calls=%fused_computation.12 | convolution fusion | flops 302841856 | bytes 1187328 | tf_op jit(solution)/shard_map/dot_general | solution.py:164
  (93 shorter events, 10.5 us)
Async XLA Ops:
  0.6 46.7 %collective-permute-start.5 = (bf16[384,1536]{1,0:T(8,128)(2,1)}, bf16[384,1536]{1,0:T(8,128)(2,1)S(1)}, u32[]{:S(2)}, u32[]{:S(2)}) collective-permute-start(bf16[384,1536]{1,0:T(8,128)(2,1)} %param.14), channel_id=1, source_target_pairs={{0,2},{1,3},{2,0},{3,1},{4,6},{5,7},{6,4},{7,5},{8,10},{9,11},{10,... | collective-permute-start | bytes 3538952 | tf_op jit(solution)/shard_map/ppermute | solution.py:50
  3.7 54.2 %collective-permute-start.6 = (bf16[384,1536]{1,0:T(8,128)(2,1)}, bf16[384,1536]{1,0:T(8,128)(2,1)}, u32[]{:S(2)}, u32[]{:S(2)}) collective-permute-start(bf16[384,1536]{1,0:T(8,128)(2,1)} %param.14), channel_id=1, source_target_pairs={{0,1},{1,0},{2,3},{3,2},{4,5},{5,4},{6,7},{7,6},{8,9},{9,8},{10,11... | collective-permute-start | bytes 3538952 | tf_op jit(solution)/shard_map/ppermute | solution.py:53
  6.6 40.2 %copy-start.6 = (bf16[384,1536]{1,0:T(8,128)(2,1)S(1)}, bf16[384,1536]{1,0:T(8,128)(2,1)}, u32[]{:S(2)}) copy-start(bf16[384,1536]{1,0:T(8,128)(2,1)} %param.15) | copy-start | bytes 3538948
  6.6 40.7 %copy-start.17 = (bf16[1,320,1536]{2,1,0:T(8,128)(2,1)S(1)}, bf16[1,320,1536]{2,1,0:T(8,128)(2,1)}, u32[]{:S(2)}) copy-start(bf16[1,320,1536]{2,1,0:T(8,128)(2,1)} %param.8) | copy-start | bytes 2949124
  8.6 0.9 copy-start.18
  10.1 11.1 %collective-permute-start.1 = (f32[1,1537]{1,0:T(1,128)S(1)}, f32[1,1537]{1,0:T(1,128)S(1)}, u32[]{:S(2)}, u32[]{:S(2)}) collective-permute-start(f32[1,1537]{1,0:T(1,128)S(1)} %pad_maximum_fusion.4), channel_id=1, source_target_pairs={{0,4},{4,8},{8,12},{12,16},{16,20},{20,24},{24,28},{1,5},{5,9},{9,... | collective-permute-start | bytes 18452 | tf_op jit(solution)/shard_map/ppermute | solution.py:16
  14.3 33.0 %collective-permute-start = (bf16[1,1536]{1,0:T(2,128)(2,1)S(1)}, bf16[1,1536]{1,0:T(2,128)(2,1)S(1)}, u32[]{:S(2)}, u32[]{:S(2)}) collective-permute-start(bf16[1,1536]{1,0:T(2,128)(2,1)S(1)} %get-tuple-element.15), channel_id=1, source_target_pairs={{0,4},{4,8},{8,12},{12,16},{16,20},{20,24},{24,28},{1,5},{5,9},{9,... | collective-permute-start | bytes 9224 | tf_op jit(solution)/shard_map/ppermute | solution.py:16
  17.7 37.5 %collective-permute-start.8 = (bf16[384,1536]{1,0:T(8,128)(2,1)}, bf16[384,1536]{1,0:T(8,128)(2,1)}, u32[]{:S(2)}, u32[]{:S(2)}) collective-permute-start(bf16[384,1536]{1,0:T(8,128)(2,1)} %param.15), channel_id=1, source_target_pairs={{0,2},{1,3},{2,0},{3,1},{4,6},{5,7},{6,4},{7,5},{8,10},{9,11},{10,... | collective-permute-start | bytes 3538952 | tf_op jit(solution)/shard_map/ppermute | solution.py:50
  23.7 4.8 %collective-permute-start.2 = (f32[1,1537]{1,0:T(1,128)S(1)}, f32[1,1537]{1,0:T(1,128)S(1)}, u32[]{:S(2)}, u32[]{:S(2)}) collective-permute-start(f32[1,1537]{1,0:T(1,128)S(1)} %pad_maximum_fusion.5), channel_id=1, source_target_pairs={{0,8},{4,12},{8,16},{12,20},{16,24},{20,28},{1,9},{5,13},{9,17},{1... | collective-permute-start | bytes 18452 | tf_op jit(solution)/shard_map/ppermute | solution.py:16
  29.8 7.3 %collective-permute-start.3 = (f32[1,1537]{1,0:T(1,128)S(1)}, f32[1,1537]{1,0:T(1,128)S(1)}, u32[]{:S(2)}, u32[]{:S(2)}) collective-permute-start(f32[1,1537]{1,0:T(1,128)S(1)} %pad_maximum_fusion.6), channel_id=1, source_target_pairs={{0,16},{4,20},{8,24},{12,28},{1,17},{5,21},{9,25},{13,29},{2,18},{... | collective-permute-start | bytes 18452 | tf_op jit(solution)/shard_map/ppermute | solution.py:16
  41.2 5.5 %collective-permute-start.4 = (f32[1,1537]{1,0:T(1,128)S(1)}, f32[1,1537]{1,0:T(1,128)S(1)}, u32[]{:S(2)}, u32[]{:S(2)}) collective-permute-start(f32[1,1537]{1,0:T(1,128)S(1)} %pad_maximum_fusion.7), channel_id=1, source_target_pairs={{4,0},{8,4},{12,8},{16,12},{20,16},{24,20},{28,24},{5,1},{9,5},{13... | collective-permute-start | bytes 18452 | tf_op jit(solution)/shard_map/ppermute | solution.py:16
  46.7 13.2 %collective-permute-start.9 = (bf16[384,1536]{1,0:T(8,128)(2,1)S(1)}, bf16[384,1536]{1,0:T(8,128)(2,1)S(1)}, u32[]{:S(2)}, u32[]{:S(2)}) collective-permute-start(bf16[384,1536]{1,0:T(8,128)(2,1)S(1)} %copy-done.6), channel_id=1, source_target_pairs={{0,1},{1,0},{2,3},{3,2},{4,5},{5,4},{6,7},{7,6},{8,9},{9,8},{10,11... | collective-permute-start | bytes 3538952 | tf_op jit(solution)/shard_map/ppermute | solution.py:53
  47.3 1.7 %copy-start.10 = (bf16[384,1536]{1,0:T(8,128)(2,1)S(1)}, bf16[384,1536]{1,0:T(8,128)(2,1)}, u32[]{:S(2)}) copy-start(bf16[384,1536]{1,0:T(8,128)(2,1)} %param.14) | copy-start | bytes 3538948
  47.4 2.4 %copy-start.4 = (bf16[384,1536]{1,0:T(8,128)(2,1)}, bf16[384,1536]{1,0:T(8,128)(2,1)S(1)}, u32[]{:S(2)}) copy-start(bf16[384,1536]{1,0:T(8,128)(2,1)S(1)} %collective-permute-done.5) | copy-start | bytes 3538948
  49.7 14.5 %collective-permute-start.7 = (bf16[384,1536]{1,0:T(8,128)(2,1)S(1)}, bf16[384,1536]{1,0:T(8,128)(2,1)S(1)}, u32[]{:S(2)}, u32[]{:S(2)}) collective-permute-start(bf16[384,1536]{1,0:T(8,128)(2,1)S(1)} %collective-permute-done.5), channel_id=1, source_target_pairs={{0,1},{1,0},{2,3},{3,2},{4,5},{5,4},{6,7},{7,6},{8,9},{9,8},{10,11... | collective-permute-start | bytes 3538952 | tf_op jit(solution)/shard_map/ppermute | solution.py:53
  55.2 5.8 %collective-permute-start.10 = (bf16[384,1536]{1,0:T(8,128)(2,1)}, bf16[384,1536]{1,0:T(8,128)(2,1)S(1)}, u32[]{:S(2)}, u32[]{:S(2)}) collective-permute-start(bf16[384,1536]{1,0:T(8,128)(2,1)} %collective-permute-done.8), channel_id=1, source_target_pairs={{0,1},{1,0},{2,3},{3,2},{4,5},{5,4},{6,7},{7,6},{8,9},{9,8},{10,11... | collective-permute-start | bytes 3538952 | tf_op jit(solution)/shard_map/ppermute | solution.py:53
  59.9 1.1 copy-start.12
  61.0 1.1 copy-start.14
  64.2 1.1 copy-start.8
  65.2 1.3 %copy-start = (f32[322,1536]{1,0:T(8,128)}, f32[322,1536]{1,0:T(8,128)S(1)}, u32[]{:S(2)}) copy-start(f32[322,1536]{1,0:T(8,128)S(1)} %convolution_add_fusion.3) | copy-start | bytes 5935108
  67.8 2.2 %copy-start.1 = (f32[322,1536]{1,0:T(8,128)S(1)}, f32[322,1536]{1,0:T(8,128)}, u32[]{:S(2)}) copy-start(f32[322,1536]{1,0:T(8,128)} %copy-done) | copy-start | bytes 5935108
  70.6 2.0 %copy-start.16 = (bf16[1,320,1536]{2,1,0:T(8,128)(2,1)S(1)}, bf16[1,320,1536]{2,1,0:T(8,128)(2,1)}, u32[]{:S(2)}) copy-start(bf16[1,320,1536]{2,1,0:T(8,128)(2,1)} %param.9) | copy-start | bytes 2949124
  73.9 0.9 copy-start.2
  75.9 36.5 %collective-permute-start.17 = (f32[1,1537]{1,0:T(1,128)S(1)}, f32[1,1537]{1,0:T(1,128)S(1)}, u32[]{:S(2)}, u32[]{:S(2)}) collective-permute-start(f32[1,1537]{1,0:T(1,128)S(1)} %pad_maximum_fusion.8), channel_id=1, source_target_pairs={{28,0},{29,1},{30,2},{31,3}} | collective-permute-start | bytes 18452 | tf_op jit(solution)/shard_map/ppermute | solution.py:16
  77.2 34.0 %collective-permute-start.16 = (f32[1,1537]{1,0:T(1,128)S(1)}, f32[1,1537]{1,0:T(1,128)S(1)}, u32[]{:S(2)}, u32[]{:S(2)}) collective-permute-start(f32[1,1537]{1,0:T(1,128)S(1)} %pad_maximum_fusion.8), channel_id=1, source_target_pairs={{24,0},{28,4},{25,1},{29,5},{26,2},{30,6},{27,3},{31,7}} | collective-permute-start | bytes 18452 | tf_op jit(solution)/shard_map/ppermute | solution.py:16
  78.5 31.4 %collective-permute-start.15 = (f32[1,1537]{1,0:T(1,128)S(1)}, f32[1,1537]{1,0:T(1,128)S(1)}, u32[]{:S(2)}, u32[]{:S(2)}) collective-permute-start(f32[1,1537]{1,0:T(1,128)S(1)} %pad_maximum_fusion.8), channel_id=1, source_target_pairs={{20,0},{24,4},{28,8},{21,1},{25,5},{29,9},{22,2},{26,6},{30,10},{2... | collective-permute-start | bytes 18452 | tf_op jit(solution)/shard_map/ppermute | solution.py:16
  79.8 18.0 %collective-permute-start.12 = (f32[1,1537]{1,0:T(1,128)S(1)}, f32[1,1537]{1,0:T(1,128)S(1)}, u32[]{:S(2)}, u32[]{:S(2)}) collective-permute-start(f32[1,1537]{1,0:T(1,128)S(1)} %pad_maximum_fusion.8), channel_id=1, source_target_pairs={{8,0},{12,4},{16,8},{20,12},{24,16},{28,20},{9,1},{13,5},{17,9},{2... | collective-permute-start | bytes 18452 | tf_op jit(solution)/shard_map/ppermute | solution.py:16
  81.1 18.2 %collective-permute-start.11 = (f32[1,1537]{1,0:T(1,128)S(1)}, f32[1,1537]{1,0:T(1,128)S(1)}, u32[]{:S(2)}, u32[]{:S(2)}) collective-permute-start(f32[1,1537]{1,0:T(1,128)S(1)} %pad_maximum_fusion.8), channel_id=1, source_target_pairs={{4,0},{8,4},{12,8},{16,12},{20,16},{24,20},{28,24},{5,1},{9,5},{13... | collective-permute-start | bytes 18452 | tf_op jit(solution)/shard_map/ppermute | solution.py:16
  86.9 1.3 %copy-start.11 = (bf16[384,1536]{1,0:T(8,128)(2,1)S(1)}, bf16[384,1536]{1,0:T(8,128)(2,1)}, u32[]{:S(2)}) copy-start(bf16[384,1536]{1,0:T(8,128)(2,1)} %param.14) | copy-start | bytes 3538948
  87.2 1.6 %copy-start.7 = (bf16[384,1536]{1,0:T(8,128)(2,1)S(1)}, bf16[384,1536]{1,0:T(8,128)(2,1)}, u32[]{:S(2)}) copy-start(bf16[384,1536]{1,0:T(8,128)(2,1)} %param.15) | copy-start | bytes 3538948
  88.9 1.3 %copy-start.15 = (bf16[384,1536]{1,0:T(8,128)(2,1)S(1)}, bf16[384,1536]{1,0:T(8,128)(2,1)}, u32[]{:S(2)}) copy-start(bf16[384,1536]{1,0:T(8,128)(2,1)} %copy-done.14) | copy-start | bytes 3538948
  90.1 1.3 %copy-start.13 = (bf16[384,1536]{1,0:T(8,128)(2,1)S(1)}, bf16[384,1536]{1,0:T(8,128)(2,1)}, u32[]{:S(2)}) copy-start(bf16[384,1536]{1,0:T(8,128)(2,1)} %copy-done.12) | copy-start | bytes 3538948
  92.1 2.1 %copy-start.9 = (bf16[384,1536]{1,0:T(8,128)(2,1)S(1)}, bf16[384,1536]{1,0:T(8,128)(2,1)}, u32[]{:S(2)}) copy-start(bf16[384,1536]{1,0:T(8,128)(2,1)} %copy-done.8) | copy-start | bytes 3538948
  94.9 2.1 %copy-start.5 = (bf16[384,1536]{1,0:T(8,128)(2,1)S(1)}, bf16[384,1536]{1,0:T(8,128)(2,1)}, u32[]{:S(2)}) copy-start(bf16[384,1536]{1,0:T(8,128)(2,1)} %copy-done.4) | copy-start | bytes 3538948
  97.7 14.7 %copy-start.3 = (f32[128,1536]{1,0:T(8,128)S(1)}, f32[128,1536]{1,0:T(8,128)}, u32[]{:S(2)}) copy-start(f32[128,1536]{1,0:T(8,128)} %copy-done.2) | copy-start | bytes 2359300
  97.9 10.9 %collective-permute-start.14 = (f32[1,1537]{1,0:T(1,128)S(1)}, f32[1,1537]{1,0:T(1,128)S(1)}, u32[]{:S(2)}, u32[]{:S(2)}) collective-permute-start(f32[1,1537]{1,0:T(1,128)S(1)} %pad_maximum_fusion.8), channel_id=1, source_target_pairs={{16,0},{20,4},{24,8},{28,12},{17,1},{21,5},{25,9},{29,13},{18,2},{... | collective-permute-start | bytes 18452 | tf_op jit(solution)/shard_map/ppermute | solution.py:16
  99.3 8.2 %collective-permute-start.13 = (f32[1,1537]{1,0:T(1,128)S(1)}, f32[1,1537]{1,0:T(1,128)S(1)}, u32[]{:S(2)}, u32[]{:S(2)}) collective-permute-start(f32[1,1537]{1,0:T(1,128)S(1)} %pad_maximum_fusion.8), channel_id=1, source_target_pairs={{12,0},{16,4},{20,8},{24,12},{28,16},{13,1},{17,5},{21,9},{25,13},... | collective-permute-start | bytes 18452 | tf_op jit(solution)/shard_map/ppermute | solution.py:16

commit v8 on v7

--- a/solution.py
+++ b/solution.py
@@ -155,10 +155,7 @@
     slot_grad = lax.dot_general(membership, weighted_grad, contract_first, precision=exact)
     lead_grad = jnp.dot(leading[None, :], weighted_grad, precision=exact)
     back_vector = lead_grad + jnp.dot(keep_all[None, :], slot_grad, precision=exact)
-    if lax.axis_size("seq") <= 8:
-        grad_in = direct_scan(last_log, back_vector, "seq")
-    else:
-        grad_in = seq_scan(last_log, back_vector, "seq", False)
+    grad_in = seq_scan(last_log, back_vector, "seq", False)
     reach_end = jnp.exp(running[slot_count - 1] - running)
     state_grad = (
         lax.dot_general(decay_table, slot_grad, contract_first, precision=exact)

time: 115 us -> 109 us (0.948)
  waiting for transfers between devices: 9.88 us -> 15.7 us
  starting transfers between devices: 30.6 us -> 25.3 us
  local copies, waits for them, and re-layouts: 13.3 us -> 9.41 us
  other arithmetic: 19.8 us -> 17.6 us
    ppermute x12 -> x8, starting transfers between devices: 26.4 us -> 21.1 us  [shifted(): return lax.ppermute(block, axis, route)]
    ppermute x12 -> x8, waiting for transfers between devices: 4.95 us -> 9.93 us  [shifted(): return lax.ppermute(block, axis, route)]
    slice x6 -> x0, local copies, waits for them, and re-layouts: 3.07 us -> none  [direct_scan(): gap = gap + got[:, -1:]]
    unnamed x38 -> x26, local copies, waits for them, and re-layouts: 6.68 us -> 4.77 us
    mul x1, other arithmetic: 1.78 us -> 0.23 us  [per_device(): prior_grad = cos_grad[:, None] * query_unit]
    concatenate x1, other arithmetic: 0.07 us -> 1.27 us  [per_device(): rows_ext = jnp.concatenate([token_rows, prev_row, next_row], axis=0)]
    reduce_sum x1, other arithmetic: 1.99 us -> 0.79 us  [per_device(): cosine = jnp.sum(query_unit * key_prior, axis=1)]
  transfers between devices with their start and end apart: 18 -> 14, of which waited for: 4 -> 5; matrix products, arithmetic and copies ran while one was open for 36% -> 31% of each run, Pallas kernels for 0% -> 0%
where the time goes in v8:
time: 109 us; the launch traced here: 108 us
  starting transfers between devices  25.3 us (23%)
  matrix products  25.2 us (23%)
  other arithmetic  17.6 us (16%)
  waiting for transfers between devices  15.7 us (14%)
  between operations  14.6 us (13%)
  local copies, waits for them, and re-layouts  9.41 us (9%)
    ppermute x8, starting transfers between devices, shifted(): return lax.ppermute(block, axis, route)  21.1 us
    ppermute x8, waiting for transfers between devices, shifted(): return lax.ppermute(block, axis, route)  9.93 us
    dot_general x8, matrix products, split_dot(): term = jnp.dot(part, block, preferred_element_type=jnp.float32)  8.07 us
    ppermute x2, waiting for transfers between devices, gather_blocks(): pairs.append(lax.ppermute(blocks, axis, route))  5.78 us
    unnamed x26, local copies, waits for them, and re-layouts  4.77 us
    dot_general x4, matrix products, per_device(): lax.dot_general(key_grad, k_block, contract_last, preferred_element_type=...  4.12 us
    dot_general x4, matrix products, per_device(): lax.dot_general(query_grad, q_block, contract_last, preferred_element_typ...  4.06 us
    ppermute x2, starting transfers between devices, gather_blocks(): pairs.append(lax.ppermute(blocks, axis, route))  3.6 us
  transfers between devices with their start and end apart: 14, of which 5 were waited for; matrix products, arithmetic and copies ran while one was open for 31% of the time, Pallas kernels for 0%

profile of v8, /device:TPU:0, one launch (start us, length us, event | category | flops | bytes accessed | tf_op | source)
XLA Modules:
  0.0 107.9 jit_solution(16018376626103659275)
XLA Ops:
  0.6 3.0 %collective-permute-start.5 = (bf16[384,1536]{1,0:T(8,128)(2,1)}, bf16[384,1536]{1,0:T(8,128)(2,1)S(1)}, u32[]{:S(2)}, u32[]{:S(2)}) collective-permute-start(bf16[384,1536]{1,0:T(8,128)(2,1)} %param.14), channel_id=1, source_target_pairs={{0,2},{1,3},{2,0},{3,1},{4,6},{5,7},{6,4},{7,5},{8,10},{9,11},{10,... | collective-permute-start | bytes 3538952 | tf_op jit(solution)/shard_map/ppermute | solution.py:50
  4.3 0.7 fusion.61
  5.3 0.5 slice.117
  5.8 0.7 bitcast_select_fusion
  6.6 2.0 %fusion.16 = f32[128,1536]{1,0:T(8,128)S(1)} fusion(bf16[1,128,1536]{2,1,0:T(8,128)(2,1)} %param.10, f32[128]{0:T(128)S(1)} %bitcast_select_fusion, f32[128]{0:T(128)S(1)} %reduce.2), kind=kOutput, calls=%fused_computation.46 | convolution fusion | flops 302448640 | bytes 1180672 | tf_op jit(solution)/shard_map/dot_general | solution.py:128
  8.6 0.7 pad_maximum_fusion.4
  9.2 3.4 %collective-permute-start.1 = (f32[1,1537]{1,0:T(1,128)S(1)}, f32[1,1537]{1,0:T(1,128)S(1)}, u32[]{:S(2)}, u32[]{:S(2)}) collective-permute-start(f32[1,1537]{1,0:T(1,128)S(1)} %pad_maximum_fusion.4), channel_id=1, source_target_pairs={{0,4},{4,8},{8,12},{12,16},{16,20},{20,24},{24,28},{1,5},{5,9},{9,... | collective-permute-start | bytes 18452 | tf_op jit(solution)/shard_map/ppermute | solution.py:16
  12.6 0.8 slice_bitcast_fusion
  13.4 3.5 %collective-permute-start = (bf16[1,1536]{1,0:T(2,128)(2,1)S(1)}, bf16[1,1536]{1,0:T(2,128)(2,1)S(1)}, u32[]{:S(2)}, u32[]{:S(2)}) collective-permute-start(bf16[1,1536]{1,0:T(2,128)(2,1)S(1)} %get-tuple-element.15), channel_id=1, source_target_pairs={{0,4},{4,8},{8,12},{12,16},{16,20},{20,24},{24,28},{1,5},{5,9},{9,... | collective-permute-start | bytes 9224 | tf_op jit(solution)/shard_map/ppermute | solution.py:16
  16.9 0.6 collective-permute-start.8
  17.4 0.8 convert_reduce_fusion
  18.3 0.7 subtract_exponential_fusion
  18.9 0.8 fusion.34
  22.3 3.5 %collective-permute-start.2 = (f32[1,1537]{1,0:T(1,128)S(1)}, f32[1,1537]{1,0:T(1,128)S(1)}, u32[]{:S(2)}, u32[]{:S(2)}) collective-permute-start(f32[1,1537]{1,0:T(1,128)S(1)} %pad_maximum_fusion.5), channel_id=1, source_target_pairs={{0,8},{4,12},{8,16},{12,20},{16,24},{20,28},{1,9},{5,13},{9,17},{1... | collective-permute-start | bytes 18452 | tf_op jit(solution)/shard_map/ppermute | solution.py:16
  25.9 1.2 %collective-permute-done.2 = f32[1,1537]{1,0:T(1,128)S(1)} collective-permute-done((f32[1,1537]{1,0:T(1,128)S(1)}, f32[1,1537]{1,0:T(1,128)S(1)}, u32[]{:S(2)}, u32[]{:S(2)}) %collective-permute-start.2) | collective-permute-done | bytes 6180 | tf_op jit(solution)/shard_map/ppermute | solution.py:16
  27.1 0.5 slice.120
  28.4 5.2 %collective-permute-start.3 = (f32[1,1537]{1,0:T(1,128)S(1)}, f32[1,1537]{1,0:T(1,128)S(1)}, u32[]{:S(2)}, u32[]{:S(2)}) collective-permute-start(f32[1,1537]{1,0:T(1,128)S(1)} %pad_maximum_fusion.6), channel_id=1, source_target_pairs={{0,16},{4,20},{8,24},{12,28},{1,17},{5,21},{9,25},{13,29},{2,18},{... | collective-permute-start | bytes 18452 | tf_op jit(solution)/shard_map/ppermute | solution.py:16
  35.7 2.6 %fusion.6 = f32[320]{0:T(512)S(1)} fusion(bf16[1,320,1536]{2,1,0:T(8,128)(2,1)} %param.9, f32[1536]{0:T(1024)S(1)} %fusion.46, f32[320]{0:T(512)S(1)} %get-tuple-element.6, f32[128,1536]{1,0:T(8,128)S(1)} %fusion.16, f32[128]{0:T(128)S(1)} %get-tuple-element.20, s32[320]{0:T(512)S(1)} %broadcast_add_fusion), kind=kOutput, calls=%fused_computation.27 | convolution fusion | flops 757866176 | bytes 1779968 | tf_op jit(solution)/shard_map/dot_general | solution.py:133
  38.4 0.5 slice.98
  38.9 0.7 pad_maximum_fusion.7
  39.6 1.5 %collective-permute-start.4 = (f32[1,1537]{1,0:T(1,128)S(1)}, f32[1,1537]{1,0:T(1,128)S(1)}, u32[]{:S(2)}, u32[]{:S(2)}) collective-permute-start(f32[1,1537]{1,0:T(1,128)S(1)} %pad_maximum_fusion.7), channel_id=1, source_target_pairs={{4,0},{8,4},{12,8},{16,12},{20,16},{24,20},{28,24},{5,1},{9,5},{13... | collective-permute-start | bytes 18452 | tf_op jit(solution)/shard_map/ppermute | solution.py:16
  41.0 0.6 fusion.66
  44.2 0.8 collective-permute-done.4
  45.6 1.3 %pad_maximum_fusion.2 = bf16[322,1536]{1,0:T(8,128)(2,1)S(1)} fusion(bf16[1,1536]{1,0:T(2,128)(2,1)S(1)} %slice.173, bf16[1,1536]{1,0:T(2,128)(2,1)S(1)} %collective-permute-done, bf16[320,1536]{1,0:T(8,128)(2,1)} %bitcast.87), kind=kLoop, calls=%fused_computation.38 | loop fusion | flops 2967552 | bytes 1978368 | tf_op jit(solution)/shard_map/concatenate | solution.py:141
  46.9 0.7 fusion.29
  47.6 0.6 copy-done.6
  48.2 0.7 convolution_add_fusion.5
  48.9 0.6 collective-permute-start.7
  49.5 5.8 %collective-permute-done.8 = bf16[384,1536]{1,0:T(8,128)(2,1)} collective-permute-done((bf16[384,1536]{1,0:T(8,128)(2,1)}, bf16[384,1536]{1,0:T(8,128)(2,1)}, u32[]{:S(2)}, u32[]{:S(2)}) %collective-permute-start.8) | collective-permute-done | bytes 1179680 | tf_op jit(solution)/shard_map/ppermute | solution.py:50
  55.2 1.9 %fusion.27 = f32[322,1536]{1,0:T(8,128)S(1)} fusion(bf16[384,1536]{1,0:T(8,128)(2,1)} %collective-permute-done.8, bf16[322,1536]{1,0:T(8,128)(2,1)S(1)} %pad_maximum_fusion.2, s32[]{:T(128)S(6)} %select_n.100), kind=kOutput, calls=%fused_computation.57 | convolution fusion | flops 379846656 | bytes 3409924 | tf_op jit(solution)/shard_map/dot_general | solution.py:75
  57.2 0.7 convolution_add_fusion.2
  57.9 2.0 %convolution_add_fusion.4 = f32[322,1536]{1,0:T(8,128)S(1)} fusion(f32[322,1536]{1,0:T(8,128)S(1)} %convolution_add_fusion.5, bf16[384,1536]{1,0:T(8,128)(2,1)} %collective-permute-done.6, bf16[322,1536]{1,0:T(8,128)(2,1)S(1)} %pad_maximum_fusion.2, s32[]{:T(128)S(6)} %select_n.101), kind=kOutput, calls=%fused_computation.4 | convolution fusion | flops 380341248 | bytes 5425156 | tf_op jit(solution)/shard_map/dot_general | solution.py:75
  59.9 0.7 convolution_add_fusion.1
  60.9 0.7 convolution_add_fusion
  62.0 0.7 multiply_reduce_fusion.6
  62.7 1.4 %multiply_reduce_fusion.3 = (f32[320]{0:T(512)S(1)}, f32[320,1536]{1,0:T(8,128)}) fusion(f32[322,1536]{1,0:T(8,128)S(1)} %convolution_add_fusion), kind=kLoop, calls=%fused_computation.24 | loop fusion | flops 982720 | bytes 3933440 | tf_op jit(solution)/shard_map/reduce_sum | solution.py:87
  64.1 0.7 convolution_add_fusion.3
  65.3 1.3 %copy-done = f32[322,1536]{1,0:T(8,128)} copy-done((f32[322,1536]{1,0:T(8,128)}, f32[322,1536]{1,0:T(8,128)S(1)}, u32[]{:S(2)}) %copy-start) | copy-done | bytes 1978392
  66.6 0.6 multiply_reduce_fusion.5
  68.6 1.4 %multiply_multiply_fusion = f32[1,1536]{1,0:T(1,128)S(1)} fusion(f32[322,1536]{1,0:T(8,128)} %copy-done, f32[]{:T(128)S(6)} %rsqrt.33, f32[]{:T(128)} %bitcast.14), kind=kLoop, calls=%fused_computation.95 | loop fusion | flops 3072 | bytes 12296 | tf_op jit(solution)/shard_map/mul | solution.py:168
  70.0 1.9 %slice_multiply_fusion.1 = f32[319,1536]{1,0:T(8,128)S(1)} fusion(f32[320,1536]{1,0:T(8,128)} %get-tuple-element.10, f32[319]{0:T(512)S(1)} %bitcast.88), kind=kLoop, calls=%fused_computation.16 | loop fusion | flops 489984 | bytes 3921148 | tf_op jit(solution)/shard_map/mul | solution.py:88
  72.2 0.6 multiply_reduce_fusion.2
  72.8 0.8 multiply_reduce_fusion
  74.5 0.9 copy-done.7
  75.4 0.7 fusion.67
  76.1 1.2 %fusion.5 = f32[128,1536]{1,0:T(8,128)S(1)} fusion(bf16[1,320,1536]{2,1,0:T(8,128)(2,1)S(1)} %copy-done.12, f32[320]{0:T(512)S(1)} %subtract_select_fusion, s32[320]{0:T(512)S(1)} %broadcast_add_fusion), kind=kOutput, calls=%fused_computation.14 | convolution fusion | flops 755998720 | bytes 1772032 | tf_op jit(solution)/shard_map/dot_general | solution.py:155
  77.4 0.9 fusion.11
  78.8 0.7 pad_maximum_fusion.8
  79.5 1.5 %collective-permute-start.11 = (f32[1,1537]{1,0:T(1,128)S(1)}, f32[1,1537]{1,0:T(1,128)S(1)}, u32[]{:S(2)}, u32[]{:S(2)}) collective-permute-start(f32[1,1537]{1,0:T(1,128)S(1)} %pad_maximum_fusion.8), channel_id=1, source_target_pairs={{4,0},{8,4},{12,8},{16,12},{20,16},{24,20},{28,24},{5,1},{9,5},{13... | collective-permute-start | bytes 18452 | tf_op jit(solution)/shard_map/ppermute | solution.py:16
  81.0 0.7 fusion.7
  81.8 0.7 fusion.70
  82.4 0.6 copy-done.9
  83.0 0.7 fusion.69
  83.7 2.1 %fusion.68 = f32[320,384]{1,0:T(8,128)S(1)} fusion(bf16[320,1536]{1,0:T(8,128)(2,1)S(1)} %subtract_convert_fusion, bf16[384,1536]{1,0:T(8,128)(2,1)} %collective-permute-done.8), kind=kOutput, calls=%fused_computation.145 | convolution fusion | flops 377487360 | bytes 2654208 | tf_op jit(solution)/shard_map/dot_general | solution.py:173
  85.8 0.7 fusion.10
  86.5 2.0 %fusion.9 = bf16[320,384]{1,0:T(8,128)(2,1)S(1)} fusion(f32[320,384]{1,0:T(8,128)S(1)} %fusion.69, bf16[320,1536]{1,0:T(8,128)(2,1)S(1)} %get-tuple-element.8, bf16[384,1536]{1,0:T(8,128)(2,1)} %collective-permute-done.6), kind=kOutput, calls=%fused_computation.34 | convolution fusion | flops 377733120 | bytes 2899968 | tf_op jit(solution)/shard_map/dot_general | solution.py:172
  88.5 0.7 fusion.8
  91.1 1.3 %collective-permute-start.12 = (f32[1,1537]{1,0:T(1,128)S(1)}, f32[1,1537]{1,0:T(1,128)S(1)}, u32[]{:S(2)}, u32[]{:S(2)}) collective-permute-start(f32[1,1537]{1,0:T(1,128)S(1)} %pad_maximum_fusion.9), channel_id=1, source_target_pairs={{8,0},{12,4},{16,8},{20,12},{24,16},{28,20},{9,1},{13,5},{17,9},{2... | collective-permute-start | bytes 18452 | tf_op jit(solution)/shard_map/ppermute | solution.py:16
  92.6 5.8 %collective-permute-done.12 = f32[1,1537]{1,0:T(1,128)S(1)} collective-permute-done((f32[1,1537]{1,0:T(1,128)S(1)}, f32[1,1537]{1,0:T(1,128)S(1)}, u32[]{:S(2)}, u32[]{:S(2)}) %collective-permute-start.12) | collective-permute-done | bytes 6180 | tf_op jit(solution)/shard_map/ppermute | solution.py:16
  98.4 0.6 slice.135
  99.7 1.3 %collective-permute-start.13 = (f32[1,1537]{1,0:T(1,128)S(1)}, f32[1,1537]{1,0:T(1,128)S(1)}, u32[]{:S(2)}, u32[]{:S(2)}) collective-permute-start(f32[1,1537]{1,0:T(1,128)S(1)} %pad_maximum_fusion.10), channel_id=1, source_target_pairs={{16,0},{20,4},{24,8},{28,12},{17,1},{21,5},{25,9},{29,13},{18,2},{... | collective-permute-start | bytes 18452 | tf_op jit(solution)/shard_map/ppermute | solution.py:16
  101.0 1.0 maximum_bitcast_fusion
  104.1 2.0 %collective-permute-done.13 = f32[1,1537]{1,0:T(1,128)S(1)} collective-permute-done((f32[1,1537]{1,0:T(1,128)S(1)}, f32[1,1537]{1,0:T(1,128)S(1)}, u32[]{:S(2)}, u32[]{:S(2)}) %collective-permute-start.13) | collective-permute-done | bytes 6180 | tf_op jit(solution)/shard_map/ppermute | solution.py:16
  106.2 1.7 %fusion.3 = bf16[1,128,1536]{2,1,0:T(8,128)(2,1)} fusion(f32[128,1536]{1,0:T(8,128)S(1)} %fusion.5, f32[1536]{0:T(1024)S(1)} %fusion.47, f32[128]{0:T(128)S(1)} %get-tuple-element.19, f32[128]{0:T(128)S(1)} %bitcast_select_fusion, f32[128]{0:T(128)S(1)} %reduce.2), kind=kOutput, calls=%fused_computation.12 | convolution fusion | flops 302841856 | bytes 1187328 | tf_op jit(solution)/shard_map/dot_general | solution.py:161
  (73 shorter events, 5.4 us)
Async XLA Ops:
  0.6 46.3 %collective-permute-start.5 = (bf16[384,1536]{1,0:T(8,128)(2,1)}, bf16[384,1536]{1,0:T(8,128)(2,1)S(1)}, u32[]{:S(2)}, u32[]{:S(2)}) collective-permute-start(bf16[384,1536]{1,0:T(8,128)(2,1)} %param.14), channel_id=1, source_target_pairs={{0,2},{1,3},{2,0},{3,1},{4,6},{5,7},{6,4},{7,5},{8,10},{9,11},{10,... | collective-permute-start | bytes 3538952 | tf_op jit(solution)/shard_map/ppermute | solution.py:50
  3.7 54.2 %collective-permute-start.6 = (bf16[384,1536]{1,0:T(8,128)(2,1)}, bf16[384,1536]{1,0:T(8,128)(2,1)}, u32[]{:S(2)}, u32[]{:S(2)}) collective-permute-start(bf16[384,1536]{1,0:T(8,128)(2,1)} %param.14), channel_id=1, source_target_pairs={{0,1},{1,0},{2,3},{3,2},{4,5},{5,4},{6,7},{7,6},{8,9},{9,8},{10,11... | collective-permute-start | bytes 3538952 | tf_op jit(solution)/shard_map/ppermute | solution.py:53
  6.6 38.5 %copy-start.2 = (bf16[384,1536]{1,0:T(8,128)(2,1)S(1)}, bf16[384,1536]{1,0:T(8,128)(2,1)}, u32[]{:S(2)}) copy-start(bf16[384,1536]{1,0:T(8,128)(2,1)} %param.15) | copy-start | bytes 3538948
  9.2 11.2 %collective-permute-start.1 = (f32[1,1537]{1,0:T(1,128)S(1)}, f32[1,1537]{1,0:T(1,128)S(1)}, u32[]{:S(2)}, u32[]{:S(2)}) collective-permute-start(f32[1,1537]{1,0:T(1,128)S(1)} %pad_maximum_fusion.4), channel_id=1, source_target_pairs={{0,4},{4,8},{8,12},{12,16},{16,20},{20,24},{24,28},{1,5},{5,9},{9,... | collective-permute-start | bytes 18452 | tf_op jit(solution)/shard_map/ppermute | solution.py:16
  13.4 32.2 %collective-permute-start = (bf16[1,1536]{1,0:T(2,128)(2,1)S(1)}, bf16[1,1536]{1,0:T(2,128)(2,1)S(1)}, u32[]{:S(2)}, u32[]{:S(2)}) collective-permute-start(bf16[1,1536]{1,0:T(2,128)(2,1)S(1)} %get-tuple-element.15), channel_id=1, source_target_pairs={{0,4},{4,8},{8,12},{12,16},{16,20},{20,24},{24,28},{1,5},{5,9},{9,... | collective-permute-start | bytes 9224 | tf_op jit(solution)/shard_map/ppermute | solution.py:16
  16.9 38.4 %collective-permute-start.8 = (bf16[384,1536]{1,0:T(8,128)(2,1)}, bf16[384,1536]{1,0:T(8,128)(2,1)}, u32[]{:S(2)}, u32[]{:S(2)}) collective-permute-start(bf16[384,1536]{1,0:T(8,128)(2,1)} %param.15), channel_id=1, source_target_pairs={{0,2},{1,3},{2,0},{3,1},{4,6},{5,7},{6,4},{7,5},{8,10},{9,11},{10,... | collective-permute-start | bytes 3538952 | tf_op jit(solution)/shard_map/ppermute | solution.py:50
  22.3 4.8 %collective-permute-start.2 = (f32[1,1537]{1,0:T(1,128)S(1)}, f32[1,1537]{1,0:T(1,128)S(1)}, u32[]{:S(2)}, u32[]{:S(2)}) collective-permute-start(f32[1,1537]{1,0:T(1,128)S(1)} %pad_maximum_fusion.5), channel_id=1, source_target_pairs={{0,8},{4,12},{8,16},{12,20},{16,24},{20,28},{1,9},{5,13},{9,17},{1... | collective-permute-start | bytes 18452 | tf_op jit(solution)/shard_map/ppermute | solution.py:16
  28.4 7.3 %collective-permute-start.3 = (f32[1,1537]{1,0:T(1,128)S(1)}, f32[1,1537]{1,0:T(1,128)S(1)}, u32[]{:S(2)}, u32[]{:S(2)}) collective-permute-start(f32[1,1537]{1,0:T(1,128)S(1)} %pad_maximum_fusion.6), channel_id=1, source_target_pairs={{0,16},{4,20},{8,24},{12,28},{1,17},{5,21},{9,25},{13,29},{2,18},{... | collective-permute-start | bytes 18452 | tf_op jit(solution)/shard_map/ppermute | solution.py:16
  39.6 5.5 %collective-permute-start.4 = (f32[1,1537]{1,0:T(1,128)S(1)}, f32[1,1537]{1,0:T(1,128)S(1)}, u32[]{:S(2)}, u32[]{:S(2)}) collective-permute-start(f32[1,1537]{1,0:T(1,128)S(1)} %pad_maximum_fusion.7), channel_id=1, source_target_pairs={{4,0},{8,4},{12,8},{16,12},{20,16},{24,20},{28,24},{5,1},{9,5},{13... | collective-permute-start | bytes 18452 | tf_op jit(solution)/shard_map/ppermute | solution.py:16
  45.1 14.8 %collective-permute-start.9 = (bf16[384,1536]{1,0:T(8,128)(2,1)S(1)}, bf16[384,1536]{1,0:T(8,128)(2,1)S(1)}, u32[]{:S(2)}, u32[]{:S(2)}) collective-permute-start(bf16[384,1536]{1,0:T(8,128)(2,1)S(1)} %copy-done.2), channel_id=1, source_target_pairs={{0,1},{1,0},{2,3},{3,2},{4,5},{5,4},{6,7},{7,6},{8,9},{9,8},{10,11... | collective-permute-start | bytes 3538952 | tf_op jit(solution)/shard_map/ppermute | solution.py:53
  46.9 1.3 %copy-start.6 = (bf16[384,1536]{1,0:T(8,128)(2,1)S(1)}, bf16[384,1536]{1,0:T(8,128)(2,1)}, u32[]{:S(2)}) copy-start(bf16[384,1536]{1,0:T(8,128)(2,1)} %param.14) | copy-start | bytes 3538948
  48.9 15.3 %collective-permute-start.7 = (bf16[384,1536]{1,0:T(8,128)(2,1)S(1)}, bf16[384,1536]{1,0:T(8,128)(2,1)S(1)}, u32[]{:S(2)}, u32[]{:S(2)}) collective-permute-start(bf16[384,1536]{1,0:T(8,128)(2,1)S(1)} %collective-permute-done.5), channel_id=1, source_target_pairs={{0,1},{1,0},{2,3},{3,2},{4,5},{5,4},{6,7},{7,6},{8,9},{9,8},{10,11... | collective-permute-start | bytes 3538952 | tf_op jit(solution)/shard_map/ppermute | solution.py:53
  55.2 5.7 %collective-permute-start.10 = (bf16[384,1536]{1,0:T(8,128)(2,1)}, bf16[384,1536]{1,0:T(8,128)(2,1)S(1)}, u32[]{:S(2)}, u32[]{:S(2)}) collective-permute-start(bf16[384,1536]{1,0:T(8,128)(2,1)} %collective-permute-done.8), channel_id=1, source_target_pairs={{0,1},{1,0},{2,3},{3,2},{4,5},{5,4},{6,7},{7,6},{8,9},{9,8},{10,11... | collective-permute-start | bytes 3538952 | tf_op jit(solution)/shard_map/ppermute | solution.py:53
  59.9 1.0 copy-start.8
  60.9 1.1 copy-start.10
  64.1 1.1 %copy-start.4 = (bf16[384,1536]{1,0:T(8,128)(2,1)}, bf16[384,1536]{1,0:T(8,128)(2,1)S(1)}, u32[]{:S(2)}) copy-start(bf16[384,1536]{1,0:T(8,128)(2,1)S(1)} %collective-permute-done.7) | copy-start | bytes 3538948
  65.3 1.3 %copy-start = (f32[322,1536]{1,0:T(8,128)}, f32[322,1536]{1,0:T(8,128)S(1)}, u32[]{:S(2)}) copy-start(f32[322,1536]{1,0:T(8,128)S(1)} %convolution_add_fusion.3) | copy-start | bytes 5935108
  70.0 2.2 %copy-start.1 = (f32[322,1536]{1,0:T(8,128)S(1)}, f32[322,1536]{1,0:T(8,128)}, u32[]{:S(2)}) copy-start(f32[322,1536]{1,0:T(8,128)} %copy-done) | copy-start | bytes 5935108
  74.1 1.3 %copy-start.7 = (bf16[384,1536]{1,0:T(8,128)(2,1)S(1)}, bf16[384,1536]{1,0:T(8,128)(2,1)}, u32[]{:S(2)}) copy-start(bf16[384,1536]{1,0:T(8,128)(2,1)} %param.14) | copy-start | bytes 3538948
  74.5 1.6 %copy-start.12 = (bf16[1,320,1536]{2,1,0:T(8,128)(2,1)S(1)}, bf16[1,320,1536]{2,1,0:T(8,128)(2,1)}, u32[]{:S(2)}) copy-start(bf16[1,320,1536]{2,1,0:T(8,128)(2,1)} %param.9) | copy-start | bytes 2949124
  76.1 4.9 %copy-start.3 = (bf16[384,1536]{1,0:T(8,128)(2,1)S(1)}, bf16[384,1536]{1,0:T(8,128)(2,1)}, u32[]{:S(2)}) copy-start(bf16[384,1536]{1,0:T(8,128)(2,1)} %param.15) | copy-start | bytes 3538948
  78.3 3.4 %copy-start.11 = (bf16[384,1536]{1,0:T(8,128)(2,1)S(1)}, bf16[384,1536]{1,0:T(8,128)(2,1)}, u32[]{:S(2)}) copy-start(bf16[384,1536]{1,0:T(8,128)(2,1)} %copy-done.10) | copy-start | bytes 3538948
  79.5 9.8 %collective-permute-start.11 = (f32[1,1537]{1,0:T(1,128)S(1)}, f32[1,1537]{1,0:T(1,128)S(1)}, u32[]{:S(2)}, u32[]{:S(2)}) collective-permute-start(f32[1,1537]{1,0:T(1,128)S(1)} %pad_maximum_fusion.8), channel_id=1, source_target_pairs={{4,0},{8,4},{12,8},{16,12},{20,16},{24,20},{28,24},{5,1},{9,5},{13... | collective-permute-start | bytes 18452 | tf_op jit(solution)/shard_map/ppermute | solution.py:16
  81.7 1.3 %copy-start.9 = (bf16[384,1536]{1,0:T(8,128)(2,1)S(1)}, bf16[384,1536]{1,0:T(8,128)(2,1)}, u32[]{:S(2)}) copy-start(bf16[384,1536]{1,0:T(8,128)(2,1)} %copy-done.8) | copy-start | bytes 3538948
  83.7 2.1 %copy-start.5 = (bf16[384,1536]{1,0:T(8,128)(2,1)S(1)}, bf16[384,1536]{1,0:T(8,128)(2,1)}, u32[]{:S(2)}) copy-start(bf16[384,1536]{1,0:T(8,128)(2,1)} %copy-done.4) | copy-start | bytes 3538948
  91.1 7.3 %collective-permute-start.12 = (f32[1,1537]{1,0:T(1,128)S(1)}, f32[1,1537]{1,0:T(1,128)S(1)}, u32[]{:S(2)}, u32[]{:S(2)}) collective-permute-start(f32[1,1537]{1,0:T(1,128)S(1)} %pad_maximum_fusion.9), channel_id=1, source_target_pairs={{8,0},{12,4},{16,8},{20,12},{24,16},{28,20},{9,1},{13,5},{17,9},{2... | collective-permute-start | bytes 18452 | tf_op jit(solution)/shard_map/ppermute | solution.py:16
  99.7 6.4 %collective-permute-start.13 = (f32[1,1537]{1,0:T(1,128)S(1)}, f32[1,1537]{1,0:T(1,128)S(1)}, u32[]{:S(2)}, u32[]{:S(2)}) collective-permute-start(f32[1,1537]{1,0:T(1,128)S(1)} %pad_maximum_fusion.10), channel_id=1, source_target_pairs={{16,0},{20,4},{24,8},{28,12},{17,1},{21,5},{25,9},{29,13},{18,2},{... | collective-permute-start | bytes 18452 | tf_op jit(solution)/shard_map/ppermute | solution.py:16

commit v9 on v8

--- a/solution.py
+++ b/solution.py
@@ -133,6 +133,11 @@
     picked = jnp.dot(membership, smoothed, precision=exact) + leading[:, None] * state_in
     conf_grad = jnp.sum(grad_rows * picked, axis=1)
     cos_grad = jnp.where(later_rows, jnp.where(starts, -0.5 * conf_grad, 0.5 * conf_grad), 0.0)
+    owner_keep = jnp.where(member_id >= 0, keep_all[jnp.maximum(member_id, 0)], 1.0)
+    level = jnp.where(later_rows, 0.5, jnp.where(starts, 1.0, 0.0))
+    rise = jnp.where(later_rows, jnp.where(starts, -0.5, 0.5), 0.0)
+    grad_wide = grad_rows.astype(jnp.float32)
+    base_vector = jnp.dot((owner_keep * level)[None, :], grad_wide, precision=exact)
     to_prev = jnp.concatenate([token_rows[:1].astype(jnp.float32), cos_grad[:1][None]], axis=1)
     from_next = shifted(to_prev, "seq", -1)
     prev_row = shifted(token_rows[token_count - 1 :], "seq", 1)
@@ -153,8 +158,9 @@
     confidence = jnp.where(starts, boundary_prob, 1.0 - boundary_prob)
     weighted_grad = confidence[:, None] * grad_rows
     slot_grad = lax.dot_general(membership, weighted_grad, contract_first, precision=exact)
-    lead_grad = jnp.dot(leading[None, :], weighted_grad, precision=exact)
-    back_vector = lead_grad + jnp.dot(keep_all[None, :], slot_grad, precision=exact)
+    back_vector = base_vector + jnp.dot(
+        (owner_keep * rise * cosine)[None, :], grad_wide, precision=exact
+    )
     grad_in = seq_scan(last_log, back_vector, "seq", False)
     reach_end = jnp.exp(running[slot_count - 1] - running)
     state_grad = (

time: 109 us -> 109 us (level)
  local copies, waits for them, and re-layouts: 9.41 us -> 11.9 us
  waiting for transfers between devices: 15.7 us -> 14 us
    gather x0 -> x1, local copies, waits for them, and re-layouts: none -> 2.36 us  [per_device(): keep_all[jnp.maximum(member_id, 0)]]
    concatenate x1, other arithmetic: 1.27 us -> 0.07 us  [per_device(): rows_ext = jnp.concatenate([token_rows, prev_row, next_row], axis=0)]
    unnamed x26 -> x30, local copies, waits for them, and re-layouts: 4.77 us -> 4.81 us
  transfers between devices with their start and end apart: 14 -> 14, of which waited for: 5 -> 4; matrix products, arithmetic and copies ran while one was open for 31% -> 33% of each run, Pallas kernels for 0% -> 0%
where the time goes in v9:
time: 109 us; the launch traced here: 108 us
  starting transfers between devices  25.3 us (23%)
  matrix products  25 us (23%)
  other arithmetic  16.7 us (15%)
  between operations  14.8 us (14%)
  waiting for transfers between devices  14 us (13%)
  local copies, waits for them, and re-layouts  11.9 us (11%)
    ppermute x8, starting transfers between devices, shifted(): return lax.ppermute(block, axis, route)  21.1 us
    ppermute x8, waiting for transfers between devices, shifted(): return lax.ppermute(block, axis, route)  9.06 us
    dot_general x8, matrix products, split_dot(): term = jnp.dot(part, block, preferred_element_type=jnp.float32)  8.06 us
    ppermute x2, waiting for transfers between devices, gather_blocks(): pairs.append(lax.ppermute(blocks, axis, route))  4.9 us
    unnamed x30, local copies, waits for them, and re-layouts  4.81 us
    dot_general x4, matrix products, per_device(): lax.dot_general(key_grad, k_block, contract_last, preferred_element_type=...  4.12 us
    dot_general x4, matrix products, per_device(): lax.dot_general(query_grad, q_block, contract_last, preferred_element_typ...  4.04 us
    ppermute x2, starting transfers between devices, gather_blocks(): pairs.append(lax.ppermute(blocks, axis, route))  3.61 us
  transfers between devices with their start and end apart: 14, of which 4 were waited for; matrix products, arithmetic and copies ran while one was open for 33% of the time, Pallas kernels for 0%

profile of v9, /device:TPU:0, one launch (start us, length us, event | category | flops | bytes accessed | tf_op | source)
XLA Modules:
  0.0 107.7 jit_solution(5345057820533622281)
XLA Ops:
  0.6 3.0 %collective-permute-start.5 = (bf16[384,1536]{1,0:T(8,128)(2,1)}, bf16[384,1536]{1,0:T(8,128)(2,1)S(1)}, u32[]{:S(2)}, u32[]{:S(2)}) collective-permute-start(bf16[384,1536]{1,0:T(8,128)(2,1)} %param.14), channel_id=1, source_target_pairs={{0,2},{1,3},{2,0},{3,1},{4,6},{5,7},{6,4},{7,5},{8,10},{9,11},{10,... | collective-permute-start | bytes 3538952 | tf_op jit(solution)/shard_map/ppermute | solution.py:50
  4.3 0.7 fusion.58
  5.3 0.6 slice.119
  5.9 0.7 bitcast_select_fusion
  6.6 1.9 %fusion.14 = f32[128,1536]{1,0:T(8,128)S(1)} fusion(bf16[1,128,1536]{2,1,0:T(8,128)(2,1)} %param.10, f32[128]{0:T(128)S(1)} %bitcast_select_fusion, f32[128]{0:T(128)S(1)} %reduce.2), kind=kOutput, calls=%fused_computation.46 | convolution fusion | flops 302448640 | bytes 1180672 | tf_op jit(solution)/shard_map/dot_general | solution.py:128
  8.6 0.7 pad_maximum_fusion.4
  9.3 3.4 %collective-permute-start.1 = (f32[1,1537]{1,0:T(1,128)S(1)}, f32[1,1537]{1,0:T(1,128)S(1)}, u32[]{:S(2)}, u32[]{:S(2)}) collective-permute-start(f32[1,1537]{1,0:T(1,128)S(1)} %pad_maximum_fusion.4), channel_id=1, source_target_pairs={{0,4},{4,8},{8,12},{12,16},{16,20},{20,24},{24,28},{1,5},{5,9},{9,... | collective-permute-start | bytes 18452 | tf_op jit(solution)/shard_map/ppermute | solution.py:16
  12.7 0.8 slice_bitcast_fusion
  13.5 3.5 %collective-permute-start = (bf16[1,1536]{1,0:T(2,128)(2,1)S(1)}, bf16[1,1536]{1,0:T(2,128)(2,1)S(1)}, u32[]{:S(2)}, u32[]{:S(2)}) collective-permute-start(bf16[1,1536]{1,0:T(2,128)(2,1)S(1)} %get-tuple-element.13), channel_id=1, source_target_pairs={{0,4},{4,8},{8,12},{12,16},{16,20},{20,24},{24,28},{1,5},{5,9},{9,... | collective-permute-start | bytes 9224 | tf_op jit(solution)/shard_map/ppermute | solution.py:16
  16.9 0.6 collective-permute-start.8
  17.5 0.8 fusion.32
  18.3 0.8 convert_reduce_fusion
  19.1 0.7 subtract_exponential_fusion
  20.7 0.5 slice.120
  22.6 3.5 %collective-permute-start.2 = (f32[1,1537]{1,0:T(1,128)S(1)}, f32[1,1537]{1,0:T(1,128)S(1)}, u32[]{:S(2)}, u32[]{:S(2)}) collective-permute-start(f32[1,1537]{1,0:T(1,128)S(1)} %pad_maximum_fusion.5), channel_id=1, source_target_pairs={{0,8},{4,12},{8,16},{12,20},{16,24},{20,28},{1,9},{5,13},{9,17},{1... | collective-permute-start | bytes 18452 | tf_op jit(solution)/shard_map/ppermute | solution.py:16
  26.2 1.2 %collective-permute-done.2 = f32[1,1537]{1,0:T(1,128)S(1)} collective-permute-done((f32[1,1537]{1,0:T(1,128)S(1)}, f32[1,1537]{1,0:T(1,128)S(1)}, u32[]{:S(2)}, u32[]{:S(2)}) %collective-permute-start.2) | collective-permute-done | bytes 6180 | tf_op jit(solution)/shard_map/ppermute | solution.py:16
  27.4 0.5 slice.122
  28.6 5.2 %collective-permute-start.3 = (f32[1,1537]{1,0:T(1,128)S(1)}, f32[1,1537]{1,0:T(1,128)S(1)}, u32[]{:S(2)}, u32[]{:S(2)}) collective-permute-start(f32[1,1537]{1,0:T(1,128)S(1)} %pad_maximum_fusion.6), channel_id=1, source_target_pairs={{0,16},{4,20},{8,24},{12,28},{1,17},{5,21},{9,25},{13,29},{2,18},{... | collective-permute-start | bytes 18452 | tf_op jit(solution)/shard_map/ppermute | solution.py:16
  33.8 0.6 fusion.61
  36.5 3.0 %fusion.5 = f32[320]{0:T(512)S(1)} fusion(bf16[1,320,1536]{2,1,0:T(8,128)(2,1)} %param.9, f32[1536]{0:T(1024)S(1)} %fusion.44, f32[320]{0:T(512)S(1)} %compare_convert_fusion, f32[128,1536]{1,0:T(8,128)} %copy-done.14, f32[128]{0:T(128)S(1)} %get-tuple-element.23, s32[320]{0:T(512)S(1)} %get-tuple-element.19), kind=kOutput, calls=%fused_computation.27 | convolution fusion | flops 757866176 | bytes 1779968 | tf_op jit(solution)/shard_map/dot_general | solution.py:133
  39.5 0.5 slice.98
  40.1 0.7 pad_maximum_fusion.7
  40.7 1.5 %collective-permute-start.4 = (f32[1,1537]{1,0:T(1,128)S(1)}, f32[1,1537]{1,0:T(1,128)S(1)}, u32[]{:S(2)}, u32[]{:S(2)}) collective-permute-start(f32[1,1537]{1,0:T(1,128)S(1)} %pad_maximum_fusion.7), channel_id=1, source_target_pairs={{4,0},{8,4},{12,8},{16,12},{20,16},{24,20},{28,24},{5,1},{9,5},{13... | collective-permute-start | bytes 18452 | tf_op jit(solution)/shard_map/ppermute | solution.py:16
  44.7 2.4 %gather_fusion = f32[320]{0:T(512)S(1)} fusion(f32[128]{0:T(128)S(1)} %get-tuple-element.23, s32[1024]{0:T(1024)S(1)} %pad_clamp_fusion), kind=kCustom, calls=%fused_computation | custom fusion | bytes 3840 | tf_op jit(solution)/shard_map/gather | solution.py:136
  47.2 0.5 slice.133
  47.8 0.7 fusion.27
  48.5 0.6 copy-done.7
  49.1 0.7 convolution_add_fusion.5
  49.8 0.6 collective-permute-start.7
  50.3 4.9 %collective-permute-done.8 = bf16[384,1536]{1,0:T(8,128)(2,1)} collective-permute-done((bf16[384,1536]{1,0:T(8,128)(2,1)}, bf16[384,1536]{1,0:T(8,128)(2,1)}, u32[]{:S(2)}, u32[]{:S(2)}) %collective-permute-start.8) | collective-permute-done | bytes 1179680 | tf_op jit(solution)/shard_map/ppermute | solution.py:50
  55.2 1.9 %fusion.25 = f32[322,1536]{1,0:T(8,128)S(1)} fusion(bf16[384,1536]{1,0:T(8,128)(2,1)} %collective-permute-done.8, bf16[322,1536]{1,0:T(8,128)(2,1)S(1)} %pad_maximum_fusion.2, s32[]{:T(128)S(6)} %select_n.131), kind=kOutput, calls=%fused_computation.57 | convolution fusion | flops 379846656 | bytes 3409924 | tf_op jit(solution)/shard_map/dot_general | solution.py:75
  57.2 0.7 convolution_add_fusion.2
  57.9 2.0 %convolution_add_fusion.4 = f32[322,1536]{1,0:T(8,128)S(1)} fusion(f32[322,1536]{1,0:T(8,128)S(1)} %convolution_add_fusion.5, bf16[384,1536]{1,0:T(8,128)(2,1)} %collective-permute-done.6, bf16[322,1536]{1,0:T(8,128)(2,1)S(1)} %pad_maximum_fusion.2, s32[]{:T(128)S(6)} %select_n.132), kind=kOutput, calls=%fused_computation.5 | convolution fusion | flops 380341248 | bytes 5425156 | tf_op jit(solution)/shard_map/dot_general | solution.py:75
  59.9 0.7 convolution_add_fusion.1
  60.9 0.7 convolution_add_fusion
  62.0 0.7 multiply_reduce_fusion.6
  62.7 1.4 %multiply_reduce_fusion.3 = (f32[320]{0:T(512)S(1)}, f32[320,1536]{1,0:T(8,128)}) fusion(f32[322,1536]{1,0:T(8,128)S(1)} %convolution_add_fusion), kind=kLoop, calls=%fused_computation.24 | loop fusion | flops 982720 | bytes 3933440 | tf_op jit(solution)/shard_map/reduce_sum | solution.py:87
  64.2 0.7 convolution_add_fusion.3
  65.3 1.3 %copy-done = f32[322,1536]{1,0:T(8,128)} copy-done((f32[322,1536]{1,0:T(8,128)}, f32[322,1536]{1,0:T(8,128)S(1)}, u32[]{:S(2)}) %copy-start) | copy-done | bytes 1978392
  66.6 0.6 multiply_reduce_fusion.5
  68.7 1.5 %multiply_multiply_fusion = f32[1,1536]{1,0:T(1,128)S(1)} fusion(f32[322,1536]{1,0:T(8,128)} %copy-done, f32[]{:T(128)S(6)} %rsqrt.33, f32[]{:T(128)} %bitcast.14), kind=kLoop, calls=%fused_computation.95 | loop fusion | flops 3072 | bytes 12296 | tf_op jit(solution)/shard_map/mul | solution.py:174
  70.1 1.9 %slice_multiply_fusion.1 = f32[319,1536]{1,0:T(8,128)S(1)} fusion(f32[320,1536]{1,0:T(8,128)} %get-tuple-element.8, f32[319]{0:T(512)S(1)} %bitcast.84), kind=kLoop, calls=%fused_computation.16 | loop fusion | flops 489984 | bytes 3921148 | tf_op jit(solution)/shard_map/mul | solution.py:88
  72.3 0.6 multiply_reduce_fusion.2
  72.9 0.8 multiply_reduce_fusion
  74.6 0.9 copy-done.8
  75.5 0.7 fusion.62
  76.2 1.2 %fusion.4 = f32[128,1536]{1,0:T(8,128)S(1)} fusion(bf16[1,320,1536]{2,1,0:T(8,128)(2,1)S(1)} %copy-done.2, f32[320]{0:T(512)S(1)} %get-tuple-element.17, s32[320]{0:T(512)S(1)} %get-tuple-element.19), kind=kOutput, calls=%fused_computation.14 | convolution fusion | flops 755998720 | bytes 1772032 | tf_op jit(solution)/shard_map/dot_general | solution.py:160
  78.5 0.7 pad_maximum_fusion.8
  79.2 1.5 %collective-permute-start.11 = (f32[1,1537]{1,0:T(1,128)S(1)}, f32[1,1537]{1,0:T(1,128)S(1)}, u32[]{:S(2)}, u32[]{:S(2)}) collective-permute-start(f32[1,1537]{1,0:T(1,128)S(1)} %pad_maximum_fusion.8), channel_id=1, source_target_pairs={{4,0},{8,4},{12,8},{16,12},{20,16},{24,20},{28,24},{5,1},{9,5},{13... | collective-permute-start | bytes 18452 | tf_op jit(solution)/shard_map/ppermute | solution.py:16
  80.8 0.7 fusion.6
  81.5 0.7 fusion.65
  82.2 0.6 copy-done.10
  82.8 0.7 fusion.64
  83.5 2.1 %fusion.63 = f32[320,384]{1,0:T(8,128)S(1)} fusion(bf16[320,1536]{1,0:T(8,128)(2,1)S(1)} %subtract_convert_fusion, bf16[384,1536]{1,0:T(8,128)(2,1)} %collective-permute-done.8), kind=kOutput, calls=%fused_computation.147 | convolution fusion | flops 377487360 | bytes 2654208 | tf_op jit(solution)/shard_map/dot_general | solution.py:179
  85.5 0.7 fusion.9
  86.2 2.0 %fusion.8 = bf16[320,384]{1,0:T(8,128)(2,1)S(1)} fusion(f32[320,384]{1,0:T(8,128)S(1)} %fusion.64, bf16[320,1536]{1,0:T(8,128)(2,1)S(1)} %get-tuple-element.6, bf16[384,1536]{1,0:T(8,128)(2,1)} %collective-permute-done.6), kind=kOutput, calls=%fused_computation.34 | convolution fusion | flops 377733120 | bytes 2899968 | tf_op jit(solution)/shard_map/dot_general | solution.py:178
  88.2 0.7 fusion.7
  90.9 1.3 %collective-permute-start.12 = (f32[1,1537]{1,0:T(1,128)S(1)}, f32[1,1537]{1,0:T(1,128)S(1)}, u32[]{:S(2)}, u32[]{:S(2)}) collective-permute-start(f32[1,1537]{1,0:T(1,128)S(1)} %pad_maximum_fusion.9), channel_id=1, source_target_pairs={{8,0},{12,4},{16,8},{20,12},{24,16},{28,20},{9,1},{13,5},{17,9},{2... | collective-permute-start | bytes 18452 | tf_op jit(solution)/shard_map/ppermute | solution.py:16
  92.4 5.8 %collective-permute-done.12 = f32[1,1537]{1,0:T(1,128)S(1)} collective-permute-done((f32[1,1537]{1,0:T(1,128)S(1)}, f32[1,1537]{1,0:T(1,128)S(1)}, u32[]{:S(2)}, u32[]{:S(2)}) %collective-permute-start.12) | collective-permute-done | bytes 6180 | tf_op jit(solution)/shard_map/ppermute | solution.py:16
  98.2 0.6 slice.137
  99.5 1.3 %collective-permute-start.13 = (f32[1,1537]{1,0:T(1,128)S(1)}, f32[1,1537]{1,0:T(1,128)S(1)}, u32[]{:S(2)}, u32[]{:S(2)}) collective-permute-start(f32[1,1537]{1,0:T(1,128)S(1)} %pad_maximum_fusion.10), channel_id=1, source_target_pairs={{16,0},{20,4},{24,8},{28,12},{17,1},{21,5},{25,9},{29,13},{18,2},{... | collective-permute-start | bytes 18452 | tf_op jit(solution)/shard_map/ppermute | solution.py:16
  100.8 1.0 maximum_bitcast_fusion
  103.9 2.0 %collective-permute-done.13 = f32[1,1537]{1,0:T(1,128)S(1)} collective-permute-done((f32[1,1537]{1,0:T(1,128)S(1)}, f32[1,1537]{1,0:T(1,128)S(1)}, u32[]{:S(2)}, u32[]{:S(2)}) %collective-permute-start.13) | collective-permute-done | bytes 6180 | tf_op jit(solution)/shard_map/ppermute | solution.py:16
  106.0 1.7 %fusion.3 = bf16[1,128,1536]{2,1,0:T(8,128)(2,1)} fusion(f32[128,1536]{1,0:T(8,128)S(1)} %fusion.4, f32[1536]{0:T(1024)S(1)} %fusion.45, f32[128]{0:T(128)S(1)} %get-tuple-element.22, f32[128]{0:T(128)S(1)} %bitcast_select_fusion, f32[128]{0:T(128)S(1)} %reduce.2), kind=kOutput, calls=%fused_computation.13 | convolution fusion | flops 302841856 | bytes 1187328 | tf_op jit(solution)/shard_map/dot_general | solution.py:167
  (80 shorter events, 5.0 us)
Async XLA Ops:
  0.6 47.2 %collective-permute-start.5 = (bf16[384,1536]{1,0:T(8,128)(2,1)}, bf16[384,1536]{1,0:T(8,128)(2,1)S(1)}, u32[]{:S(2)}, u32[]{:S(2)}) collective-permute-start(bf16[384,1536]{1,0:T(8,128)(2,1)} %param.14), channel_id=1, source_target_pairs={{0,2},{1,3},{2,0},{3,1},{4,6},{5,7},{6,4},{7,5},{8,10},{9,11},{10,... | collective-permute-start | bytes 3538952 | tf_op jit(solution)/shard_map/ppermute | solution.py:50
  3.7 54.2 %collective-permute-start.6 = (bf16[384,1536]{1,0:T(8,128)(2,1)}, bf16[384,1536]{1,0:T(8,128)(2,1)}, u32[]{:S(2)}, u32[]{:S(2)}) collective-permute-start(bf16[384,1536]{1,0:T(8,128)(2,1)} %param.14), channel_id=1, source_target_pairs={{0,1},{1,0},{2,3},{3,2},{4,5},{5,4},{6,7},{7,6},{8,9},{9,8},{10,11... | collective-permute-start | bytes 3538952 | tf_op jit(solution)/shard_map/ppermute | solution.py:53
  8.5 27.9 %copy-start.14 = (f32[128,1536]{1,0:T(8,128)}, f32[128,1536]{1,0:T(8,128)S(1)}, u32[]{:S(2)}) copy-start(f32[128,1536]{1,0:T(8,128)S(1)} %fusion.14) | copy-start | bytes 2359300
  9.3 11.4 %collective-permute-start.1 = (f32[1,1537]{1,0:T(1,128)S(1)}, f32[1,1537]{1,0:T(1,128)S(1)}, u32[]{:S(2)}, u32[]{:S(2)}) collective-permute-start(f32[1,1537]{1,0:T(1,128)S(1)} %pad_maximum_fusion.4), channel_id=1, source_target_pairs={{0,4},{4,8},{8,12},{12,16},{16,20},{20,24},{24,28},{1,5},{5,9},{9,... | collective-permute-start | bytes 18452 | tf_op jit(solution)/shard_map/ppermute | solution.py:16
  13.5 34.3 %collective-permute-start = (bf16[1,1536]{1,0:T(2,128)(2,1)S(1)}, bf16[1,1536]{1,0:T(2,128)(2,1)S(1)}, u32[]{:S(2)}, u32[]{:S(2)}) collective-permute-start(bf16[1,1536]{1,0:T(2,128)(2,1)S(1)} %get-tuple-element.13), channel_id=1, source_target_pairs={{0,4},{4,8},{8,12},{12,16},{16,20},{20,24},{24,28},{1,5},{5,9},{9,... | collective-permute-start | bytes 9224 | tf_op jit(solution)/shard_map/ppermute | solution.py:16
  16.9 38.3 %collective-permute-start.8 = (bf16[384,1536]{1,0:T(8,128)(2,1)}, bf16[384,1536]{1,0:T(8,128)(2,1)}, u32[]{:S(2)}, u32[]{:S(2)}) collective-permute-start(bf16[384,1536]{1,0:T(8,128)(2,1)} %param.15), channel_id=1, source_target_pairs={{0,2},{1,3},{2,0},{3,1},{4,6},{5,7},{6,4},{7,5},{8,10},{9,11},{10,... | collective-permute-start | bytes 3538952 | tf_op jit(solution)/shard_map/ppermute | solution.py:50
  22.6 4.8 %collective-permute-start.2 = (f32[1,1537]{1,0:T(1,128)S(1)}, f32[1,1537]{1,0:T(1,128)S(1)}, u32[]{:S(2)}, u32[]{:S(2)}) collective-permute-start(f32[1,1537]{1,0:T(1,128)S(1)} %pad_maximum_fusion.5), channel_id=1, source_target_pairs={{0,8},{4,12},{8,16},{12,20},{16,24},{20,28},{1,9},{5,13},{9,17},{1... | collective-permute-start | bytes 18452 | tf_op jit(solution)/shard_map/ppermute | solution.py:16
  28.6 7.8 %collective-permute-start.3 = (f32[1,1537]{1,0:T(1,128)S(1)}, f32[1,1537]{1,0:T(1,128)S(1)}, u32[]{:S(2)}, u32[]{:S(2)}) collective-permute-start(f32[1,1537]{1,0:T(1,128)S(1)} %pad_maximum_fusion.6), channel_id=1, source_target_pairs={{0,16},{4,20},{8,24},{12,28},{1,17},{5,21},{9,25},{13,29},{2,18},{... | collective-permute-start | bytes 18452 | tf_op jit(solution)/shard_map/ppermute | solution.py:16
  36.5 10.7 %copy-start.3 = (bf16[384,1536]{1,0:T(8,128)(2,1)S(1)}, bf16[384,1536]{1,0:T(8,128)(2,1)}, u32[]{:S(2)}) copy-start(bf16[384,1536]{1,0:T(8,128)(2,1)} %param.15) | copy-start | bytes 3538948
  36.5 11.2 %copy-start.13 = (bf16[1,320,1536]{2,1,0:T(8,128)(2,1)S(1)}, bf16[1,320,1536]{2,1,0:T(8,128)(2,1)}, u32[]{:S(2)}) copy-start(bf16[1,320,1536]{2,1,0:T(8,128)(2,1)} %param.8) | copy-start | bytes 2949124
  40.7 6.4 %collective-permute-start.4 = (f32[1,1537]{1,0:T(1,128)S(1)}, f32[1,1537]{1,0:T(1,128)S(1)}, u32[]{:S(2)}, u32[]{:S(2)}) collective-permute-start(f32[1,1537]{1,0:T(1,128)S(1)} %pad_maximum_fusion.7), channel_id=1, source_target_pairs={{4,0},{8,4},{12,8},{16,12},{20,16},{24,20},{28,24},{5,1},{9,5},{13... | collective-permute-start | bytes 18452 | tf_op jit(solution)/shard_map/ppermute | solution.py:16
  47.2 12.7 %collective-permute-start.9 = (bf16[384,1536]{1,0:T(8,128)(2,1)S(1)}, bf16[384,1536]{1,0:T(8,128)(2,1)S(1)}, u32[]{:S(2)}, u32[]{:S(2)}) collective-permute-start(bf16[384,1536]{1,0:T(8,128)(2,1)S(1)} %copy-done.3), channel_id=1, source_target_pairs={{0,1},{1,0},{2,3},{3,2},{4,5},{5,4},{6,7},{7,6},{8,9},{9,8},{10,11... | collective-permute-start | bytes 3538952 | tf_op jit(solution)/shard_map/ppermute | solution.py:53
  47.8 1.3 %copy-start.7 = (bf16[384,1536]{1,0:T(8,128)(2,1)S(1)}, bf16[384,1536]{1,0:T(8,128)(2,1)}, u32[]{:S(2)}) copy-start(bf16[384,1536]{1,0:T(8,128)(2,1)} %param.14) | copy-start | bytes 3538948
  49.8 14.4 %collective-permute-start.7 = (bf16[384,1536]{1,0:T(8,128)(2,1)S(1)}, bf16[384,1536]{1,0:T(8,128)(2,1)S(1)}, u32[]{:S(2)}, u32[]{:S(2)}) collective-permute-start(bf16[384,1536]{1,0:T(8,128)(2,1)S(1)} %collective-permute-done.5), channel_id=1, source_target_pairs={{0,1},{1,0},{2,3},{3,2},{4,5},{5,4},{6,7},{7,6},{8,9},{9,8},{10,11... | collective-permute-start | bytes 3538952 | tf_op jit(solution)/shard_map/ppermute | solution.py:53
  55.2 5.7 %collective-permute-start.10 = (bf16[384,1536]{1,0:T(8,128)(2,1)}, bf16[384,1536]{1,0:T(8,128)(2,1)S(1)}, u32[]{:S(2)}, u32[]{:S(2)}) collective-permute-start(bf16[384,1536]{1,0:T(8,128)(2,1)} %collective-permute-done.8), channel_id=1, source_target_pairs={{0,1},{1,0},{2,3},{3,2},{4,5},{5,4},{6,7},{7,6},{8,9},{9,8},{10,11... | collective-permute-start | bytes 3538952 | tf_op jit(solution)/shard_map/ppermute | solution.py:53
  59.9 1.0 copy-start.9
  60.9 1.1 copy-start.11
  64.2 1.1 %copy-start.5 = (bf16[384,1536]{1,0:T(8,128)(2,1)}, bf16[384,1536]{1,0:T(8,128)(2,1)S(1)}, u32[]{:S(2)}) copy-start(bf16[384,1536]{1,0:T(8,128)(2,1)S(1)} %collective-permute-done.7) | copy-start | bytes 3538948
  65.3 1.3 %copy-start = (f32[322,1536]{1,0:T(8,128)}, f32[322,1536]{1,0:T(8,128)S(1)}, u32[]{:S(2)}) copy-start(f32[322,1536]{1,0:T(8,128)S(1)} %convolution_add_fusion.3) | copy-start | bytes 5935108
  70.1 2.2 %copy-start.1 = (f32[322,1536]{1,0:T(8,128)S(1)}, f32[322,1536]{1,0:T(8,128)}, u32[]{:S(2)}) copy-start(f32[322,1536]{1,0:T(8,128)} %copy-done) | copy-start | bytes 5935108
  74.2 1.3 %copy-start.8 = (bf16[384,1536]{1,0:T(8,128)(2,1)S(1)}, bf16[384,1536]{1,0:T(8,128)(2,1)}, u32[]{:S(2)}) copy-start(bf16[384,1536]{1,0:T(8,128)(2,1)} %param.14) | copy-start | bytes 3538948
  74.6 1.6 %copy-start.2 = (bf16[1,320,1536]{2,1,0:T(8,128)(2,1)S(1)}, bf16[1,320,1536]{2,1,0:T(8,128)(2,1)}, u32[]{:S(2)}) copy-start(bf16[1,320,1536]{2,1,0:T(8,128)(2,1)} %param.9) | copy-start | bytes 2949124
  76.2 4.6 %copy-start.4 = (bf16[384,1536]{1,0:T(8,128)(2,1)S(1)}, bf16[384,1536]{1,0:T(8,128)(2,1)}, u32[]{:S(2)}) copy-start(bf16[384,1536]{1,0:T(8,128)(2,1)} %param.15) | copy-start | bytes 3538948
  78.0 3.5 %copy-start.12 = (bf16[384,1536]{1,0:T(8,128)(2,1)S(1)}, bf16[384,1536]{1,0:T(8,128)(2,1)}, u32[]{:S(2)}) copy-start(bf16[384,1536]{1,0:T(8,128)(2,1)} %copy-done.11) | copy-start | bytes 3538948
  79.2 9.8 %collective-permute-start.11 = (f32[1,1537]{1,0:T(1,128)S(1)}, f32[1,1537]{1,0:T(1,128)S(1)}, u32[]{:S(2)}, u32[]{:S(2)}) collective-permute-start(f32[1,1537]{1,0:T(1,128)S(1)} %pad_maximum_fusion.8), channel_id=1, source_target_pairs={{4,0},{8,4},{12,8},{16,12},{20,16},{24,20},{28,24},{5,1},{9,5},{13... | collective-permute-start | bytes 18452 | tf_op jit(solution)/shard_map/ppermute | solution.py:16
  81.5 1.3 %copy-start.10 = (bf16[384,1536]{1,0:T(8,128)(2,1)S(1)}, bf16[384,1536]{1,0:T(8,128)(2,1)}, u32[]{:S(2)}) copy-start(bf16[384,1536]{1,0:T(8,128)(2,1)} %copy-done.9) | copy-start | bytes 3538948
  83.4 2.1 %copy-start.6 = (bf16[384,1536]{1,0:T(8,128)(2,1)S(1)}, bf16[384,1536]{1,0:T(8,128)(2,1)}, u32[]{:S(2)}) copy-start(bf16[384,1536]{1,0:T(8,128)(2,1)} %copy-done.5) | copy-start | bytes 3538948
  90.9 7.3 %collective-permute-start.12 = (f32[1,1537]{1,0:T(1,128)S(1)}, f32[1,1537]{1,0:T(1,128)S(1)}, u32[]{:S(2)}, u32[]{:S(2)}) collective-permute-start(f32[1,1537]{1,0:T(1,128)S(1)} %pad_maximum_fusion.9), channel_id=1, source_target_pairs={{8,0},{12,4},{16,8},{20,12},{24,16},{28,20},{9,1},{13,5},{17,9},{2... | collective-permute-start | bytes 18452 | tf_op jit(solution)/shard_map/ppermute | solution.py:16
  99.5 6.4 %collective-permute-start.13 = (f32[1,1537]{1,0:T(1,128)S(1)}, f32[1,1537]{1,0:T(1,128)S(1)}, u32[]{:S(2)}, u32[]{:S(2)}) collective-permute-start(f32[1,1537]{1,0:T(1,128)S(1)} %pad_maximum_fusion.10), channel_id=1, source_target_pairs={{16,0},{20,4},{24,8},{28,12},{17,1},{21,5},{25,9},{29,13},{18,2},{... | collective-permute-start | bytes 18452 | tf_op jit(solution)/shard_map/ppermute | solution.py:16

commit v10 on v9

--- a/solution.py
+++ b/solution.py
@@ -161,6 +161,11 @@
     back_vector = base_vector + jnp.dot(
         (owner_keep * rise * cosine)[None, :], grad_wide, precision=exact
     )
+    back_vector, queries, query_scale, key_rows, key_scale, key_prior, query_unit, query_next = (
+        lax.optimization_barrier(
+            (back_vector, queries, query_scale, key_rows, key_scale, key_prior, query_unit, query_next)
+        )
+    )
     grad_in = seq_scan(last_log, back_vector, "seq", False)
     reach_end = jnp.exp(running[slot_count - 1] - running)
     state_grad = (

time: 109 us -> 113 us (1.037)
  other arithmetic: 16.7 us -> 21.7 us
  local copies, waits for them, and re-layouts: 11.9 us -> 16 us
  matrix products: 25 us -> 22.3 us
  waiting for transfers between devices: 14 us -> 11.3 us
    unnamed x30 -> x42, local copies, waits for them, and re-layouts: 4.81 us -> 8.78 us
    ppermute x2, waiting for transfers between devices: 4.9 us -> 2.23 us  [gather_blocks(): pairs.append(lax.ppermute(blocks, axis, route))]
    mul x1, other arithmetic: 0.23 us -> 1.93 us  [per_device(): prior_grad = cos_grad[:, None] * query_unit]
    slice x0 -> x1, other arithmetic: none -> 1.68 us  [per_device(): queries = queries_ext[:token_count]]
    reduce_sum x1, other arithmetic: 0.79 us -> 2.31 us  [per_device(): cosine = jnp.sum(query_unit * key_prior, axis=1)]
    dot_general x4, matrix products: 4.04 us -> 2.76 us  [per_device(): lax.dot_general(query_grad, q_block, contract_last, preferred_element_typ...]
    dot_general x8, matrix products: 8.06 us -> 6.78 us  [split_dot(): term = jnp.dot(part, block, preferred_element_type=jnp.float32)]
    concatenate x1, other arithmetic: 0.07 us -> 1.28 us  [per_device(): rows_ext = jnp.concatenate([token_rows, prev_row, next_row], axis=0)]
  transfers between devices with their start and end apart: 14 -> 14, of which waited for: 4 -> 4; matrix products, arithmetic and copies ran while one was open for 33% -> 30% of each run, Pallas kernels for 0% -> 0%
where the time goes in v10:
time: 113 us; the launch traced here: 112 us
  starting transfers between devices  25.4 us (22%)
  matrix products  22.3 us (20%)
  other arithmetic  21.7 us (19%)
  local copies, waits for them, and re-layouts  16 us (14%)
  between operations  14.9 us (13%)
  waiting for transfers between devices  11.3 us (10%)
    ppermute x8, starting transfers between devices, shifted(): return lax.ppermute(block, axis, route)  21.1 us
    ppermute x8, waiting for transfers between devices, shifted(): return lax.ppermute(block, axis, route)  9.05 us
    unnamed x42, local copies, waits for them, and re-layouts  8.78 us
    dot_general x8, matrix products, split_dot(): term = jnp.dot(part, block, preferred_element_type=jnp.float32)  6.78 us
    dot_general x4, matrix products, per_device(): lax.dot_general(key_grad, k_block, contract_last, preferred_element_type=...  4.12 us
    ppermute x2, starting transfers between devices, gather_blocks(): pairs.append(lax.ppermute(blocks, axis, route))  3.6 us
    dot_general x1, matrix products, per_device(): jnp.dot(membership, smoothed, precision=exact) + leading[:, None] * state_in  2.88 us
    dot_general x4, matrix products, per_device(): lax.dot_general(query_grad, q_block, contract_last, preferred_element_typ...  2.76 us
  transfers between devices with their start and end apart: 14, of which 4 were waited for; matrix products, arithmetic and copies ran while one was open for 30% of the time, Pallas kernels for 0%

profile of v10, /device:TPU:0, one launch (start us, length us, event | category | flops | bytes accessed | tf_op | source)
XLA Modules:
  0.0 111.6 jit_solution(18164227077889031000)
XLA Ops:
  0.6 3.0 %collective-permute-start.8 = (bf16[384,1536]{1,0:T(8,128)(2,1)}, bf16[384,1536]{1,0:T(8,128)(2,1)S(1)}, u32[]{:S(2)}, u32[]{:S(2)}) collective-permute-start(bf16[384,1536]{1,0:T(8,128)(2,1)} %param.15), channel_id=1, source_target_pairs={{0,2},{1,3},{2,0},{3,1},{4,6},{5,7},{6,4},{7,5},{8,10},{9,11},{10,... | collective-permute-start | bytes 3538952 | tf_op jit(solution)/shard_map/ppermute | solution.py:50
  4.3 0.7 fusion.60
  5.3 0.6 slice.119
  5.9 0.7 bitcast_select_fusion
  6.6 1.9 %fusion.14 = f32[128,1536]{1,0:T(8,128)S(1)} fusion(bf16[1,128,1536]{2,1,0:T(8,128)(2,1)} %param.10, f32[128]{0:T(128)S(1)} %bitcast_select_fusion, f32[128]{0:T(128)S(1)} %reduce.2), kind=kOutput, calls=%fused_computation.46 | convolution fusion | flops 302448640 | bytes 1180672 | tf_op jit(solution)/shard_map/dot_general | solution.py:128
  8.6 0.7 pad_maximum_fusion.4
  9.3 3.4 %collective-permute-start.1 = (f32[1,1537]{1,0:T(1,128)S(1)}, f32[1,1537]{1,0:T(1,128)S(1)}, u32[]{:S(2)}, u32[]{:S(2)}) collective-permute-start(f32[1,1537]{1,0:T(1,128)S(1)} %pad_maximum_fusion.4), channel_id=1, source_target_pairs={{0,4},{4,8},{8,12},{12,16},{16,20},{20,24},{24,28},{1,5},{5,9},{9,... | collective-permute-start | bytes 18452 | tf_op jit(solution)/shard_map/ppermute | solution.py:16
  12.7 0.8 slice_bitcast_fusion
  13.5 3.5 %collective-permute-start = (bf16[1,1536]{1,0:T(2,128)(2,1)S(1)}, bf16[1,1536]{1,0:T(2,128)(2,1)S(1)}, u32[]{:S(2)}, u32[]{:S(2)}) collective-permute-start(bf16[1,1536]{1,0:T(2,128)(2,1)S(1)} %get-tuple-element.33), channel_id=1, source_target_pairs={{0,4},{4,8},{8,12},{12,16},{16,20},{20,24},{24,28},{1,5},{5,9},{9,... | collective-permute-start | bytes 9224 | tf_op jit(solution)/shard_map/ppermute | solution.py:16
  17.5 0.8 fusion.33
  18.3 0.8 convert_reduce_fusion
  19.2 0.7 subtract_exponential_fusion
  22.6 0.8 multiply_add_fusion.3
  23.4 3.5 %collective-permute-start.2 = (f32[1,1537]{1,0:T(1,128)S(1)}, f32[1,1537]{1,0:T(1,128)S(1)}, u32[]{:S(2)}, u32[]{:S(2)}) collective-permute-start(f32[1,1537]{1,0:T(1,128)S(1)} %pad_maximum_fusion.5), channel_id=1, source_target_pairs={{0,8},{4,12},{8,16},{12,20},{16,24},{20,28},{1,9},{5,13},{9,17},{1... | collective-permute-start | bytes 18452 | tf_op jit(solution)/shard_map/ppermute | solution.py:16
  27.0 1.2 %collective-permute-done.2 = f32[1,1537]{1,0:T(1,128)S(1)} collective-permute-done((f32[1,1537]{1,0:T(1,128)S(1)}, f32[1,1537]{1,0:T(1,128)S(1)}, u32[]{:S(2)}, u32[]{:S(2)}) %collective-permute-start.2) | collective-permute-done | bytes 6180 | tf_op jit(solution)/shard_map/ppermute | solution.py:16
  28.2 0.6 slice.122
  29.5 5.2 %collective-permute-start.3 = (f32[1,1537]{1,0:T(1,128)S(1)}, f32[1,1537]{1,0:T(1,128)S(1)}, u32[]{:S(2)}, u32[]{:S(2)}) collective-permute-start(f32[1,1537]{1,0:T(1,128)S(1)} %pad_maximum_fusion.6), channel_id=1, source_target_pairs={{0,16},{4,20},{8,24},{12,28},{1,17},{5,21},{9,25},{13,29},{2,18},{... | collective-permute-start | bytes 18452 | tf_op jit(solution)/shard_map/ppermute | solution.py:16
  34.7 0.7 fusion.66
  37.5 2.9 %fusion.5 = f32[320]{0:T(512)S(1)} fusion(bf16[1,320,1536]{2,1,0:T(8,128)(2,1)} %param.9, f32[1536]{0:T(1024)S(1)} %fusion.44, f32[320]{0:T(512)S(1)} %compare_convert_fusion, f32[128,1536]{1,0:T(8,128)} %copy-done.20, f32[128]{0:T(128)S(1)} %get-tuple-element.41, s32[320]{0:T(512)S(1)} %get-tuple-element.38), kind=kOutput, calls=%fused_computation.26 | convolution fusion | flops 757866176 | bytes 1779968 | tf_op jit(solution)/shard_map/dot_general | solution.py:133
  40.9 0.7 pad_maximum_fusion.7
  41.6 1.5 %collective-permute-start.4 = (f32[1,1537]{1,0:T(1,128)S(1)}, f32[1,1537]{1,0:T(1,128)S(1)}, u32[]{:S(2)}, u32[]{:S(2)}) collective-permute-start(f32[1,1537]{1,0:T(1,128)S(1)} %pad_maximum_fusion.7), channel_id=1, source_target_pairs={{4,0},{8,4},{12,8},{16,12},{20,16},{24,20},{28,24},{5,1},{9,5},{13... | collective-permute-start | bytes 18452 | tf_op jit(solution)/shard_map/ppermute | solution.py:16
  45.6 2.4 %gather_fusion = f32[320]{0:T(512)S(1)} fusion(f32[128]{0:T(128)S(1)} %get-tuple-element.41, s32[1024]{0:T(1024)S(1)} %pad_clamp_fusion), kind=kCustom, calls=%fused_computation | custom fusion | bytes 3840 | tf_op jit(solution)/shard_map/gather | solution.py:136
  48.6 1.3 %pad_maximum_fusion.2 = bf16[322,1536]{1,0:T(8,128)(2,1)S(1)} fusion(bf16[1,1536]{1,0:T(2,128)(2,1)S(1)} %slice.171, bf16[1,1536]{1,0:T(2,128)(2,1)S(1)} %collective-permute-done, bf16[320,1536]{1,0:T(8,128)(2,1)} %bitcast.83), kind=kLoop, calls=%fused_computation.37 | loop fusion | flops 2967552 | bytes 1978368 | tf_op jit(solution)/shard_map/concatenate | solution.py:146
  50.0 0.7 fusion.25
  50.7 1.0 copy-done.8
  51.6 0.7 convolution_add_fusion.2
  52.9 2.2 %collective-permute-done.5 = bf16[384,1536]{1,0:T(8,128)(2,1)S(1)} collective-permute-done((bf16[384,1536]{1,0:T(8,128)(2,1)}, bf16[384,1536]{1,0:T(8,128)(2,1)S(1)}, u32[]{:S(2)}, u32[]{:S(2)}) %collective-permute-start.5) | collective-permute-done | bytes 1179680 | tf_op jit(solution)/shard_map/ppermute | solution.py:50
  55.1 0.7 fusion.27
  55.9 0.7 convolution_add_fusion.5
  56.6 2.0 %convolution_add_fusion.1 = f32[322,1536]{1,0:T(8,128)S(1)} fusion(f32[322,1536]{1,0:T(8,128)S(1)} %convolution_add_fusion.2, bf16[384,1536]{1,0:T(8,128)(2,1)} %collective-permute-done.9, bf16[322,1536]{1,0:T(8,128)(2,1)S(1)} %pad_maximum_fusion.2, s32[]{:T(128)S(6)} %select_n.137), kind=kOutput, calls=%fused_computation.2 | convolution fusion | flops 380341248 | bytes 5425156 | tf_op jit(solution)/shard_map/dot_general | solution.py:75
  58.6 0.7 convolution_add_fusion.4
  59.6 0.7 convolution_add_fusion
  60.7 0.7 multiply_reduce_fusion.6
  62.0 0.7 convolution_add_fusion.3
  63.0 1.7 %fusion.65 = (f32[320,1536]{1,0:T(8,128)}, f32[320]{0:T(512)S(1)}) fusion(f32[322,1536]{1,0:T(8,128)S(1)} %convolution_add_fusion.3), kind=kLoop, calls=%fused_computation.150 | loop fusion | flops 982720 | bytes 3933440 | tf_op jit(solution)/shard_map/slice | solution.py:149
  65.0 0.6 multiply_reduce_fusion.5
  66.3 0.8 slice_multiply_fusion.5
  67.3 1.4 %copy-done.3 = f32[322,1536]{1,0:T(8,128)S(1)} copy-done((f32[322,1536]{1,0:T(8,128)S(1)}, f32[322,1536]{1,0:T(8,128)}, u32[]{:S(2)}) %copy-start.3) | copy-done | bytes 1978392
  68.7 2.3 %multiply_reduce_fusion.2 = (f32[320]{0:T(512)S(1)}, f32[320,1536]{1,0:T(8,128)}, f32[320,1536]{1,0:T(8,128)}) fusion(f32[319,1536]{1,0:T(8,128)S(1)} %slice_multiply_fusion.1, f32[1,1536]{1,0:T(1,128)S(1)} %slice_multiply_fusion.5, f32[320]{0:T(512)S(1)} %add_rsqrt_fusion.1, f32[322,1536]{1,0:T(8,128)S(1)} %copy-done.3), kind=kLoop, calls=%fused_computation.23 | loop fusion | flops 1965760 | bytes 7866880 | tf_op jit(solution)/shard_map/reduce_sum | solution.py:156
  72.8 0.8 slice_multiply_fusion.4
  73.6 0.7 broadcast_multiply_fusion.1
  74.2 1.9 %slice_multiply_fusion = f32[319,1536]{1,0:T(8,128)S(1)} fusion(f32[320,1536]{1,0:T(8,128)} %get-tuple-element.14, f32[319]{0:T(512)S(1)} %slice.132), kind=kLoop, calls=%fused_computation.15 | loop fusion | flops 489984 | bytes 3921148 | tf_op jit(solution)/shard_map/mul | solution.py:177
  76.4 0.6 copy-done.1
  78.0 0.9 copy-done.17
  78.9 0.7 fusion.67
  79.6 1.2 %fusion.4 = f32[128,1536]{1,0:T(8,128)S(1)} fusion(bf16[1,320,1536]{2,1,0:T(8,128)(2,1)S(1)} %copy-done.4, f32[320]{0:T(512)S(1)} %get-tuple-element.37, s32[320]{0:T(512)S(1)} %get-tuple-element.38), kind=kOutput, calls=%fused_computation.14 | convolution fusion | flops 755998720 | bytes 1772032 | tf_op jit(solution)/shard_map/dot_general | solution.py:160
  80.8 0.7 pad_maximum_fusion.8
  81.5 1.5 %collective-permute-start.11 = (f32[1,1537]{1,0:T(1,128)S(1)}, f32[1,1537]{1,0:T(1,128)S(1)}, u32[]{:S(2)}, u32[]{:S(2)}) collective-permute-start(f32[1,1537]{1,0:T(1,128)S(1)} %pad_maximum_fusion.8), channel_id=1, source_target_pairs={{4,0},{8,4},{12,8},{16,12},{20,16},{24,20},{28,24},{5,1},{9,5},{13... | collective-permute-start | bytes 18452 | tf_op jit(solution)/shard_map/ppermute | solution.py:16
  83.4 0.9 copy-done.9
  84.3 0.7 fusion.6
  85.6 0.7 fusion.70
  86.3 2.0 %fusion.69 = f32[320,384]{1,0:T(8,128)S(1)} fusion(bf16[320,1536]{1,0:T(8,128)(2,1)S(1)} %subtract_convert_fusion, bf16[384,1536]{1,0:T(8,128)(2,1)} %collective-permute-done.9), kind=kOutput, calls=%fused_computation.154 | convolution fusion | flops 377487360 | bytes 2654208 | tf_op jit(solution)/shard_map/dot_general | solution.py:184
  88.4 0.7 fusion.68
  89.6 0.7 fusion.9
  90.9 0.7 fusion.8
  91.6 0.6 copy-done.7
  92.2 0.7 fusion.7
  94.9 1.3 %collective-permute-start.12 = (f32[1,1537]{1,0:T(1,128)S(1)}, f32[1,1537]{1,0:T(1,128)S(1)}, u32[]{:S(2)}, u32[]{:S(2)}) collective-permute-start(f32[1,1537]{1,0:T(1,128)S(1)} %pad_maximum_fusion.9), channel_id=1, source_target_pairs={{8,0},{12,4},{16,8},{20,12},{24,16},{28,20},{9,1},{13,5},{17,9},{2... | collective-permute-start | bytes 18452 | tf_op jit(solution)/shard_map/ppermute | solution.py:16
  96.3 5.8 %collective-permute-done.12 = f32[1,1537]{1,0:T(1,128)S(1)} collective-permute-done((f32[1,1537]{1,0:T(1,128)S(1)}, f32[1,1537]{1,0:T(1,128)S(1)}, u32[]{:S(2)}, u32[]{:S(2)}) %collective-permute-start.12) | collective-permute-done | bytes 6180 | tf_op jit(solution)/shard_map/ppermute | solution.py:16
  102.2 0.6 slice.137
  103.5 1.3 %collective-permute-start.13 = (f32[1,1537]{1,0:T(1,128)S(1)}, f32[1,1537]{1,0:T(1,128)S(1)}, u32[]{:S(2)}, u32[]{:S(2)}) collective-permute-start(f32[1,1537]{1,0:T(1,128)S(1)} %pad_maximum_fusion.10), channel_id=1, source_target_pairs={{16,0},{20,4},{24,8},{28,12},{17,1},{21,5},{25,9},{29,13},{18,2},{... | collective-permute-start | bytes 18452 | tf_op jit(solution)/shard_map/ppermute | solution.py:16
  104.8 1.0 maximum_bitcast_fusion
  107.9 2.0 %collective-permute-done.13 = f32[1,1537]{1,0:T(1,128)S(1)} collective-permute-done((f32[1,1537]{1,0:T(1,128)S(1)}, f32[1,1537]{1,0:T(1,128)S(1)}, u32[]{:S(2)}, u32[]{:S(2)}) %collective-permute-start.13) | collective-permute-done | bytes 6180 | tf_op jit(solution)/shard_map/ppermute | solution.py:16
  109.9 1.7 %fusion.3 = bf16[1,128,1536]{2,1,0:T(8,128)(2,1)} fusion(f32[128,1536]{1,0:T(8,128)S(1)} %fusion.4, f32[1536]{0:T(1024)S(1)} %fusion.45, f32[128]{0:T(128)S(1)} %get-tuple-element.40, f32[128]{0:T(128)S(1)} %bitcast_select_fusion, f32[128]{0:T(128)S(1)} %reduce.2), kind=kOutput, calls=%fused_computation.13 | convolution fusion | flops 302841856 | bytes 1187328 | tf_op jit(solution)/shard_map/dot_general | solution.py:172
  (97 shorter events, 10.8 us)
Async XLA Ops:
  0.6 49.3 %collective-permute-start.8 = (bf16[384,1536]{1,0:T(8,128)(2,1)}, bf16[384,1536]{1,0:T(8,128)(2,1)S(1)}, u32[]{:S(2)}, u32[]{:S(2)}) collective-permute-start(bf16[384,1536]{1,0:T(8,128)(2,1)} %param.15), channel_id=1, source_target_pairs={{0,2},{1,3},{2,0},{3,1},{4,6},{5,7},{6,4},{7,5},{8,10},{9,11},{10,... | collective-permute-start | bytes 3538952 | tf_op jit(solution)/shard_map/ppermute | solution.py:50
  3.7 52.9 %collective-permute-start.9 = (bf16[384,1536]{1,0:T(8,128)(2,1)}, bf16[384,1536]{1,0:T(8,128)(2,1)}, u32[]{:S(2)}, u32[]{:S(2)}) collective-permute-start(bf16[384,1536]{1,0:T(8,128)(2,1)} %param.15), channel_id=1, source_target_pairs={{0,1},{1,0},{2,3},{3,2},{4,5},{5,4},{6,7},{7,6},{8,9},{9,8},{10,11... | collective-permute-start | bytes 3538952 | tf_op jit(solution)/shard_map/ppermute | solution.py:53
  8.5 4.9 %copy-start.20 = (f32[128,1536]{1,0:T(8,128)}, f32[128,1536]{1,0:T(8,128)S(1)}, u32[]{:S(2)}) copy-start(f32[128,1536]{1,0:T(8,128)S(1)} %fusion.14) | copy-start | bytes 2359300
  9.3 11.4 %collective-permute-start.1 = (f32[1,1537]{1,0:T(1,128)S(1)}, f32[1,1537]{1,0:T(1,128)S(1)}, u32[]{:S(2)}, u32[]{:S(2)}) collective-permute-start(f32[1,1537]{1,0:T(1,128)S(1)} %pad_maximum_fusion.4), channel_id=1, source_target_pairs={{0,4},{4,8},{8,12},{12,16},{16,20},{20,24},{24,28},{1,5},{5,9},{9,... | collective-permute-start | bytes 18452 | tf_op jit(solution)/shard_map/ppermute | solution.py:16
  13.5 35.2 %collective-permute-start = (bf16[1,1536]{1,0:T(2,128)(2,1)S(1)}, bf16[1,1536]{1,0:T(2,128)(2,1)S(1)}, u32[]{:S(2)}, u32[]{:S(2)}) collective-permute-start(bf16[1,1536]{1,0:T(2,128)(2,1)S(1)} %get-tuple-element.33), channel_id=1, source_target_pairs={{0,4},{4,8},{8,12},{12,16},{16,20},{20,24},{24,28},{1,5},{5,9},{9,... | collective-permute-start | bytes 9224 | tf_op jit(solution)/shard_map/ppermute | solution.py:16
  16.9 38.2 %collective-permute-start.5 = (bf16[384,1536]{1,0:T(8,128)(2,1)}, bf16[384,1536]{1,0:T(8,128)(2,1)S(1)}, u32[]{:S(2)}, u32[]{:S(2)}) collective-permute-start(bf16[384,1536]{1,0:T(8,128)(2,1)} %param.14), channel_id=1, source_target_pairs={{0,2},{1,3},{2,0},{3,1},{4,6},{5,7},{6,4},{7,5},{8,10},{9,11},{10,... | collective-permute-start | bytes 3538952 | tf_op jit(solution)/shard_map/ppermute | solution.py:50
  23.4 4.8 %collective-permute-start.2 = (f32[1,1537]{1,0:T(1,128)S(1)}, f32[1,1537]{1,0:T(1,128)S(1)}, u32[]{:S(2)}, u32[]{:S(2)}) collective-permute-start(f32[1,1537]{1,0:T(1,128)S(1)} %pad_maximum_fusion.5), channel_id=1, source_target_pairs={{0,8},{4,12},{8,16},{12,20},{16,24},{20,28},{1,9},{5,13},{9,17},{1... | collective-permute-start | bytes 18452 | tf_op jit(solution)/shard_map/ppermute | solution.py:16
  29.5 7.9 %collective-permute-start.3 = (f32[1,1537]{1,0:T(1,128)S(1)}, f32[1,1537]{1,0:T(1,128)S(1)}, u32[]{:S(2)}, u32[]{:S(2)}) collective-permute-start(f32[1,1537]{1,0:T(1,128)S(1)} %pad_maximum_fusion.6), channel_id=1, source_target_pairs={{0,16},{4,20},{8,24},{12,28},{1,17},{5,21},{9,25},{13,29},{2,18},{... | collective-permute-start | bytes 18452 | tf_op jit(solution)/shard_map/ppermute | solution.py:16
  41.6 6.5 %collective-permute-start.4 = (f32[1,1537]{1,0:T(1,128)S(1)}, f32[1,1537]{1,0:T(1,128)S(1)}, u32[]{:S(2)}, u32[]{:S(2)}) collective-permute-start(f32[1,1537]{1,0:T(1,128)S(1)} %pad_maximum_fusion.7), channel_id=1, source_target_pairs={{4,0},{8,4},{12,8},{16,12},{20,16},{24,20},{28,24},{5,1},{9,5},{13... | collective-permute-start | bytes 18452 | tf_op jit(solution)/shard_map/ppermute | solution.py:16
  48.1 10.5 %collective-permute-start.6 = (bf16[384,1536]{1,0:T(8,128)(2,1)}, bf16[384,1536]{1,0:T(8,128)(2,1)S(1)}, u32[]{:S(2)}, u32[]{:S(2)}) collective-permute-start(bf16[384,1536]{1,0:T(8,128)(2,1)} %param.14), channel_id=1, source_target_pairs={{0,1},{1,0},{2,3},{3,2},{4,5},{5,4},{6,7},{7,6},{8,9},{9,8},{10,11... | collective-permute-start | bytes 3538952 | tf_op jit(solution)/shard_map/ppermute | solution.py:53
  49.9 1.7 %copy-start.8 = (bf16[384,1536]{1,0:T(8,128)(2,1)S(1)}, bf16[384,1536]{1,0:T(8,128)(2,1)}, u32[]{:S(2)}) copy-start(bf16[384,1536]{1,0:T(8,128)(2,1)} %param.15) | copy-start | bytes 3538948
  49.9 2.4 %copy-start.10 = (bf16[384,1536]{1,0:T(8,128)(2,1)}, bf16[384,1536]{1,0:T(8,128)(2,1)S(1)}, u32[]{:S(2)}) copy-start(bf16[384,1536]{1,0:T(8,128)(2,1)S(1)} %collective-permute-done.8) | copy-start | bytes 3538948
  52.3 3.6 %copy-start.16 = (bf16[384,1536]{1,0:T(8,128)(2,1)S(1)}, bf16[384,1536]{1,0:T(8,128)(2,1)}, u32[]{:S(2)}) copy-start(bf16[384,1536]{1,0:T(8,128)(2,1)} %param.14) | copy-start | bytes 3538948
  52.3 7.3 %collective-permute-start.10 = (bf16[384,1536]{1,0:T(8,128)(2,1)S(1)}, bf16[384,1536]{1,0:T(8,128)(2,1)S(1)}, u32[]{:S(2)}, u32[]{:S(2)}) collective-permute-start(bf16[384,1536]{1,0:T(8,128)(2,1)S(1)} %collective-permute-done.8), channel_id=1, source_target_pairs={{0,1},{1,0},{2,3},{3,2},{4,5},{5,4},{6,7},{7,6},{8,9},{9,8},{10,11... | collective-permute-start | bytes 3538952 | tf_op jit(solution)/shard_map/ppermute | solution.py:53
  55.1 1.5 %copy-start.6 = (bf16[384,1536]{1,0:T(8,128)(2,1)}, bf16[384,1536]{1,0:T(8,128)(2,1)S(1)}, u32[]{:S(2)}) copy-start(bf16[384,1536]{1,0:T(8,128)(2,1)S(1)} %collective-permute-done.5) | copy-start | bytes 3538948
  55.8 6.2 %collective-permute-start.7 = (bf16[384,1536]{1,0:T(8,128)(2,1)S(1)}, bf16[384,1536]{1,0:T(8,128)(2,1)S(1)}, u32[]{:S(2)}, u32[]{:S(2)}) collective-permute-start(bf16[384,1536]{1,0:T(8,128)(2,1)S(1)} %collective-permute-done.5), channel_id=1, source_target_pairs={{0,1},{1,0},{2,3},{3,2},{4,5},{5,4},{6,7},{7,6},{8,9},{9,8},{10,11... | collective-permute-start | bytes 3538952 | tf_op jit(solution)/shard_map/ppermute | solution.py:53
  58.6 1.0 copy-start.12
  59.6 1.1 copy-start.18
  60.7 1.3 %copy-start.5 = (f32[322,1536]{1,0:T(8,128)}, f32[322,1536]{1,0:T(8,128)S(1)}, u32[]{:S(2)}) copy-start(f32[322,1536]{1,0:T(8,128)S(1)} %convolution_add_fusion) | copy-start | bytes 5935108
  62.0 1.0 copy-start.14
  63.0 2.0 %copy-start.2 = (f32[322,1536]{1,0:T(8,128)}, f32[322,1536]{1,0:T(8,128)S(1)}, u32[]{:S(2)}) copy-start(f32[322,1536]{1,0:T(8,128)S(1)} %convolution_add_fusion.3) | copy-start | bytes 5935108
  67.1 1.6 %copy-start.3 = (f32[322,1536]{1,0:T(8,128)S(1)}, f32[322,1536]{1,0:T(8,128)}, u32[]{:S(2)}) copy-start(f32[322,1536]{1,0:T(8,128)} %copy-done.2) | copy-start | bytes 5935108
  68.7 2.3 %copy-start.4 = (bf16[1,320,1536]{2,1,0:T(8,128)(2,1)S(1)}, bf16[1,320,1536]{2,1,0:T(8,128)(2,1)}, u32[]{:S(2)}) copy-start(bf16[1,320,1536]{2,1,0:T(8,128)(2,1)} %param.9) | copy-start | bytes 2949124
  74.2 2.1 %copy-start = (f32[320,1536]{1,0:T(8,128)S(1)}, f32[320,1536]{1,0:T(8,128)}, u32[]{:S(2)}) copy-start(f32[320,1536]{1,0:T(8,128)} %get-tuple-element.12) | copy-start | bytes 5898244
  74.2 2.7 %copy-start.1 = (f32[320,1536]{1,0:T(8,128)S(1)}, f32[320,1536]{1,0:T(8,128)}, u32[]{:S(2)}) copy-start(f32[320,1536]{1,0:T(8,128)} %get-tuple-element.11) | copy-start | bytes 5898244
  77.6 1.3 %copy-start.17 = (bf16[384,1536]{1,0:T(8,128)(2,1)S(1)}, bf16[384,1536]{1,0:T(8,128)(2,1)}, u32[]{:S(2)}) copy-start(bf16[384,1536]{1,0:T(8,128)(2,1)} %param.14) | copy-start | bytes 3538948
  81.5 11.4 %collective-permute-start.11 = (f32[1,1537]{1,0:T(1,128)S(1)}, f32[1,1537]{1,0:T(1,128)S(1)}, u32[]{:S(2)}, u32[]{:S(2)}) collective-permute-start(f32[1,1537]{1,0:T(1,128)S(1)} %pad_maximum_fusion.8), channel_id=1, source_target_pairs={{4,0},{8,4},{12,8},{16,12},{20,16},{24,20},{28,24},{5,1},{9,5},{13... | collective-permute-start | bytes 18452 | tf_op jit(solution)/shard_map/ppermute | solution.py:16
  83.0 1.3 %copy-start.9 = (bf16[384,1536]{1,0:T(8,128)(2,1)S(1)}, bf16[384,1536]{1,0:T(8,128)(2,1)}, u32[]{:S(2)}) copy-start(bf16[384,1536]{1,0:T(8,128)(2,1)} %param.15) | copy-start | bytes 3538948
  84.3 1.3 %copy-start.19 = (bf16[384,1536]{1,0:T(8,128)(2,1)S(1)}, bf16[384,1536]{1,0:T(8,128)(2,1)}, u32[]{:S(2)}) copy-start(bf16[384,1536]{1,0:T(8,128)(2,1)} %copy-done.18) | copy-start | bytes 3538948
  86.3 2.1 %copy-start.11 = (bf16[384,1536]{1,0:T(8,128)(2,1)S(1)}, bf16[384,1536]{1,0:T(8,128)(2,1)}, u32[]{:S(2)}) copy-start(bf16[384,1536]{1,0:T(8,128)(2,1)} %copy-done.10) | copy-start | bytes 3538948
  88.4 1.3 %copy-start.15 = (bf16[384,1536]{1,0:T(8,128)(2,1)S(1)}, bf16[384,1536]{1,0:T(8,128)(2,1)}, u32[]{:S(2)}) copy-start(bf16[384,1536]{1,0:T(8,128)(2,1)} %copy-done.14) | copy-start | bytes 3538948
  89.6 1.3 %copy-start.13 = (bf16[384,1536]{1,0:T(8,128)(2,1)S(1)}, bf16[384,1536]{1,0:T(8,128)(2,1)}, u32[]{:S(2)}) copy-start(bf16[384,1536]{1,0:T(8,128)(2,1)} %copy-done.12) | copy-start | bytes 3538948
  90.9 1.3 %copy-start.7 = (bf16[384,1536]{1,0:T(8,128)(2,1)S(1)}, bf16[384,1536]{1,0:T(8,128)(2,1)}, u32[]{:S(2)}) copy-start(bf16[384,1536]{1,0:T(8,128)(2,1)} %copy-done.6) | copy-start | bytes 3538948
  94.9 7.3 %collective-permute-start.12 = (f32[1,1537]{1,0:T(1,128)S(1)}, f32[1,1537]{1,0:T(1,128)S(1)}, u32[]{:S(2)}, u32[]{:S(2)}) collective-permute-start(f32[1,1537]{1,0:T(1,128)S(1)} %pad_maximum_fusion.9), channel_id=1, source_target_pairs={{8,0},{12,4},{16,8},{20,12},{24,16},{28,20},{9,1},{13,5},{17,9},{2... | collective-permute-start | bytes 18452 | tf_op jit(solution)/shard_map/ppermute | solution.py:16
  103.5 6.4 %collective-permute-start.13 = (f32[1,1537]{1,0:T(1,128)S(1)}, f32[1,1537]{1,0:T(1,128)S(1)}, u32[]{:S(2)}, u32[]{:S(2)}) collective-permute-start(f32[1,1537]{1,0:T(1,128)S(1)} %pad_maximum_fusion.10), channel_id=1, source_target_pairs={{16,0},{20,4},{24,8},{28,12},{17,1},{21,5},{25,9},{29,13},{18,2},{... | collective-permute-start | bytes 18452 | tf_op jit(solution)/shard_map/ppermute | solution.py:16

commit v11 on v9

--- a/solution.py
+++ b/solution.py
@@ -153,7 +153,13 @@
     key_before, _ = unit_of(keys_ext[token_count : token_count + 1])
     query_next, _ = unit_of(queries_ext[token_count + 1 :])
     key_prior = jnp.concatenate([key_before, key_unit[:-1]], axis=0)
-    cosine = jnp.sum(query_unit * key_prior, axis=1)
+    key_shift = keys_ext[token_count : token_count + 1]
+    raw_prior = jnp.concatenate([key_shift, key_rows[:-1]], axis=0)
+    prior_sq = jnp.sum(raw_prior * raw_prior, axis=1)
+    query_sq = jnp.sum(queries * queries, axis=1)
+    cosine = (
+        jnp.sum(queries * raw_prior, axis=1) * lax.rsqrt(query_sq + norm_eps) * lax.rsqrt(prior_sq + norm_eps)
+    )
     boundary_prob = jnp.where(later_rows, 0.5 * (1.0 - cosine), 1.0)
     confidence = jnp.where(starts, boundary_prob, 1.0 - boundary_prob)
     weighted_grad = confidence[:, None] * grad_rows

time: 109 us -> 111 us (1.018)
  other arithmetic: 16.7 us -> 18.9 us
    reduce_sum x1, other arithmetic: 0.79 us -> 2.8 us  [per_device(): jnp.sum(queries * raw_prior, axis=1) * lax.rsqrt(query_sq + norm_eps)]
    concatenate x1, other arithmetic: 0.07 us -> 1.28 us  [per_device(): rows_ext = jnp.concatenate([token_rows, prev_row, next_row], axis=0)]
where the time goes in v11:
time: 111 us; the launch traced here: 110 us
  starting transfers between devices  25.3 us (23%)
  matrix products  24.8 us (22%)
  other arithmetic  18.9 us (17%)
  between operations  14.6 us (13%)
  waiting for transfers between devices  13.3 us (12%)
  local copies, waits for them, and re-layouts  13 us (12%)
    ppermute x8, starting transfers between devices, shifted(): return lax.ppermute(block, axis, route)  21.1 us
    ppermute x8, waiting for transfers between devices, shifted(): return lax.ppermute(block, axis, route)  9.06 us
    dot_general x8, matrix products, split_dot(): term = jnp.dot(part, block, preferred_element_type=jnp.float32)  8.07 us
    unnamed x30, local copies, waits for them, and re-layouts  5.63 us
    ppermute x2, waiting for transfers between devices, gather_blocks(): pairs.append(lax.ppermute(blocks, axis, route))  4.22 us
    dot_general x4, matrix products, per_device(): lax.dot_general(key_grad, k_block, contract_last, preferred_element_type=...  4.11 us
    dot_general x4, matrix products, per_device(): lax.dot_general(query_grad, q_block, contract_last, preferred_element_typ...  4.05 us
    ppermute x2, starting transfers between devices, gather_blocks(): pairs.append(lax.ppermute(blocks, axis, route))  3.6 us
  transfers between devices with their start and end apart: 14, of which 4 were waited for; matrix products, arithmetic and copies ran while one was open for 33% of the time, Pallas kernels for 0%

profile of v11, /device:TPU:0, one launch (start us, length us, event | category | flops | bytes accessed | tf_op | source)
XLA Modules:
  0.0 109.8 jit_solution(6405254880210544357)
XLA Ops:
  0.6 3.0 %collective-permute-start.5 = (bf16[384,1536]{1,0:T(8,128)(2,1)}, bf16[384,1536]{1,0:T(8,128)(2,1)S(1)}, u32[]{:S(2)}, u32[]{:S(2)}) collective-permute-start(bf16[384,1536]{1,0:T(8,128)(2,1)} %param.14), channel_id=1, source_target_pairs={{0,2},{1,3},{2,0},{3,1},{4,6},{5,7},{6,4},{7,5},{8,10},{9,11},{10,... | collective-permute-start | bytes 3538952 | tf_op jit(solution)/shard_map/ppermute | solution.py:50
  4.3 0.7 fusion.59
  5.3 0.5 slice.125
  5.8 0.7 bitcast_select_fusion
  6.6 1.9 %fusion.15 = f32[128,1536]{1,0:T(8,128)S(1)} fusion(bf16[1,128,1536]{2,1,0:T(8,128)(2,1)} %param.10, f32[128]{0:T(128)S(1)} %bitcast_select_fusion, f32[128]{0:T(128)S(1)} %reduce.2), kind=kOutput, calls=%fused_computation.48 | convolution fusion | flops 302448640 | bytes 1180672 | tf_op jit(solution)/shard_map/dot_general | solution.py:128
  8.5 0.7 pad_maximum_fusion.4
  9.1 3.4 %collective-permute-start.1 = (f32[1,1537]{1,0:T(1,128)S(1)}, f32[1,1537]{1,0:T(1,128)S(1)}, u32[]{:S(2)}, u32[]{:S(2)}) collective-permute-start(f32[1,1537]{1,0:T(1,128)S(1)} %pad_maximum_fusion.4), channel_id=1, source_target_pairs={{0,4},{4,8},{8,12},{12,16},{16,20},{20,24},{24,28},{1,5},{5,9},{9,... | collective-permute-start | bytes 18452 | tf_op jit(solution)/shard_map/ppermute | solution.py:16
  12.5 0.8 slice_bitcast_fusion
  13.3 3.5 %collective-permute-start = (bf16[1,1536]{1,0:T(2,128)(2,1)S(1)}, bf16[1,1536]{1,0:T(2,128)(2,1)S(1)}, u32[]{:S(2)}, u32[]{:S(2)}) collective-permute-start(bf16[1,1536]{1,0:T(2,128)(2,1)S(1)} %get-tuple-element.16), channel_id=1, source_target_pairs={{0,4},{4,8},{8,12},{12,16},{16,20},{20,24},{24,28},{1,5},{5,9},{9,... | collective-permute-start | bytes 9224 | tf_op jit(solution)/shard_map/ppermute | solution.py:16
  16.8 0.6 collective-permute-start.8
  17.3 0.8 fusion.33
  18.2 0.8 convert_reduce_fusion
  19.0 0.7 subtract_exponential_fusion
  20.5 0.5 slice.126
  22.3 3.5 %collective-permute-start.2 = (f32[1,1537]{1,0:T(1,128)S(1)}, f32[1,1537]{1,0:T(1,128)S(1)}, u32[]{:S(2)}, u32[]{:S(2)}) collective-permute-start(f32[1,1537]{1,0:T(1,128)S(1)} %pad_maximum_fusion.5), channel_id=1, source_target_pairs={{0,8},{4,12},{8,16},{12,20},{16,24},{20,28},{1,9},{5,13},{9,17},{1... | collective-permute-start | bytes 18452 | tf_op jit(solution)/shard_map/ppermute | solution.py:16
  26.0 1.2 %collective-permute-done.2 = f32[1,1537]{1,0:T(1,128)S(1)} collective-permute-done((f32[1,1537]{1,0:T(1,128)S(1)}, f32[1,1537]{1,0:T(1,128)S(1)}, u32[]{:S(2)}, u32[]{:S(2)}) %collective-permute-start.2) | collective-permute-done | bytes 6180 | tf_op jit(solution)/shard_map/ppermute | solution.py:16
  27.1 0.6 slice.128
  28.4 5.2 %collective-permute-start.3 = (f32[1,1537]{1,0:T(1,128)S(1)}, f32[1,1537]{1,0:T(1,128)S(1)}, u32[]{:S(2)}, u32[]{:S(2)}) collective-permute-start(f32[1,1537]{1,0:T(1,128)S(1)} %pad_maximum_fusion.6), channel_id=1, source_target_pairs={{0,16},{4,20},{8,24},{12,28},{1,17},{5,21},{9,25},{13,29},{2,18},{... | collective-permute-start | bytes 18452 | tf_op jit(solution)/shard_map/ppermute | solution.py:16
  33.6 0.6 fusion.62
  36.2 2.7 %fusion.6 = f32[320]{0:T(512)S(1)} fusion(bf16[1,320,1536]{2,1,0:T(8,128)(2,1)} %param.9, f32[1536]{0:T(1024)S(1)} %fusion.45, f32[320]{0:T(512)S(1)} %compare_convert_fusion, f32[128,1536]{1,0:T(8,128)S(1)} %fusion.15, f32[128]{0:T(128)S(1)} %get-tuple-element.26, s32[320]{0:T(512)S(1)} %get-tuple-element.24), kind=kOutput, calls=%fused_computation.29 | convolution fusion | flops 757866176 | bytes 1779968 | tf_op jit(solution)/shard_map/dot_general | solution.py:133
  39.0 0.5 slice.103
  39.5 0.7 pad_maximum_fusion.7
  40.2 1.5 %collective-permute-start.4 = (f32[1,1537]{1,0:T(1,128)S(1)}, f32[1,1537]{1,0:T(1,128)S(1)}, u32[]{:S(2)}, u32[]{:S(2)}) collective-permute-start(f32[1,1537]{1,0:T(1,128)S(1)} %pad_maximum_fusion.7), channel_id=1, source_target_pairs={{4,0},{8,4},{12,8},{16,12},{20,16},{24,20},{28,24},{5,1},{9,5},{13... | collective-permute-start | bytes 18452 | tf_op jit(solution)/shard_map/ppermute | solution.py:16
  44.2 2.4 %gather_fusion = f32[320]{0:T(512)S(1)} fusion(f32[128]{0:T(128)S(1)} %get-tuple-element.26, s32[1024]{0:T(1024)S(1)} %pad_clamp_fusion), kind=kCustom, calls=%fused_computation | custom fusion | bytes 3840 | tf_op jit(solution)/shard_map/gather | solution.py:136
  47.2 1.3 %pad_maximum_fusion.2 = bf16[322,1536]{1,0:T(8,128)(2,1)S(1)} fusion(bf16[1,1536]{1,0:T(2,128)(2,1)S(1)} %slice.185, bf16[1,1536]{1,0:T(2,128)(2,1)S(1)} %collective-permute-done, bf16[320,1536]{1,0:T(8,128)(2,1)} %bitcast.83), kind=kLoop, calls=%fused_computation.40 | loop fusion | flops 2967552 | bytes 1978368 | tf_op jit(solution)/shard_map/concatenate | solution.py:146
  48.5 0.7 fusion.28
  49.2 0.6 copy-done.9
  49.8 0.7 convolution_add_fusion.5
  50.5 0.5 collective-permute-start.7
  51.0 4.2 %collective-permute-done.8 = bf16[384,1536]{1,0:T(8,128)(2,1)} collective-permute-done((bf16[384,1536]{1,0:T(8,128)(2,1)}, bf16[384,1536]{1,0:T(8,128)(2,1)}, u32[]{:S(2)}, u32[]{:S(2)}) %collective-permute-start.8) | collective-permute-done | bytes 1179680 | tf_op jit(solution)/shard_map/ppermute | solution.py:50
  55.2 1.9 %fusion.26 = f32[322,1536]{1,0:T(8,128)S(1)} fusion(bf16[384,1536]{1,0:T(8,128)(2,1)} %collective-permute-done.8, bf16[322,1536]{1,0:T(8,128)(2,1)S(1)} %pad_maximum_fusion.2, s32[]{:T(128)S(6)} %select_n.131), kind=kOutput, calls=%fused_computation.59 | convolution fusion | flops 379846656 | bytes 3409924 | tf_op jit(solution)/shard_map/dot_general | solution.py:75
  57.2 0.7 convolution_add_fusion.2
  57.9 2.0 %convolution_add_fusion.4 = f32[322,1536]{1,0:T(8,128)S(1)} fusion(f32[322,1536]{1,0:T(8,128)S(1)} %convolution_add_fusion.5, bf16[384,1536]{1,0:T(8,128)(2,1)} %collective-permute-done.6, bf16[322,1536]{1,0:T(8,128)(2,1)S(1)} %pad_maximum_fusion.2, s32[]{:T(128)S(6)} %select_n.132), kind=kOutput, calls=%fused_computation.5 | convolution fusion | flops 380341248 | bytes 5425156 | tf_op jit(solution)/shard_map/dot_general | solution.py:75
  59.9 0.7 convolution_add_fusion.1
  61.0 0.7 convolution_add_fusion
  62.0 0.8 multiply_reduce_fusion.7
  62.8 1.5 %multiply_reduce_fusion.4 = (f32[320]{0:T(512)S(1)}, f32[320,1536]{1,0:T(8,128)}) fusion(f32[322,1536]{1,0:T(8,128)S(1)} %convolution_add_fusion), kind=kLoop, calls=%fused_computation.27 | loop fusion | flops 982720 | bytes 3933440 | tf_op jit(solution)/shard_map/reduce_sum | solution.py:87
  64.2 0.7 convolution_add_fusion.3
  65.3 1.3 %copy-done.2 = f32[322,1536]{1,0:T(8,128)} copy-done((f32[322,1536]{1,0:T(8,128)}, f32[322,1536]{1,0:T(8,128)S(1)}, u32[]{:S(2)}) %copy-start.2) | copy-done | bytes 1978392
  66.5 0.6 multiply_reduce_fusion.6
  68.6 1.9 %slice_multiply_fusion.1 = f32[319,1536]{1,0:T(8,128)S(1)} fusion(f32[320,1536]{1,0:T(8,128)} %get-tuple-element.11, f32[319]{0:T(512)S(1)} %bitcast.84), kind=kLoop, calls=%fused_computation.17 | loop fusion | flops 489984 | bytes 3921148 | tf_op jit(solution)/shard_map/mul | solution.py:88
  70.7 2.8 %multiply_reduce_fusion.1 = (f32[320]{0:T(512)S(1)}, f32[320]{0:T(512)S(1)}, f32[320]{0:T(512)S(1)}, f32[320]{0:T(512)S(1)}) fusion(f32[319,1536]{1,0:T(8,128)S(1)} %slice-done, f32[1,1536]{1,0:T(1,128)S(1)} %get-tuple-element.9, f32[322,1536]{1,0:T(8,128)} %copy-done.2, f32[319,1536]{1,0:T(8,128)S(1)} %slice_multiply_fusion.1, ...), kind=kLoop, calls=%fused_computation.22 | loop fusion | flops 5405440 | bytes 5904640 | tf_op jit(solution)/shard_map/reduce_sum | solution.py:161
  74.1 0.6 multiply_multiply_fusion
  75.0 1.2 %copy-done.1 = f32[322,1536]{1,0:T(8,128)S(1)} copy-done((f32[322,1536]{1,0:T(8,128)S(1)}, f32[322,1536]{1,0:T(8,128)}, u32[]{:S(2)}) %copy-start.1) | copy-done | bytes 1978392
  76.9 0.9 copy-done.10
  77.8 0.7 fusion.63
  78.5 1.2 %fusion.4 = f32[128,1536]{1,0:T(8,128)S(1)} fusion(bf16[1,320,1536]{2,1,0:T(8,128)(2,1)S(1)} %copy-done.4, f32[320]{0:T(512)S(1)} %get-tuple-element.19, s32[320]{0:T(512)S(1)} %get-tuple-element.24), kind=kOutput, calls=%fused_computation.14 | convolution fusion | flops 755998720 | bytes 1772032 | tf_op jit(solution)/shard_map/dot_general | solution.py:166
  80.8 0.7 pad_maximum_fusion.8
  81.5 1.5 %collective-permute-start.11 = (f32[1,1537]{1,0:T(1,128)S(1)}, f32[1,1537]{1,0:T(1,128)S(1)}, u32[]{:S(2)}, u32[]{:S(2)}) collective-permute-start(f32[1,1537]{1,0:T(1,128)S(1)} %pad_maximum_fusion.8), channel_id=1, source_target_pairs={{4,0},{8,4},{12,8},{16,12},{20,16},{24,20},{28,24},{5,1},{9,5},{13... | collective-permute-start | bytes 18452 | tf_op jit(solution)/shard_map/ppermute | solution.py:16
  83.0 0.7 fusion.7
  83.7 0.7 fusion.66
  84.4 0.6 copy-done.12
  85.0 0.7 fusion.65
  85.7 2.0 %fusion.64 = f32[320,384]{1,0:T(8,128)S(1)} fusion(bf16[320,1536]{1,0:T(8,128)(2,1)S(1)} %subtract_convert_fusion, bf16[384,1536]{1,0:T(8,128)(2,1)} %collective-permute-done.8), kind=kOutput, calls=%fused_computation.150 | convolution fusion | flops 377487360 | bytes 2654208 | tf_op jit(solution)/shard_map/dot_general | solution.py:185
  87.8 0.7 fusion.10
  88.5 2.0 %fusion.9 = bf16[320,384]{1,0:T(8,128)(2,1)S(1)} fusion(f32[320,384]{1,0:T(8,128)S(1)} %fusion.65, bf16[320,1536]{1,0:T(8,128)(2,1)S(1)} %get-tuple-element.6, bf16[384,1536]{1,0:T(8,128)(2,1)} %collective-permute-done.6), kind=kOutput, calls=%fused_computation.36 | convolution fusion | flops 377733120 | bytes 2899968 | tf_op jit(solution)/shard_map/dot_general | solution.py:184
  90.4 0.7 fusion.8
  93.1 1.3 %collective-permute-start.12 = (f32[1,1537]{1,0:T(1,128)S(1)}, f32[1,1537]{1,0:T(1,128)S(1)}, u32[]{:S(2)}, u32[]{:S(2)}) collective-permute-start(f32[1,1537]{1,0:T(1,128)S(1)} %pad_maximum_fusion.9), channel_id=1, source_target_pairs={{8,0},{12,4},{16,8},{20,12},{24,16},{28,20},{9,1},{13,5},{17,9},{2... | collective-permute-start | bytes 18452 | tf_op jit(solution)/shard_map/ppermute | solution.py:16
  94.6 5.8 %collective-permute-done.12 = f32[1,1537]{1,0:T(1,128)S(1)} collective-permute-done((f32[1,1537]{1,0:T(1,128)S(1)}, f32[1,1537]{1,0:T(1,128)S(1)}, u32[]{:S(2)}, u32[]{:S(2)}) %collective-permute-start.12) | collective-permute-done | bytes 6180 | tf_op jit(solution)/shard_map/ppermute | solution.py:16
  100.4 0.6 slice.145
  101.7 1.3 %collective-permute-start.13 = (f32[1,1537]{1,0:T(1,128)S(1)}, f32[1,1537]{1,0:T(1,128)S(1)}, u32[]{:S(2)}, u32[]{:S(2)}) collective-permute-start(f32[1,1537]{1,0:T(1,128)S(1)} %pad_maximum_fusion.10), channel_id=1, source_target_pairs={{16,0},{20,4},{24,8},{28,12},{17,1},{21,5},{25,9},{29,13},{18,2},{... | collective-permute-start | bytes 18452 | tf_op jit(solution)/shard_map/ppermute | solution.py:16
  103.0 1.0 maximum_bitcast_fusion
  106.1 2.0 %collective-permute-done.13 = f32[1,1537]{1,0:T(1,128)S(1)} collective-permute-done((f32[1,1537]{1,0:T(1,128)S(1)}, f32[1,1537]{1,0:T(1,128)S(1)}, u32[]{:S(2)}, u32[]{:S(2)}) %collective-permute-start.13) | collective-permute-done | bytes 6180 | tf_op jit(solution)/shard_map/ppermute | solution.py:16
  108.2 1.7 %fusion.3 = bf16[1,128,1536]{2,1,0:T(8,128)(2,1)} fusion(f32[128,1536]{1,0:T(8,128)S(1)} %fusion.4, f32[1536]{0:T(1024)S(1)} %fusion.46, f32[128]{0:T(128)S(1)} %get-tuple-element.25, f32[128]{0:T(128)S(1)} %bitcast_select_fusion, f32[128]{0:T(128)S(1)} %reduce.2), kind=kOutput, calls=%fused_computation.13 | convolution fusion | flops 302841856 | bytes 1187328 | tf_op jit(solution)/shard_map/dot_general | solution.py:173
  (82 shorter events, 6.0 us)
Async XLA Ops:
  0.6 47.9 %collective-permute-start.5 = (bf16[384,1536]{1,0:T(8,128)(2,1)}, bf16[384,1536]{1,0:T(8,128)(2,1)S(1)}, u32[]{:S(2)}, u32[]{:S(2)}) collective-permute-start(bf16[384,1536]{1,0:T(8,128)(2,1)} %param.14), channel_id=1, source_target_pairs={{0,2},{1,3},{2,0},{3,1},{4,6},{5,7},{6,4},{7,5},{8,10},{9,11},{10,... | collective-permute-start | bytes 3538952 | tf_op jit(solution)/shard_map/ppermute | solution.py:50
  3.7 54.2 %collective-permute-start.6 = (bf16[384,1536]{1,0:T(8,128)(2,1)}, bf16[384,1536]{1,0:T(8,128)(2,1)}, u32[]{:S(2)}, u32[]{:S(2)}) collective-permute-start(bf16[384,1536]{1,0:T(8,128)(2,1)} %param.14), channel_id=1, source_target_pairs={{0,1},{1,0},{2,3},{3,2},{4,5},{5,4},{6,7},{7,6},{8,9},{9,8},{10,11... | collective-permute-start | bytes 3538952 | tf_op jit(solution)/shard_map/ppermute | solution.py:53
  9.1 11.3 %collective-permute-start.1 = (f32[1,1537]{1,0:T(1,128)S(1)}, f32[1,1537]{1,0:T(1,128)S(1)}, u32[]{:S(2)}, u32[]{:S(2)}) collective-permute-start(f32[1,1537]{1,0:T(1,128)S(1)} %pad_maximum_fusion.4), channel_id=1, source_target_pairs={{0,4},{4,8},{8,12},{12,16},{16,20},{20,24},{24,28},{1,5},{5,9},{9,... | collective-permute-start | bytes 18452 | tf_op jit(solution)/shard_map/ppermute | solution.py:16
  13.3 33.9 %collective-permute-start = (bf16[1,1536]{1,0:T(2,128)(2,1)S(1)}, bf16[1,1536]{1,0:T(2,128)(2,1)S(1)}, u32[]{:S(2)}, u32[]{:S(2)}) collective-permute-start(bf16[1,1536]{1,0:T(2,128)(2,1)S(1)} %get-tuple-element.16), channel_id=1, source_target_pairs={{0,4},{4,8},{8,12},{12,16},{16,20},{20,24},{24,28},{1,5},{5,9},{9,... | collective-permute-start | bytes 9224 | tf_op jit(solution)/shard_map/ppermute | solution.py:16
  16.8 38.5 %collective-permute-start.8 = (bf16[384,1536]{1,0:T(8,128)(2,1)}, bf16[384,1536]{1,0:T(8,128)(2,1)}, u32[]{:S(2)}, u32[]{:S(2)}) collective-permute-start(bf16[384,1536]{1,0:T(8,128)(2,1)} %param.15), channel_id=1, source_target_pairs={{0,2},{1,3},{2,0},{3,1},{4,6},{5,7},{6,4},{7,5},{8,10},{9,11},{10,... | collective-permute-start | bytes 3538952 | tf_op jit(solution)/shard_map/ppermute | solution.py:50
  22.3 4.8 %collective-permute-start.2 = (f32[1,1537]{1,0:T(1,128)S(1)}, f32[1,1537]{1,0:T(1,128)S(1)}, u32[]{:S(2)}, u32[]{:S(2)}) collective-permute-start(f32[1,1537]{1,0:T(1,128)S(1)} %pad_maximum_fusion.5), channel_id=1, source_target_pairs={{0,8},{4,12},{8,16},{12,20},{16,24},{20,28},{1,9},{5,13},{9,17},{1... | collective-permute-start | bytes 18452 | tf_op jit(solution)/shard_map/ppermute | solution.py:16
  28.4 7.8 %collective-permute-start.3 = (f32[1,1537]{1,0:T(1,128)S(1)}, f32[1,1537]{1,0:T(1,128)S(1)}, u32[]{:S(2)}, u32[]{:S(2)}) collective-permute-start(f32[1,1537]{1,0:T(1,128)S(1)} %pad_maximum_fusion.6), channel_id=1, source_target_pairs={{0,16},{4,20},{8,24},{12,28},{1,17},{5,21},{9,25},{13,29},{2,18},{... | collective-permute-start | bytes 18452 | tf_op jit(solution)/shard_map/ppermute | solution.py:16
  36.2 10.4 %copy-start.5 = (bf16[384,1536]{1,0:T(8,128)(2,1)S(1)}, bf16[384,1536]{1,0:T(8,128)(2,1)}, u32[]{:S(2)}) copy-start(bf16[384,1536]{1,0:T(8,128)(2,1)} %param.15) | copy-start | bytes 3538948
  40.2 6.5 %collective-permute-start.4 = (f32[1,1537]{1,0:T(1,128)S(1)}, f32[1,1537]{1,0:T(1,128)S(1)}, u32[]{:S(2)}, u32[]{:S(2)}) collective-permute-start(f32[1,1537]{1,0:T(1,128)S(1)} %pad_maximum_fusion.7), channel_id=1, source_target_pairs={{4,0},{8,4},{12,8},{16,12},{20,16},{24,20},{28,24},{5,1},{9,5},{13... | collective-permute-start | bytes 18452 | tf_op jit(solution)/shard_map/ppermute | solution.py:16
  46.6 13.2 %collective-permute-start.9 = (bf16[384,1536]{1,0:T(8,128)(2,1)S(1)}, bf16[384,1536]{1,0:T(8,128)(2,1)S(1)}, u32[]{:S(2)}, u32[]{:S(2)}) collective-permute-start(bf16[384,1536]{1,0:T(8,128)(2,1)S(1)} %copy-done.5), channel_id=1, source_target_pairs={{0,1},{1,0},{2,3},{3,2},{4,5},{5,4},{6,7},{7,6},{8,9},{9,8},{10,11... | collective-permute-start | bytes 3538952 | tf_op jit(solution)/shard_map/ppermute | solution.py:53
  48.5 1.3 %copy-start.9 = (bf16[384,1536]{1,0:T(8,128)(2,1)S(1)}, bf16[384,1536]{1,0:T(8,128)(2,1)}, u32[]{:S(2)}) copy-start(bf16[384,1536]{1,0:T(8,128)(2,1)} %param.14) | copy-start | bytes 3538948
  50.5 13.8 %collective-permute-start.7 = (bf16[384,1536]{1,0:T(8,128)(2,1)S(1)}, bf16[384,1536]{1,0:T(8,128)(2,1)S(1)}, u32[]{:S(2)}, u32[]{:S(2)}) collective-permute-start(bf16[384,1536]{1,0:T(8,128)(2,1)S(1)} %collective-permute-done.5), channel_id=1, source_target_pairs={{0,1},{1,0},{2,3},{3,2},{4,5},{5,4},{6,7},{7,6},{8,9},{9,8},{10,11... | collective-permute-start | bytes 3538952 | tf_op jit(solution)/shard_map/ppermute | solution.py:53
  55.2 5.8 %collective-permute-start.10 = (bf16[384,1536]{1,0:T(8,128)(2,1)}, bf16[384,1536]{1,0:T(8,128)(2,1)S(1)}, u32[]{:S(2)}, u32[]{:S(2)}) collective-permute-start(bf16[384,1536]{1,0:T(8,128)(2,1)} %collective-permute-done.8), channel_id=1, source_target_pairs={{0,1},{1,0},{2,3},{3,2},{4,5},{5,4},{6,7},{7,6},{8,9},{9,8},{10,11... | collective-permute-start | bytes 3538952 | tf_op jit(solution)/shard_map/ppermute | solution.py:53
  59.9 1.1 %copy-start.11 = (bf16[384,1536]{1,0:T(8,128)(2,1)}, bf16[384,1536]{1,0:T(8,128)(2,1)S(1)}, u32[]{:S(2)}) copy-start(bf16[384,1536]{1,0:T(8,128)(2,1)S(1)} %collective-permute-done.9) | copy-start | bytes 3538948
  61.0 1.0 copy-start.13
  62.0 6.5 %copy-start = (f32[322,1536]{1,0:T(8,128)}, f32[322,1536]{1,0:T(8,128)S(1)}, u32[]{:S(2)}) copy-start(f32[322,1536]{1,0:T(8,128)S(1)} %convolution_add_fusion) | copy-start | bytes 5935108
  64.2 1.0 copy-start.7
  65.3 1.3 %copy-start.2 = (f32[322,1536]{1,0:T(8,128)}, f32[322,1536]{1,0:T(8,128)S(1)}, u32[]{:S(2)}) copy-start(f32[322,1536]{1,0:T(8,128)S(1)} %convolution_add_fusion.3) | copy-start | bytes 5935108
  68.5 2.1 %slice-start = ((f32[322,1536]{1,0:T(8,128)}), f32[319,1536]{1,0:T(8,128)S(1)}, s32[]{:S(2)}) async-start(f32[322,1536]{1,0:T(8,128)} %copy-done), calls=%async_computation | async-start | bytes 3932160 | tf_op jit(solution)/shard_map/slice | solution.py:157
  70.7 2.9 %copy-start.3 = (f32[322,1536]{1,0:T(8,128)S(1)}, f32[322,1536]{1,0:T(8,128)}, u32[]{:S(2)}) copy-start(f32[322,1536]{1,0:T(8,128)} %copy-done.2) | copy-start | bytes 5935108
  74.7 1.6 %copy-start.1 = (f32[322,1536]{1,0:T(8,128)S(1)}, f32[322,1536]{1,0:T(8,128)}, u32[]{:S(2)}) copy-start(f32[322,1536]{1,0:T(8,128)} %copy-done) | copy-start | bytes 5935108
  76.5 1.3 %copy-start.10 = (bf16[384,1536]{1,0:T(8,128)(2,1)S(1)}, bf16[384,1536]{1,0:T(8,128)(2,1)}, u32[]{:S(2)}) copy-start(bf16[384,1536]{1,0:T(8,128)(2,1)} %param.14) | copy-start | bytes 3538948
  76.9 1.6 %copy-start.4 = (bf16[1,320,1536]{2,1,0:T(8,128)(2,1)S(1)}, bf16[1,320,1536]{2,1,0:T(8,128)(2,1)}, u32[]{:S(2)}) copy-start(bf16[1,320,1536]{2,1,0:T(8,128)(2,1)} %param.9) | copy-start | bytes 2949124
  78.5 4.5 %copy-start.6 = (bf16[384,1536]{1,0:T(8,128)(2,1)S(1)}, bf16[384,1536]{1,0:T(8,128)(2,1)}, u32[]{:S(2)}) copy-start(bf16[384,1536]{1,0:T(8,128)(2,1)} %param.15) | copy-start | bytes 3538948
  80.3 3.4 %copy-start.14 = (bf16[384,1536]{1,0:T(8,128)(2,1)S(1)}, bf16[384,1536]{1,0:T(8,128)(2,1)}, u32[]{:S(2)}) copy-start(bf16[384,1536]{1,0:T(8,128)(2,1)} %copy-done.13) | copy-start | bytes 3538948
  81.5 9.8 %collective-permute-start.11 = (f32[1,1537]{1,0:T(1,128)S(1)}, f32[1,1537]{1,0:T(1,128)S(1)}, u32[]{:S(2)}, u32[]{:S(2)}) collective-permute-start(f32[1,1537]{1,0:T(1,128)S(1)} %pad_maximum_fusion.8), channel_id=1, source_target_pairs={{4,0},{8,4},{12,8},{16,12},{20,16},{24,20},{28,24},{5,1},{9,5},{13... | collective-permute-start | bytes 18452 | tf_op jit(solution)/shard_map/ppermute | solution.py:16
  83.7 1.3 %copy-start.12 = (bf16[384,1536]{1,0:T(8,128)(2,1)S(1)}, bf16[384,1536]{1,0:T(8,128)(2,1)}, u32[]{:S(2)}) copy-start(bf16[384,1536]{1,0:T(8,128)(2,1)} %copy-done.11) | copy-start | bytes 3538948
  85.7 2.1 %copy-start.8 = (bf16[384,1536]{1,0:T(8,128)(2,1)S(1)}, bf16[384,1536]{1,0:T(8,128)(2,1)}, u32[]{:S(2)}) copy-start(bf16[384,1536]{1,0:T(8,128)(2,1)} %copy-done.7) | copy-start | bytes 3538948
  93.1 7.3 %collective-permute-start.12 = (f32[1,1537]{1,0:T(1,128)S(1)}, f32[1,1537]{1,0:T(1,128)S(1)}, u32[]{:S(2)}, u32[]{:S(2)}) collective-permute-start(f32[1,1537]{1,0:T(1,128)S(1)} %pad_maximum_fusion.9), channel_id=1, source_target_pairs={{8,0},{12,4},{16,8},{20,12},{24,16},{28,20},{9,1},{13,5},{17,9},{2... | collective-permute-start | bytes 18452 | tf_op jit(solution)/shard_map/ppermute | solution.py:16
  101.7 6.4 %collective-permute-start.13 = (f32[1,1537]{1,0:T(1,128)S(1)}, f32[1,1537]{1,0:T(1,128)S(1)}, u32[]{:S(2)}, u32[]{:S(2)}) collective-permute-start(f32[1,1537]{1,0:T(1,128)S(1)} %pad_maximum_fusion.10), channel_id=1, source_target_pairs={{16,0},{20,4},{24,8},{28,12},{17,1},{21,5},{25,9},{29,13},{18,2},{... | collective-permute-start | bytes 18452 | tf_op jit(solution)/shard_map/ppermute | solution.py:16

commit v12 on v11

--- a/solution.py
+++ b/solution.py
@@ -137,7 +137,8 @@
     level = jnp.where(later_rows, 0.5, jnp.where(starts, 1.0, 0.0))
     rise = jnp.where(later_rows, jnp.where(starts, -0.5, 0.5), 0.0)
     grad_wide = grad_rows.astype(jnp.float32)
-    base_vector = jnp.dot((owner_keep * level)[None, :], grad_wide, precision=exact)
+    base_vector = jnp.sum(grad_wide * (owner_keep * level)[:, None], axis=0, keepdims=True)
+    rise_rows = lax.optimization_barrier(grad_wide * (owner_keep * rise)[:, None])
     to_prev = jnp.concatenate([token_rows[:1].astype(jnp.float32), cos_grad[:1][None]], axis=1)
     from_next = shifted(to_prev, "seq", -1)
     prev_row = shifted(token_rows[token_count - 1 :], "seq", 1)
@@ -164,9 +165,7 @@
     confidence = jnp.where(starts, boundary_prob, 1.0 - boundary_prob)
     weighted_grad = confidence[:, None] * grad_rows
     slot_grad = lax.dot_general(membership, weighted_grad, contract_first, precision=exact)
-    back_vector = base_vector + jnp.dot(
-        (owner_keep * rise * cosine)[None, :], grad_wide, precision=exact
-    )
+    back_vector = base_vector + jnp.sum(rise_rows * cosine[:, None], axis=0, keepdims=True)
     grad_in = seq_scan(last_log, back_vector, "seq", False)
     reach_end = jnp.exp(running[slot_count - 1] - running)
     state_grad = (

time: 111 us -> 110 us (level)
  no operation moved by 1% of the time
where the time goes in v12:
time: 110 us; the launch traced here: 109 us
  starting transfers between devices  25.3 us (23%)
  matrix products  23.8 us (22%)
  other arithmetic  19.4 us (18%)
  between operations  14.6 us (13%)
  waiting for transfers between devices  13.3 us (12%)
  local copies, waits for them, and re-layouts  13 us (12%)
    ppermute x8, starting transfers between devices, shifted(): return lax.ppermute(block, axis, route)  21.1 us
    ppermute x8, waiting for transfers between devices, shifted(): return lax.ppermute(block, axis, route)  9.05 us
    dot_general x8, matrix products, split_dot(): term = jnp.dot(part, block, preferred_element_type=jnp.float32)  8.06 us
    unnamed x30, local copies, waits for them, and re-layouts  5.65 us
    ppermute x2, waiting for transfers between devices, gather_blocks(): pairs.append(lax.ppermute(blocks, axis, route))  4.22 us
    dot_general x4, matrix products, per_device(): lax.dot_general(key_grad, k_block, contract_last, preferred_element_type=...  4.12 us
    dot_general x4, matrix products, per_device(): lax.dot_general(query_grad, q_block, contract_last, preferred_element_typ...  4.06 us
    ppermute x2, starting transfers between devices, gather_blocks(): pairs.append(lax.ppermute(blocks, axis, route))  3.6 us
  transfers between devices with their start and end apart: 14, of which 4 were waited for; matrix products, arithmetic and copies ran while one was open for 33% of the time, Pallas kernels for 0%

profile of v12, /device:TPU:0, one launch (start us, length us, event | category | flops | bytes accessed | tf_op | source)
XLA Modules:
  0.0 109.4 jit_solution(1063227259846215271)
XLA Ops:
  0.6 3.0 %collective-permute-start.5 = (bf16[384,1536]{1,0:T(8,128)(2,1)}, bf16[384,1536]{1,0:T(8,128)(2,1)S(1)}, u32[]{:S(2)}, u32[]{:S(2)}) collective-permute-start(bf16[384,1536]{1,0:T(8,128)(2,1)} %param.14), channel_id=1, source_target_pairs={{0,2},{1,3},{2,0},{3,1},{4,6},{5,7},{6,4},{7,5},{8,10},{9,11},{10,... | collective-permute-start | bytes 3538952 | tf_op jit(solution)/shard_map/ppermute | solution.py:50
  4.3 0.7 fusion.57
  5.3 0.5 slice.125
  5.8 0.7 bitcast_select_fusion
  6.6 1.9 %fusion.13 = f32[128,1536]{1,0:T(8,128)S(1)} fusion(bf16[1,128,1536]{2,1,0:T(8,128)(2,1)} %param.10, f32[128]{0:T(128)S(1)} %bitcast_select_fusion, f32[128]{0:T(128)S(1)} %reduce.2), kind=kOutput, calls=%fused_computation.48 | convolution fusion | flops 302448640 | bytes 1180672 | tf_op jit(solution)/shard_map/dot_general | solution.py:128
  8.5 0.7 pad_maximum_fusion.4
  9.1 3.4 %collective-permute-start.1 = (f32[1,1537]{1,0:T(1,128)S(1)}, f32[1,1537]{1,0:T(1,128)S(1)}, u32[]{:S(2)}, u32[]{:S(2)}) collective-permute-start(f32[1,1537]{1,0:T(1,128)S(1)} %pad_maximum_fusion.4), channel_id=1, source_target_pairs={{0,4},{4,8},{8,12},{12,16},{16,20},{20,24},{24,28},{1,5},{5,9},{9,... | collective-permute-start | bytes 18452 | tf_op jit(solution)/shard_map/ppermute | solution.py:16
  12.5 0.8 slice_bitcast_fusion
  13.3 3.5 %collective-permute-start = (bf16[1,1536]{1,0:T(2,128)(2,1)S(1)}, bf16[1,1536]{1,0:T(2,128)(2,1)S(1)}, u32[]{:S(2)}, u32[]{:S(2)}) collective-permute-start(bf16[1,1536]{1,0:T(2,128)(2,1)S(1)} %get-tuple-element.20), channel_id=1, source_target_pairs={{0,4},{4,8},{8,12},{12,16},{16,20},{20,24},{24,28},{1,5},{5,9},{9,... | collective-permute-start | bytes 9224 | tf_op jit(solution)/shard_map/ppermute | solution.py:16
  16.8 0.6 collective-permute-start.8
  17.3 0.8 fusion.31
  18.2 0.8 convert_reduce_fusion
  19.0 0.7 subtract_exponential_fusion
  22.3 3.5 %collective-permute-start.2 = (f32[1,1537]{1,0:T(1,128)S(1)}, f32[1,1537]{1,0:T(1,128)S(1)}, u32[]{:S(2)}, u32[]{:S(2)}) collective-permute-start(f32[1,1537]{1,0:T(1,128)S(1)} %pad_maximum_fusion.5), channel_id=1, source_target_pairs={{0,8},{4,12},{8,16},{12,20},{16,24},{20,28},{1,9},{5,13},{9,17},{1... | collective-permute-start | bytes 18452 | tf_op jit(solution)/shard_map/ppermute | solution.py:16
  26.0 1.2 %collective-permute-done.2 = f32[1,1537]{1,0:T(1,128)S(1)} collective-permute-done((f32[1,1537]{1,0:T(1,128)S(1)}, f32[1,1537]{1,0:T(1,128)S(1)}, u32[]{:S(2)}, u32[]{:S(2)}) %collective-permute-start.2) | collective-permute-done | bytes 6180 | tf_op jit(solution)/shard_map/ppermute | solution.py:16
  27.1 0.6 slice.128
  28.4 5.2 %collective-permute-start.3 = (f32[1,1537]{1,0:T(1,128)S(1)}, f32[1,1537]{1,0:T(1,128)S(1)}, u32[]{:S(2)}, u32[]{:S(2)}) collective-permute-start(f32[1,1537]{1,0:T(1,128)S(1)} %pad_maximum_fusion.6), channel_id=1, source_target_pairs={{0,16},{4,20},{8,24},{12,28},{1,17},{5,21},{9,25},{13,29},{2,18},{... | collective-permute-start | bytes 18452 | tf_op jit(solution)/shard_map/ppermute | solution.py:16
  33.6 0.6 fusion.60
  36.2 2.7 %fusion.6 = f32[320]{0:T(512)S(1)} fusion(bf16[1,320,1536]{2,1,0:T(8,128)(2,1)} %param.9, f32[1536]{0:T(1024)S(1)} %fusion.43, f32[320]{0:T(512)S(1)} %compare_convert_fusion, f32[128,1536]{1,0:T(8,128)S(1)} %fusion.13, f32[128]{0:T(128)S(1)} %get-tuple-element.29, s32[320]{0:T(512)S(1)} %get-tuple-element.25), kind=kOutput, calls=%fused_computation.33 | convolution fusion | flops 757866176 | bytes 1779968 | tf_op jit(solution)/shard_map/dot_general | solution.py:133
  39.0 0.5 slice.103
  39.5 0.7 pad_maximum_fusion.7
  40.2 1.5 %collective-permute-start.4 = (f32[1,1537]{1,0:T(1,128)S(1)}, f32[1,1537]{1,0:T(1,128)S(1)}, u32[]{:S(2)}, u32[]{:S(2)}) collective-permute-start(f32[1,1537]{1,0:T(1,128)S(1)} %pad_maximum_fusion.7), channel_id=1, source_target_pairs={{4,0},{8,4},{12,8},{16,12},{20,16},{24,20},{28,24},{5,1},{9,5},{13... | collective-permute-start | bytes 18452 | tf_op jit(solution)/shard_map/ppermute | solution.py:16
  44.2 2.4 %gather_fusion = f32[320]{0:T(512)S(1)} fusion(f32[128]{0:T(128)S(1)} %get-tuple-element.29, s32[1024]{0:T(1024)S(1)} %pad_clamp_fusion), kind=kCustom, calls=%fused_computation | custom fusion | bytes 3840 | tf_op jit(solution)/shard_map/gather | solution.py:136
  47.2 1.3 %pad_maximum_fusion.2 = bf16[322,1536]{1,0:T(8,128)(2,1)S(1)} fusion(bf16[1,1536]{1,0:T(2,128)(2,1)S(1)} %slice.185, bf16[1,1536]{1,0:T(2,128)(2,1)S(1)} %collective-permute-done, bf16[320,1536]{1,0:T(8,128)(2,1)} %bitcast.80), kind=kLoop, calls=%fused_computation.42 | loop fusion | flops 2967552 | bytes 1978368 | tf_op jit(solution)/shard_map/concatenate | solution.py:147
  48.5 0.7 fusion.26
  49.2 0.6 copy-done.8
  49.8 0.7 convolution_add_fusion.5
  50.5 0.6 collective-permute-start.7
  51.0 4.2 %collective-permute-done.8 = bf16[384,1536]{1,0:T(8,128)(2,1)} collective-permute-done((bf16[384,1536]{1,0:T(8,128)(2,1)}, bf16[384,1536]{1,0:T(8,128)(2,1)}, u32[]{:S(2)}, u32[]{:S(2)}) %collective-permute-start.8) | collective-permute-done | bytes 1179680 | tf_op jit(solution)/shard_map/ppermute | solution.py:50
  55.2 1.9 %fusion.24 = f32[322,1536]{1,0:T(8,128)S(1)} fusion(bf16[384,1536]{1,0:T(8,128)(2,1)} %collective-permute-done.8, bf16[322,1536]{1,0:T(8,128)(2,1)S(1)} %pad_maximum_fusion.2, s32[]{:T(128)S(6)} %select_n.142), kind=kOutput, calls=%fused_computation.59 | convolution fusion | flops 379846656 | bytes 3409924 | tf_op jit(solution)/shard_map/dot_general | solution.py:75
  57.2 0.7 convolution_add_fusion.2
  57.9 2.0 %convolution_add_fusion.4 = f32[322,1536]{1,0:T(8,128)S(1)} fusion(f32[322,1536]{1,0:T(8,128)S(1)} %convolution_add_fusion.5, bf16[384,1536]{1,0:T(8,128)(2,1)} %collective-permute-done.6, bf16[322,1536]{1,0:T(8,128)(2,1)S(1)} %pad_maximum_fusion.2, s32[]{:T(128)S(6)} %select_n.143), kind=kOutput, calls=%fused_computation.9 | convolution fusion | flops 380341248 | bytes 5425156 | tf_op jit(solution)/shard_map/dot_general | solution.py:75
  59.9 0.7 convolution_add_fusion.1
  61.0 0.7 convolution_add_fusion
  62.0 0.8 multiply_reduce_fusion.8
  62.8 1.5 %multiply_reduce_fusion.5 = (f32[320]{0:T(512)S(1)}, f32[320,1536]{1,0:T(8,128)}) fusion(f32[322,1536]{1,0:T(8,128)S(1)} %convolution_add_fusion), kind=kLoop, calls=%fused_computation.31 | loop fusion | flops 982720 | bytes 3933440 | tf_op jit(solution)/shard_map/reduce_sum | solution.py:87
  64.2 0.7 convolution_add_fusion.3
  65.3 1.3 %copy-done.2 = f32[322,1536]{1,0:T(8,128)} copy-done((f32[322,1536]{1,0:T(8,128)}, f32[322,1536]{1,0:T(8,128)S(1)}, u32[]{:S(2)}) %copy-start.2) | copy-done | bytes 1978392
  66.5 0.6 multiply_reduce_fusion.7
  68.5 1.9 %slice_multiply_fusion.1 = f32[319,1536]{1,0:T(8,128)S(1)} fusion(f32[320,1536]{1,0:T(8,128)} %get-tuple-element.13, f32[319]{0:T(512)S(1)} %bitcast.81), kind=kLoop, calls=%fused_computation.20 | loop fusion | flops 489984 | bytes 3921148 | tf_op jit(solution)/shard_map/mul | solution.py:88
  70.7 2.7 %multiply_reduce_fusion.2 = (f32[320]{0:T(512)S(1)}, f32[320]{0:T(512)S(1)}, f32[320]{0:T(512)S(1)}, f32[320]{0:T(512)S(1)}) fusion(f32[319,1536]{1,0:T(8,128)S(1)} %slice-done, f32[1,1536]{1,0:T(1,128)S(1)} %get-tuple-element.11, f32[322,1536]{1,0:T(8,128)} %copy-done.2, f32[319,1536]{1,0:T(8,128)S(1)} %slice_multiply_fusion.1, ...), kind=kLoop, calls=%fused_computation.26 | loop fusion | flops 5405440 | bytes 5904640 | tf_op jit(solution)/shard_map/reduce_sum | solution.py:162
  73.5 0.6 multiply_multiply_fusion
  74.1 0.9 convert_multiply_fusion
  75.3 1.2 %copy-done.1 = f32[322,1536]{1,0:T(8,128)S(1)} copy-done((f32[322,1536]{1,0:T(8,128)S(1)}, f32[322,1536]{1,0:T(8,128)}, u32[]{:S(2)}) %copy-start.1) | copy-done | bytes 1978392
  77.1 1.0 copy-done.9
  78.1 0.7 fusion.61
  78.8 1.2 %fusion.3 = f32[128,1536]{1,0:T(8,128)S(1)} fusion(bf16[1,320,1536]{2,1,0:T(8,128)(2,1)S(1)} %copy-done.14, f32[320]{0:T(512)S(1)} %get-tuple-element.32, s32[320]{0:T(512)S(1)} %get-tuple-element.25), kind=kOutput, calls=%fused_computation.16 | convolution fusion | flops 755998720 | bytes 1772032 | tf_op jit(solution)/shard_map/dot_general | solution.py:167
  80.3 0.7 pad_maximum_fusion.8
  81.0 1.5 %collective-permute-start.11 = (f32[1,1537]{1,0:T(1,128)S(1)}, f32[1,1537]{1,0:T(1,128)S(1)}, u32[]{:S(2)}, u32[]{:S(2)}) collective-permute-start(f32[1,1537]{1,0:T(1,128)S(1)} %pad_maximum_fusion.8), channel_id=1, source_target_pairs={{4,0},{8,4},{12,8},{16,12},{20,16},{24,20},{28,24},{5,1},{9,5},{13... | collective-permute-start | bytes 18452 | tf_op jit(solution)/shard_map/ppermute | solution.py:16
  82.5 0.7 fusion.7
  83.3 0.7 fusion.64
  84.0 0.6 copy-done.11
  84.5 0.7 fusion.63
  85.2 2.1 %fusion.62 = f32[320,384]{1,0:T(8,128)S(1)} fusion(bf16[320,1536]{1,0:T(8,128)(2,1)S(1)} %subtract_convert_fusion, bf16[384,1536]{1,0:T(8,128)(2,1)} %collective-permute-done.8), kind=kOutput, calls=%fused_computation.150 | convolution fusion | flops 377487360 | bytes 2654208 | tf_op jit(solution)/shard_map/dot_general | solution.py:184
  87.3 0.7 fusion.10
  88.0 2.0 %fusion.9 = bf16[320,384]{1,0:T(8,128)(2,1)S(1)} fusion(f32[320,384]{1,0:T(8,128)S(1)} %fusion.63, bf16[320,1536]{1,0:T(8,128)(2,1)S(1)} %get-tuple-element.39, bf16[384,1536]{1,0:T(8,128)(2,1)} %collective-permute-done.6), kind=kOutput, calls=%fused_computation.40 | convolution fusion | flops 377733120 | bytes 2899968 | tf_op jit(solution)/shard_map/dot_general | solution.py:183
  90.0 0.7 fusion.8
  92.6 1.3 %collective-permute-start.12 = (f32[1,1537]{1,0:T(1,128)S(1)}, f32[1,1537]{1,0:T(1,128)S(1)}, u32[]{:S(2)}, u32[]{:S(2)}) collective-permute-start(f32[1,1537]{1,0:T(1,128)S(1)} %pad_maximum_fusion.9), channel_id=1, source_target_pairs={{8,0},{12,4},{16,8},{20,12},{24,16},{28,20},{9,1},{13,5},{17,9},{2... | collective-permute-start | bytes 18452 | tf_op jit(solution)/shard_map/ppermute | solution.py:16
  94.1 5.8 %collective-permute-done.12 = f32[1,1537]{1,0:T(1,128)S(1)} collective-permute-done((f32[1,1537]{1,0:T(1,128)S(1)}, f32[1,1537]{1,0:T(1,128)S(1)}, u32[]{:S(2)}, u32[]{:S(2)}) %collective-permute-start.12) | collective-permute-done | bytes 6180 | tf_op jit(solution)/shard_map/ppermute | solution.py:16
  99.9 0.6 slice.145
  101.3 1.3 %collective-permute-start.13 = (f32[1,1537]{1,0:T(1,128)S(1)}, f32[1,1537]{1,0:T(1,128)S(1)}, u32[]{:S(2)}, u32[]{:S(2)}) collective-permute-start(f32[1,1537]{1,0:T(1,128)S(1)} %pad_maximum_fusion.10), channel_id=1, source_target_pairs={{16,0},{20,4},{24,8},{28,12},{17,1},{21,5},{25,9},{29,13},{18,2},{... | collective-permute-start | bytes 18452 | tf_op jit(solution)/shard_map/ppermute | solution.py:16
  102.6 1.0 maximum_bitcast_fusion
  105.6 2.0 %collective-permute-done.13 = f32[1,1537]{1,0:T(1,128)S(1)} collective-permute-done((f32[1,1537]{1,0:T(1,128)S(1)}, f32[1,1537]{1,0:T(1,128)S(1)}, u32[]{:S(2)}, u32[]{:S(2)}) %collective-permute-start.13) | collective-permute-done | bytes 6180 | tf_op jit(solution)/shard_map/ppermute | solution.py:16
  107.7 1.7 %fusion.2 = bf16[1,128,1536]{2,1,0:T(8,128)(2,1)} fusion(f32[128,1536]{1,0:T(8,128)S(1)} %fusion.3, f32[1536]{0:T(1024)S(1)} %fusion.44, f32[128]{0:T(128)S(1)} %get-tuple-element.28, f32[128]{0:T(128)S(1)} %bitcast_select_fusion, f32[128]{0:T(128)S(1)} %reduce.2), kind=kOutput, calls=%fused_computation.15 | convolution fusion | flops 302841856 | bytes 1187328 | tf_op jit(solution)/shard_map/dot_general | solution.py:172
  (79 shorter events, 5.2 us)
Async XLA Ops:
  0.6 47.9 %collective-permute-start.5 = (bf16[384,1536]{1,0:T(8,128)(2,1)}, bf16[384,1536]{1,0:T(8,128)(2,1)S(1)}, u32[]{:S(2)}, u32[]{:S(2)}) collective-permute-start(bf16[384,1536]{1,0:T(8,128)(2,1)} %param.14), channel_id=1, source_target_pairs={{0,2},{1,3},{2,0},{3,1},{4,6},{5,7},{6,4},{7,5},{8,10},{9,11},{10,... | collective-permute-start | bytes 3538952 | tf_op jit(solution)/shard_map/ppermute | solution.py:50
  3.7 54.2 %collective-permute-start.6 = (bf16[384,1536]{1,0:T(8,128)(2,1)}, bf16[384,1536]{1,0:T(8,128)(2,1)}, u32[]{:S(2)}, u32[]{:S(2)}) collective-permute-start(bf16[384,1536]{1,0:T(8,128)(2,1)} %param.14), channel_id=1, source_target_pairs={{0,1},{1,0},{2,3},{3,2},{4,5},{5,4},{6,7},{7,6},{8,9},{9,8},{10,11... | collective-permute-start | bytes 3538952 | tf_op jit(solution)/shard_map/ppermute | solution.py:53
  9.1 11.3 %collective-permute-start.1 = (f32[1,1537]{1,0:T(1,128)S(1)}, f32[1,1537]{1,0:T(1,128)S(1)}, u32[]{:S(2)}, u32[]{:S(2)}) collective-permute-start(f32[1,1537]{1,0:T(1,128)S(1)} %pad_maximum_fusion.4), channel_id=1, source_target_pairs={{0,4},{4,8},{8,12},{12,16},{16,20},{20,24},{24,28},{1,5},{5,9},{9,... | collective-permute-start | bytes 18452 | tf_op jit(solution)/shard_map/ppermute | solution.py:16
  13.3 33.9 %collective-permute-start = (bf16[1,1536]{1,0:T(2,128)(2,1)S(1)}, bf16[1,1536]{1,0:T(2,128)(2,1)S(1)}, u32[]{:S(2)}, u32[]{:S(2)}) collective-permute-start(bf16[1,1536]{1,0:T(2,128)(2,1)S(1)} %get-tuple-element.20), channel_id=1, source_target_pairs={{0,4},{4,8},{8,12},{12,16},{16,20},{20,24},{24,28},{1,5},{5,9},{9,... | collective-permute-start | bytes 9224 | tf_op jit(solution)/shard_map/ppermute | solution.py:16
  16.8 38.5 %collective-permute-start.8 = (bf16[384,1536]{1,0:T(8,128)(2,1)}, bf16[384,1536]{1,0:T(8,128)(2,1)}, u32[]{:S(2)}, u32[]{:S(2)}) collective-permute-start(bf16[384,1536]{1,0:T(8,128)(2,1)} %param.15), channel_id=1, source_target_pairs={{0,2},{1,3},{2,0},{3,1},{4,6},{5,7},{6,4},{7,5},{8,10},{9,11},{10,... | collective-permute-start | bytes 3538952 | tf_op jit(solution)/shard_map/ppermute | solution.py:50
  22.3 4.8 %collective-permute-start.2 = (f32[1,1537]{1,0:T(1,128)S(1)}, f32[1,1537]{1,0:T(1,128)S(1)}, u32[]{:S(2)}, u32[]{:S(2)}) collective-permute-start(f32[1,1537]{1,0:T(1,128)S(1)} %pad_maximum_fusion.5), channel_id=1, source_target_pairs={{0,8},{4,12},{8,16},{12,20},{16,24},{20,28},{1,9},{5,13},{9,17},{1... | collective-permute-start | bytes 18452 | tf_op jit(solution)/shard_map/ppermute | solution.py:16
  28.4 7.8 %collective-permute-start.3 = (f32[1,1537]{1,0:T(1,128)S(1)}, f32[1,1537]{1,0:T(1,128)S(1)}, u32[]{:S(2)}, u32[]{:S(2)}) collective-permute-start(f32[1,1537]{1,0:T(1,128)S(1)} %pad_maximum_fusion.6), channel_id=1, source_target_pairs={{0,16},{4,20},{8,24},{12,28},{1,17},{5,21},{9,25},{13,29},{2,18},{... | collective-permute-start | bytes 18452 | tf_op jit(solution)/shard_map/ppermute | solution.py:16
  36.2 10.4 %copy-start.4 = (bf16[384,1536]{1,0:T(8,128)(2,1)S(1)}, bf16[384,1536]{1,0:T(8,128)(2,1)}, u32[]{:S(2)}) copy-start(bf16[384,1536]{1,0:T(8,128)(2,1)} %param.15) | copy-start | bytes 3538948
  40.2 6.5 %collective-permute-start.4 = (f32[1,1537]{1,0:T(1,128)S(1)}, f32[1,1537]{1,0:T(1,128)S(1)}, u32[]{:S(2)}, u32[]{:S(2)}) collective-permute-start(f32[1,1537]{1,0:T(1,128)S(1)} %pad_maximum_fusion.7), channel_id=1, source_target_pairs={{4,0},{8,4},{12,8},{16,12},{20,16},{24,20},{28,24},{5,1},{9,5},{13... | collective-permute-start | bytes 18452 | tf_op jit(solution)/shard_map/ppermute | solution.py:16
  46.6 13.2 %collective-permute-start.9 = (bf16[384,1536]{1,0:T(8,128)(2,1)S(1)}, bf16[384,1536]{1,0:T(8,128)(2,1)S(1)}, u32[]{:S(2)}, u32[]{:S(2)}) collective-permute-start(bf16[384,1536]{1,0:T(8,128)(2,1)S(1)} %copy-done.4), channel_id=1, source_target_pairs={{0,1},{1,0},{2,3},{3,2},{4,5},{5,4},{6,7},{7,6},{8,9},{9,8},{10,11... | collective-permute-start | bytes 3538952 | tf_op jit(solution)/shard_map/ppermute | solution.py:53
  48.5 1.3 %copy-start.8 = (bf16[384,1536]{1,0:T(8,128)(2,1)S(1)}, bf16[384,1536]{1,0:T(8,128)(2,1)}, u32[]{:S(2)}) copy-start(bf16[384,1536]{1,0:T(8,128)(2,1)} %param.14) | copy-start | bytes 3538948
  50.5 13.8 %collective-permute-start.7 = (bf16[384,1536]{1,0:T(8,128)(2,1)S(1)}, bf16[384,1536]{1,0:T(8,128)(2,1)S(1)}, u32[]{:S(2)}, u32[]{:S(2)}) collective-permute-start(bf16[384,1536]{1,0:T(8,128)(2,1)S(1)} %collective-permute-done.5), channel_id=1, source_target_pairs={{0,1},{1,0},{2,3},{3,2},{4,5},{5,4},{6,7},{7,6},{8,9},{9,8},{10,11... | collective-permute-start | bytes 3538952 | tf_op jit(solution)/shard_map/ppermute | solution.py:53
  55.2 5.8 %collective-permute-start.10 = (bf16[384,1536]{1,0:T(8,128)(2,1)}, bf16[384,1536]{1,0:T(8,128)(2,1)S(1)}, u32[]{:S(2)}, u32[]{:S(2)}) collective-permute-start(bf16[384,1536]{1,0:T(8,128)(2,1)} %collective-permute-done.8), channel_id=1, source_target_pairs={{0,1},{1,0},{2,3},{3,2},{4,5},{5,4},{6,7},{7,6},{8,9},{9,8},{10,11... | collective-permute-start | bytes 3538952 | tf_op jit(solution)/shard_map/ppermute | solution.py:53
  59.9 1.1 %copy-start.10 = (bf16[384,1536]{1,0:T(8,128)(2,1)}, bf16[384,1536]{1,0:T(8,128)(2,1)S(1)}, u32[]{:S(2)}) copy-start(bf16[384,1536]{1,0:T(8,128)(2,1)S(1)} %collective-permute-done.9) | copy-start | bytes 3538948
  61.0 1.0 copy-start.12
  62.0 6.5 %copy-start = (f32[322,1536]{1,0:T(8,128)}, f32[322,1536]{1,0:T(8,128)S(1)}, u32[]{:S(2)}) copy-start(f32[322,1536]{1,0:T(8,128)S(1)} %convolution_add_fusion) | copy-start | bytes 5935108
  64.2 1.0 copy-start.6
  65.3 1.3 %copy-start.2 = (f32[322,1536]{1,0:T(8,128)}, f32[322,1536]{1,0:T(8,128)S(1)}, u32[]{:S(2)}) copy-start(f32[322,1536]{1,0:T(8,128)S(1)} %convolution_add_fusion.3) | copy-start | bytes 5935108
  68.5 2.1 %slice-start = ((f32[322,1536]{1,0:T(8,128)}), f32[319,1536]{1,0:T(8,128)S(1)}, s32[]{:S(2)}) async-start(f32[322,1536]{1,0:T(8,128)} %copy-done), calls=%async_computation | async-start | bytes 3932160 | tf_op jit(solution)/shard_map/slice | solution.py:158
  70.7 2.8 %copy-start.3 = (f32[322,1536]{1,0:T(8,128)S(1)}, f32[322,1536]{1,0:T(8,128)}, u32[]{:S(2)}) copy-start(f32[322,1536]{1,0:T(8,128)} %copy-done.2) | copy-start | bytes 5935108
  70.7 3.4 %copy-start.14 = (bf16[1,320,1536]{2,1,0:T(8,128)(2,1)S(1)}, bf16[1,320,1536]{2,1,0:T(8,128)(2,1)}, u32[]{:S(2)}) copy-start(bf16[1,320,1536]{2,1,0:T(8,128)(2,1)} %param.9) | copy-start | bytes 2949124
  74.9 1.6 %copy-start.1 = (f32[322,1536]{1,0:T(8,128)S(1)}, f32[322,1536]{1,0:T(8,128)}, u32[]{:S(2)}) copy-start(f32[322,1536]{1,0:T(8,128)} %copy-done) | copy-start | bytes 5935108
  76.8 1.3 %copy-start.9 = (bf16[384,1536]{1,0:T(8,128)(2,1)S(1)}, bf16[384,1536]{1,0:T(8,128)(2,1)}, u32[]{:S(2)}) copy-start(bf16[384,1536]{1,0:T(8,128)(2,1)} %param.14) | copy-start | bytes 3538948
  78.8 3.8 %copy-start.5 = (bf16[384,1536]{1,0:T(8,128)(2,1)S(1)}, bf16[384,1536]{1,0:T(8,128)(2,1)}, u32[]{:S(2)}) copy-start(bf16[384,1536]{1,0:T(8,128)(2,1)} %param.15) | copy-start | bytes 3538948
  80.2 3.0 %copy-start.13 = (bf16[384,1536]{1,0:T(8,128)(2,1)S(1)}, bf16[384,1536]{1,0:T(8,128)(2,1)}, u32[]{:S(2)}) copy-start(bf16[384,1536]{1,0:T(8,128)(2,1)} %copy-done.12) | copy-start | bytes 3538948
  81.0 9.8 %collective-permute-start.11 = (f32[1,1537]{1,0:T(1,128)S(1)}, f32[1,1537]{1,0:T(1,128)S(1)}, u32[]{:S(2)}, u32[]{:S(2)}) collective-permute-start(f32[1,1537]{1,0:T(1,128)S(1)} %pad_maximum_fusion.8), channel_id=1, source_target_pairs={{4,0},{8,4},{12,8},{16,12},{20,16},{24,20},{28,24},{5,1},{9,5},{13... | collective-permute-start | bytes 18452 | tf_op jit(solution)/shard_map/ppermute | solution.py:16
  83.3 1.3 %copy-start.11 = (bf16[384,1536]{1,0:T(8,128)(2,1)S(1)}, bf16[384,1536]{1,0:T(8,128)(2,1)}, u32[]{:S(2)}) copy-start(bf16[384,1536]{1,0:T(8,128)(2,1)} %copy-done.10) | copy-start | bytes 3538948
  85.2 2.1 %copy-start.7 = (bf16[384,1536]{1,0:T(8,128)(2,1)S(1)}, bf16[384,1536]{1,0:T(8,128)(2,1)}, u32[]{:S(2)}) copy-start(bf16[384,1536]{1,0:T(8,128)(2,1)} %copy-done.6) | copy-start | bytes 3538948
  92.6 7.3 %collective-permute-start.12 = (f32[1,1537]{1,0:T(1,128)S(1)}, f32[1,1537]{1,0:T(1,128)S(1)}, u32[]{:S(2)}, u32[]{:S(2)}) collective-permute-start(f32[1,1537]{1,0:T(1,128)S(1)} %pad_maximum_fusion.9), channel_id=1, source_target_pairs={{8,0},{12,4},{16,8},{20,12},{24,16},{28,20},{9,1},{13,5},{17,9},{2... | collective-permute-start | bytes 18452 | tf_op jit(solution)/shard_map/ppermute | solution.py:16
  101.3 6.4 %collective-permute-start.13 = (f32[1,1537]{1,0:T(1,128)S(1)}, f32[1,1537]{1,0:T(1,128)S(1)}, u32[]{:S(2)}, u32[]{:S(2)}) collective-permute-start(f32[1,1537]{1,0:T(1,128)S(1)} %pad_maximum_fusion.10), channel_id=1, source_target_pairs={{16,0},{20,4},{24,8},{28,12},{17,1},{21,5},{25,9},{29,13},{18,2},{... | collective-permute-start | bytes 18452 | tf_op jit(solution)/shard_map/ppermute | solution.py:16

commit v13 on v12

--- a/solution.py
+++ b/solution.py
@@ -165,7 +165,7 @@
     confidence = jnp.where(starts, boundary_prob, 1.0 - boundary_prob)
     weighted_grad = confidence[:, None] * grad_rows
     slot_grad = lax.dot_general(membership, weighted_grad, contract_first, precision=exact)
-    back_vector = base_vector + jnp.sum(rise_rows * cosine[:, None], axis=0, keepdims=True)
+    back_vector = base_vector + jnp.dot(cosine[None, :], rise_rows, precision=exact)
     grad_in = seq_scan(last_log, back_vector, "seq", False)
     reach_end = jnp.exp(running[slot_count - 1] - running)
     state_grad = (

time: 110 us -> 111 us (level)
  no operation moved by 1% of the time
where the time goes in v13:
time: 111 us; the launch traced here: 110 us
  starting transfers between devices  25.3 us (23%)
  matrix products  24.8 us (22%)
  other arithmetic  19.2 us (17%)
  between operations  14.6 us (13%)
  waiting for transfers between devices  13.3 us (12%)
  local copies, waits for them, and re-layouts  13 us (12%)
    ppermute x8, starting transfers between devices, shifted(): return lax.ppermute(block, axis, route)  21.1 us
    ppermute x8, waiting for transfers between devices, shifted(): return lax.ppermute(block, axis, route)  9.05 us
    dot_general x8, matrix products, split_dot(): term = jnp.dot(part, block, preferred_element_type=jnp.float32)  8.06 us
    unnamed x30, local copies, waits for them, and re-layouts  5.65 us
    ppermute x2, waiting for transfers between devices, gather_blocks(): pairs.append(lax.ppermute(blocks, axis, route))  4.22 us
    dot_general x4, matrix products, per_device(): lax.dot_general(key_grad, k_block, contract_last, preferred_element_type=...  4.11 us
    dot_general x4, matrix products, per_device(): lax.dot_general(query_grad, q_block, contract_last, preferred_element_typ...  4.06 us
    ppermute x2, starting transfers between devices, gather_blocks(): pairs.append(lax.ppermute(blocks, axis, route))  3.6 us
  transfers between devices with their start and end apart: 14, of which 4 were waited for; matrix products, arithmetic and copies ran while one was open for 33% of the time, Pallas kernels for 0%

profile of v13, /device:TPU:0, one launch (start us, length us, event | category | flops | bytes accessed | tf_op | source)
XLA Modules:
  0.0 110.2 jit_solution(3430185293566567686)
XLA Ops:
  0.6 3.0 %collective-permute-start.5 = (bf16[384,1536]{1,0:T(8,128)(2,1)}, bf16[384,1536]{1,0:T(8,128)(2,1)S(1)}, u32[]{:S(2)}, u32[]{:S(2)}) collective-permute-start(bf16[384,1536]{1,0:T(8,128)(2,1)} %param.14), channel_id=1, source_target_pairs={{0,2},{1,3},{2,0},{3,1},{4,6},{5,7},{6,4},{7,5},{8,10},{9,11},{10,... | collective-permute-start | bytes 3538952 | tf_op jit(solution)/shard_map/ppermute | solution.py:50
  4.3 0.7 fusion.57
  5.3 0.5 slice.125
  5.8 0.7 bitcast_select_fusion
  6.6 1.9 %fusion.13 = f32[128,1536]{1,0:T(8,128)S(1)} fusion(bf16[1,128,1536]{2,1,0:T(8,128)(2,1)} %param.10, f32[128]{0:T(128)S(1)} %bitcast_select_fusion, f32[128]{0:T(128)S(1)} %reduce.2), kind=kOutput, calls=%fused_computation.48 | convolution fusion | flops 302448640 | bytes 1180672 | tf_op jit(solution)/shard_map/dot_general | solution.py:128
  8.5 0.7 pad_maximum_fusion.4
  9.1 3.4 %collective-permute-start.1 = (f32[1,1537]{1,0:T(1,128)S(1)}, f32[1,1537]{1,0:T(1,128)S(1)}, u32[]{:S(2)}, u32[]{:S(2)}) collective-permute-start(f32[1,1537]{1,0:T(1,128)S(1)} %pad_maximum_fusion.4), channel_id=1, source_target_pairs={{0,4},{4,8},{8,12},{12,16},{16,20},{20,24},{24,28},{1,5},{5,9},{9,... | collective-permute-start | bytes 18452 | tf_op jit(solution)/shard_map/ppermute | solution.py:16
  12.5 0.8 slice_bitcast_fusion
  13.3 3.5 %collective-permute-start = (bf16[1,1536]{1,0:T(2,128)(2,1)S(1)}, bf16[1,1536]{1,0:T(2,128)(2,1)S(1)}, u32[]{:S(2)}, u32[]{:S(2)}) collective-permute-start(bf16[1,1536]{1,0:T(2,128)(2,1)S(1)} %get-tuple-element.20), channel_id=1, source_target_pairs={{0,4},{4,8},{8,12},{12,16},{16,20},{20,24},{24,28},{1,5},{5,9},{9,... | collective-permute-start | bytes 9224 | tf_op jit(solution)/shard_map/ppermute | solution.py:16
  16.8 0.6 collective-permute-start.8
  17.3 0.8 fusion.31
  18.2 0.8 convert_reduce_fusion
  19.0 0.7 subtract_exponential_fusion
  22.3 3.5 %collective-permute-start.2 = (f32[1,1537]{1,0:T(1,128)S(1)}, f32[1,1537]{1,0:T(1,128)S(1)}, u32[]{:S(2)}, u32[]{:S(2)}) collective-permute-start(f32[1,1537]{1,0:T(1,128)S(1)} %pad_maximum_fusion.5), channel_id=1, source_target_pairs={{0,8},{4,12},{8,16},{12,20},{16,24},{20,28},{1,9},{5,13},{9,17},{1... | collective-permute-start | bytes 18452 | tf_op jit(solution)/shard_map/ppermute | solution.py:16
  26.0 1.2 %collective-permute-done.2 = f32[1,1537]{1,0:T(1,128)S(1)} collective-permute-done((f32[1,1537]{1,0:T(1,128)S(1)}, f32[1,1537]{1,0:T(1,128)S(1)}, u32[]{:S(2)}, u32[]{:S(2)}) %collective-permute-start.2) | collective-permute-done | bytes 6180 | tf_op jit(solution)/shard_map/ppermute | solution.py:16
  27.1 0.6 slice.128
  28.4 5.2 %collective-permute-start.3 = (f32[1,1537]{1,0:T(1,128)S(1)}, f32[1,1537]{1,0:T(1,128)S(1)}, u32[]{:S(2)}, u32[]{:S(2)}) collective-permute-start(f32[1,1537]{1,0:T(1,128)S(1)} %pad_maximum_fusion.6), channel_id=1, source_target_pairs={{0,16},{4,20},{8,24},{12,28},{1,17},{5,21},{9,25},{13,29},{2,18},{... | collective-permute-start | bytes 18452 | tf_op jit(solution)/shard_map/ppermute | solution.py:16
  33.6 0.6 fusion.60
  36.2 2.7 %fusion.6 = f32[320]{0:T(512)S(1)} fusion(bf16[1,320,1536]{2,1,0:T(8,128)(2,1)} %param.9, f32[1536]{0:T(1024)S(1)} %fusion.43, f32[320]{0:T(512)S(1)} %compare_convert_fusion, f32[128,1536]{1,0:T(8,128)S(1)} %fusion.13, f32[128]{0:T(128)S(1)} %get-tuple-element.29, s32[320]{0:T(512)S(1)} %get-tuple-element.25), kind=kOutput, calls=%fused_computation.32 | convolution fusion | flops 757866176 | bytes 1779968 | tf_op jit(solution)/shard_map/dot_general | solution.py:133
  39.5 0.7 pad_maximum_fusion.7
  40.2 1.5 %collective-permute-start.4 = (f32[1,1537]{1,0:T(1,128)S(1)}, f32[1,1537]{1,0:T(1,128)S(1)}, u32[]{:S(2)}, u32[]{:S(2)}) collective-permute-start(f32[1,1537]{1,0:T(1,128)S(1)} %pad_maximum_fusion.7), channel_id=1, source_target_pairs={{4,0},{8,4},{12,8},{16,12},{20,16},{24,20},{28,24},{5,1},{9,5},{13... | collective-permute-start | bytes 18452 | tf_op jit(solution)/shard_map/ppermute | solution.py:16
  44.2 2.4 %gather_fusion = f32[320]{0:T(512)S(1)} fusion(f32[128]{0:T(128)S(1)} %get-tuple-element.29, s32[1024]{0:T(1024)S(1)} %pad_clamp_fusion), kind=kCustom, calls=%fused_computation | custom fusion | bytes 3840 | tf_op jit(solution)/shard_map/gather | solution.py:136
  47.2 1.3 %pad_maximum_fusion.2 = bf16[322,1536]{1,0:T(8,128)(2,1)S(1)} fusion(bf16[1,1536]{1,0:T(2,128)(2,1)S(1)} %slice.185, bf16[1,1536]{1,0:T(2,128)(2,1)S(1)} %collective-permute-done, bf16[320,1536]{1,0:T(8,128)(2,1)} %bitcast.82), kind=kLoop, calls=%fused_computation.42 | loop fusion | flops 2967552 | bytes 1978368 | tf_op jit(solution)/shard_map/concatenate | solution.py:147
  48.5 0.7 fusion.26
  49.2 0.6 copy-done.8
  49.8 0.7 convolution_add_fusion.5
  50.5 0.6 collective-permute-start.7
  51.0 4.2 %collective-permute-done.8 = bf16[384,1536]{1,0:T(8,128)(2,1)} collective-permute-done((bf16[384,1536]{1,0:T(8,128)(2,1)}, bf16[384,1536]{1,0:T(8,128)(2,1)}, u32[]{:S(2)}, u32[]{:S(2)}) %collective-permute-start.8) | collective-permute-done | bytes 1179680 | tf_op jit(solution)/shard_map/ppermute | solution.py:50
  55.2 1.9 %fusion.24 = f32[322,1536]{1,0:T(8,128)S(1)} fusion(bf16[384,1536]{1,0:T(8,128)(2,1)} %collective-permute-done.8, bf16[322,1536]{1,0:T(8,128)(2,1)S(1)} %pad_maximum_fusion.2, s32[]{:T(128)S(6)} %select_n.142), kind=kOutput, calls=%fused_computation.59 | convolution fusion | flops 379846656 | bytes 3409924 | tf_op jit(solution)/shard_map/dot_general | solution.py:75
  57.2 0.7 convolution_add_fusion.2
  57.9 2.0 %convolution_add_fusion.4 = f32[322,1536]{1,0:T(8,128)S(1)} fusion(f32[322,1536]{1,0:T(8,128)S(1)} %convolution_add_fusion.5, bf16[384,1536]{1,0:T(8,128)(2,1)} %collective-permute-done.6, bf16[322,1536]{1,0:T(8,128)(2,1)S(1)} %pad_maximum_fusion.2, s32[]{:T(128)S(6)} %select_n.143), kind=kOutput, calls=%fused_computation.9 | convolution fusion | flops 380341248 | bytes 5425156 | tf_op jit(solution)/shard_map/dot_general | solution.py:75
  59.9 0.7 convolution_add_fusion.1
  61.0 0.7 convolution_add_fusion
  62.0 0.8 multiply_reduce_fusion.7
  62.8 1.5 %multiply_reduce_fusion.4 = (f32[320]{0:T(512)S(1)}, f32[320,1536]{1,0:T(8,128)}) fusion(f32[322,1536]{1,0:T(8,128)S(1)} %convolution_add_fusion), kind=kLoop, calls=%fused_computation.30 | loop fusion | flops 982720 | bytes 3933440 | tf_op jit(solution)/shard_map/reduce_sum | solution.py:87
  64.2 0.7 convolution_add_fusion.3
  65.3 1.3 %copy-done.2 = f32[322,1536]{1,0:T(8,128)} copy-done((f32[322,1536]{1,0:T(8,128)}, f32[322,1536]{1,0:T(8,128)S(1)}, u32[]{:S(2)}) %copy-start.2) | copy-done | bytes 1978392
  66.5 0.6 multiply_reduce_fusion.6
  68.5 1.9 %slice_multiply_fusion.1 = f32[319,1536]{1,0:T(8,128)S(1)} fusion(f32[320,1536]{1,0:T(8,128)} %get-tuple-element.13, f32[319]{0:T(512)S(1)} %bitcast.83), kind=kLoop, calls=%fused_computation.20 | loop fusion | flops 489984 | bytes 3921148 | tf_op jit(solution)/shard_map/mul | solution.py:88
  70.7 2.7 %multiply_reduce_fusion.1 = (f32[320]{0:T(512)S(1)}, f32[320]{0:T(512)S(1)}, f32[320]{0:T(512)S(1)}, f32[320]{0:T(512)S(1)}) fusion(f32[319,1536]{1,0:T(8,128)S(1)} %slice-done, f32[1,1536]{1,0:T(1,128)S(1)} %get-tuple-element.11, f32[322,1536]{1,0:T(8,128)} %copy-done.2, f32[319,1536]{1,0:T(8,128)S(1)} %slice_multiply_fusion.1, ...), kind=kLoop, calls=%fused_computation.25 | loop fusion | flops 5405440 | bytes 5904640 | tf_op jit(solution)/shard_map/reduce_sum | solution.py:162
  73.5 0.6 multiply_multiply_fusion
  74.1 0.9 convert_multiply_fusion
  75.3 1.2 %copy-done.1 = f32[322,1536]{1,0:T(8,128)S(1)} copy-done((f32[322,1536]{1,0:T(8,128)S(1)}, f32[322,1536]{1,0:T(8,128)}, u32[]{:S(2)}) %copy-start.1) | copy-done | bytes 1978392
  77.1 1.0 copy-done.9
  78.1 0.7 fusion.61
  78.8 1.2 %fusion.3 = f32[128,1536]{1,0:T(8,128)S(1)} fusion(bf16[1,320,1536]{2,1,0:T(8,128)(2,1)S(1)} %copy-done.14, f32[320]{0:T(512)S(1)} %get-tuple-element.32, s32[320]{0:T(512)S(1)} %get-tuple-element.25), kind=kOutput, calls=%fused_computation.16 | convolution fusion | flops 755998720 | bytes 1772032 | tf_op jit(solution)/shard_map/dot_general | solution.py:167
  80.0 1.0 convolution_reduce_fusion
  81.1 0.7 pad_maximum_fusion.8
  81.9 1.5 %collective-permute-start.11 = (f32[1,1537]{1,0:T(1,128)S(1)}, f32[1,1537]{1,0:T(1,128)S(1)}, u32[]{:S(2)}, u32[]{:S(2)}) collective-permute-start(f32[1,1537]{1,0:T(1,128)S(1)} %pad_maximum_fusion.8), channel_id=1, source_target_pairs={{4,0},{8,4},{12,8},{16,12},{20,16},{24,20},{28,24},{5,1},{9,5},{13... | collective-permute-start | bytes 18452 | tf_op jit(solution)/shard_map/ppermute | solution.py:16
  83.4 0.7 fusion.7
  84.1 0.7 fusion.64
  84.8 0.6 copy-done.11
  85.4 0.7 fusion.63
  86.1 2.1 %fusion.62 = f32[320,384]{1,0:T(8,128)S(1)} fusion(bf16[320,1536]{1,0:T(8,128)(2,1)S(1)} %subtract_convert_fusion, bf16[384,1536]{1,0:T(8,128)(2,1)} %collective-permute-done.8), kind=kOutput, calls=%fused_computation.150 | convolution fusion | flops 377487360 | bytes 2654208 | tf_op jit(solution)/shard_map/dot_general | solution.py:184
  88.1 0.7 fusion.10
  88.8 2.0 %fusion.9 = bf16[320,384]{1,0:T(8,128)(2,1)S(1)} fusion(f32[320,384]{1,0:T(8,128)S(1)} %fusion.63, bf16[320,1536]{1,0:T(8,128)(2,1)S(1)} %get-tuple-element.39, bf16[384,1536]{1,0:T(8,128)(2,1)} %collective-permute-done.6), kind=kOutput, calls=%fused_computation.39 | convolution fusion | flops 377733120 | bytes 2899968 | tf_op jit(solution)/shard_map/dot_general | solution.py:183
  90.8 0.7 fusion.8
  93.5 1.3 %collective-permute-start.12 = (f32[1,1537]{1,0:T(1,128)S(1)}, f32[1,1537]{1,0:T(1,128)S(1)}, u32[]{:S(2)}, u32[]{:S(2)}) collective-permute-start(f32[1,1537]{1,0:T(1,128)S(1)} %pad_maximum_fusion.9), channel_id=1, source_target_pairs={{8,0},{12,4},{16,8},{20,12},{24,16},{28,20},{9,1},{13,5},{17,9},{2... | collective-permute-start | bytes 18452 | tf_op jit(solution)/shard_map/ppermute | solution.py:16
  94.9 5.8 %collective-permute-done.12 = f32[1,1537]{1,0:T(1,128)S(1)} collective-permute-done((f32[1,1537]{1,0:T(1,128)S(1)}, f32[1,1537]{1,0:T(1,128)S(1)}, u32[]{:S(2)}, u32[]{:S(2)}) %collective-permute-start.12) | collective-permute-done | bytes 6180 | tf_op jit(solution)/shard_map/ppermute | solution.py:16
  100.8 0.6 slice.145
  102.1 1.3 %collective-permute-start.13 = (f32[1,1537]{1,0:T(1,128)S(1)}, f32[1,1537]{1,0:T(1,128)S(1)}, u32[]{:S(2)}, u32[]{:S(2)}) collective-permute-start(f32[1,1537]{1,0:T(1,128)S(1)} %pad_maximum_fusion.10), channel_id=1, source_target_pairs={{16,0},{20,4},{24,8},{28,12},{17,1},{21,5},{25,9},{29,13},{18,2},{... | collective-permute-start | bytes 18452 | tf_op jit(solution)/shard_map/ppermute | solution.py:16
  103.4 1.0 maximum_bitcast_fusion
  106.5 2.0 %collective-permute-done.13 = f32[1,1537]{1,0:T(1,128)S(1)} collective-permute-done((f32[1,1537]{1,0:T(1,128)S(1)}, f32[1,1537]{1,0:T(1,128)S(1)}, u32[]{:S(2)}, u32[]{:S(2)}) %collective-permute-start.13) | collective-permute-done | bytes 6180 | tf_op jit(solution)/shard_map/ppermute | solution.py:16
  108.5 1.7 %fusion.2 = bf16[1,128,1536]{2,1,0:T(8,128)(2,1)} fusion(f32[128,1536]{1,0:T(8,128)S(1)} %fusion.3, f32[1536]{0:T(1024)S(1)} %fusion.44, f32[128]{0:T(128)S(1)} %get-tuple-element.28, f32[128]{0:T(128)S(1)} %bitcast_select_fusion, f32[128]{0:T(128)S(1)} %reduce.2), kind=kOutput, calls=%fused_computation.15 | convolution fusion | flops 302841856 | bytes 1187328 | tf_op jit(solution)/shard_map/dot_general | solution.py:172
  (80 shorter events, 5.5 us)
Async XLA Ops:
  0.6 47.9 %collective-permute-start.5 = (bf16[384,1536]{1,0:T(8,128)(2,1)}, bf16[384,1536]{1,0:T(8,128)(2,1)S(1)}, u32[]{:S(2)}, u32[]{:S(2)}) collective-permute-start(bf16[384,1536]{1,0:T(8,128)(2,1)} %param.14), channel_id=1, source_target_pairs={{0,2},{1,3},{2,0},{3,1},{4,6},{5,7},{6,4},{7,5},{8,10},{9,11},{10,... | collective-permute-start | bytes 3538952 | tf_op jit(solution)/shard_map/ppermute | solution.py:50
  3.7 54.2 %collective-permute-start.6 = (bf16[384,1536]{1,0:T(8,128)(2,1)}, bf16[384,1536]{1,0:T(8,128)(2,1)}, u32[]{:S(2)}, u32[]{:S(2)}) collective-permute-start(bf16[384,1536]{1,0:T(8,128)(2,1)} %param.14), channel_id=1, source_target_pairs={{0,1},{1,0},{2,3},{3,2},{4,5},{5,4},{6,7},{7,6},{8,9},{9,8},{10,11... | collective-permute-start | bytes 3538952 | tf_op jit(solution)/shard_map/ppermute | solution.py:53
  9.1 11.3 %collective-permute-start.1 = (f32[1,1537]{1,0:T(1,128)S(1)}, f32[1,1537]{1,0:T(1,128)S(1)}, u32[]{:S(2)}, u32[]{:S(2)}) collective-permute-start(f32[1,1537]{1,0:T(1,128)S(1)} %pad_maximum_fusion.4), channel_id=1, source_target_pairs={{0,4},{4,8},{8,12},{12,16},{16,20},{20,24},{24,28},{1,5},{5,9},{9,... | collective-permute-start | bytes 18452 | tf_op jit(solution)/shard_map/ppermute | solution.py:16
  13.3 33.9 %collective-permute-start = (bf16[1,1536]{1,0:T(2,128)(2,1)S(1)}, bf16[1,1536]{1,0:T(2,128)(2,1)S(1)}, u32[]{:S(2)}, u32[]{:S(2)}) collective-permute-start(bf16[1,1536]{1,0:T(2,128)(2,1)S(1)} %get-tuple-element.20), channel_id=1, source_target_pairs={{0,4},{4,8},{8,12},{12,16},{16,20},{20,24},{24,28},{1,5},{5,9},{9,... | collective-permute-start | bytes 9224 | tf_op jit(solution)/shard_map/ppermute | solution.py:16
  16.8 38.5 %collective-permute-start.8 = (bf16[384,1536]{1,0:T(8,128)(2,1)}, bf16[384,1536]{1,0:T(8,128)(2,1)}, u32[]{:S(2)}, u32[]{:S(2)}) collective-permute-start(bf16[384,1536]{1,0:T(8,128)(2,1)} %param.15), channel_id=1, source_target_pairs={{0,2},{1,3},{2,0},{3,1},{4,6},{5,7},{6,4},{7,5},{8,10},{9,11},{10,... | collective-permute-start | bytes 3538952 | tf_op jit(solution)/shard_map/ppermute | solution.py:50
  22.3 4.8 %collective-permute-start.2 = (f32[1,1537]{1,0:T(1,128)S(1)}, f32[1,1537]{1,0:T(1,128)S(1)}, u32[]{:S(2)}, u32[]{:S(2)}) collective-permute-start(f32[1,1537]{1,0:T(1,128)S(1)} %pad_maximum_fusion.5), channel_id=1, source_target_pairs={{0,8},{4,12},{8,16},{12,20},{16,24},{20,28},{1,9},{5,13},{9,17},{1... | collective-permute-start | bytes 18452 | tf_op jit(solution)/shard_map/ppermute | solution.py:16
  28.4 7.8 %collective-permute-start.3 = (f32[1,1537]{1,0:T(1,128)S(1)}, f32[1,1537]{1,0:T(1,128)S(1)}, u32[]{:S(2)}, u32[]{:S(2)}) collective-permute-start(f32[1,1537]{1,0:T(1,128)S(1)} %pad_maximum_fusion.6), channel_id=1, source_target_pairs={{0,16},{4,20},{8,24},{12,28},{1,17},{5,21},{9,25},{13,29},{2,18},{... | collective-permute-start | bytes 18452 | tf_op jit(solution)/shard_map/ppermute | solution.py:16
  36.2 10.4 %copy-start.4 = (bf16[384,1536]{1,0:T(8,128)(2,1)S(1)}, bf16[384,1536]{1,0:T(8,128)(2,1)}, u32[]{:S(2)}) copy-start(bf16[384,1536]{1,0:T(8,128)(2,1)} %param.15) | copy-start | bytes 3538948
  40.2 6.5 %collective-permute-start.4 = (f32[1,1537]{1,0:T(1,128)S(1)}, f32[1,1537]{1,0:T(1,128)S(1)}, u32[]{:S(2)}, u32[]{:S(2)}) collective-permute-start(f32[1,1537]{1,0:T(1,128)S(1)} %pad_maximum_fusion.7), channel_id=1, source_target_pairs={{4,0},{8,4},{12,8},{16,12},{20,16},{24,20},{28,24},{5,1},{9,5},{13... | collective-permute-start | bytes 18452 | tf_op jit(solution)/shard_map/ppermute | solution.py:16
  46.6 13.2 %collective-permute-start.9 = (bf16[384,1536]{1,0:T(8,128)(2,1)S(1)}, bf16[384,1536]{1,0:T(8,128)(2,1)S(1)}, u32[]{:S(2)}, u32[]{:S(2)}) collective-permute-start(bf16[384,1536]{1,0:T(8,128)(2,1)S(1)} %copy-done.4), channel_id=1, source_target_pairs={{0,1},{1,0},{2,3},{3,2},{4,5},{5,4},{6,7},{7,6},{8,9},{9,8},{10,11... | collective-permute-start | bytes 3538952 | tf_op jit(solution)/shard_map/ppermute | solution.py:53
  48.5 1.3 %copy-start.8 = (bf16[384,1536]{1,0:T(8,128)(2,1)S(1)}, bf16[384,1536]{1,0:T(8,128)(2,1)}, u32[]{:S(2)}) copy-start(bf16[384,1536]{1,0:T(8,128)(2,1)} %param.14) | copy-start | bytes 3538948
  50.5 13.8 %collective-permute-start.7 = (bf16[384,1536]{1,0:T(8,128)(2,1)S(1)}, bf16[384,1536]{1,0:T(8,128)(2,1)S(1)}, u32[]{:S(2)}, u32[]{:S(2)}) collective-permute-start(bf16[384,1536]{1,0:T(8,128)(2,1)S(1)} %collective-permute-done.5), channel_id=1, source_target_pairs={{0,1},{1,0},{2,3},{3,2},{4,5},{5,4},{6,7},{7,6},{8,9},{9,8},{10,11... | collective-permute-start | bytes 3538952 | tf_op jit(solution)/shard_map/ppermute | solution.py:53
  55.2 5.8 %collective-permute-start.10 = (bf16[384,1536]{1,0:T(8,128)(2,1)}, bf16[384,1536]{1,0:T(8,128)(2,1)S(1)}, u32[]{:S(2)}, u32[]{:S(2)}) collective-permute-start(bf16[384,1536]{1,0:T(8,128)(2,1)} %collective-permute-done.8), channel_id=1, source_target_pairs={{0,1},{1,0},{2,3},{3,2},{4,5},{5,4},{6,7},{7,6},{8,9},{9,8},{10,11... | collective-permute-start | bytes 3538952 | tf_op jit(solution)/shard_map/ppermute | solution.py:53
  59.9 1.1 %copy-start.10 = (bf16[384,1536]{1,0:T(8,128)(2,1)}, bf16[384,1536]{1,0:T(8,128)(2,1)S(1)}, u32[]{:S(2)}) copy-start(bf16[384,1536]{1,0:T(8,128)(2,1)S(1)} %collective-permute-done.9) | copy-start | bytes 3538948
  61.0 1.0 copy-start.12
  62.0 6.5 %copy-start = (f32[322,1536]{1,0:T(8,128)}, f32[322,1536]{1,0:T(8,128)S(1)}, u32[]{:S(2)}) copy-start(f32[322,1536]{1,0:T(8,128)S(1)} %convolution_add_fusion) | copy-start | bytes 5935108
  64.2 1.0 copy-start.6
  65.3 1.3 %copy-start.2 = (f32[322,1536]{1,0:T(8,128)}, f32[322,1536]{1,0:T(8,128)S(1)}, u32[]{:S(2)}) copy-start(f32[322,1536]{1,0:T(8,128)S(1)} %convolution_add_fusion.3) | copy-start | bytes 5935108
  68.5 2.1 %slice-start = ((f32[322,1536]{1,0:T(8,128)}), f32[319,1536]{1,0:T(8,128)S(1)}, s32[]{:S(2)}) async-start(f32[322,1536]{1,0:T(8,128)} %copy-done), calls=%async_computation | async-start | bytes 3932160 | tf_op jit(solution)/shard_map/slice | solution.py:158
  70.7 2.8 %copy-start.3 = (f32[322,1536]{1,0:T(8,128)S(1)}, f32[322,1536]{1,0:T(8,128)}, u32[]{:S(2)}) copy-start(f32[322,1536]{1,0:T(8,128)} %copy-done.2) | copy-start | bytes 5935108
  70.7 3.4 %copy-start.14 = (bf16[1,320,1536]{2,1,0:T(8,128)(2,1)S(1)}, bf16[1,320,1536]{2,1,0:T(8,128)(2,1)}, u32[]{:S(2)}) copy-start(bf16[1,320,1536]{2,1,0:T(8,128)(2,1)} %param.9) | copy-start | bytes 2949124
  74.9 1.6 %copy-start.1 = (f32[322,1536]{1,0:T(8,128)S(1)}, f32[322,1536]{1,0:T(8,128)}, u32[]{:S(2)}) copy-start(f32[322,1536]{1,0:T(8,128)} %copy-done) | copy-start | bytes 5935108
  76.8 1.3 %copy-start.9 = (bf16[384,1536]{1,0:T(8,128)(2,1)S(1)}, bf16[384,1536]{1,0:T(8,128)(2,1)}, u32[]{:S(2)}) copy-start(bf16[384,1536]{1,0:T(8,128)(2,1)} %param.14) | copy-start | bytes 3538948
  78.8 4.6 %copy-start.5 = (bf16[384,1536]{1,0:T(8,128)(2,1)S(1)}, bf16[384,1536]{1,0:T(8,128)(2,1)}, u32[]{:S(2)}) copy-start(bf16[384,1536]{1,0:T(8,128)(2,1)} %param.15) | copy-start | bytes 3538948
  81.1 3.0 %copy-start.13 = (bf16[384,1536]{1,0:T(8,128)(2,1)S(1)}, bf16[384,1536]{1,0:T(8,128)(2,1)}, u32[]{:S(2)}) copy-start(bf16[384,1536]{1,0:T(8,128)(2,1)} %copy-done.12) | copy-start | bytes 3538948
  81.9 9.8 %collective-permute-start.11 = (f32[1,1537]{1,0:T(1,128)S(1)}, f32[1,1537]{1,0:T(1,128)S(1)}, u32[]{:S(2)}, u32[]{:S(2)}) collective-permute-start(f32[1,1537]{1,0:T(1,128)S(1)} %pad_maximum_fusion.8), channel_id=1, source_target_pairs={{4,0},{8,4},{12,8},{16,12},{20,16},{24,20},{28,24},{5,1},{9,5},{13... | collective-permute-start | bytes 18452 | tf_op jit(solution)/shard_map/ppermute | solution.py:16
  84.1 1.3 %copy-start.11 = (bf16[384,1536]{1,0:T(8,128)(2,1)S(1)}, bf16[384,1536]{1,0:T(8,128)(2,1)}, u32[]{:S(2)}) copy-start(bf16[384,1536]{1,0:T(8,128)(2,1)} %copy-done.10) | copy-start | bytes 3538948
  86.0 2.1 %copy-start.7 = (bf16[384,1536]{1,0:T(8,128)(2,1)S(1)}, bf16[384,1536]{1,0:T(8,128)(2,1)}, u32[]{:S(2)}) copy-start(bf16[384,1536]{1,0:T(8,128)(2,1)} %copy-done.6) | copy-start | bytes 3538948
  93.5 7.3 %collective-permute-start.12 = (f32[1,1537]{1,0:T(1,128)S(1)}, f32[1,1537]{1,0:T(1,128)S(1)}, u32[]{:S(2)}, u32[]{:S(2)}) collective-permute-start(f32[1,1537]{1,0:T(1,128)S(1)} %pad_maximum_fusion.9), channel_id=1, source_target_pairs={{8,0},{12,4},{16,8},{20,12},{24,16},{28,20},{9,1},{13,5},{17,9},{2... | collective-permute-start | bytes 18452 | tf_op jit(solution)/shard_map/ppermute | solution.py:16
  102.1 6.4 %collective-permute-start.13 = (f32[1,1537]{1,0:T(1,128)S(1)}, f32[1,1537]{1,0:T(1,128)S(1)}, u32[]{:S(2)}, u32[]{:S(2)}) collective-permute-start(f32[1,1537]{1,0:T(1,128)S(1)} %pad_maximum_fusion.10), channel_id=1, source_target_pairs={{16,0},{20,4},{24,8},{28,12},{17,1},{21,5},{25,9},{29,13},{18,2},{... | collective-permute-start | bytes 18452 | tf_op jit(solution)/shard_map/ppermute | solution.py:16

commit v14 on v13

--- a/solution.py
+++ b/solution.py
@@ -21,7 +21,7 @@
     return scales * unit_grad - scales * scales * scales * inner_prod * vectors
 
 
-def seq_scan(log_keep, vectors, axis, from_lower):
+def seq_scan(log_keep, vectors, axis, from_lower, held=None):
     size = lax.axis_size(axis)
     step = 1
     incl_log, incl_vec = log_keep, vectors
@@ -30,6 +30,8 @@
     while step < size:
         packed = jnp.concatenate([incl_vec, incl_log], axis=-1)
         got = shifted(packed, axis, step if from_lower else -step)
+        if held is not None and step == 1:
+            got, held = lax.optimization_barrier((got, held))
         got_log, got_vec = got[:, -1:], got[:, :-1]
         excl_vec = jnp.exp(excl_log) * got_vec + excl_vec
         excl_log = excl_log + got_log
@@ -37,6 +39,8 @@
             incl_vec = jnp.exp(incl_log) * got_vec + incl_vec
             incl_log = incl_log + got_log
         step *= 2
+    if held is not None:
+        return excl_vec, held
     return excl_vec
 
 
@@ -166,7 +170,9 @@
     weighted_grad = confidence[:, None] * grad_rows
     slot_grad = lax.dot_general(membership, weighted_grad, contract_first, precision=exact)
     back_vector = base_vector + jnp.dot(cosine[None, :], rise_rows, precision=exact)
-    grad_in = seq_scan(last_log, back_vector, "seq", False)
+    held = (queries, query_scale, key_rows, key_scale, key_prior, query_unit, query_next)
+    grad_in, held = seq_scan(last_log, back_vector, "seq", False, held)
+    queries, query_scale, key_rows, key_scale, key_prior, query_unit, query_next = held
     reach_end = jnp.exp(running[slot_count - 1] - running)
     state_grad = (
         lax.dot_general(decay_table, slot_grad, contract_first, precision=exact)

time: 111 us -> 119 us (1.072)
  matrix products: 24.8 us -> 31.1 us
    dot_general x8, matrix products: 8.06 us -> 11.9 us  [split_dot(): term = jnp.dot(part, block, preferred_element_type=jnp.float32)]
    ppermute x8, waiting for transfers between devices: 9.05 us -> 6 us  [shifted(): return lax.ppermute(block, axis, route)]
    ppermute x2, waiting for transfers between devices: 4.22 us -> 7.01 us  [gather_blocks(): pairs.append(lax.ppermute(blocks, axis, route))]
    dot_general x4, matrix products: 4.06 us -> 5.42 us  [per_device(): lax.dot_general(query_grad, q_block, contract_last, preferred_element_typ...]
    slice x2 -> x1, local copies, waits for them, and re-layouts: 0.24 us -> 1.52 us  [per_device(): raw_prior = jnp.concatenate([key_shift, key_rows[:-1]], axis=0)]
    unnamed x30 -> x26, local copies, waits for them, and re-layouts: 5.65 us -> 5.38 us
  transfers between devices with their start and end apart: 14 -> 14, of which waited for: 4 -> 4; matrix products, arithmetic and copies ran while one was open for 33% -> 41% of each run, Pallas kernels for 0% -> 0%
where the time goes in v14:
time: 119 us; the launch traced here: 117 us
  matrix products  31.1 us (26%)
  starting transfers between devices  25.1 us (21%)
  other arithmetic  19.6 us (16%)
  between operations  14.6 us (12%)
  local copies, waits for them, and re-layouts  14 us (12%)
  waiting for transfers between devices  13 us (11%)
    ppermute x8, starting transfers between devices, shifted(): return lax.ppermute(block, axis, route)  20.9 us
    dot_general x8, matrix products, split_dot(): term = jnp.dot(part, block, preferred_element_type=jnp.float32)  11.9 us
    ppermute x2, waiting for transfers between devices, gather_blocks(): pairs.append(lax.ppermute(blocks, axis, route))  7.01 us
    ppermute x8, waiting for transfers between devices, shifted(): return lax.ppermute(block, axis, route)  6 us
    dot_general x4, matrix products, per_device(): lax.dot_general(query_grad, q_block, contract_last, preferred_element_typ...  5.42 us
    unnamed x26, local copies, waits for them, and re-layouts  5.38 us
    dot_general x4, matrix products, per_device(): lax.dot_general(key_grad, k_block, contract_last, preferred_element_type=...  5.28 us
    ppermute x2, starting transfers between devices, gather_blocks(): pairs.append(lax.ppermute(blocks, axis, route))  3.6 us
  transfers between devices with their start and end apart: 14, of which 4 were waited for; matrix products, arithmetic and copies ran while one was open for 41% of the time, Pallas kernels for 0%

profile of v14, /device:TPU:0, one launch (start us, length us, event | category | flops | bytes accessed | tf_op | source)
XLA Modules:
  0.0 117.4 jit_solution(16941102877763098343)
XLA Ops:
  0.6 3.0 %collective-permute-start.5 = (bf16[384,1536]{1,0:T(8,128)(2,1)}, bf16[384,1536]{1,0:T(8,128)(2,1)}, u32[]{:S(2)}, u32[]{:S(2)}) collective-permute-start(bf16[384,1536]{1,0:T(8,128)(2,1)} %param.14), channel_id=1, source_target_pairs={{0,2},{1,3},{2,0},{3,1},{4,6},{5,7},{6,4},{7,5},{8,10},{9,11},{10,... | collective-permute-start | bytes 3538952 | tf_op jit(solution)/shard_map/ppermute | solution.py:54
  3.7 0.8 slice_bitcast_fusion
  4.4 3.4 %collective-permute-start = (bf16[1,1536]{1,0:T(2,128)(2,1)S(1)}, bf16[1,1536]{1,0:T(2,128)(2,1)S(1)}, u32[]{:S(2)}, u32[]{:S(2)}) collective-permute-start(bf16[1,1536]{1,0:T(2,128)(2,1)S(1)} %get-tuple-element.39), channel_id=1, source_target_pairs={{0,4},{4,8},{8,12},{12,16},{16,20},{20,24},{24,28},{1,5},{5,9},{9,... | collective-permute-start | bytes 9224 | tf_op jit(solution)/shard_map/ppermute | solution.py:16
  8.5 0.7 bitcast_select_fusion
  9.1 0.7 fusion.58
  10.1 0.5 slice.125
  10.7 1.9 %fusion.12 = f32[128,1536]{1,0:T(8,128)S(1)} fusion(bf16[1,128,1536]{2,1,0:T(8,128)(2,1)} %param.10, f32[128]{0:T(128)S(1)} %bitcast_select_fusion, f32[128]{0:T(128)S(1)} %reduce.2), kind=kOutput, calls=%fused_computation.48 | convolution fusion | flops 302448640 | bytes 1180672 | tf_op jit(solution)/shard_map/dot_general | solution.py:132
  12.6 0.7 pad_maximum_fusion.5
  13.3 3.5 %collective-permute-start.1 = (f32[1,1537]{1,0:T(1,128)S(1)}, f32[1,1537]{1,0:T(1,128)S(1)}, u32[]{:S(2)}, u32[]{:S(2)}) collective-permute-start(f32[1,1537]{1,0:T(1,128)S(1)} %pad_maximum_fusion.5), channel_id=1, source_target_pairs={{0,4},{4,8},{8,12},{12,16},{16,20},{20,24},{24,28},{1,5},{5,9},{9,... | collective-permute-start | bytes 18452 | tf_op jit(solution)/shard_map/ppermute | solution.py:16
  16.8 0.6 collective-permute-start.8
  17.3 0.8 fusion.31
  18.1 0.8 convert_reduce_fusion
  19.0 0.7 subtract_exponential_fusion
  22.3 3.5 %collective-permute-start.2 = (f32[1,1537]{1,0:T(1,128)S(1)}, f32[1,1537]{1,0:T(1,128)S(1)}, u32[]{:S(2)}, u32[]{:S(2)}) collective-permute-start(f32[1,1537]{1,0:T(1,128)S(1)} %pad_maximum_fusion.6), channel_id=1, source_target_pairs={{0,8},{4,12},{8,16},{12,20},{16,24},{20,28},{1,9},{5,13},{9,17},{1... | collective-permute-start | bytes 18452 | tf_op jit(solution)/shard_map/ppermute | solution.py:16
  25.9 1.2 collective-permute-done.2
  27.1 0.6 slice.128
  28.3 5.2 %collective-permute-start.3 = (f32[1,1537]{1,0:T(1,128)S(1)}, f32[1,1537]{1,0:T(1,128)S(1)}, u32[]{:S(2)}, u32[]{:S(2)}) collective-permute-start(f32[1,1537]{1,0:T(1,128)S(1)} %pad_maximum_fusion.7), channel_id=1, source_target_pairs={{0,16},{4,20},{8,24},{12,28},{1,17},{5,21},{9,25},{13,29},{2,18},{... | collective-permute-start | bytes 18452 | tf_op jit(solution)/shard_map/ppermute | solution.py:16
  33.5 0.7 fusion.63
  36.2 2.7 %fusion.5 = f32[320]{0:T(512)S(1)} fusion(bf16[1,320,1536]{2,1,0:T(8,128)(2,1)} %param.9, f32[1536]{0:T(1024)S(1)} %fusion.42, f32[320]{0:T(512)S(1)} %compare_convert_fusion, f32[128,1536]{1,0:T(8,128)S(1)} %fusion.12, f32[128]{0:T(128)S(1)} %get-tuple-element.49, s32[320]{0:T(512)S(1)} %get-tuple-element.44), kind=kOutput, calls=%fused_computation.31 | convolution fusion | flops 757866176 | bytes 1779968 | tf_op jit(solution)/shard_map/dot_general | solution.py:137
  39.4 0.7 pad_maximum_fusion.8
  40.1 1.3 %collective-permute-start.4 = (f32[1,1537]{1,0:T(1,128)S(1)}, f32[1,1537]{1,0:T(1,128)S(1)}, u32[]{:S(2)}, u32[]{:S(2)}) collective-permute-start(f32[1,1537]{1,0:T(1,128)S(1)} %pad_maximum_fusion.8), channel_id=1, source_target_pairs={{4,0},{8,4},{12,8},{16,12},{20,16},{24,20},{28,24},{5,1},{9,5},{13... | collective-permute-start | bytes 18452 | tf_op jit(solution)/shard_map/ppermute | solution.py:16
  43.8 2.4 %gather_fusion = f32[320]{0:T(512)S(1)} fusion(f32[128]{0:T(128)S(1)} %get-tuple-element.49, s32[1024]{0:T(1024)S(1)} %pad_clamp_fusion), kind=kCustom, calls=%fused_computation | custom fusion | bytes 3840 | tf_op jit(solution)/shard_map/gather | solution.py:140
  46.4 0.6 slice.141
  46.9 1.3 %pad_maximum_fusion.3 = bf16[322,1536]{1,0:T(8,128)(2,1)S(1)} fusion(bf16[1,1536]{1,0:T(2,128)(2,1)S(1)} %slice.177, bf16[1,1536]{1,0:T(2,128)(2,1)S(1)} %collective-permute-done, bf16[320,1536]{1,0:T(8,128)(2,1)} %bitcast.82), kind=kLoop, calls=%fused_computation.41 | loop fusion | flops 2967552 | bytes 1978368 | tf_op jit(solution)/shard_map/concatenate | solution.py:151
  48.2 7.0 %collective-permute-done.8 = bf16[384,1536]{1,0:T(8,128)(2,1)} collective-permute-done((bf16[384,1536]{1,0:T(8,128)(2,1)}, bf16[384,1536]{1,0:T(8,128)(2,1)}, u32[]{:S(2)}, u32[]{:S(2)}) %collective-permute-start.8) | collective-permute-done | bytes 1179680 | tf_op jit(solution)/shard_map/ppermute | solution.py:54
  55.2 2.0 %fusion.23 = f32[322,1536]{1,0:T(8,128)S(1)} fusion(bf16[384,1536]{1,0:T(8,128)(2,1)} %collective-permute-done.8, bf16[322,1536]{1,0:T(8,128)(2,1)S(1)} %pad_maximum_fusion.3, s32[]{:T(128)S(6)} %select_n.145), kind=kOutput, calls=%fused_computation.59 | convolution fusion | flops 379846656 | bytes 3409924 | tf_op jit(solution)/shard_map/dot_general | solution.py:79
  57.2 2.0 %convolution_add_fusion.2 = f32[322,1536]{1,0:T(8,128)S(1)} fusion(f32[322,1536]{1,0:T(8,128)S(1)} %fusion.23, bf16[384,1536]{1,0:T(8,128)(2,1)} %param.15, bf16[322,1536]{1,0:T(8,128)(2,1)S(1)} %pad_maximum_fusion.3, s32[]{:T(128)S(6)} %select_n.143), kind=kOutput, calls=%fused_computation.7 | convolution fusion | flops 380341248 | bytes 5425156 | tf_op jit(solution)/shard_map/dot_general | solution.py:79
  59.7 2.0 %fusion.25 = f32[322,1536]{1,0:T(8,128)S(1)} fusion(bf16[384,1536]{1,0:T(8,128)(2,1)} %collective-permute-done.5, bf16[322,1536]{1,0:T(8,128)(2,1)S(1)} %pad_maximum_fusion.3, s32[]{:T(128)S(6)} %select_n.145), kind=kOutput, calls=%fused_computation.61 | convolution fusion | flops 379846656 | bytes 3409924 | tf_op jit(solution)/shard_map/dot_general | solution.py:79
  61.7 0.7 convolution_add_fusion.5
  62.4 0.7 convolution_add_fusion.1
  63.5 2.0 %convolution_add_fusion.4 = f32[322,1536]{1,0:T(8,128)} fusion(f32[322,1536]{1,0:T(8,128)S(1)} %convolution_add_fusion.5, bf16[384,1536]{1,0:T(8,128)(2,1)S(1)} %collective-permute-done.6, bf16[322,1536]{1,0:T(8,128)(2,1)S(1)} %pad_maximum_fusion.3, s32[]{:T(128)S(6)} %select_n.146), kind=kOutput, calls=%fused_computation.9 | convolution fusion | flops 380341248 | bytes 5425156 | tf_op jit(solution)/shard_map/dot_general | solution.py:79
  65.5 0.7 convolution_add_fusion
  66.5 1.5 %slice.134 = f32[319,1536]{1,0:T(8,128)} slice(f32[322,1536]{1,0:T(8,128)S(1)} %convolution_add_fusion), slice={[0:319], [0:1536]} | slice | bytes 3919872 | tf_op jit(solution)/shard_map/slice | solution.py:162
  68.5 0.6 multiply_reduce_fusion.7
  69.8 2.0 %multiply_reduce_fusion.2 = (f32[320]{0:T(512)S(1)}, f32[320,1536]{1,0:T(8,128)S(1)}) fusion(f32[322,1536]{1,0:T(8,128)} %copy-done.2), kind=kLoop, calls=%fused_computation.27 | loop fusion | flops 982720 | bytes 3933440 | tf_op jit(solution)/shard_map/reduce_sum | solution.py:91
  71.8 0.8 broadcast_multiply_fusion.2
  72.6 2.0 %convolution_add_fusion.3 = f32[322,1536]{1,0:T(8,128)S(1)} fusion(f32[322,1536]{1,0:T(8,128)S(1)} %copy-done.3, bf16[384,1536]{1,0:T(8,128)(2,1)} %collective-permute-done.7, bf16[322,1536]{1,0:T(8,128)(2,1)S(1)} %pad_maximum_fusion.3, s32[]{:T(128)S(6)} %select_n.147), kind=kOutput, calls=%fused_computation.8 | convolution fusion | flops 380341248 | bytes 5425156 | tf_op jit(solution)/shard_map/dot_general | solution.py:79
  74.6 1.3 %copy-done = f32[322,1536]{1,0:T(8,128)} copy-done((f32[322,1536]{1,0:T(8,128)}, f32[322,1536]{1,0:T(8,128)S(1)}, u32[]{:S(2)}) %copy-start) | copy-done | bytes 1978392
  75.9 0.6 multiply_reduce_fusion.6
  77.2 2.9 %multiply_reduce_fusion.4 = (f32[320]{0:T(512)S(1)}, f32[320]{0:T(512)S(1)}, f32[320]{0:T(512)S(1)}) fusion(f32[322,1536]{1,0:T(8,128)} %copy-done, f32[319,1536]{1,0:T(8,128)} %slice.134, f32[1,1536]{1,0:T(1,128)S(1)} %get-tuple-element.30), kind=kLoop, calls=%fused_computation.29 | loop fusion | flops 3439680 | bytes 3936000 | tf_op jit(solution)/shard_map/reduce_sum | solution.py:164
  80.5 0.9 copy-done.12
  81.8 1.0 convolution_reduce_fusion
  82.9 0.7 pad_maximum_fusion.9
  83.6 1.5 %collective-permute-start.11 = (f32[1,1537]{1,0:T(1,128)S(1)}, f32[1,1537]{1,0:T(1,128)S(1)}, u32[]{:S(2)}, u32[]{:S(2)}) collective-permute-start(f32[1,1537]{1,0:T(1,128)S(1)} %pad_maximum_fusion.9), channel_id=1, source_target_pairs={{4,0},{8,4},{12,8},{16,12},{20,16},{24,20},{28,24},{5,1},{9,5},{13... | collective-permute-start | bytes 18452 | tf_op jit(solution)/shard_map/ppermute | solution.py:16
  85.5 1.2 %fusion.4 = f32[128,1536]{1,0:T(8,128)S(1)} fusion(bf16[1,320,1536]{2,1,0:T(8,128)(2,1)S(1)} %copy-done.12, f32[320]{0:T(512)S(1)} %get-tuple-element.25, s32[320]{0:T(512)S(1)} %get-tuple-element.44), kind=kOutput, calls=%fused_computation.17 | convolution fusion | flops 755998720 | bytes 1772032 | tf_op jit(solution)/shard_map/dot_general | solution.py:171
  86.7 2.4 %collective-permute-done.11 = f32[1,1537]{1,0:T(1,128)S(1)} collective-permute-done((f32[1,1537]{1,0:T(1,128)S(1)}, f32[1,1537]{1,0:T(1,128)S(1)}, u32[]{:S(2)}, u32[]{:S(2)}) %collective-permute-start.11) | collective-permute-done | bytes 6180 | tf_op jit(solution)/shard_map/ppermute | solution.py:16
  90.9 1.3 %collective-permute-start.12 = (f32[1,1537]{1,0:T(1,128)S(1)}, f32[1,1537]{1,0:T(1,128)S(1)}, u32[]{:S(2)}, u32[]{:S(2)}) collective-permute-start(f32[1,1537]{1,0:T(1,128)S(1)} %pad_maximum_fusion.10), channel_id=1, source_target_pairs={{8,0},{12,4},{16,8},{20,12},{24,16},{28,20},{9,1},{13,5},{17,9},{2... | collective-permute-start | bytes 18452 | tf_op jit(solution)/shard_map/ppermute | solution.py:16
  92.6 0.6 broadcast_multiply_fusion.1
  94.1 2.0 %fusion.64 = f32[320,384]{1,0:T(8,128)S(1)} fusion(bf16[320,1536]{1,0:T(8,128)(2,1)S(1)} %subtract_convert_fusion, bf16[384,1536]{1,0:T(8,128)(2,1)} %param.15), kind=kOutput, calls=%fused_computation.154 | convolution fusion | flops 377487360 | bytes 2654208 | tf_op jit(solution)/shard_map/dot_general | solution.py:190
  96.5 0.9 copy-done.5
  97.4 0.7 fusion.6
  98.1 0.6 copy-done.11
  98.6 0.7 fusion.67
  99.3 0.6 copy-done.9
  99.9 0.7 fusion.66
  100.6 2.0 %fusion.65 = f32[320,384]{1,0:T(8,128)S(1)} fusion(bf16[320,1536]{1,0:T(8,128)(2,1)S(1)} %subtract_convert_fusion, bf16[384,1536]{1,0:T(8,128)(2,1)} %collective-permute-done.8), kind=kOutput, calls=%fused_computation.155 | convolution fusion | flops 377487360 | bytes 2654208 | tf_op jit(solution)/shard_map/dot_general | solution.py:190
  102.6 2.1 %fusion.9 = bf16[320,384]{1,0:T(8,128)(2,1)S(1)} fusion(f32[320,384]{1,0:T(8,128)S(1)} %fusion.67, bf16[320,1536]{1,0:T(8,128)(2,1)S(1)} %subtract_convert_fusion.1, bf16[384,1536]{1,0:T(8,128)(2,1)} %collective-permute-done.7), kind=kOutput, calls=%fused_computation.39 | convolution fusion | flops 377733120 | bytes 2899968 | tf_op jit(solution)/shard_map/dot_general | solution.py:189
  104.6 0.7 fusion.8
  105.4 2.0 %fusion.7 = bf16[320,384]{1,0:T(8,128)(2,1)S(1)} fusion(f32[320,384]{1,0:T(8,128)S(1)} %fusion.65, bf16[320,1536]{1,0:T(8,128)(2,1)S(1)} %subtract_convert_fusion.1, bf16[384,1536]{1,0:T(8,128)(2,1)} %collective-permute-done.5), kind=kOutput, calls=%fused_computation.37 | convolution fusion | flops 377733120 | bytes 2899968 | tf_op jit(solution)/shard_map/dot_general | solution.py:189
  107.6 0.6 slice.142
  108.9 1.3 %collective-permute-start.13 = (f32[1,1537]{1,0:T(1,128)S(1)}, f32[1,1537]{1,0:T(1,128)S(1)}, u32[]{:S(2)}, u32[]{:S(2)}) collective-permute-start(f32[1,1537]{1,0:T(1,128)S(1)} %pad_maximum_fusion.11), channel_id=1, source_target_pairs={{16,0},{20,4},{24,8},{28,12},{17,1},{21,5},{25,9},{29,13},{18,2},{... | collective-permute-start | bytes 18452 | tf_op jit(solution)/shard_map/ppermute | solution.py:16
  110.2 1.0 maximum_bitcast_fusion
  113.3 2.4 %collective-permute-done.13 = f32[1,1537]{1,0:T(1,128)S(1)} collective-permute-done((f32[1,1537]{1,0:T(1,128)S(1)}, f32[1,1537]{1,0:T(1,128)S(1)}, u32[]{:S(2)}, u32[]{:S(2)}) %collective-permute-start.13) | collective-permute-done | bytes 6180 | tf_op jit(solution)/shard_map/ppermute | solution.py:16
  115.8 1.7 %fusion.2 = bf16[1,128,1536]{2,1,0:T(8,128)(2,1)} fusion(f32[128,1536]{1,0:T(8,128)S(1)} %fusion.4, f32[1536]{0:T(1024)S(1)} %fusion.43, f32[128]{0:T(128)S(1)} %get-tuple-element.48, f32[128]{0:T(128)S(1)} %bitcast_select_fusion, f32[128]{0:T(128)S(1)} %reduce.2), kind=kOutput, calls=%fused_computation.15 | convolution fusion | flops 302841856 | bytes 1187328 | tf_op jit(solution)/shard_map/dot_general | solution.py:178
  (81 shorter events, 7.0 us)
Async XLA Ops:
  0.6 58.6 %collective-permute-start.5 = (bf16[384,1536]{1,0:T(8,128)(2,1)}, bf16[384,1536]{1,0:T(8,128)(2,1)}, u32[]{:S(2)}, u32[]{:S(2)}) collective-permute-start(bf16[384,1536]{1,0:T(8,128)(2,1)} %param.14), channel_id=1, source_target_pairs={{0,2},{1,3},{2,0},{3,1},{4,6},{5,7},{6,4},{7,5},{8,10},{9,11},{10,... | collective-permute-start | bytes 3538952 | tf_op jit(solution)/shard_map/ppermute | solution.py:54
  3.7 59.8 %collective-permute-start.6 = (bf16[384,1536]{1,0:T(8,128)(2,1)}, bf16[384,1536]{1,0:T(8,128)(2,1)S(1)}, u32[]{:S(2)}, u32[]{:S(2)}) collective-permute-start(bf16[384,1536]{1,0:T(8,128)(2,1)} %param.14), channel_id=1, source_target_pairs={{0,1},{1,0},{2,3},{3,2},{4,5},{5,4},{6,7},{7,6},{8,9},{9,8},{10,11... | collective-permute-start | bytes 3538952 | tf_op jit(solution)/shard_map/ppermute | solution.py:57
  4.4 42.5 %collective-permute-start = (bf16[1,1536]{1,0:T(2,128)(2,1)S(1)}, bf16[1,1536]{1,0:T(2,128)(2,1)S(1)}, u32[]{:S(2)}, u32[]{:S(2)}) collective-permute-start(bf16[1,1536]{1,0:T(2,128)(2,1)S(1)} %get-tuple-element.39), channel_id=1, source_target_pairs={{0,4},{4,8},{8,12},{12,16},{16,20},{20,24},{24,28},{1,5},{5,9},{9,... | collective-permute-start | bytes 9224 | tf_op jit(solution)/shard_map/ppermute | solution.py:16
  13.3 7.1 %collective-permute-start.1 = (f32[1,1537]{1,0:T(1,128)S(1)}, f32[1,1537]{1,0:T(1,128)S(1)}, u32[]{:S(2)}, u32[]{:S(2)}) collective-permute-start(f32[1,1537]{1,0:T(1,128)S(1)} %pad_maximum_fusion.5), channel_id=1, source_target_pairs={{0,4},{4,8},{8,12},{12,16},{16,20},{20,24},{24,28},{1,5},{5,9},{9,... | collective-permute-start | bytes 18452 | tf_op jit(solution)/shard_map/ppermute | solution.py:16
  16.8 38.5 %collective-permute-start.8 = (bf16[384,1536]{1,0:T(8,128)(2,1)}, bf16[384,1536]{1,0:T(8,128)(2,1)}, u32[]{:S(2)}, u32[]{:S(2)}) collective-permute-start(bf16[384,1536]{1,0:T(8,128)(2,1)} %param.15), channel_id=1, source_target_pairs={{0,2},{1,3},{2,0},{3,1},{4,6},{5,7},{6,4},{7,5},{8,10},{9,11},{10,... | collective-permute-start | bytes 3538952 | tf_op jit(solution)/shard_map/ppermute | solution.py:54
  22.3 4.8 %collective-permute-start.2 = (f32[1,1537]{1,0:T(1,128)S(1)}, f32[1,1537]{1,0:T(1,128)S(1)}, u32[]{:S(2)}, u32[]{:S(2)}) collective-permute-start(f32[1,1537]{1,0:T(1,128)S(1)} %pad_maximum_fusion.6), channel_id=1, source_target_pairs={{0,8},{4,12},{8,16},{12,20},{16,24},{20,28},{1,9},{5,13},{9,17},{1... | collective-permute-start | bytes 18452 | tf_op jit(solution)/shard_map/ppermute | solution.py:16
  28.3 7.9 %collective-permute-start.3 = (f32[1,1537]{1,0:T(1,128)S(1)}, f32[1,1537]{1,0:T(1,128)S(1)}, u32[]{:S(2)}, u32[]{:S(2)}) collective-permute-start(f32[1,1537]{1,0:T(1,128)S(1)} %pad_maximum_fusion.7), channel_id=1, source_target_pairs={{0,16},{4,20},{8,24},{12,28},{1,17},{5,21},{9,25},{13,29},{2,18},{... | collective-permute-start | bytes 18452 | tf_op jit(solution)/shard_map/ppermute | solution.py:16
  40.1 6.2 %collective-permute-start.4 = (f32[1,1537]{1,0:T(1,128)S(1)}, f32[1,1537]{1,0:T(1,128)S(1)}, u32[]{:S(2)}, u32[]{:S(2)}) collective-permute-start(f32[1,1537]{1,0:T(1,128)S(1)} %pad_maximum_fusion.8), channel_id=1, source_target_pairs={{4,0},{8,4},{12,8},{16,12},{20,16},{24,20},{28,24},{5,1},{9,5},{13... | collective-permute-start | bytes 18452 | tf_op jit(solution)/shard_map/ppermute | solution.py:16
  46.3 16.1 %collective-permute-start.9 = (bf16[384,1536]{1,0:T(8,128)(2,1)}, bf16[384,1536]{1,0:T(8,128)(2,1)S(1)}, u32[]{:S(2)}, u32[]{:S(2)}) collective-permute-start(bf16[384,1536]{1,0:T(8,128)(2,1)} %param.15), channel_id=1, source_target_pairs={{0,1},{1,0},{2,3},{3,2},{4,5},{5,4},{6,7},{7,6},{8,9},{9,8},{10,11... | collective-permute-start | bytes 3538952 | tf_op jit(solution)/shard_map/ppermute | solution.py:57
  59.2 2.6 %copy-start.4 = (bf16[384,1536]{1,0:T(8,128)(2,1)S(1)}, bf16[384,1536]{1,0:T(8,128)(2,1)}, u32[]{:S(2)}) copy-start(bf16[384,1536]{1,0:T(8,128)(2,1)} %param.14) | copy-start | bytes 3538948
  59.2 6.3 %collective-permute-start.10 = (bf16[384,1536]{1,0:T(8,128)(2,1)}, bf16[384,1536]{1,0:T(8,128)(2,1)S(1)}, u32[]{:S(2)}, u32[]{:S(2)}) collective-permute-start(bf16[384,1536]{1,0:T(8,128)(2,1)} %collective-permute-done.8), channel_id=1, source_target_pairs={{0,1},{1,0},{2,3},{3,2},{4,5},{5,4},{6,7},{7,6},{8,9},{9,8},{10,11... | collective-permute-start | bytes 3538952 | tf_op jit(solution)/shard_map/ppermute | solution.py:57
  59.3 13.3 %collective-permute-start.7 = (bf16[384,1536]{1,0:T(8,128)(2,1)}, bf16[384,1536]{1,0:T(8,128)(2,1)}, u32[]{:S(2)}, u32[]{:S(2)}) collective-permute-start(bf16[384,1536]{1,0:T(8,128)(2,1)} %collective-permute-done.5), channel_id=1, source_target_pairs={{0,1},{1,0},{2,3},{3,2},{4,5},{5,4},{6,7},{7,6},{8,9},{9,8},{10,11... | collective-permute-start | bytes 3538952 | tf_op jit(solution)/shard_map/ppermute | solution.py:57
  62.4 1.0 copy-start.8
  63.4 2.0 %copy-start.6 = (bf16[384,1536]{1,0:T(8,128)(2,1)}, bf16[384,1536]{1,0:T(8,128)(2,1)S(1)}, u32[]{:S(2)}) copy-start(bf16[384,1536]{1,0:T(8,128)(2,1)S(1)} %collective-permute-done.6) | copy-start | bytes 3538948
  65.5 1.1 copy-start.10
  66.5 1.9 %copy-start.2 = (f32[322,1536]{1,0:T(8,128)}, f32[322,1536]{1,0:T(8,128)S(1)}, u32[]{:S(2)}) copy-start(f32[322,1536]{1,0:T(8,128)S(1)} %convolution_add_fusion) | copy-start | bytes 5935108
  69.8 2.8 %copy-start.3 = (f32[322,1536]{1,0:T(8,128)S(1)}, f32[322,1536]{1,0:T(8,128)}, u32[]{:S(2)}) copy-start(f32[322,1536]{1,0:T(8,128)} %convolution_add_fusion.4) | copy-start | bytes 5935108
  74.6 1.3 %copy-start = (f32[322,1536]{1,0:T(8,128)}, f32[322,1536]{1,0:T(8,128)S(1)}, u32[]{:S(2)}) copy-start(f32[322,1536]{1,0:T(8,128)S(1)} %convolution_add_fusion.3) | copy-start | bytes 5935108
  77.2 3.0 %copy-start.1 = (f32[322,1536]{1,0:T(8,128)S(1)}, f32[322,1536]{1,0:T(8,128)}, u32[]{:S(2)}) copy-start(f32[322,1536]{1,0:T(8,128)} %copy-done) | copy-start | bytes 5935108
  80.2 1.2 %copy-start.12 = (bf16[1,320,1536]{2,1,0:T(8,128)(2,1)S(1)}, bf16[1,320,1536]{2,1,0:T(8,128)(2,1)}, u32[]{:S(2)}) copy-start(bf16[1,320,1536]{2,1,0:T(8,128)(2,1)} %param.9) | copy-start | bytes 2949124
  83.6 5.5 %collective-permute-start.11 = (f32[1,1537]{1,0:T(1,128)S(1)}, f32[1,1537]{1,0:T(1,128)S(1)}, u32[]{:S(2)}, u32[]{:S(2)}) collective-permute-start(f32[1,1537]{1,0:T(1,128)S(1)} %pad_maximum_fusion.9), channel_id=1, source_target_pairs={{4,0},{8,4},{12,8},{16,12},{20,16},{24,20},{28,24},{5,1},{9,5},{13... | collective-permute-start | bytes 18452 | tf_op jit(solution)/shard_map/ppermute | solution.py:16
  90.9 16.6 %collective-permute-start.12 = (f32[1,1537]{1,0:T(1,128)S(1)}, f32[1,1537]{1,0:T(1,128)S(1)}, u32[]{:S(2)}, u32[]{:S(2)}) collective-permute-start(f32[1,1537]{1,0:T(1,128)S(1)} %pad_maximum_fusion.10), channel_id=1, source_target_pairs={{8,0},{12,4},{16,8},{20,12},{24,16},{28,20},{9,1},{13,5},{17,9},{2... | collective-permute-start | bytes 18452 | tf_op jit(solution)/shard_map/ppermute | solution.py:16
  96.1 1.3 %copy-start.5 = (bf16[384,1536]{1,0:T(8,128)(2,1)S(1)}, bf16[384,1536]{1,0:T(8,128)(2,1)}, u32[]{:S(2)}) copy-start(bf16[384,1536]{1,0:T(8,128)(2,1)} %param.14) | copy-start | bytes 3538948
  97.4 1.3 %copy-start.11 = (bf16[384,1536]{1,0:T(8,128)(2,1)S(1)}, bf16[384,1536]{1,0:T(8,128)(2,1)}, u32[]{:S(2)}) copy-start(bf16[384,1536]{1,0:T(8,128)(2,1)} %copy-done.10) | copy-start | bytes 3538948
  98.6 1.3 %copy-start.9 = (bf16[384,1536]{1,0:T(8,128)(2,1)S(1)}, bf16[384,1536]{1,0:T(8,128)(2,1)}, u32[]{:S(2)}) copy-start(bf16[384,1536]{1,0:T(8,128)(2,1)} %copy-done.8) | copy-start | bytes 3538948
  102.6 2.1 %copy-start.7 = (bf16[384,1536]{1,0:T(8,128)(2,1)S(1)}, bf16[384,1536]{1,0:T(8,128)(2,1)}, u32[]{:S(2)}) copy-start(bf16[384,1536]{1,0:T(8,128)(2,1)} %copy-done.6) | copy-start | bytes 3538948
  108.9 6.8 %collective-permute-start.13 = (f32[1,1537]{1,0:T(1,128)S(1)}, f32[1,1537]{1,0:T(1,128)S(1)}, u32[]{:S(2)}, u32[]{:S(2)}) collective-permute-start(f32[1,1537]{1,0:T(1,128)S(1)} %pad_maximum_fusion.11), channel_id=1, source_target_pairs={{16,0},{20,4},{24,8},{28,12},{17,1},{21,5},{25,9},{29,13},{18,2},{... | collective-permute-start | bytes 18452 | tf_op jit(solution)/shard_map/ppermute | solution.py:16

commit v15 on v9

--- a/solution.py
+++ b/solution.py
@@ -40,19 +40,36 @@
     return excl_vec
 
 
-def gather_blocks(blocks, axis):
+def gather_blocks(blocks, axis, pair_axis):
     size = lax.axis_size(axis)
     own = lax.axis_index(axis)
-    pairs = [blocks]
-    index = [own]
+    side = lax.axis_index(pair_axis) % 2
+    cols = blocks[0].shape[1] // 2
+    swap = [(i, i ^ 1) for i in range(size)]
+    swap_pair = [(i, i ^ 1) for i in range(lax.axis_size(pair_axis))]
+    partner_own = lax.ppermute(blocks, axis, swap)
+    pairs = [blocks, partner_own]
+    index = [own, own ^ 1]
+    last = None
     for k in range(1, size // 2):
         route = [(i, (i + 2 * k) % size) for i in range(size)]
-        pairs.append(lax.ppermute(blocks, axis, route))
-        index.append((own - 2 * k) % size)
-    swap = [(i, i ^ 1) for i in range(size)]
-    partner = lax.ppermute(pairs, axis, swap)
-    pairs = pairs + partner
-    index = index + [i ^ 1 for i in index]
+        mine, theirs = [], []
+        for block in blocks:
+            half = lax.dynamic_slice_in_dim(block, side * cols, cols, axis=1)
+            if last is not None:
+                half, _ = lax.optimization_barrier((half, last))
+            fetched = lax.ppermute(half, axis, route)
+            last = fetched
+            other = lax.ppermute(fetched, pair_axis, swap_pair)
+            fetched_fwd = lax.ppermute(fetched, axis, swap)
+            other_fwd = lax.ppermute(other, axis, swap)
+            first = side == 0
+            mine.append(jnp.where(first, jnp.concatenate([fetched, other], 1), jnp.concatenate([other, fetched], 1)))
+            theirs.append(
+                jnp.where(first, jnp.concatenate([fetched_fwd, other_fwd], 1), jnp.concatenate([other_fwd, fetched_fwd], 1))
+            )
+        pairs += [tuple(mine), tuple(theirs)]
+        index += [(own - 2 * k) % size, ((own - 2 * k) % size) ^ 1]
     return pairs, index
 
 
@@ -104,7 +121,7 @@
     slot_count = segment_states.shape[1]
     width = query_weight.shape[0]
     shard_index = lax.axis_index("seq")
-    pairs, index = gather_blocks((query_weight, key_weight), "dp")
+    pairs, index = gather_blocks((query_weight, key_weight), "dp", "seq")
     query_blocks = [p[0] for p in pairs]
     key_blocks = [p[1] for p in pairs]
     position = jnp.arange(token_count)

time: 109 us -> 135 us (1.24)
  waiting for transfers between devices: 14 us -> 27 us
  matrix products: 25 us -> 35.4 us
  starting transfers between devices: 25.3 us -> 28.4 us
    ppermute x8, waiting for transfers between devices: 9.06 us -> 19.8 us  [shifted(): return lax.ppermute(block, axis, route)]
    dot_general x8, matrix products: 8.06 us -> 14.1 us  [split_dot(): term = jnp.dot(part, block, preferred_element_type=jnp.float32)]
    ppermute x6 -> x10, starting transfers between devices: 4.19 us -> 8.24 us  [the longest x2 5.11 us: gather_blocks(): other = lax.ppermute(fetched, pair_axis, swap_pair)]
    unnamed x30, local copies, waits for them, and re-layouts: 4.81 us -> 1.41 us
    dot_general x4, matrix products: 4.12 us -> 7.45 us  [per_device(): lax.dot_general(key_grad, k_block, contract_last, preferred_element_type=...]
    dynamic_slice x0 -> x2, local copies, waits for them, and re-layouts: none -> 2.8 us  [gather_blocks(): half = lax.dynamic_slice_in_dim(block, side * cols, cols, axis=1)]
    ppermute x6 -> x10, waiting for transfers between devices: 4.91 us -> 7.21 us  [the longest x2 7.18 us: gather_blocks(): other = lax.ppermute(fetched, pair_axis, swap_pair)]
  transfers between devices with their start and end apart: 14 -> 18, of which waited for: 4 -> 5; matrix products, arithmetic and copies ran while one was open for 33% -> 35% of each run, Pallas kernels for 0% -> 0%
where the time goes in v15:
time: 135 us; the launch traced here: 134 us
  matrix products  35.4 us (26%)
  starting transfers between devices  28.4 us (21%)
  waiting for transfers between devices  27 us (20%)
  other arithmetic  16.3 us (12%)
  between operations  14.6 us (11%)
  local copies, waits for them, and re-layouts  12.1 us (9%)
    ppermute x8, starting transfers between devices, shifted(): return lax.ppermute(block, axis, route)  20.2 us
    ppermute x8, waiting for transfers between devices, shifted(): return lax.ppermute(block, axis, route)  19.8 us
    dot_general x8, matrix products, split_dot(): term = jnp.dot(part, block, preferred_element_type=jnp.float32)  14.1 us
    dot_general x4, matrix products, per_device(): lax.dot_general(key_grad, k_block, contract_last, preferred_element_type=...  7.45 us
    ppermute x2, waiting for transfers between devices, gather_blocks(): other = lax.ppermute(fetched, pair_axis, swap_pair)  7.18 us
    ppermute x2, starting transfers between devices, gather_blocks(): other = lax.ppermute(fetched, pair_axis, swap_pair)  5.11 us
    dot_general x4, matrix products, per_device(): lax.dot_general(query_grad, q_block, contract_last, preferred_element_typ...  4.52 us
    dynamic_slice x2, local copies, waits for them, and re-layouts, gather_blocks(): half = lax.dynamic_slice_in_dim(block, side * cols, cols, axis=1)  2.8 us
  transfers between devices with their start and end apart: 18, of which 5 were waited for; matrix products, arithmetic and copies ran while one was open for 35% of the time, Pallas kernels for 0%

profile of v15, /device:TPU:0, one launch (start us, length us, event | category | flops | bytes accessed | tf_op | source)
XLA Modules:
  0.0 133.8 jit_solution(4316662080980399321)
XLA Ops:
  1.8 0.7 fusion.60
  2.8 0.5 slice.119
  3.3 0.7 bitcast_select_fusion
  4.1 2.8 %fusion.14 = f32[128,1536]{1,0:T(8,128)} fusion(bf16[1,128,1536]{2,1,0:T(8,128)(2,1)} %param.10, f32[128]{0:T(128)S(1)} %bitcast_select_fusion, f32[128]{0:T(128)S(1)} %reduce.2), kind=kOutput, calls=%fused_computation.50 | convolution fusion | flops 302448640 | bytes 1180672 | tf_op jit(solution)/shard_map/dot_general | solution.py:145
  6.9 0.8 slice.118
  7.7 0.6 pad_maximum_fusion.4
  8.3 4.5 %collective-permute-start.1 = (f32[1,1537]{1,0:T(1,128)S(1)}, f32[1,1537]{1,0:T(1,128)S(1)}, u32[]{:S(2)}, u32[]{:S(2)}) collective-permute-start(f32[1,1537]{1,0:T(1,128)S(1)} %pad_maximum_fusion.4), channel_id=1, source_target_pairs={{0,4},{4,8},{8,12},{12,16},{16,20},{20,24},{24,28},{1,5},{5,9},{9,... | collective-permute-start | bytes 18452 | tf_op jit(solution)/shard_map/ppermute | solution.py:16
  12.8 1.9 %constant_dynamic-slice_fusion.5 = bf16[384,768]{1,0:T(8,128)(2,1)} fusion(bf16[384,1536]{1,0:T(8,128)(2,1)} %param.14, s32[]{:T(128)S(6)} %select_n.165), kind=kLoop, calls=%fused_computation.124 | loop fusion | bytes 1179652 | tf_op jit(solution)/shard_map/dynamic_slice | solution.py:58
  14.7 1.5 %collective-permute-start.6 = (bf16[384,768]{1,0:T(8,128)(2,1)}, bf16[384,768]{1,0:T(8,128)(2,1)}, u32[]{:S(2)}, u32[]{:S(2)}) collective-permute-start(bf16[384,768]{1,0:T(8,128)(2,1)} %constant_dynamic-slice_fusion.5), channel_id=1, source_target_pairs={{0,2},{1,3},{2,0},{3,1},{4,6},{5,7},{6,4},{7,5},{8,10},{9,11},{10,... | collective-permute-start | bytes 1769480 | tf_op jit(solution)/shard_map/ppermute | solution.py:61
  16.4 0.9 constant_dynamic-slice_fusion.4
  17.3 0.6 subtract_exponential_fusion
  17.9 0.8 slice_bitcast_fusion
  21.3 0.8 multiply_add_fusion.3
  22.1 3.5 %collective-permute-start.2 = (f32[1,1537]{1,0:T(1,128)S(1)}, f32[1,1537]{1,0:T(1,128)S(1)}, u32[]{:S(2)}, u32[]{:S(2)}) collective-permute-start(f32[1,1537]{1,0:T(1,128)S(1)} %pad_maximum_fusion.5), channel_id=1, source_target_pairs={{0,8},{4,12},{8,16},{12,20},{16,24},{20,28},{1,9},{5,13},{9,17},{1... | collective-permute-start | bytes 18452 | tf_op jit(solution)/shard_map/ppermute | solution.py:16
  25.8 1.2 collective-permute-done.2
  27.0 0.5 slice.122
  28.2 5.2 %collective-permute-start.3 = (f32[1,1537]{1,0:T(1,128)S(1)}, f32[1,1537]{1,0:T(1,128)S(1)}, u32[]{:S(2)}, u32[]{:S(2)}) collective-permute-start(f32[1,1537]{1,0:T(1,128)S(1)} %pad_maximum_fusion.6), channel_id=1, source_target_pairs={{0,16},{4,20},{8,24},{12,28},{1,17},{5,21},{9,25},{13,29},{2,18},{... | collective-permute-start | bytes 18452 | tf_op jit(solution)/shard_map/ppermute | solution.py:16
  35.6 2.6 %fusion.5 = f32[320]{0:T(512)S(1)} fusion(bf16[1,320,1536]{2,1,0:T(8,128)(2,1)S(1)} %copy-done, f32[1536]{0:T(1024)S(1)} %fusion.46, f32[320]{0:T(512)S(1)} %compare_convert_fusion, f32[128,1536]{1,0:T(8,128)} %fusion.14, f32[128]{0:T(128)S(1)} %get-tuple-element.25, s32[320]{0:T(512)S(1)} %get-tuple-element.21), kind=kOutput, calls=%fused_computation.27 | convolution fusion | flops 757866176 | bytes 1779968 | tf_op jit(solution)/shard_map/dot_general | solution.py:150
  38.2 0.5 slice.98
  39.2 1.5 %collective-permute-start.7 = (bf16[384,768]{1,0:T(8,128)(2,1)}, bf16[384,768]{1,0:T(8,128)(2,1)}, u32[]{:S(2)}, u32[]{:S(2)}) collective-permute-start(bf16[384,768]{1,0:T(8,128)(2,1)} %collective-permute-done.6), channel_id=1, source_target_pairs={{0,4},{4,0},{8,12},{12,8},{16,20},{20,16},{24,28},{28,24},{1,5},{5... | collective-permute-start | bytes 1769480 | tf_op jit(solution)/shard_map/ppermute | solution.py:63
  40.7 0.7 pad_maximum_fusion.7
  41.4 1.3 collective-permute-start.4
  42.7 0.6 fusion.71
  43.3 10.7 %collective-permute-done.4 = f32[1,1537]{1,0:T(1,128)S(1)} collective-permute-done((f32[1,1537]{1,0:T(1,128)S(1)}, f32[1,1537]{1,0:T(1,128)S(1)}, u32[]{:S(2)}, u32[]{:S(2)}) %collective-permute-start.4) | collective-permute-done | bytes 6180 | tf_op jit(solution)/shard_map/ppermute | solution.py:16
  54.0 1.6 %collective-permute-start = (bf16[1,1536]{1,0:T(2,128)(2,1)S(1)}, bf16[1,1536]{1,0:T(2,128)(2,1)S(1)}, u32[]{:S(2)}, u32[]{:S(2)}) collective-permute-start(bf16[1,1536]{1,0:T(2,128)(2,1)S(1)} %get-tuple-element.15), channel_id=1, source_target_pairs={{0,4},{4,8},{8,12},{12,16},{16,20},{20,24},{24,28},{1,5},{5,9},{9,... | collective-permute-start | bytes 9224 | tf_op jit(solution)/shard_map/ppermute | solution.py:16
  58.2 2.4 %gather_fusion = f32[320]{0:T(512)S(1)} fusion(f32[128]{0:T(128)S(1)} %get-tuple-element.25, s32[1024]{0:T(1024)S(1)} %pad_clamp_fusion), kind=kCustom, calls=%fused_computation | custom fusion | bytes 3840 | tf_op jit(solution)/shard_map/gather | solution.py:153
  60.6 0.5 slice.133
  61.2 1.3 pad_maximum_fusion.2
  62.6 3.6 %collective-permute-start.12 = (bf16[384,768]{1,0:T(8,128)(2,1)}, bf16[384,768]{1,0:T(8,128)(2,1)}, u32[]{:S(2)}, u32[]{:S(2)}) collective-permute-start(bf16[384,768]{1,0:T(8,128)(2,1)} %collective-permute-done.11), channel_id=1, source_target_pairs={{0,4},{4,0},{8,12},{12,8},{16,20},{20,16},{24,28},{28,24},{1,5},{5... | collective-permute-start | bytes 1769480 | tf_op jit(solution)/shard_map/ppermute | solution.py:63
  66.7 0.7 fusion.27
  67.4 0.7 convolution_add_fusion.5
  68.1 2.0 %fusion.25 = f32[322,1536]{1,0:T(8,128)S(1)} fusion(bf16[384,1536]{1,0:T(8,128)(2,1)} %collective-permute-done.10, bf16[322,1536]{1,0:T(8,128)(2,1)S(1)} %pad_maximum_fusion.2, s32[]{:T(128)S(6)} %select_n.160), kind=kOutput, calls=%fused_computation.61 | convolution fusion | flops 379846656 | bytes 3409924 | tf_op jit(solution)/shard_map/dot_general | solution.py:92
  70.1 0.7 convolution_add_fusion.2
  70.8 2.4 %convolution_add_fusion.4 = f32[322,1536]{1,0:T(8,128)S(1)} fusion(f32[322,1536]{1,0:T(8,128)S(1)} %convolution_add_fusion.5, bf16[322,1536]{1,0:T(8,128)(2,1)S(1)} %pad_maximum_fusion.2, s32[]{:T(128)S(6)} %select_n.162, bf16[384,768]{1,0:T(8,128)(2,1)} %collective-permute-done.7, bf16[384,768]{1,0:T(8,128)(2,1)} %collective-permute-done.6, pred[]{:T(512)S(6)} %eq.59), kind=kOutput, calls=%fused_computation.5 | convolution fusion | flops 385649664 | bytes 5425157 | tf_op jit(solution)/shard_map/dot_general | solution.py:92
  73.2 7.2 %collective-permute-done.12 = bf16[384,768]{1,0:T(8,128)(2,1)} collective-permute-done((bf16[384,768]{1,0:T(8,128)(2,1)}, bf16[384,768]{1,0:T(8,128)(2,1)}, u32[]{:S(2)}, u32[]{:S(2)}) %collective-permute-start.12) | collective-permute-done | bytes 589856 | tf_op jit(solution)/shard_map/ppermute | solution.py:63
  80.4 3.7 %convolution_add_fusion.1 = f32[322,1536]{1,0:T(8,128)} fusion(f32[322,1536]{1,0:T(8,128)S(1)} %convolution_add_fusion.2, bf16[322,1536]{1,0:T(8,128)(2,1)S(1)} %pad_maximum_fusion.2, s32[]{:T(128)S(6)} %select_n.162, bf16[384,768]{1,0:T(8,128)(2,1)} %collective-permute-done.12, bf16[384,768]{1,0:T(8,128)(2,1)} %collective-permute-done.11, pred[]{:T(512)S(6)} %eq.59), kind=kOutput, calls=%fused_computation.2 | convolution fusion | flops 385649664 | bytes 5425157 | tf_op jit(solution)/shard_map/dot_general | solution.py:92
  84.1 0.8 convolution_add_fusion.3
  85.1 0.7 multiply_reduce_fusion.5
  86.5 0.6 multiply_multiply_fusion
  87.2 3.2 %convolution_add_fusion = f32[322,1536]{1,0:T(8,128)S(1)} fusion(f32[322,1536]{1,0:T(8,128)} %convolution_add_fusion.1, bf16[322,1536]{1,0:T(8,128)(2,1)} %copy-done.9, s32[]{:T(128)S(6)} %select_n.167, bf16[384,768]{1,0:T(8,128)(2,1)} %collective-permute-done.14, bf16[384,768]{1,0:T(8,128)(2,1)} %collective-permute-done.13, pred[]{:T(512)S(6)} %eq.59), kind=kOutput, calls=%fused_computation.1 | convolution fusion | flops 385649664 | bytes 5425157 | tf_op jit(solution)/shard_map/dot_general | solution.py:92
  90.4 1.4 %multiply_reduce_fusion.3 = (f32[320]{0:T(512)S(1)}, f32[320,1536]{1,0:T(8,128)}) fusion(f32[322,1536]{1,0:T(8,128)S(1)} %convolution_add_fusion), kind=kLoop, calls=%fused_computation.24 | loop fusion | flops 982720 | bytes 3933440 | tf_op jit(solution)/shard_map/reduce_sum | solution.py:104
  91.8 0.6 multiply_reduce_fusion.6
  93.2 1.9 %slice_multiply_fusion.1 = f32[319,1536]{1,0:T(8,128)S(1)} fusion(f32[320,1536]{1,0:T(8,128)} %get-tuple-element.10, f32[319]{0:T(512)S(1)} %bitcast.76), kind=kLoop, calls=%fused_computation.16 | loop fusion | flops 489984 | bytes 3921148 | tf_op jit(solution)/shard_map/mul | solution.py:105
  95.3 0.6 multiply_reduce_fusion.2
  95.9 0.8 multiply_reduce_fusion
  97.6 0.9 copy-done.6
  98.5 0.7 fusion.72
  99.3 1.2 fusion.4
  101.6 0.6 pad_maximum_fusion.8
  102.2 1.5 %collective-permute-start.15 = (f32[1,1537]{1,0:T(1,128)S(1)}, f32[1,1537]{1,0:T(1,128)S(1)}, u32[]{:S(2)}, u32[]{:S(2)}) collective-permute-start(f32[1,1537]{1,0:T(1,128)S(1)} %pad_maximum_fusion.8), channel_id=1, source_target_pairs={{4,0},{8,4},{12,8},{16,12},{20,16},{24,20},{28,24},{5,1},{9,5},{13... | collective-permute-start | bytes 18452 | tf_op jit(solution)/shard_map/ppermute | solution.py:16
  103.7 0.7 fusion.6
  104.4 2.3 %fusion.31 = f32[320,384]{1,0:T(8,128)S(1)} fusion(bf16[320,1536]{1,0:T(8,128)(2,1)S(1)} %subtract_convert_fusion, bf16[384,768]{1,0:T(8,128)(2,1)} %collective-permute-done.14, bf16[384,768]{1,0:T(8,128)(2,1)} %collective-permute-done.13, pred[]{:T(512)S(6)} %eq.59), kind=kOutput, calls=%fused_computation.67 | convolution fusion | flops 382795776 | bytes 2654209 | tf_op jit(solution)/shard_map/dot_general | solution.py:196
  106.7 2.4 %fusion.32 = f32[320,384]{1,0:T(8,128)S(1)} fusion(bf16[320,1536]{1,0:T(8,128)(2,1)S(1)} %subtract_convert_fusion, bf16[384,768]{1,0:T(8,128)(2,1)} %collective-permute-done.12, bf16[384,768]{1,0:T(8,128)(2,1)} %collective-permute-done.11, pred[]{:T(512)S(6)} %eq.59), kind=kOutput, calls=%fused_computation.68 | convolution fusion | flops 382795776 | bytes 2654209 | tf_op jit(solution)/shard_map/dot_general | solution.py:196
  109.1 2.0 %fusion.73 = f32[320,384]{1,0:T(8,128)S(1)} fusion(bf16[320,1536]{1,0:T(8,128)(2,1)S(1)} %subtract_convert_fusion, bf16[384,1536]{1,0:T(8,128)(2,1)} %collective-permute-done.10), kind=kOutput, calls=%fused_computation.163 | convolution fusion | flops 377487360 | bytes 2654208 | tf_op jit(solution)/shard_map/dot_general | solution.py:196
  111.2 0.7 fusion.9
  111.9 2.4 %fusion.8 = bf16[320,384]{1,0:T(8,128)(2,1)S(1)} fusion(f32[320,384]{1,0:T(8,128)S(1)} %fusion.32, bf16[320,1536]{1,0:T(8,128)(2,1)S(1)} %get-tuple-element.8, bf16[384,768]{1,0:T(8,128)(2,1)} %collective-permute-done.7, bf16[384,768]{1,0:T(8,128)(2,1)} %collective-permute-done.6, pred[]{:T(512)S(6)} %eq.59), kind=kOutput, calls=%fused_computation.34 | convolution fusion | flops 383041536 | bytes 2899969 | tf_op jit(solution)/shard_map/dot_general | solution.py:195
  114.4 0.7 fusion.7
  117.0 1.3 collective-permute-start.16
  118.5 5.9 %collective-permute-done.16 = f32[1,1537]{1,0:T(1,128)S(1)} collective-permute-done((f32[1,1537]{1,0:T(1,128)S(1)}, f32[1,1537]{1,0:T(1,128)S(1)}, u32[]{:S(2)}, u32[]{:S(2)}) %collective-permute-start.16) | collective-permute-done | bytes 6180 | tf_op jit(solution)/shard_map/ppermute | solution.py:16
  124.3 0.6 slice.137
  125.7 1.3 collective-permute-start.17
  127.0 1.0 maximum_bitcast_fusion
  130.1 2.0 %collective-permute-done.17 = f32[1,1537]{1,0:T(1,128)S(1)} collective-permute-done((f32[1,1537]{1,0:T(1,128)S(1)}, f32[1,1537]{1,0:T(1,128)S(1)}, u32[]{:S(2)}, u32[]{:S(2)}) %collective-permute-start.17) | collective-permute-done | bytes 6180 | tf_op jit(solution)/shard_map/ppermute | solution.py:16
  132.1 1.7 %fusion.3 = bf16[1,128,1536]{2,1,0:T(8,128)(2,1)} fusion(f32[128,1536]{1,0:T(8,128)S(1)} %fusion.4, f32[1536]{0:T(1024)S(1)} %fusion.47, f32[128]{0:T(128)S(1)} %get-tuple-element.24, f32[128]{0:T(128)S(1)} %bitcast_select_fusion, f32[128]{0:T(128)S(1)} %reduce.2), kind=kOutput, calls=%fused_computation.13 | convolution fusion | flops 302841856 | bytes 1187328 | tf_op jit(solution)/shard_map/dot_general | solution.py:184
  (90 shorter events, 6.4 us)
Async XLA Ops:
  0.6 15.6 %copy-start.3 = (bf16[384,1536]{1,0:T(8,128)(2,1)S(1)}, bf16[384,1536]{1,0:T(8,128)(2,1)}, u32[]{:S(2)}) copy-start(bf16[384,1536]{1,0:T(8,128)(2,1)} %param.15) | copy-start | bytes 3538948
  0.6 15.6 %copy-start.10 = (s32[1,128]{1,0:T(1,128)S(1)}, s32[1,128]{1,0:T(1,128)}, u32[]{:S(2)}) copy-start(s32[1,128]{1,0:T(1,128)} %param.11) | copy-start | bytes 1540
  0.7 65.5 %collective-permute-start.5 = (bf16[384,1536]{1,0:T(8,128)(2,1)}, bf16[384,1536]{1,0:T(8,128)(2,1)S(1)}, u32[]{:S(2)}, u32[]{:S(2)}) collective-permute-start(bf16[384,1536]{1,0:T(8,128)(2,1)} %param.14), channel_id=1, source_target_pairs={{0,1},{1,0},{2,3},{3,2},{4,5},{5,4},{6,7},{7,6},{8,9},{9,8},{10,11... | collective-permute-start | bytes 3538952 | tf_op jit(solution)/shard_map/ppermute | solution.py:50
  2.8 32.8 %copy-start = (bf16[1,320,1536]{2,1,0:T(8,128)(2,1)S(1)}, bf16[1,320,1536]{2,1,0:T(8,128)(2,1)}, u32[]{:S(2)}) copy-start(bf16[1,320,1536]{2,1,0:T(8,128)(2,1)} %param.9) | copy-start | bytes 2949124
  8.3 11.2 %collective-permute-start.1 = (f32[1,1537]{1,0:T(1,128)S(1)}, f32[1,1537]{1,0:T(1,128)S(1)}, u32[]{:S(2)}, u32[]{:S(2)}) collective-permute-start(f32[1,1537]{1,0:T(1,128)S(1)} %pad_maximum_fusion.4), channel_id=1, source_target_pairs={{0,4},{4,8},{8,12},{12,16},{16,20},{20,24},{24,28},{1,5},{5,9},{9,... | collective-permute-start | bytes 18452 | tf_op jit(solution)/shard_map/ppermute | solution.py:16
  14.7 24.0 %collective-permute-start.6 = (bf16[384,768]{1,0:T(8,128)(2,1)}, bf16[384,768]{1,0:T(8,128)(2,1)}, u32[]{:S(2)}, u32[]{:S(2)}) collective-permute-start(bf16[384,768]{1,0:T(8,128)(2,1)} %constant_dynamic-slice_fusion.5), channel_id=1, source_target_pairs={{0,2},{1,3},{2,0},{3,1},{4,6},{5,7},{6,4},{7,5},{8,10},{9,11},{10,... | collective-permute-start | bytes 1769480 | tf_op jit(solution)/shard_map/ppermute | solution.py:61
  16.2 51.8 %collective-permute-start.10 = (bf16[384,1536]{1,0:T(8,128)(2,1)S(1)}, bf16[384,1536]{1,0:T(8,128)(2,1)}, u32[]{:S(2)}, u32[]{:S(2)}) collective-permute-start(bf16[384,1536]{1,0:T(8,128)(2,1)S(1)} %copy-done.3), channel_id=1, source_target_pairs={{0,1},{1,0},{2,3},{3,2},{4,5},{5,4},{6,7},{7,6},{8,9},{9,8},{10,11... | collective-permute-start | bytes 3538952 | tf_op jit(solution)/shard_map/ppermute | solution.py:50
  22.1 4.8 %collective-permute-start.2 = (f32[1,1537]{1,0:T(1,128)S(1)}, f32[1,1537]{1,0:T(1,128)S(1)}, u32[]{:S(2)}, u32[]{:S(2)}) collective-permute-start(f32[1,1537]{1,0:T(1,128)S(1)} %pad_maximum_fusion.5), channel_id=1, source_target_pairs={{0,8},{4,12},{8,16},{12,20},{16,24},{20,28},{1,9},{5,13},{9,17},{1... | collective-permute-start | bytes 18452 | tf_op jit(solution)/shard_map/ppermute | solution.py:16
  28.2 7.3 %collective-permute-start.3 = (f32[1,1537]{1,0:T(1,128)S(1)}, f32[1,1537]{1,0:T(1,128)S(1)}, u32[]{:S(2)}, u32[]{:S(2)}) collective-permute-start(f32[1,1537]{1,0:T(1,128)S(1)} %pad_maximum_fusion.6), channel_id=1, source_target_pairs={{0,16},{4,20},{8,24},{12,28},{1,17},{5,21},{9,25},{13,29},{2,18},{... | collective-permute-start | bytes 18452 | tf_op jit(solution)/shard_map/ppermute | solution.py:16
  38.7 23.9 %collective-permute-start.11 = (bf16[384,768]{1,0:T(8,128)(2,1)}, bf16[384,768]{1,0:T(8,128)(2,1)}, u32[]{:S(2)}, u32[]{:S(2)}) collective-permute-start(bf16[384,768]{1,0:T(8,128)(2,1)} %constant_dynamic-slice_fusion.4), channel_id=1, source_target_pairs={{0,2},{1,3},{2,0},{3,1},{4,6},{5,7},{6,4},{7,5},{8,10},{9,11},{10,... | collective-permute-start | bytes 1769480 | tf_op jit(solution)/shard_map/ppermute | solution.py:61
  39.2 27.1 %collective-permute-start.7 = (bf16[384,768]{1,0:T(8,128)(2,1)}, bf16[384,768]{1,0:T(8,128)(2,1)}, u32[]{:S(2)}, u32[]{:S(2)}) collective-permute-start(bf16[384,768]{1,0:T(8,128)(2,1)} %collective-permute-done.6), channel_id=1, source_target_pairs={{0,4},{4,0},{8,12},{12,8},{16,20},{20,16},{24,28},{28,24},{1,5},{5... | collective-permute-start | bytes 1769480 | tf_op jit(solution)/shard_map/ppermute | solution.py:63
  41.4 12.6 %collective-permute-start.4 = (f32[1,1537]{1,0:T(1,128)S(1)}, f32[1,1537]{1,0:T(1,128)S(1)}, u32[]{:S(2)}, u32[]{:S(2)}) collective-permute-start(f32[1,1537]{1,0:T(1,128)S(1)} %pad_maximum_fusion.7), channel_id=1, source_target_pairs={{4,0},{8,4},{12,8},{16,12},{20,16},{24,20},{28,24},{5,1},{9,5},{13... | collective-permute-start | bytes 18452 | tf_op jit(solution)/shard_map/ppermute | solution.py:16
  54.0 7.2 %collective-permute-start = (bf16[1,1536]{1,0:T(2,128)(2,1)S(1)}, bf16[1,1536]{1,0:T(2,128)(2,1)S(1)}, u32[]{:S(2)}, u32[]{:S(2)}) collective-permute-start(bf16[1,1536]{1,0:T(2,128)(2,1)S(1)} %get-tuple-element.15), channel_id=1, source_target_pairs={{0,4},{4,8},{8,12},{12,16},{16,20},{20,24},{24,28},{1,5},{5,9},{9,... | collective-permute-start | bytes 9224 | tf_op jit(solution)/shard_map/ppermute | solution.py:16
  62.5 21.6 %copy-start.9 = (bf16[322,1536]{1,0:T(8,128)(2,1)}, bf16[322,1536]{1,0:T(8,128)(2,1)S(1)}, u32[]{:S(2)}) copy-start(bf16[322,1536]{1,0:T(8,128)(2,1)S(1)} %pad_maximum_fusion.2) | copy-start | bytes 2967556
  62.5 4.9 %copy-start.5 = (bf16[384,1536]{1,0:T(8,128)(2,1)S(1)}, bf16[384,1536]{1,0:T(8,128)(2,1)}, u32[]{:S(2)}) copy-start(bf16[384,1536]{1,0:T(8,128)(2,1)} %param.14) | copy-start | bytes 3538948
  62.5 21.6 %collective-permute-start.8 = (bf16[384,768]{1,0:T(8,128)(2,1)}, bf16[384,768]{1,0:T(8,128)(2,1)S(1)}, u32[]{:S(2)}, u32[]{:S(2)}) collective-permute-start(bf16[384,768]{1,0:T(8,128)(2,1)} %collective-permute-done.6), channel_id=1, source_target_pairs={{0,1},{1,0},{2,3},{3,2},{4,5},{5,4},{6,7},{7,6},{8,9},{9,8},{10,11... | collective-permute-start | bytes 1769480 | tf_op jit(solution)/shard_map/ppermute | solution.py:64
  62.6 17.8 %collective-permute-start.12 = (bf16[384,768]{1,0:T(8,128)(2,1)}, bf16[384,768]{1,0:T(8,128)(2,1)}, u32[]{:S(2)}, u32[]{:S(2)}) collective-permute-start(bf16[384,768]{1,0:T(8,128)(2,1)} %collective-permute-done.11), channel_id=1, source_target_pairs={{0,4},{4,0},{8,12},{12,8},{16,20},{20,16},{24,28},{28,24},{1,5},{5... | collective-permute-start | bytes 1769480 | tf_op jit(solution)/shard_map/ppermute | solution.py:63
  66.2 1.9 %copy-start.7 = (bf16[384,1536]{1,0:T(8,128)(2,1)}, bf16[384,1536]{1,0:T(8,128)(2,1)S(1)}, u32[]{:S(2)}) copy-start(bf16[384,1536]{1,0:T(8,128)(2,1)S(1)} %collective-permute-done.5) | copy-start | bytes 3538948
  66.2 21.0 %collective-permute-start.13 = (bf16[384,768]{1,0:T(8,128)(2,1)}, bf16[384,768]{1,0:T(8,128)(2,1)}, u32[]{:S(2)}, u32[]{:S(2)}) collective-permute-start(bf16[384,768]{1,0:T(8,128)(2,1)} %collective-permute-done.11), channel_id=1, source_target_pairs={{0,1},{1,0},{2,3},{3,2},{4,5},{5,4},{6,7},{7,6},{8,9},{9,8},{10,11... | collective-permute-start | bytes 1769480 | tf_op jit(solution)/shard_map/ppermute | solution.py:64
  66.3 17.8 %collective-permute-start.9 = (bf16[384,768]{1,0:T(8,128)(2,1)}, bf16[384,768]{1,0:T(8,128)(2,1)S(1)}, u32[]{:S(2)}, u32[]{:S(2)}) collective-permute-start(bf16[384,768]{1,0:T(8,128)(2,1)} %collective-permute-done.7), channel_id=1, source_target_pairs={{0,1},{1,0},{2,3},{3,2},{4,5},{5,4},{6,7},{7,6},{8,9},{9,8},{10,11... | collective-permute-start | bytes 1769480 | tf_op jit(solution)/shard_map/ppermute | solution.py:65
  80.4 6.8 %collective-permute-start.14 = (bf16[384,768]{1,0:T(8,128)(2,1)}, bf16[384,768]{1,0:T(8,128)(2,1)}, u32[]{:S(2)}, u32[]{:S(2)}) collective-permute-start(bf16[384,768]{1,0:T(8,128)(2,1)} %collective-permute-done.12), channel_id=1, source_target_pairs={{0,1},{1,0},{2,3},{3,2},{4,5},{5,4},{6,7},{7,6},{8,9},{9,8},{10,11... | collective-permute-start | bytes 1769480 | tf_op jit(solution)/shard_map/ppermute | solution.py:65
  84.1 0.8 copy-start.11
  84.1 1.0 copy-start.13
  85.1 2.1 %copy-start.1 = (f32[322,1536]{1,0:T(8,128)}, f32[322,1536]{1,0:T(8,128)S(1)}, u32[]{:S(2)}) copy-start(f32[322,1536]{1,0:T(8,128)S(1)} %convolution_add_fusion.3) | copy-start | bytes 5935108
  93.1 2.2 %copy-start.2 = (f32[322,1536]{1,0:T(8,128)S(1)}, f32[322,1536]{1,0:T(8,128)}, u32[]{:S(2)}) copy-start(f32[322,1536]{1,0:T(8,128)} %copy-done.1) | copy-start | bytes 5935108
  97.3 1.3 copy-start.6
  99.2 4.5 %copy-start.4 = (bf16[384,1536]{1,0:T(8,128)(2,1)S(1)}, bf16[384,1536]{1,0:T(8,128)(2,1)}, u32[]{:S(2)}) copy-start(bf16[384,1536]{1,0:T(8,128)(2,1)} %param.15) | copy-start | bytes 3538948
  102.2 13.0 %collective-permute-start.15 = (f32[1,1537]{1,0:T(1,128)S(1)}, f32[1,1537]{1,0:T(1,128)S(1)}, u32[]{:S(2)}, u32[]{:S(2)}) collective-permute-start(f32[1,1537]{1,0:T(1,128)S(1)} %pad_maximum_fusion.8), channel_id=1, source_target_pairs={{4,0},{8,4},{12,8},{16,12},{20,16},{24,20},{28,24},{5,1},{9,5},{13... | collective-permute-start | bytes 18452 | tf_op jit(solution)/shard_map/ppermute | solution.py:16
  109.1 2.1 %copy-start.12 = (bf16[384,768]{1,0:T(8,128)(2,1)S(1)}, bf16[384,768]{1,0:T(8,128)(2,1)}, u32[]{:S(2)}) copy-start(bf16[384,768]{1,0:T(8,128)(2,1)} %copy-done.11) | copy-start | bytes 1769476
  109.1 2.1 %copy-start.14 = (bf16[384,768]{1,0:T(8,128)(2,1)S(1)}, bf16[384,768]{1,0:T(8,128)(2,1)}, u32[]{:S(2)}) copy-start(bf16[384,768]{1,0:T(8,128)(2,1)} %copy-done.13) | copy-start | bytes 1769476
  111.9 2.4 %copy-start.8 = (bf16[384,1536]{1,0:T(8,128)(2,1)S(1)}, bf16[384,1536]{1,0:T(8,128)(2,1)}, u32[]{:S(2)}) copy-start(bf16[384,1536]{1,0:T(8,128)(2,1)} %copy-done.7) | copy-start | bytes 3538948
  117.0 7.3 %collective-permute-start.16 = (f32[1,1537]{1,0:T(1,128)S(1)}, f32[1,1537]{1,0:T(1,128)S(1)}, u32[]{:S(2)}, u32[]{:S(2)}) collective-permute-start(f32[1,1537]{1,0:T(1,128)S(1)} %pad_maximum_fusion.9), channel_id=1, source_target_pairs={{8,0},{12,4},{16,8},{20,12},{24,16},{28,20},{9,1},{13,5},{17,9},{2... | collective-permute-start | bytes 18452 | tf_op jit(solution)/shard_map/ppermute | solution.py:16
  125.7 6.4 %collective-permute-start.17 = (f32[1,1537]{1,0:T(1,128)S(1)}, f32[1,1537]{1,0:T(1,128)S(1)}, u32[]{:S(2)}, u32[]{:S(2)}) collective-permute-start(f32[1,1537]{1,0:T(1,128)S(1)} %pad_maximum_fusion.10), channel_id=1, source_target_pairs={{16,0},{20,4},{24,8},{28,12},{17,1},{21,5},{25,9},{29,13},{18,2},{... | collective-permute-start | bytes 18452 | tf_op jit(solution)/shard_map/ppermute | solution.py:16

commit v16 on v9

--- a/solution.py
+++ b/solution.py
@@ -23,21 +23,19 @@
 
 def seq_scan(log_keep, vectors, axis, from_lower):
     size = lax.axis_size(axis)
+    width = vectors.shape[-1]
+    tail = jnp.zeros(vectors.shape[:-1] + (128,), vectors.dtype)
+    is_vec = jnp.arange(width + 128) < width
+    incl = jnp.concatenate([vectors, tail + log_keep], axis=-1)
+    excl = jnp.zeros_like(incl)
     step = 1
-    incl_log, incl_vec = log_keep, vectors
-    excl_log = jnp.zeros_like(log_keep)
-    excl_vec = jnp.zeros_like(vectors)
     while step < size:
-        packed = jnp.concatenate([incl_vec, incl_log], axis=-1)
-        got = shifted(packed, axis, step if from_lower else -step)
-        got_log, got_vec = got[:, -1:], got[:, :-1]
-        excl_vec = jnp.exp(excl_log) * got_vec + excl_vec
-        excl_log = excl_log + got_log
+        got = shifted(incl, axis, step if from_lower else -step)
+        excl = jnp.where(is_vec, jnp.exp(excl[:, width:width + 1]) * got, got) + excl
         if 2 * step < size:
-            incl_vec = jnp.exp(incl_log) * got_vec + incl_vec
-            incl_log = incl_log + got_log
+            incl = jnp.where(is_vec, jnp.exp(incl[:, width:width + 1]) * got, got) + incl
         step *= 2
-    return excl_vec
+    return excl[:, :width]
 
 
 def gather_blocks(blocks, axis):

time: 109 us -> 106 us (0.972)
  between operations: 14.8 us -> 10.6 us
  local copies, waits for them, and re-layouts: 11.9 us -> 14.2 us
  starting transfers between devices: 25.3 us -> 24.2 us
    ppermute x2, waiting for transfers between devices: 4.9 us -> 8.07 us  [gather_blocks(): pairs.append(lax.ppermute(blocks, axis, route))]
    ppermute x8, waiting for transfers between devices: 9.06 us -> 6.37 us  [shifted(): return lax.ppermute(block, axis, route)]
    concatenate x6 -> x0, other arithmetic: 1.45 us -> none  [seq_scan(): packed = jnp.concatenate([incl_vec, incl_log], axis=-1)]
    concatenate x0 -> x2, local copies, waits for them, and re-layouts: none -> 1.41 us  [seq_scan(): incl = jnp.concatenate([vectors, tail + log_keep], axis=-1)]
    add x6 -> x4, other arithmetic: 0.1 us -> 1.42 us  [seq_scan(): jnp.where(is_vec, jnp.exp(incl[:, width:width + 1]) * got, got) + incl]
    ppermute x8, starting transfers between devices: 21.1 us -> 20 us  [shifted(): return lax.ppermute(block, axis, route)]
    slice x4 -> x6, local copies, waits for them, and re-layouts: 2.14 us -> 3.08 us  [the longest x4 2.03 us: seq_scan(): excl[:, width:width + 1]]
  transfers between devices with their start and end apart: 14 -> 14, of which waited for: 4 -> 3; matrix products, arithmetic and copies ran while one was open for 33% -> 36% of each run, Pallas kernels for 0% -> 0%
where the time goes in v16:
time: 106 us; the launch traced here: 105 us
  matrix products  25 us (24%)
  starting transfers between devices  24.2 us (23%)
  other arithmetic  16.5 us (16%)
  waiting for transfers between devices  14.4 us (14%)
  local copies, waits for them, and re-layouts  14.2 us (13%)
  between operations  10.6 us (10%)
    ppermute x8, starting transfers between devices, shifted(): return lax.ppermute(block, axis, route)  20 us
    ppermute x2, waiting for transfers between devices, gather_blocks(): pairs.append(lax.ppermute(blocks, axis, route))  8.07 us
    dot_general x8, matrix products, split_dot(): term = jnp.dot(part, block, preferred_element_type=jnp.float32)  8.06 us
    ppermute x8, waiting for transfers between devices, shifted(): return lax.ppermute(block, axis, route)  6.37 us
    unnamed x30, local copies, waits for them, and re-layouts  4.81 us
    dot_general x4, matrix products, per_device(): lax.dot_general(key_grad, k_block, contract_last, preferred_element_type=...  4.12 us
    dot_general x4, matrix products, per_device(): lax.dot_general(query_grad, q_block, contract_last, preferred_element_typ...  4.05 us
    ppermute x2, starting transfers between devices, gather_blocks(): pairs.append(lax.ppermute(blocks, axis, route))  3.61 us
  transfers between devices with their start and end apart: 14, of which 3 were waited for; matrix products, arithmetic and copies ran while one was open for 36% of the time, Pallas kernels for 0%

profile of v16, /device:TPU:0, one launch (start us, length us, event | category | flops | bytes accessed | tf_op | source)
XLA Modules:
  0.0 105.1 jit_solution(12827642862096141317)
XLA Ops:
  0.6 3.0 %collective-permute-start.5 = (bf16[384,1536]{1,0:T(8,128)(2,1)}, bf16[384,1536]{1,0:T(8,128)(2,1)S(1)}, u32[]{:S(2)}, u32[]{:S(2)}) collective-permute-start(bf16[384,1536]{1,0:T(8,128)(2,1)} %param.14), channel_id=1, source_target_pairs={{0,2},{1,3},{2,0},{3,1},{4,6},{5,7},{6,4},{7,5},{8,10},{9,11},{10,... | collective-permute-start | bytes 3538952 | tf_op jit(solution)/shard_map/ppermute | solution.py:48
  4.3 0.7 bitcast_select_fusion
  5.0 0.7 fusion.64
  5.9 0.6 slice.113
  6.6 1.9 %fusion.14 = f32[128,1536]{1,0:T(8,128)S(1)} fusion(bf16[1,128,1536]{2,1,0:T(8,128)(2,1)} %param.10, f32[128]{0:T(128)S(1)} %bitcast_select_fusion, f32[128]{0:T(128)S(1)} %reduce.2), kind=kOutput, calls=%fused_computation.46 | convolution fusion | flops 302448640 | bytes 1180672 | tf_op jit(solution)/shard_map/dot_general | solution.py:126
  8.6 0.7 concatenate.24
  9.3 3.4 %collective-permute-start.1 = (f32[1,1664]{1,0:T(1,128)S(1)}, f32[1,1664]{1,0:T(1,128)S(1)}, u32[]{:S(2)}, u32[]{:S(2)}) collective-permute-start(f32[1,1664]{1,0:T(1,128)S(1)} %concatenate.24), channel_id=1, source_target_pairs={{0,4},{4,8},{8,12},{12,16},{16,20},{20,24},{24,28},{1,5},{5,9},{9,... | collective-permute-start | bytes 19976 | tf_op jit(solution)/shard_map/ppermute | solution.py:16
  12.7 0.8 slice_bitcast_fusion
  13.5 3.5 %collective-permute-start = (bf16[1,1536]{1,0:T(2,128)(2,1)S(1)}, bf16[1,1536]{1,0:T(2,128)(2,1)S(1)}, u32[]{:S(2)}, u32[]{:S(2)}) collective-permute-start(bf16[1,1536]{1,0:T(2,128)(2,1)S(1)} %get-tuple-element.13), channel_id=1, source_target_pairs={{0,4},{4,8},{8,12},{12,16},{16,20},{20,24},{24,28},{1,5},{5,9},{9,... | collective-permute-start | bytes 9224 | tf_op jit(solution)/shard_map/ppermute | solution.py:16
  16.9 0.6 collective-permute-start.8
  17.5 0.8 fusion.32
  18.3 0.8 convert_reduce_fusion
  19.1 0.7 subtract_exponential_fusion
  20.7 0.7 fusion.42
  21.4 3.5 %collective-permute-start.2 = (f32[1,1664]{1,0:T(1,128)S(1)}, f32[1,1664]{1,0:T(1,128)S(1)}, u32[]{:S(2)}, u32[]{:S(2)}) collective-permute-start(f32[1,1664]{1,0:T(1,128)S(1)} %fusion.42), channel_id=1, source_target_pairs={{0,8},{4,12},{8,16},{12,20},{16,24},{20,28},{1,9},{5,13},{9,17},{1... | collective-permute-start | bytes 19976 | tf_op jit(solution)/shard_map/ppermute | solution.py:16
  25.0 0.5 slice.116
  27.3 4.1 %collective-permute-start.3 = (f32[1,1664]{1,0:T(1,128)S(1)}, f32[1,1664]{1,0:T(1,128)S(1)}, u32[]{:S(2)}, u32[]{:S(2)}) collective-permute-start(f32[1,1664]{1,0:T(1,128)S(1)} %get-tuple-element.17), channel_id=1, source_target_pairs={{0,16},{4,20},{8,24},{12,28},{1,17},{5,21},{9,25},{13,29},{2,18},{... | collective-permute-start | bytes 19976 | tf_op jit(solution)/shard_map/ppermute | solution.py:16
  31.5 0.6 fusion.67
  32.1 0.5 slice.115
  33.3 3.0 %fusion.5 = f32[320]{0:T(512)S(1)} fusion(bf16[1,320,1536]{2,1,0:T(8,128)(2,1)} %param.9, f32[1536]{0:T(1024)S(1)} %fusion.51, f32[320]{0:T(512)S(1)} %compare_convert_fusion, f32[128,1536]{1,0:T(8,128)} %copy-done.14, f32[128]{0:T(128)S(1)} %get-tuple-element.27, s32[320]{0:T(512)S(1)} %get-tuple-element.23), kind=kOutput, calls=%fused_computation.27 | convolution fusion | flops 757866176 | bytes 1779968 | tf_op jit(solution)/shard_map/dot_general | solution.py:131
  36.4 0.5 slice.93
  36.9 0.7 pad_maximum_fusion.4
  37.5 1.5 %collective-permute-start.4 = (f32[1,1537]{1,0:T(1,128)S(1)}, f32[1,1537]{1,0:T(1,128)S(1)}, u32[]{:S(2)}, u32[]{:S(2)}) collective-permute-start(f32[1,1537]{1,0:T(1,128)S(1)} %pad_maximum_fusion.4), channel_id=1, source_target_pairs={{4,0},{8,4},{12,8},{16,12},{20,16},{24,20},{28,24},{5,1},{9,5},{13... | collective-permute-start | bytes 18452 | tf_op jit(solution)/shard_map/ppermute | solution.py:16
  41.5 2.4 %gather_fusion = f32[320]{0:T(512)S(1)} fusion(f32[128]{0:T(128)S(1)} %get-tuple-element.27, s32[1024]{0:T(1024)S(1)} %pad_clamp_fusion), kind=kCustom, calls=%fused_computation | custom fusion | bytes 3840 | tf_op jit(solution)/shard_map/gather | solution.py:134
  44.0 0.5 slice.128
  44.7 0.7 fusion.27
  45.3 0.6 copy-done.7
  45.9 0.7 convolution_add_fusion.5
  46.6 0.5 collective-permute-start.7
  47.2 8.1 %collective-permute-done.8 = bf16[384,1536]{1,0:T(8,128)(2,1)} collective-permute-done((bf16[384,1536]{1,0:T(8,128)(2,1)}, bf16[384,1536]{1,0:T(8,128)(2,1)}, u32[]{:S(2)}, u32[]{:S(2)}) %collective-permute-start.8) | collective-permute-done | bytes 1179680 | tf_op jit(solution)/shard_map/ppermute | solution.py:48
  55.2 1.9 %fusion.25 = f32[322,1536]{1,0:T(8,128)S(1)} fusion(bf16[384,1536]{1,0:T(8,128)(2,1)} %collective-permute-done.8, bf16[322,1536]{1,0:T(8,128)(2,1)S(1)} %pad_maximum_fusion.2, s32[]{:T(128)S(6)} %select_n.162), kind=kOutput, calls=%fused_computation.57 | convolution fusion | flops 379846656 | bytes 3409924 | tf_op jit(solution)/shard_map/dot_general | solution.py:73
  57.2 0.7 convolution_add_fusion.2
  57.9 2.0 %convolution_add_fusion.4 = f32[322,1536]{1,0:T(8,128)S(1)} fusion(f32[322,1536]{1,0:T(8,128)S(1)} %convolution_add_fusion.5, bf16[384,1536]{1,0:T(8,128)(2,1)} %collective-permute-done.6, bf16[322,1536]{1,0:T(8,128)(2,1)S(1)} %pad_maximum_fusion.2, s32[]{:T(128)S(6)} %select_n.163), kind=kOutput, calls=%fused_computation.5 | convolution fusion | flops 380341248 | bytes 5425156 | tf_op jit(solution)/shard_map/dot_general | solution.py:73
  59.9 0.7 convolution_add_fusion.1
  60.9 0.7 convolution_add_fusion
  62.0 0.7 multiply_reduce_fusion.6
  62.7 1.4 %multiply_reduce_fusion.3 = (f32[320]{0:T(512)S(1)}, f32[320,1536]{1,0:T(8,128)}) fusion(f32[322,1536]{1,0:T(8,128)S(1)} %convolution_add_fusion), kind=kLoop, calls=%fused_computation.24 | loop fusion | flops 982720 | bytes 3933440 | tf_op jit(solution)/shard_map/reduce_sum | solution.py:85
  64.2 0.7 convolution_add_fusion.3
  65.3 1.3 %copy-done = f32[322,1536]{1,0:T(8,128)} copy-done((f32[322,1536]{1,0:T(8,128)}, f32[322,1536]{1,0:T(8,128)S(1)}, u32[]{:S(2)}) %copy-start) | copy-done | bytes 1978392
  66.6 0.6 multiply_reduce_fusion.5
  68.7 1.4 %multiply_multiply_fusion = f32[1,1536]{1,0:T(1,128)S(1)} fusion(f32[322,1536]{1,0:T(8,128)} %copy-done, f32[]{:T(128)S(6)} %rsqrt.33, f32[]{:T(128)} %bitcast.15), kind=kLoop, calls=%fused_computation.100 | loop fusion | flops 3072 | bytes 12296 | tf_op jit(solution)/shard_map/mul | solution.py:172
  70.0 1.9 %slice_multiply_fusion.1 = f32[319,1536]{1,0:T(8,128)S(1)} fusion(f32[320,1536]{1,0:T(8,128)} %get-tuple-element.8, f32[319]{0:T(512)S(1)} %bitcast.84), kind=kLoop, calls=%fused_computation.16 | loop fusion | flops 489984 | bytes 3921148 | tf_op jit(solution)/shard_map/mul | solution.py:86
  72.2 0.6 multiply_reduce_fusion.2
  72.8 0.8 multiply_reduce_fusion
  74.5 0.9 copy-done.8
  75.4 0.7 fusion.68
  76.2 1.2 %fusion.4 = f32[128,1536]{1,0:T(8,128)S(1)} fusion(bf16[1,320,1536]{2,1,0:T(8,128)(2,1)S(1)} %copy-done.2, f32[320]{0:T(512)S(1)} %get-tuple-element.21, s32[320]{0:T(512)S(1)} %get-tuple-element.23), kind=kOutput, calls=%fused_computation.14 | convolution fusion | flops 755998720 | bytes 1772032 | tf_op jit(solution)/shard_map/dot_general | solution.py:158
  78.5 0.7 concatenate.31
  79.2 1.5 %collective-permute-start.11 = (f32[1,1664]{1,0:T(1,128)S(1)}, f32[1,1664]{1,0:T(1,128)S(1)}, u32[]{:S(2)}, u32[]{:S(2)}) collective-permute-start(f32[1,1664]{1,0:T(1,128)S(1)} %concatenate.31), channel_id=1, source_target_pairs={{4,0},{8,4},{12,8},{16,12},{20,16},{24,20},{28,24},{5,1},{9,5},{13... | collective-permute-start | bytes 19976 | tf_op jit(solution)/shard_map/ppermute | solution.py:16
  80.7 0.7 fusion.6
  81.4 0.7 fusion.71
  82.1 0.6 copy-done.10
  82.7 0.7 fusion.70
  83.4 2.1 %fusion.69 = f32[320,384]{1,0:T(8,128)S(1)} fusion(bf16[320,1536]{1,0:T(8,128)(2,1)S(1)} %subtract_convert_fusion, bf16[384,1536]{1,0:T(8,128)(2,1)} %collective-permute-done.8), kind=kOutput, calls=%fused_computation.150 | convolution fusion | flops 377487360 | bytes 2654208 | tf_op jit(solution)/shard_map/dot_general | solution.py:177
  85.5 0.7 fusion.9
  86.2 2.0 %fusion.8 = bf16[320,384]{1,0:T(8,128)(2,1)S(1)} fusion(f32[320,384]{1,0:T(8,128)S(1)} %fusion.70, bf16[320,1536]{1,0:T(8,128)(2,1)S(1)} %get-tuple-element.6, bf16[384,1536]{1,0:T(8,128)(2,1)} %collective-permute-done.6), kind=kOutput, calls=%fused_computation.34 | convolution fusion | flops 377733120 | bytes 2899968 | tf_op jit(solution)/shard_map/dot_general | solution.py:176
  88.1 0.7 fusion.7
  88.9 0.7 fusion.45
  89.6 1.3 %collective-permute-start.12 = (f32[1,1664]{1,0:T(1,128)S(1)}, f32[1,1664]{1,0:T(1,128)S(1)}, u32[]{:S(2)}, u32[]{:S(2)}) collective-permute-start(f32[1,1664]{1,0:T(1,128)S(1)} %fusion.45), channel_id=1, source_target_pairs={{8,0},{12,4},{16,8},{20,12},{24,16},{28,20},{9,1},{13,5},{17,9},{2... | collective-permute-start | bytes 19976 | tf_op jit(solution)/shard_map/ppermute | solution.py:16
  93.5 3.5 %collective-permute-done.12 = f32[1,1664]{1,0:T(1,128)S(1)} collective-permute-done((f32[1,1664]{1,0:T(1,128)S(1)}, f32[1,1664]{1,0:T(1,128)S(1)}, u32[]{:S(2)}, u32[]{:S(2)}) %collective-permute-start.12) | collective-permute-done | bytes 6688 | tf_op jit(solution)/shard_map/ppermute | solution.py:16
  96.9 1.3 %collective-permute-start.13 = (f32[1,1664]{1,0:T(1,128)S(1)}, f32[1,1664]{1,0:T(1,128)S(1)}, u32[]{:S(2)}, u32[]{:S(2)}) collective-permute-start(f32[1,1664]{1,0:T(1,128)S(1)} %get-tuple-element.15), channel_id=1, source_target_pairs={{16,0},{20,4},{24,8},{28,12},{17,1},{21,5},{25,9},{29,13},{18,2},{... | collective-permute-start | bytes 19976 | tf_op jit(solution)/shard_map/ppermute | solution.py:16
  98.2 1.0 maximum_bitcast_fusion
  100.5 2.9 %collective-permute-done.13 = f32[1,1664]{1,0:T(1,128)S(1)} collective-permute-done((f32[1,1664]{1,0:T(1,128)S(1)}, f32[1,1664]{1,0:T(1,128)S(1)}, u32[]{:S(2)}, u32[]{:S(2)}) %collective-permute-start.13) | collective-permute-done | bytes 6688 | tf_op jit(solution)/shard_map/ppermute | solution.py:16
  103.4 1.7 %fusion.3 = bf16[1,128,1536]{2,1,0:T(8,128)(2,1)} fusion(f32[128,1536]{1,0:T(8,128)S(1)} %fusion.4, f32[1536]{0:T(1024)S(1)} %fusion.50, f32[128]{0:T(128)S(1)} %get-tuple-element.26, f32[128]{0:T(128)S(1)} %bitcast_select_fusion, f32[128]{0:T(128)S(1)} %reduce.2), kind=kOutput, calls=%fused_computation.13 | convolution fusion | flops 302841856 | bytes 1187328 | tf_op jit(solution)/shard_map/dot_general | solution.py:165
  (79 shorter events, 6.5 us)
Async XLA Ops:
  0.6 44.0 %collective-permute-start.5 = (bf16[384,1536]{1,0:T(8,128)(2,1)}, bf16[384,1536]{1,0:T(8,128)(2,1)S(1)}, u32[]{:S(2)}, u32[]{:S(2)}) collective-permute-start(bf16[384,1536]{1,0:T(8,128)(2,1)} %param.14), channel_id=1, source_target_pairs={{0,2},{1,3},{2,0},{3,1},{4,6},{5,7},{6,4},{7,5},{8,10},{9,11},{10,... | collective-permute-start | bytes 3538952 | tf_op jit(solution)/shard_map/ppermute | solution.py:48
  3.7 54.2 %collective-permute-start.6 = (bf16[384,1536]{1,0:T(8,128)(2,1)}, bf16[384,1536]{1,0:T(8,128)(2,1)}, u32[]{:S(2)}, u32[]{:S(2)}) collective-permute-start(bf16[384,1536]{1,0:T(8,128)(2,1)} %param.14), channel_id=1, source_target_pairs={{0,1},{1,0},{2,3},{3,2},{4,5},{5,4},{6,7},{7,6},{8,9},{9,8},{10,11... | collective-permute-start | bytes 3538952 | tf_op jit(solution)/shard_map/ppermute | solution.py:51
  8.5 9.8 %copy-start.14 = (f32[128,1536]{1,0:T(8,128)}, f32[128,1536]{1,0:T(8,128)S(1)}, u32[]{:S(2)}) copy-start(f32[128,1536]{1,0:T(8,128)S(1)} %fusion.14) | copy-start | bytes 2359300
  9.3 11.4 %collective-permute-start.1 = (f32[1,1664]{1,0:T(1,128)S(1)}, f32[1,1664]{1,0:T(1,128)S(1)}, u32[]{:S(2)}, u32[]{:S(2)}) collective-permute-start(f32[1,1664]{1,0:T(1,128)S(1)} %concatenate.24), channel_id=1, source_target_pairs={{0,4},{4,8},{8,12},{12,16},{16,20},{20,24},{24,28},{1,5},{5,9},{9,... | collective-permute-start | bytes 19976 | tf_op jit(solution)/shard_map/ppermute | solution.py:16
  13.5 31.1 %collective-permute-start = (bf16[1,1536]{1,0:T(2,128)(2,1)S(1)}, bf16[1,1536]{1,0:T(2,128)(2,1)S(1)}, u32[]{:S(2)}, u32[]{:S(2)}) collective-permute-start(bf16[1,1536]{1,0:T(2,128)(2,1)S(1)} %get-tuple-element.13), channel_id=1, source_target_pairs={{0,4},{4,8},{8,12},{12,16},{16,20},{20,24},{24,28},{1,5},{5,9},{9,... | collective-permute-start | bytes 9224 | tf_op jit(solution)/shard_map/ppermute | solution.py:16
  16.9 38.3 %collective-permute-start.8 = (bf16[384,1536]{1,0:T(8,128)(2,1)}, bf16[384,1536]{1,0:T(8,128)(2,1)}, u32[]{:S(2)}, u32[]{:S(2)}) collective-permute-start(bf16[384,1536]{1,0:T(8,128)(2,1)} %param.15), channel_id=1, source_target_pairs={{0,2},{1,3},{2,0},{3,1},{4,6},{5,7},{6,4},{7,5},{8,10},{9,11},{10,... | collective-permute-start | bytes 3538952 | tf_op jit(solution)/shard_map/ppermute | solution.py:48
  21.4 5.9 %collective-permute-start.2 = (f32[1,1664]{1,0:T(1,128)S(1)}, f32[1,1664]{1,0:T(1,128)S(1)}, u32[]{:S(2)}, u32[]{:S(2)}) collective-permute-start(f32[1,1664]{1,0:T(1,128)S(1)} %fusion.42), channel_id=1, source_target_pairs={{0,8},{4,12},{8,16},{12,20},{16,24},{20,28},{1,9},{5,13},{9,17},{1... | collective-permute-start | bytes 19976 | tf_op jit(solution)/shard_map/ppermute | solution.py:16
  27.3 5.9 %collective-permute-start.3 = (f32[1,1664]{1,0:T(1,128)S(1)}, f32[1,1664]{1,0:T(1,128)S(1)}, u32[]{:S(2)}, u32[]{:S(2)}) collective-permute-start(f32[1,1664]{1,0:T(1,128)S(1)} %get-tuple-element.17), channel_id=1, source_target_pairs={{0,16},{4,20},{8,24},{12,28},{1,17},{5,21},{9,25},{13,29},{2,18},{... | collective-permute-start | bytes 19976 | tf_op jit(solution)/shard_map/ppermute | solution.py:16
  33.3 10.7 %copy-start.3 = (bf16[384,1536]{1,0:T(8,128)(2,1)S(1)}, bf16[384,1536]{1,0:T(8,128)(2,1)}, u32[]{:S(2)}) copy-start(bf16[384,1536]{1,0:T(8,128)(2,1)} %param.15) | copy-start | bytes 3538948
  33.3 11.2 %copy-start.13 = (bf16[1,320,1536]{2,1,0:T(8,128)(2,1)S(1)}, bf16[1,320,1536]{2,1,0:T(8,128)(2,1)}, u32[]{:S(2)}) copy-start(bf16[1,320,1536]{2,1,0:T(8,128)(2,1)} %param.8) | copy-start | bytes 2949124
  37.5 6.4 %collective-permute-start.4 = (f32[1,1537]{1,0:T(1,128)S(1)}, f32[1,1537]{1,0:T(1,128)S(1)}, u32[]{:S(2)}, u32[]{:S(2)}) collective-permute-start(f32[1,1537]{1,0:T(1,128)S(1)} %pad_maximum_fusion.4), channel_id=1, source_target_pairs={{4,0},{8,4},{12,8},{16,12},{20,16},{24,20},{28,24},{5,1},{9,5},{13... | collective-permute-start | bytes 18452 | tf_op jit(solution)/shard_map/ppermute | solution.py:16
  44.0 15.9 %collective-permute-start.9 = (bf16[384,1536]{1,0:T(8,128)(2,1)S(1)}, bf16[384,1536]{1,0:T(8,128)(2,1)S(1)}, u32[]{:S(2)}, u32[]{:S(2)}) collective-permute-start(bf16[384,1536]{1,0:T(8,128)(2,1)S(1)} %copy-done.3), channel_id=1, source_target_pairs={{0,1},{1,0},{2,3},{3,2},{4,5},{5,4},{6,7},{7,6},{8,9},{9,8},{10,11... | collective-permute-start | bytes 3538952 | tf_op jit(solution)/shard_map/ppermute | solution.py:51
  44.6 1.3 %copy-start.7 = (bf16[384,1536]{1,0:T(8,128)(2,1)S(1)}, bf16[384,1536]{1,0:T(8,128)(2,1)}, u32[]{:S(2)}) copy-start(bf16[384,1536]{1,0:T(8,128)(2,1)} %param.14) | copy-start | bytes 3538948
  46.6 17.5 %collective-permute-start.7 = (bf16[384,1536]{1,0:T(8,128)(2,1)S(1)}, bf16[384,1536]{1,0:T(8,128)(2,1)S(1)}, u32[]{:S(2)}, u32[]{:S(2)}) collective-permute-start(bf16[384,1536]{1,0:T(8,128)(2,1)S(1)} %collective-permute-done.5), channel_id=1, source_target_pairs={{0,1},{1,0},{2,3},{3,2},{4,5},{5,4},{6,7},{7,6},{8,9},{9,8},{10,11... | collective-permute-start | bytes 3538952 | tf_op jit(solution)/shard_map/ppermute | solution.py:51
  55.2 5.7 %collective-permute-start.10 = (bf16[384,1536]{1,0:T(8,128)(2,1)}, bf16[384,1536]{1,0:T(8,128)(2,1)S(1)}, u32[]{:S(2)}, u32[]{:S(2)}) collective-permute-start(bf16[384,1536]{1,0:T(8,128)(2,1)} %collective-permute-done.8), channel_id=1, source_target_pairs={{0,1},{1,0},{2,3},{3,2},{4,5},{5,4},{6,7},{7,6},{8,9},{9,8},{10,11... | collective-permute-start | bytes 3538952 | tf_op jit(solution)/shard_map/ppermute | solution.py:51
  59.9 1.0 copy-start.9
  60.9 1.1 %copy-start.11 = (bf16[384,1536]{1,0:T(8,128)(2,1)}, bf16[384,1536]{1,0:T(8,128)(2,1)S(1)}, u32[]{:S(2)}) copy-start(bf16[384,1536]{1,0:T(8,128)(2,1)S(1)} %collective-permute-done.10) | copy-start | bytes 3538948
  64.2 1.1 %copy-start.5 = (bf16[384,1536]{1,0:T(8,128)(2,1)}, bf16[384,1536]{1,0:T(8,128)(2,1)S(1)}, u32[]{:S(2)}) copy-start(bf16[384,1536]{1,0:T(8,128)(2,1)S(1)} %collective-permute-done.7) | copy-start | bytes 3538948
  65.3 1.3 %copy-start = (f32[322,1536]{1,0:T(8,128)}, f32[322,1536]{1,0:T(8,128)S(1)}, u32[]{:S(2)}) copy-start(f32[322,1536]{1,0:T(8,128)S(1)} %convolution_add_fusion.3) | copy-start | bytes 5935108
  70.0 2.2 %copy-start.1 = (f32[322,1536]{1,0:T(8,128)S(1)}, f32[322,1536]{1,0:T(8,128)}, u32[]{:S(2)}) copy-start(f32[322,1536]{1,0:T(8,128)} %copy-done) | copy-start | bytes 5935108
  74.2 1.3 %copy-start.8 = (bf16[384,1536]{1,0:T(8,128)(2,1)S(1)}, bf16[384,1536]{1,0:T(8,128)(2,1)}, u32[]{:S(2)}) copy-start(bf16[384,1536]{1,0:T(8,128)(2,1)} %param.14) | copy-start | bytes 3538948
  74.5 1.6 %copy-start.2 = (bf16[1,320,1536]{2,1,0:T(8,128)(2,1)S(1)}, bf16[1,320,1536]{2,1,0:T(8,128)(2,1)}, u32[]{:S(2)}) copy-start(bf16[1,320,1536]{2,1,0:T(8,128)(2,1)} %param.9) | copy-start | bytes 2949124
  76.1 4.6 %copy-start.4 = (bf16[384,1536]{1,0:T(8,128)(2,1)S(1)}, bf16[384,1536]{1,0:T(8,128)(2,1)}, u32[]{:S(2)}) copy-start(bf16[384,1536]{1,0:T(8,128)(2,1)} %param.15) | copy-start | bytes 3538948
  77.9 3.5 %copy-start.12 = (bf16[384,1536]{1,0:T(8,128)(2,1)S(1)}, bf16[384,1536]{1,0:T(8,128)(2,1)}, u32[]{:S(2)}) copy-start(bf16[384,1536]{1,0:T(8,128)(2,1)} %copy-done.11) | copy-start | bytes 3538948
  79.2 9.8 %collective-permute-start.11 = (f32[1,1664]{1,0:T(1,128)S(1)}, f32[1,1664]{1,0:T(1,128)S(1)}, u32[]{:S(2)}, u32[]{:S(2)}) collective-permute-start(f32[1,1664]{1,0:T(1,128)S(1)} %concatenate.31), channel_id=1, source_target_pairs={{4,0},{8,4},{12,8},{16,12},{20,16},{24,20},{28,24},{5,1},{9,5},{13... | collective-permute-start | bytes 19976 | tf_op jit(solution)/shard_map/ppermute | solution.py:16
  81.4 1.3 %copy-start.10 = (bf16[384,1536]{1,0:T(8,128)(2,1)S(1)}, bf16[384,1536]{1,0:T(8,128)(2,1)}, u32[]{:S(2)}) copy-start(bf16[384,1536]{1,0:T(8,128)(2,1)} %copy-done.9) | copy-start | bytes 3538948
  83.4 2.1 %copy-start.6 = (bf16[384,1536]{1,0:T(8,128)(2,1)S(1)}, bf16[384,1536]{1,0:T(8,128)(2,1)}, u32[]{:S(2)}) copy-start(bf16[384,1536]{1,0:T(8,128)(2,1)} %copy-done.5) | copy-start | bytes 3538948
  89.6 7.3 %collective-permute-start.12 = (f32[1,1664]{1,0:T(1,128)S(1)}, f32[1,1664]{1,0:T(1,128)S(1)}, u32[]{:S(2)}, u32[]{:S(2)}) collective-permute-start(f32[1,1664]{1,0:T(1,128)S(1)} %fusion.45), channel_id=1, source_target_pairs={{8,0},{12,4},{16,8},{20,12},{24,16},{28,20},{9,1},{13,5},{17,9},{2... | collective-permute-start | bytes 19976 | tf_op jit(solution)/shard_map/ppermute | solution.py:16
  96.9 6.4 %collective-permute-start.13 = (f32[1,1664]{1,0:T(1,128)S(1)}, f32[1,1664]{1,0:T(1,128)S(1)}, u32[]{:S(2)}, u32[]{:S(2)}) collective-permute-start(f32[1,1664]{1,0:T(1,128)S(1)} %get-tuple-element.15), channel_id=1, source_target_pairs={{16,0},{20,4},{24,8},{28,12},{17,1},{21,5},{25,9},{29,13},{18,2},{... | collective-permute-start | bytes 19976 | tf_op jit(solution)/shard_map/ppermute | solution.py:16

commit v17 on v16

--- a/solution.py
+++ b/solution.py
@@ -24,9 +24,8 @@
 def seq_scan(log_keep, vectors, axis, from_lower):
     size = lax.axis_size(axis)
     width = vectors.shape[-1]
-    tail = jnp.zeros(vectors.shape[:-1] + (128,), vectors.dtype)
     is_vec = jnp.arange(width + 128) < width
-    incl = jnp.concatenate([vectors, tail + log_keep], axis=-1)
+    incl = jnp.pad(vectors, ((0, 0), (0, 128))) + jnp.where(is_vec, 0.0, log_keep)
     excl = jnp.zeros_like(incl)
     step = 1
     while step < size:

time: 106 us -> 107 us (level)
  other arithmetic: 16.5 us -> 17.9 us
    concatenate x2 -> x0, local copies, waits for them, and re-layouts: 1.41 us -> none  [seq_scan(): incl = jnp.concatenate([vectors, tail + log_keep], axis=-1)]
    add x0 -> x2, other arithmetic: none -> 1.4 us  [seq_scan(): jnp.pad(vectors, ((0, 0), (0, 128))) + jnp.where(is_vec, 0.0, log_keep)]
  transfers between devices with their start and end apart: 14 -> 14, of which waited for: 3 -> 3; matrix products, arithmetic and copies ran while one was open for 36% -> 37% of each run, Pallas kernels for 0% -> 0%
where the time goes in v17:
time: 107 us; the launch traced here: 106 us
  matrix products  25 us (23%)
  starting transfers between devices  24.1 us (23%)
  other arithmetic  17.9 us (17%)
  waiting for transfers between devices  14 us (13%)
  local copies, waits for them, and re-layouts  13.8 us (13%)
  between operations  11.3 us (11%)
    ppermute x8, starting transfers between devices, shifted(): return lax.ppermute(block, axis, route)  19.9 us
    dot_general x8, matrix products, split_dot(): term = jnp.dot(part, block, preferred_element_type=jnp.float32)  8.06 us
    ppermute x2, waiting for transfers between devices, gather_blocks(): pairs.append(lax.ppermute(blocks, axis, route))  7.6 us
    ppermute x8, waiting for transfers between devices, shifted(): return lax.ppermute(block, axis, route)  6.38 us
    unnamed x30, local copies, waits for them, and re-layouts  4.8 us
    dot_general x4, matrix products, per_device(): lax.dot_general(key_grad, k_block, contract_last, preferred_element_type=...  4.12 us
    dot_general x4, matrix products, per_device(): lax.dot_general(query_grad, q_block, contract_last, preferred_element_typ...  4.05 us
    ppermute x2, starting transfers between devices, gather_blocks(): pairs.append(lax.ppermute(blocks, axis, route))  3.61 us
  transfers between devices with their start and end apart: 14, of which 3 were waited for; matrix products, arithmetic and copies ran while one was open for 37% of the time, Pallas kernels for 0%

profile of v17, /device:TPU:0, one launch (start us, length us, event | category | flops | bytes accessed | tf_op | source)
XLA Modules:
  0.0 106.2 jit_solution(11048901061961415531)
XLA Ops:
  0.6 3.0 %collective-permute-start.5 = (bf16[384,1536]{1,0:T(8,128)(2,1)}, bf16[384,1536]{1,0:T(8,128)(2,1)S(1)}, u32[]{:S(2)}, u32[]{:S(2)}) collective-permute-start(bf16[384,1536]{1,0:T(8,128)(2,1)} %param.14), channel_id=1, source_target_pairs={{0,2},{1,3},{2,0},{3,1},{4,6},{5,7},{6,4},{7,5},{8,10},{9,11},{10,... | collective-permute-start | bytes 3538952 | tf_op jit(solution)/shard_map/ppermute | solution.py:47
  4.3 0.7 bitcast_select_fusion
  5.0 0.7 fusion.65
  5.9 0.6 slice.119
  6.6 1.9 %fusion.14 = f32[128,1536]{1,0:T(8,128)S(1)} fusion(bf16[1,128,1536]{2,1,0:T(8,128)(2,1)} %param.10, f32[128]{0:T(128)S(1)} %bitcast_select_fusion, f32[128]{0:T(128)S(1)} %reduce.2), kind=kOutput, calls=%fused_computation.46 | convolution fusion | flops 302448640 | bytes 1180672 | tf_op jit(solution)/shard_map/dot_general | solution.py:125
  8.6 0.7 pad_add_fusion.1
  9.3 3.4 %collective-permute-start.1 = (f32[1,1664]{1,0:T(1,128)S(1)}, f32[1,1664]{1,0:T(1,128)S(1)}, u32[]{:S(2)}, u32[]{:S(2)}) collective-permute-start(f32[1,1664]{1,0:T(1,128)S(1)} %pad_add_fusion.1), channel_id=1, source_target_pairs={{0,4},{4,8},{8,12},{12,16},{16,20},{20,24},{24,28},{1,5},{5,9},{9,... | collective-permute-start | bytes 19976 | tf_op jit(solution)/shard_map/ppermute | solution.py:16
  12.7 0.8 slice_bitcast_fusion
  13.4 3.5 %collective-permute-start = (bf16[1,1536]{1,0:T(2,128)(2,1)S(1)}, bf16[1,1536]{1,0:T(2,128)(2,1)S(1)}, u32[]{:S(2)}, u32[]{:S(2)}) collective-permute-start(bf16[1,1536]{1,0:T(2,128)(2,1)S(1)} %get-tuple-element.13), channel_id=1, source_target_pairs={{0,4},{4,8},{8,12},{12,16},{16,20},{20,24},{24,28},{1,5},{5,9},{9,... | collective-permute-start | bytes 9224 | tf_op jit(solution)/shard_map/ppermute | solution.py:16
  16.9 0.6 collective-permute-start.8
  17.5 0.8 fusion.32
  18.3 0.8 convert_reduce_fusion
  19.1 0.7 subtract_exponential_fusion
  19.9 0.5 slice.121
  21.2 0.7 fusion.42
  21.9 3.5 %collective-permute-start.2 = (f32[1,1664]{1,0:T(1,128)S(1)}, f32[1,1664]{1,0:T(1,128)S(1)}, u32[]{:S(2)}, u32[]{:S(2)}) collective-permute-start(f32[1,1664]{1,0:T(1,128)S(1)} %fusion.42), channel_id=1, source_target_pairs={{0,8},{4,12},{8,16},{12,20},{16,24},{20,28},{1,9},{5,13},{9,17},{1... | collective-permute-start | bytes 19976 | tf_op jit(solution)/shard_map/ppermute | solution.py:16
  25.5 0.5 slice.123
  26.7 0.5 slice.120
  27.9 4.0 %collective-permute-start.3 = (f32[1,1664]{1,0:T(1,128)S(1)}, f32[1,1664]{1,0:T(1,128)S(1)}, u32[]{:S(2)}, u32[]{:S(2)}) collective-permute-start(f32[1,1664]{1,0:T(1,128)S(1)} %get-tuple-element.17), channel_id=1, source_target_pairs={{0,16},{4,20},{8,24},{12,28},{1,17},{5,21},{9,25},{13,29},{2,18},{... | collective-permute-start | bytes 19976 | tf_op jit(solution)/shard_map/ppermute | solution.py:16
  31.9 0.6 fusion.68
  33.8 3.0 %fusion.5 = f32[320]{0:T(512)S(1)} fusion(bf16[1,320,1536]{2,1,0:T(8,128)(2,1)} %param.9, f32[1536]{0:T(1024)S(1)} %fusion.51, f32[320]{0:T(512)S(1)} %compare_convert_fusion, f32[128,1536]{1,0:T(8,128)} %copy-done.14, f32[128]{0:T(128)S(1)} %get-tuple-element.27, s32[320]{0:T(512)S(1)} %get-tuple-element.23), kind=kOutput, calls=%fused_computation.27 | convolution fusion | flops 757866176 | bytes 1779968 | tf_op jit(solution)/shard_map/dot_general | solution.py:130
  36.8 0.5 slice.98
  37.4 0.7 pad_maximum_fusion.4
  38.0 1.5 %collective-permute-start.4 = (f32[1,1537]{1,0:T(1,128)S(1)}, f32[1,1537]{1,0:T(1,128)S(1)}, u32[]{:S(2)}, u32[]{:S(2)}) collective-permute-start(f32[1,1537]{1,0:T(1,128)S(1)} %pad_maximum_fusion.4), channel_id=1, source_target_pairs={{4,0},{8,4},{12,8},{16,12},{20,16},{24,20},{28,24},{5,1},{9,5},{13... | collective-permute-start | bytes 18452 | tf_op jit(solution)/shard_map/ppermute | solution.py:16
  42.0 2.4 %gather_fusion = f32[320]{0:T(512)S(1)} fusion(f32[128]{0:T(128)S(1)} %get-tuple-element.27, s32[1024]{0:T(1024)S(1)} %pad_clamp_fusion), kind=kCustom, calls=%fused_computation | custom fusion | bytes 3840 | tf_op jit(solution)/shard_map/gather | solution.py:133
  45.1 0.7 fusion.27
  45.8 0.6 copy-done.7
  46.4 0.7 convolution_add_fusion.5
  47.1 0.6 collective-permute-start.7
  47.6 7.6 %collective-permute-done.8 = bf16[384,1536]{1,0:T(8,128)(2,1)} collective-permute-done((bf16[384,1536]{1,0:T(8,128)(2,1)}, bf16[384,1536]{1,0:T(8,128)(2,1)}, u32[]{:S(2)}, u32[]{:S(2)}) %collective-permute-start.8) | collective-permute-done | bytes 1179680 | tf_op jit(solution)/shard_map/ppermute | solution.py:47
  55.2 1.9 %fusion.25 = f32[322,1536]{1,0:T(8,128)S(1)} fusion(bf16[384,1536]{1,0:T(8,128)(2,1)} %collective-permute-done.8, bf16[322,1536]{1,0:T(8,128)(2,1)S(1)} %pad_maximum_fusion.2, s32[]{:T(128)S(6)} %select_n.176), kind=kOutput, calls=%fused_computation.57 | convolution fusion | flops 379846656 | bytes 3409924 | tf_op jit(solution)/shard_map/dot_general | solution.py:72
  57.2 0.7 convolution_add_fusion.2
  57.9 2.0 %convolution_add_fusion.4 = f32[322,1536]{1,0:T(8,128)S(1)} fusion(f32[322,1536]{1,0:T(8,128)S(1)} %convolution_add_fusion.5, bf16[384,1536]{1,0:T(8,128)(2,1)} %collective-permute-done.6, bf16[322,1536]{1,0:T(8,128)(2,1)S(1)} %pad_maximum_fusion.2, s32[]{:T(128)S(6)} %select_n.177), kind=kOutput, calls=%fused_computation.5 | convolution fusion | flops 380341248 | bytes 5425156 | tf_op jit(solution)/shard_map/dot_general | solution.py:72
  59.9 0.7 convolution_add_fusion.1
  60.9 0.7 convolution_add_fusion
  62.0 0.6 multiply_reduce_fusion.6
  62.6 1.4 %multiply_reduce_fusion.3 = (f32[320]{0:T(512)S(1)}, f32[320,1536]{1,0:T(8,128)}) fusion(f32[322,1536]{1,0:T(8,128)S(1)} %convolution_add_fusion), kind=kLoop, calls=%fused_computation.24 | loop fusion | flops 982720 | bytes 3933440 | tf_op jit(solution)/shard_map/reduce_sum | solution.py:84
  64.1 0.7 convolution_add_fusion.3
  65.2 1.3 %copy-done = f32[322,1536]{1,0:T(8,128)} copy-done((f32[322,1536]{1,0:T(8,128)}, f32[322,1536]{1,0:T(8,128)S(1)}, u32[]{:S(2)}) %copy-start) | copy-done | bytes 1978392
  66.5 0.6 multiply_reduce_fusion.5
  68.5 1.5 %multiply_multiply_fusion = f32[1,1536]{1,0:T(1,128)S(1)} fusion(f32[322,1536]{1,0:T(8,128)} %copy-done, f32[]{:T(128)S(6)} %rsqrt.33, f32[]{:T(128)} %bitcast.15), kind=kLoop, calls=%fused_computation.102 | loop fusion | flops 3072 | bytes 12296 | tf_op jit(solution)/shard_map/mul | solution.py:171
  69.9 1.9 %slice_multiply_fusion.1 = f32[319,1536]{1,0:T(8,128)S(1)} fusion(f32[320,1536]{1,0:T(8,128)} %get-tuple-element.8, f32[319]{0:T(512)S(1)} %bitcast.85), kind=kLoop, calls=%fused_computation.16 | loop fusion | flops 489984 | bytes 3921148 | tf_op jit(solution)/shard_map/mul | solution.py:85
  72.1 0.6 multiply_reduce_fusion.2
  72.7 0.8 multiply_reduce_fusion
  74.4 0.9 copy-done.8
  75.3 0.7 fusion.69
  76.1 1.2 %fusion.4 = f32[128,1536]{1,0:T(8,128)S(1)} fusion(bf16[1,320,1536]{2,1,0:T(8,128)(2,1)S(1)} %copy-done.2, f32[320]{0:T(512)S(1)} %get-tuple-element.21, s32[320]{0:T(512)S(1)} %get-tuple-element.23), kind=kOutput, calls=%fused_computation.14 | convolution fusion | flops 755998720 | bytes 1772032 | tf_op jit(solution)/shard_map/dot_general | solution.py:157
  78.4 0.7 pad_add_fusion
  79.1 1.5 %collective-permute-start.11 = (f32[1,1664]{1,0:T(1,128)S(1)}, f32[1,1664]{1,0:T(1,128)S(1)}, u32[]{:S(2)}, u32[]{:S(2)}) collective-permute-start(f32[1,1664]{1,0:T(1,128)S(1)} %pad_add_fusion), channel_id=1, source_target_pairs={{4,0},{8,4},{12,8},{16,12},{20,16},{24,20},{28,24},{5,1},{9,5},{13... | collective-permute-start | bytes 19976 | tf_op jit(solution)/shard_map/ppermute | solution.py:16
  80.6 0.7 fusion.6
  81.3 0.7 fusion.72
  82.0 0.6 copy-done.10
  82.6 0.7 fusion.71
  83.3 2.1 %fusion.70 = f32[320,384]{1,0:T(8,128)S(1)} fusion(bf16[320,1536]{1,0:T(8,128)(2,1)S(1)} %subtract_convert_fusion, bf16[384,1536]{1,0:T(8,128)(2,1)} %collective-permute-done.8), kind=kOutput, calls=%fused_computation.153 | convolution fusion | flops 377487360 | bytes 2654208 | tf_op jit(solution)/shard_map/dot_general | solution.py:176
  85.3 0.7 fusion.9
  86.0 2.0 %fusion.8 = bf16[320,384]{1,0:T(8,128)(2,1)S(1)} fusion(f32[320,384]{1,0:T(8,128)S(1)} %fusion.71, bf16[320,1536]{1,0:T(8,128)(2,1)S(1)} %get-tuple-element.6, bf16[384,1536]{1,0:T(8,128)(2,1)} %collective-permute-done.6), kind=kOutput, calls=%fused_computation.34 | convolution fusion | flops 377733120 | bytes 2899968 | tf_op jit(solution)/shard_map/dot_general | solution.py:175
  88.0 0.7 fusion.7
  90.0 0.7 fusion.45
  90.7 1.3 %collective-permute-start.12 = (f32[1,1664]{1,0:T(1,128)S(1)}, f32[1,1664]{1,0:T(1,128)S(1)}, u32[]{:S(2)}, u32[]{:S(2)}) collective-permute-start(f32[1,1664]{1,0:T(1,128)S(1)} %fusion.45), channel_id=1, source_target_pairs={{8,0},{12,4},{16,8},{20,12},{24,16},{28,20},{9,1},{13,5},{17,9},{2... | collective-permute-start | bytes 19976 | tf_op jit(solution)/shard_map/ppermute | solution.py:16
  94.6 3.5 %collective-permute-done.12 = f32[1,1664]{1,0:T(1,128)S(1)} collective-permute-done((f32[1,1664]{1,0:T(1,128)S(1)}, f32[1,1664]{1,0:T(1,128)S(1)}, u32[]{:S(2)}, u32[]{:S(2)}) %collective-permute-start.12) | collective-permute-done | bytes 6688 | tf_op jit(solution)/shard_map/ppermute | solution.py:16
  98.0 1.3 %collective-permute-start.13 = (f32[1,1664]{1,0:T(1,128)S(1)}, f32[1,1664]{1,0:T(1,128)S(1)}, u32[]{:S(2)}, u32[]{:S(2)}) collective-permute-start(f32[1,1664]{1,0:T(1,128)S(1)} %get-tuple-element.15), channel_id=1, source_target_pairs={{16,0},{20,4},{24,8},{28,12},{17,1},{21,5},{25,9},{29,13},{18,2},{... | collective-permute-start | bytes 19976 | tf_op jit(solution)/shard_map/ppermute | solution.py:16
  99.3 1.0 maximum_bitcast_fusion
  101.6 2.9 %collective-permute-done.13 = f32[1,1664]{1,0:T(1,128)S(1)} collective-permute-done((f32[1,1664]{1,0:T(1,128)S(1)}, f32[1,1664]{1,0:T(1,128)S(1)}, u32[]{:S(2)}, u32[]{:S(2)}) %collective-permute-start.13) | collective-permute-done | bytes 6688 | tf_op jit(solution)/shard_map/ppermute | solution.py:16
  104.5 1.7 %fusion.3 = bf16[1,128,1536]{2,1,0:T(8,128)(2,1)} fusion(f32[128,1536]{1,0:T(8,128)S(1)} %fusion.4, f32[1536]{0:T(1024)S(1)} %fusion.50, f32[128]{0:T(128)S(1)} %get-tuple-element.26, f32[128]{0:T(128)S(1)} %bitcast_select_fusion, f32[128]{0:T(128)S(1)} %reduce.2), kind=kOutput, calls=%fused_computation.13 | convolution fusion | flops 302841856 | bytes 1187328 | tf_op jit(solution)/shard_map/dot_general | solution.py:164
  (81 shorter events, 7.5 us)
Async XLA Ops:
  0.6 44.5 %collective-permute-start.5 = (bf16[384,1536]{1,0:T(8,128)(2,1)}, bf16[384,1536]{1,0:T(8,128)(2,1)S(1)}, u32[]{:S(2)}, u32[]{:S(2)}) collective-permute-start(bf16[384,1536]{1,0:T(8,128)(2,1)} %param.14), channel_id=1, source_target_pairs={{0,2},{1,3},{2,0},{3,1},{4,6},{5,7},{6,4},{7,5},{8,10},{9,11},{10,... | collective-permute-start | bytes 3538952 | tf_op jit(solution)/shard_map/ppermute | solution.py:47
  3.7 54.2 %collective-permute-start.6 = (bf16[384,1536]{1,0:T(8,128)(2,1)}, bf16[384,1536]{1,0:T(8,128)(2,1)}, u32[]{:S(2)}, u32[]{:S(2)}) collective-permute-start(bf16[384,1536]{1,0:T(8,128)(2,1)} %param.14), channel_id=1, source_target_pairs={{0,1},{1,0},{2,3},{3,2},{4,5},{5,4},{6,7},{7,6},{8,9},{9,8},{10,11... | collective-permute-start | bytes 3538952 | tf_op jit(solution)/shard_map/ppermute | solution.py:50
  8.5 9.8 %copy-start.14 = (f32[128,1536]{1,0:T(8,128)}, f32[128,1536]{1,0:T(8,128)S(1)}, u32[]{:S(2)}) copy-start(f32[128,1536]{1,0:T(8,128)S(1)} %fusion.14) | copy-start | bytes 2359300
  9.3 11.9 %collective-permute-start.1 = (f32[1,1664]{1,0:T(1,128)S(1)}, f32[1,1664]{1,0:T(1,128)S(1)}, u32[]{:S(2)}, u32[]{:S(2)}) collective-permute-start(f32[1,1664]{1,0:T(1,128)S(1)} %pad_add_fusion.1), channel_id=1, source_target_pairs={{0,4},{4,8},{8,12},{12,16},{16,20},{20,24},{24,28},{1,5},{5,9},{9,... | collective-permute-start | bytes 19976 | tf_op jit(solution)/shard_map/ppermute | solution.py:16
  13.4 31.6 %collective-permute-start = (bf16[1,1536]{1,0:T(2,128)(2,1)S(1)}, bf16[1,1536]{1,0:T(2,128)(2,1)S(1)}, u32[]{:S(2)}, u32[]{:S(2)}) collective-permute-start(bf16[1,1536]{1,0:T(2,128)(2,1)S(1)} %get-tuple-element.13), channel_id=1, source_target_pairs={{0,4},{4,8},{8,12},{12,16},{16,20},{20,24},{24,28},{1,5},{5,9},{9,... | collective-permute-start | bytes 9224 | tf_op jit(solution)/shard_map/ppermute | solution.py:16
  16.9 38.3 %collective-permute-start.8 = (bf16[384,1536]{1,0:T(8,128)(2,1)}, bf16[384,1536]{1,0:T(8,128)(2,1)}, u32[]{:S(2)}, u32[]{:S(2)}) collective-permute-start(bf16[384,1536]{1,0:T(8,128)(2,1)} %param.15), channel_id=1, source_target_pairs={{0,2},{1,3},{2,0},{3,1},{4,6},{5,7},{6,4},{7,5},{8,10},{9,11},{10,... | collective-permute-start | bytes 3538952 | tf_op jit(solution)/shard_map/ppermute | solution.py:47
  21.9 6.0 %collective-permute-start.2 = (f32[1,1664]{1,0:T(1,128)S(1)}, f32[1,1664]{1,0:T(1,128)S(1)}, u32[]{:S(2)}, u32[]{:S(2)}) collective-permute-start(f32[1,1664]{1,0:T(1,128)S(1)} %fusion.42), channel_id=1, source_target_pairs={{0,8},{4,12},{8,16},{12,20},{16,24},{20,28},{1,9},{5,13},{9,17},{1... | collective-permute-start | bytes 19976 | tf_op jit(solution)/shard_map/ppermute | solution.py:16
  27.9 5.8 %collective-permute-start.3 = (f32[1,1664]{1,0:T(1,128)S(1)}, f32[1,1664]{1,0:T(1,128)S(1)}, u32[]{:S(2)}, u32[]{:S(2)}) collective-permute-start(f32[1,1664]{1,0:T(1,128)S(1)} %get-tuple-element.17), channel_id=1, source_target_pairs={{0,16},{4,20},{8,24},{12,28},{1,17},{5,21},{9,25},{13,29},{2,18},{... | collective-permute-start | bytes 19976 | tf_op jit(solution)/shard_map/ppermute | solution.py:16
  33.8 10.7 %copy-start.3 = (bf16[384,1536]{1,0:T(8,128)(2,1)S(1)}, bf16[384,1536]{1,0:T(8,128)(2,1)}, u32[]{:S(2)}) copy-start(bf16[384,1536]{1,0:T(8,128)(2,1)} %param.15) | copy-start | bytes 3538948
  33.8 11.2 %copy-start.13 = (bf16[1,320,1536]{2,1,0:T(8,128)(2,1)S(1)}, bf16[1,320,1536]{2,1,0:T(8,128)(2,1)}, u32[]{:S(2)}) copy-start(bf16[1,320,1536]{2,1,0:T(8,128)(2,1)} %param.8) | copy-start | bytes 2949124
  38.0 6.4 %collective-permute-start.4 = (f32[1,1537]{1,0:T(1,128)S(1)}, f32[1,1537]{1,0:T(1,128)S(1)}, u32[]{:S(2)}, u32[]{:S(2)}) collective-permute-start(f32[1,1537]{1,0:T(1,128)S(1)} %pad_maximum_fusion.4), channel_id=1, source_target_pairs={{4,0},{8,4},{12,8},{16,12},{20,16},{24,20},{28,24},{5,1},{9,5},{13... | collective-permute-start | bytes 18452 | tf_op jit(solution)/shard_map/ppermute | solution.py:16
  44.5 15.4 %collective-permute-start.9 = (bf16[384,1536]{1,0:T(8,128)(2,1)S(1)}, bf16[384,1536]{1,0:T(8,128)(2,1)S(1)}, u32[]{:S(2)}, u32[]{:S(2)}) collective-permute-start(bf16[384,1536]{1,0:T(8,128)(2,1)S(1)} %copy-done.3), channel_id=1, source_target_pairs={{0,1},{1,0},{2,3},{3,2},{4,5},{5,4},{6,7},{7,6},{8,9},{9,8},{10,11... | collective-permute-start | bytes 3538952 | tf_op jit(solution)/shard_map/ppermute | solution.py:50
  45.1 1.3 %copy-start.7 = (bf16[384,1536]{1,0:T(8,128)(2,1)S(1)}, bf16[384,1536]{1,0:T(8,128)(2,1)}, u32[]{:S(2)}) copy-start(bf16[384,1536]{1,0:T(8,128)(2,1)} %param.14) | copy-start | bytes 3538948
  47.1 17.0 %collective-permute-start.7 = (bf16[384,1536]{1,0:T(8,128)(2,1)S(1)}, bf16[384,1536]{1,0:T(8,128)(2,1)S(1)}, u32[]{:S(2)}, u32[]{:S(2)}) collective-permute-start(bf16[384,1536]{1,0:T(8,128)(2,1)S(1)} %collective-permute-done.5), channel_id=1, source_target_pairs={{0,1},{1,0},{2,3},{3,2},{4,5},{5,4},{6,7},{7,6},{8,9},{9,8},{10,11... | collective-permute-start | bytes 3538952 | tf_op jit(solution)/shard_map/ppermute | solution.py:50
  55.2 5.7 %collective-permute-start.10 = (bf16[384,1536]{1,0:T(8,128)(2,1)}, bf16[384,1536]{1,0:T(8,128)(2,1)S(1)}, u32[]{:S(2)}, u32[]{:S(2)}) collective-permute-start(bf16[384,1536]{1,0:T(8,128)(2,1)} %collective-permute-done.8), channel_id=1, source_target_pairs={{0,1},{1,0},{2,3},{3,2},{4,5},{5,4},{6,7},{7,6},{8,9},{9,8},{10,11... | collective-permute-start | bytes 3538952 | tf_op jit(solution)/shard_map/ppermute | solution.py:50
  59.9 1.0 copy-start.9
  60.9 1.1 %copy-start.11 = (bf16[384,1536]{1,0:T(8,128)(2,1)}, bf16[384,1536]{1,0:T(8,128)(2,1)S(1)}, u32[]{:S(2)}) copy-start(bf16[384,1536]{1,0:T(8,128)(2,1)S(1)} %collective-permute-done.10) | copy-start | bytes 3538948
  64.1 1.1 %copy-start.5 = (bf16[384,1536]{1,0:T(8,128)(2,1)}, bf16[384,1536]{1,0:T(8,128)(2,1)S(1)}, u32[]{:S(2)}) copy-start(bf16[384,1536]{1,0:T(8,128)(2,1)S(1)} %collective-permute-done.7) | copy-start | bytes 3538948
  65.2 1.3 %copy-start = (f32[322,1536]{1,0:T(8,128)}, f32[322,1536]{1,0:T(8,128)S(1)}, u32[]{:S(2)}) copy-start(f32[322,1536]{1,0:T(8,128)S(1)} %convolution_add_fusion.3) | copy-start | bytes 5935108
  69.9 2.2 %copy-start.1 = (f32[322,1536]{1,0:T(8,128)S(1)}, f32[322,1536]{1,0:T(8,128)}, u32[]{:S(2)}) copy-start(f32[322,1536]{1,0:T(8,128)} %copy-done) | copy-start | bytes 5935108
  74.0 1.3 %copy-start.8 = (bf16[384,1536]{1,0:T(8,128)(2,1)S(1)}, bf16[384,1536]{1,0:T(8,128)(2,1)}, u32[]{:S(2)}) copy-start(bf16[384,1536]{1,0:T(8,128)(2,1)} %param.14) | copy-start | bytes 3538948
  74.4 1.6 %copy-start.2 = (bf16[1,320,1536]{2,1,0:T(8,128)(2,1)S(1)}, bf16[1,320,1536]{2,1,0:T(8,128)(2,1)}, u32[]{:S(2)}) copy-start(bf16[1,320,1536]{2,1,0:T(8,128)(2,1)} %param.9) | copy-start | bytes 2949124
  76.0 4.6 %copy-start.4 = (bf16[384,1536]{1,0:T(8,128)(2,1)S(1)}, bf16[384,1536]{1,0:T(8,128)(2,1)}, u32[]{:S(2)}) copy-start(bf16[384,1536]{1,0:T(8,128)(2,1)} %param.15) | copy-start | bytes 3538948
  77.8 3.5 %copy-start.12 = (bf16[384,1536]{1,0:T(8,128)(2,1)S(1)}, bf16[384,1536]{1,0:T(8,128)(2,1)}, u32[]{:S(2)}) copy-start(bf16[384,1536]{1,0:T(8,128)(2,1)} %copy-done.11) | copy-start | bytes 3538948
  79.1 11.0 %collective-permute-start.11 = (f32[1,1664]{1,0:T(1,128)S(1)}, f32[1,1664]{1,0:T(1,128)S(1)}, u32[]{:S(2)}, u32[]{:S(2)}) collective-permute-start(f32[1,1664]{1,0:T(1,128)S(1)} %pad_add_fusion), channel_id=1, source_target_pairs={{4,0},{8,4},{12,8},{16,12},{20,16},{24,20},{28,24},{5,1},{9,5},{13... | collective-permute-start | bytes 19976 | tf_op jit(solution)/shard_map/ppermute | solution.py:16
  81.3 1.3 %copy-start.10 = (bf16[384,1536]{1,0:T(8,128)(2,1)S(1)}, bf16[384,1536]{1,0:T(8,128)(2,1)}, u32[]{:S(2)}) copy-start(bf16[384,1536]{1,0:T(8,128)(2,1)} %copy-done.9) | copy-start | bytes 3538948
  83.3 2.1 %copy-start.6 = (bf16[384,1536]{1,0:T(8,128)(2,1)S(1)}, bf16[384,1536]{1,0:T(8,128)(2,1)}, u32[]{:S(2)}) copy-start(bf16[384,1536]{1,0:T(8,128)(2,1)} %copy-done.5) | copy-start | bytes 3538948
  90.7 7.3 %collective-permute-start.12 = (f32[1,1664]{1,0:T(1,128)S(1)}, f32[1,1664]{1,0:T(1,128)S(1)}, u32[]{:S(2)}, u32[]{:S(2)}) collective-permute-start(f32[1,1664]{1,0:T(1,128)S(1)} %fusion.45), channel_id=1, source_target_pairs={{8,0},{12,4},{16,8},{20,12},{24,16},{28,20},{9,1},{13,5},{17,9},{2... | collective-permute-start | bytes 19976 | tf_op jit(solution)/shard_map/ppermute | solution.py:16
  98.0 6.4 %collective-permute-start.13 = (f32[1,1664]{1,0:T(1,128)S(1)}, f32[1,1664]{1,0:T(1,128)S(1)}, u32[]{:S(2)}, u32[]{:S(2)}) collective-permute-start(f32[1,1664]{1,0:T(1,128)S(1)} %get-tuple-element.15), channel_id=1, source_target_pairs={{16,0},{20,4},{24,8},{28,12},{17,1},{21,5},{25,9},{29,13},{18,2},{... | collective-permute-start | bytes 19976 | tf_op jit(solution)/shard_map/ppermute | solution.py:16

commit v18 on v16

--- a/solution.py
+++ b/solution.py
@@ -161,10 +161,10 @@
     )
     grad_in = seq_scan(last_log, back_vector, "seq", False)
     reach_end = jnp.exp(running[slot_count - 1] - running)
-    state_grad = (
+    state_local = lax.optimization_barrier(
         lax.dot_general(decay_table, slot_grad, contract_first, precision=exact)
-        + reach_end[:, None] * grad_in
-    )
+    )
+    state_grad = state_local + reach_end[:, None] * grad_in
     segment_grad = (smoothing[:, None] * state_grad).astype(jnp.bfloat16)
     unit_q_grad = cos_grad[:, None] * key_prior
     prior_grad = cos_grad[:, None] * query_unit

time: 106 us -> 106 us (level)
  no operation moved by 1% of the time
where the time goes in v18:
time: 106 us; the launch traced here: 105 us
  matrix products  24.3 us (23%)
  starting transfers between devices  24.2 us (23%)
  other arithmetic  17.5 us (17%)
  waiting for transfers between devices  14.5 us (14%)
  local copies, waits for them, and re-layouts  14.2 us (13%)
  between operations  10.7 us (10%)
    ppermute x8, starting transfers between devices, shifted(): return lax.ppermute(block, axis, route)  20 us
    ppermute x2, waiting for transfers between devices, gather_blocks(): pairs.append(lax.ppermute(blocks, axis, route))  8.07 us
    dot_general x8, matrix products, split_dot(): term = jnp.dot(part, block, preferred_element_type=jnp.float32)  8.06 us
    ppermute x8, waiting for transfers between devices, shifted(): return lax.ppermute(block, axis, route)  6.37 us
    unnamed x30, local copies, waits for them, and re-layouts  4.81 us
    dot_general x4, matrix products, per_device(): lax.dot_general(key_grad, k_block, contract_last, preferred_element_type=...  4.12 us
    dot_general x4, matrix products, per_device(): lax.dot_general(query_grad, q_block, contract_last, preferred_element_typ...  4.06 us
    ppermute x2, starting transfers between devices, gather_blocks(): pairs.append(lax.ppermute(blocks, axis, route))  3.61 us
  transfers between devices with their start and end apart: 14, of which 3 were waited for; matrix products, arithmetic and copies ran while one was open for 36% of the time, Pallas kernels for 0%

profile of v18, /device:TPU:0, one launch (start us, length us, event | category | flops | bytes accessed | tf_op | source)
XLA Modules:
  0.0 105.3 jit_solution(13936906346871672171)
XLA Ops:
  0.6 3.0 %collective-permute-start.5 = (bf16[384,1536]{1,0:T(8,128)(2,1)}, bf16[384,1536]{1,0:T(8,128)(2,1)S(1)}, u32[]{:S(2)}, u32[]{:S(2)}) collective-permute-start(bf16[384,1536]{1,0:T(8,128)(2,1)} %param.14), channel_id=1, source_target_pairs={{0,2},{1,3},{2,0},{3,1},{4,6},{5,7},{6,4},{7,5},{8,10},{9,11},{10,... | collective-permute-start | bytes 3538952 | tf_op jit(solution)/shard_map/ppermute | solution.py:48
  4.3 0.7 bitcast_select_fusion
  5.0 0.7 fusion.63
  5.9 0.6 slice.113
  6.6 1.9 %fusion.11 = f32[128,1536]{1,0:T(8,128)S(1)} fusion(bf16[1,128,1536]{2,1,0:T(8,128)(2,1)} %param.10, f32[128]{0:T(128)S(1)} %bitcast_select_fusion, f32[128]{0:T(128)S(1)} %reduce.2), kind=kOutput, calls=%fused_computation.42 | convolution fusion | flops 302448640 | bytes 1180672 | tf_op jit(solution)/shard_map/dot_general | solution.py:126
  8.6 0.7 concatenate.24
  9.3 3.4 %collective-permute-start.1 = (f32[1,1664]{1,0:T(1,128)S(1)}, f32[1,1664]{1,0:T(1,128)S(1)}, u32[]{:S(2)}, u32[]{:S(2)}) collective-permute-start(f32[1,1664]{1,0:T(1,128)S(1)} %concatenate.24), channel_id=1, source_target_pairs={{0,4},{4,8},{8,12},{12,16},{16,20},{20,24},{24,28},{1,5},{5,9},{9,... | collective-permute-start | bytes 19976 | tf_op jit(solution)/shard_map/ppermute | solution.py:16
  12.7 0.8 slice_bitcast_fusion
  13.5 3.5 %collective-permute-start = (bf16[1,1536]{1,0:T(2,128)(2,1)S(1)}, bf16[1,1536]{1,0:T(2,128)(2,1)S(1)}, u32[]{:S(2)}, u32[]{:S(2)}) collective-permute-start(bf16[1,1536]{1,0:T(2,128)(2,1)S(1)} %get-tuple-element.13), channel_id=1, source_target_pairs={{0,4},{4,8},{8,12},{12,16},{16,20},{20,24},{24,28},{1,5},{5,9},{9,... | collective-permute-start | bytes 9224 | tf_op jit(solution)/shard_map/ppermute | solution.py:16
  16.9 0.6 collective-permute-start.8
  17.5 0.8 fusion.30
  18.3 0.8 convert_reduce_fusion
  19.1 0.7 subtract_exponential_fusion
  20.7 0.7 fusion.41
  21.4 3.5 %collective-permute-start.2 = (f32[1,1664]{1,0:T(1,128)S(1)}, f32[1,1664]{1,0:T(1,128)S(1)}, u32[]{:S(2)}, u32[]{:S(2)}) collective-permute-start(f32[1,1664]{1,0:T(1,128)S(1)} %fusion.41), channel_id=1, source_target_pairs={{0,8},{4,12},{8,16},{12,20},{16,24},{20,28},{1,9},{5,13},{9,17},{1... | collective-permute-start | bytes 19976 | tf_op jit(solution)/shard_map/ppermute | solution.py:16
  25.0 0.5 slice.116
  27.3 4.1 %collective-permute-start.3 = (f32[1,1664]{1,0:T(1,128)S(1)}, f32[1,1664]{1,0:T(1,128)S(1)}, u32[]{:S(2)}, u32[]{:S(2)}) collective-permute-start(f32[1,1664]{1,0:T(1,128)S(1)} %get-tuple-element.17), channel_id=1, source_target_pairs={{0,16},{4,20},{8,24},{12,28},{1,17},{5,21},{9,25},{13,29},{2,18},{... | collective-permute-start | bytes 19976 | tf_op jit(solution)/shard_map/ppermute | solution.py:16
  31.5 0.6 fusion.66
  32.1 0.5 slice.115
  33.3 3.0 %fusion.2 = f32[320]{0:T(512)S(1)} fusion(bf16[1,320,1536]{2,1,0:T(8,128)(2,1)} %param.9, f32[1536]{0:T(1024)S(1)} %fusion.50, f32[320]{0:T(512)S(1)} %compare_convert_fusion, f32[128,1536]{1,0:T(8,128)} %copy-done.14, f32[128]{0:T(128)S(1)} %get-tuple-element.27, s32[320]{0:T(512)S(1)} %get-tuple-element.23), kind=kOutput, calls=%fused_computation.23 | convolution fusion | flops 757866176 | bytes 1779968 | tf_op jit(solution)/shard_map/dot_general | solution.py:131
  36.9 0.7 pad_maximum_fusion.4
  37.5 1.5 %collective-permute-start.4 = (f32[1,1537]{1,0:T(1,128)S(1)}, f32[1,1537]{1,0:T(1,128)S(1)}, u32[]{:S(2)}, u32[]{:S(2)}) collective-permute-start(f32[1,1537]{1,0:T(1,128)S(1)} %pad_maximum_fusion.4), channel_id=1, source_target_pairs={{4,0},{8,4},{12,8},{16,12},{20,16},{24,20},{28,24},{5,1},{9,5},{13... | collective-permute-start | bytes 18452 | tf_op jit(solution)/shard_map/ppermute | solution.py:16
  41.5 2.4 %gather_fusion = f32[320]{0:T(512)S(1)} fusion(f32[128]{0:T(128)S(1)} %get-tuple-element.27, s32[1024]{0:T(1024)S(1)} %pad_clamp_fusion), kind=kCustom, calls=%fused_computation | custom fusion | bytes 3840 | tf_op jit(solution)/shard_map/gather | solution.py:134
  44.0 0.5 slice.128
  44.7 0.7 fusion.25
  45.3 0.6 copy-done.7
  45.9 0.7 convolution_add_fusion.5
  46.6 0.5 collective-permute-start.7
  47.2 8.1 %collective-permute-done.8 = bf16[384,1536]{1,0:T(8,128)(2,1)} collective-permute-done((bf16[384,1536]{1,0:T(8,128)(2,1)}, bf16[384,1536]{1,0:T(8,128)(2,1)}, u32[]{:S(2)}, u32[]{:S(2)}) %collective-permute-start.8) | collective-permute-done | bytes 1179680 | tf_op jit(solution)/shard_map/ppermute | solution.py:48
  55.2 1.9 %fusion.23 = f32[322,1536]{1,0:T(8,128)S(1)} fusion(bf16[384,1536]{1,0:T(8,128)(2,1)} %collective-permute-done.8, bf16[322,1536]{1,0:T(8,128)(2,1)S(1)} %pad_maximum_fusion.2, s32[]{:T(128)S(6)} %select_n.162), kind=kOutput, calls=%fused_computation.55 | convolution fusion | flops 379846656 | bytes 3409924 | tf_op jit(solution)/shard_map/dot_general | solution.py:73
  57.2 0.7 convolution_add_fusion.2
  57.9 2.0 %convolution_add_fusion.4 = f32[322,1536]{1,0:T(8,128)S(1)} fusion(f32[322,1536]{1,0:T(8,128)S(1)} %convolution_add_fusion.5, bf16[384,1536]{1,0:T(8,128)(2,1)} %collective-permute-done.6, bf16[322,1536]{1,0:T(8,128)(2,1)S(1)} %pad_maximum_fusion.2, s32[]{:T(128)S(6)} %select_n.163), kind=kOutput, calls=%fused_computation.5 | convolution fusion | flops 380341248 | bytes 5425156 | tf_op jit(solution)/shard_map/dot_general | solution.py:73
  59.9 0.7 convolution_add_fusion.1
  60.9 0.7 convolution_add_fusion
  62.0 0.7 multiply_reduce_fusion.6
  62.7 1.4 %multiply_reduce_fusion.3 = (f32[320]{0:T(512)S(1)}, f32[320,1536]{1,0:T(8,128)}) fusion(f32[322,1536]{1,0:T(8,128)S(1)} %convolution_add_fusion), kind=kLoop, calls=%fused_computation.20 | loop fusion | flops 982720 | bytes 3933440 | tf_op jit(solution)/shard_map/reduce_sum | solution.py:85
  64.2 0.7 convolution_add_fusion.3
  65.3 1.3 %copy-done = f32[322,1536]{1,0:T(8,128)} copy-done((f32[322,1536]{1,0:T(8,128)}, f32[322,1536]{1,0:T(8,128)S(1)}, u32[]{:S(2)}) %copy-start) | copy-done | bytes 1978392
  66.6 0.6 multiply_reduce_fusion.5
  68.7 1.4 %multiply_multiply_fusion = f32[1,1536]{1,0:T(1,128)S(1)} fusion(f32[322,1536]{1,0:T(8,128)} %copy-done, f32[]{:T(128)S(6)} %rsqrt.33, f32[]{:T(128)} %bitcast.15), kind=kLoop, calls=%fused_computation.99 | loop fusion | flops 3072 | bytes 12296 | tf_op jit(solution)/shard_map/mul | solution.py:172
  70.0 1.9 %slice_multiply_fusion.1 = f32[319,1536]{1,0:T(8,128)S(1)} fusion(f32[320,1536]{1,0:T(8,128)} %get-tuple-element.8, f32[319]{0:T(512)S(1)} %bitcast.84), kind=kLoop, calls=%fused_computation.12 | loop fusion | flops 489984 | bytes 3921148 | tf_op jit(solution)/shard_map/mul | solution.py:86
  72.2 0.6 multiply_reduce_fusion.2
  72.8 0.8 multiply_reduce_fusion
  74.5 0.9 copy-done.8
  75.4 0.7 fusion.67
  76.2 1.2 %fusion.1 = f32[128,1536]{1,0:T(8,128)S(1)} fusion(bf16[1,320,1536]{2,1,0:T(8,128)(2,1)S(1)} %copy-done.2, f32[320]{0:T(512)S(1)} %get-tuple-element.21, s32[320]{0:T(512)S(1)} %get-tuple-element.23), kind=kOutput, calls=%fused_computation.10 | convolution fusion | flops 755998720 | bytes 1772032 | tf_op jit(solution)/shard_map/dot_general | solution.py:158
  77.4 0.9 fusion.34
  79.4 0.7 concatenate.31
  80.1 1.5 %collective-permute-start.11 = (f32[1,1664]{1,0:T(1,128)S(1)}, f32[1,1664]{1,0:T(1,128)S(1)}, u32[]{:S(2)}, u32[]{:S(2)}) collective-permute-start(f32[1,1664]{1,0:T(1,128)S(1)} %concatenate.31), channel_id=1, source_target_pairs={{4,0},{8,4},{12,8},{16,12},{20,16},{24,20},{28,24},{5,1},{9,5},{13... | collective-permute-start | bytes 19976 | tf_op jit(solution)/shard_map/ppermute | solution.py:16
  81.6 0.7 fusion.3
  82.4 0.7 fusion.70
  83.0 0.6 copy-done.10
  83.6 0.7 fusion.69
  84.3 2.1 %fusion.68 = f32[320,384]{1,0:T(8,128)S(1)} fusion(bf16[320,1536]{1,0:T(8,128)(2,1)S(1)} %subtract_convert_fusion, bf16[384,1536]{1,0:T(8,128)(2,1)} %collective-permute-done.8), kind=kOutput, calls=%fused_computation.149 | convolution fusion | flops 377487360 | bytes 2654208 | tf_op jit(solution)/shard_map/dot_general | solution.py:177
  86.4 0.7 fusion.6
  87.1 2.0 %fusion.5 = bf16[320,384]{1,0:T(8,128)(2,1)S(1)} fusion(f32[320,384]{1,0:T(8,128)S(1)} %fusion.69, bf16[320,1536]{1,0:T(8,128)(2,1)S(1)} %get-tuple-element.6, bf16[384,1536]{1,0:T(8,128)(2,1)} %collective-permute-done.6), kind=kOutput, calls=%fused_computation.30 | convolution fusion | flops 377733120 | bytes 2899968 | tf_op jit(solution)/shard_map/dot_general | solution.py:176
  89.1 0.7 fusion.4
  89.9 0.7 fusion.44
  90.6 1.3 %collective-permute-start.12 = (f32[1,1664]{1,0:T(1,128)S(1)}, f32[1,1664]{1,0:T(1,128)S(1)}, u32[]{:S(2)}, u32[]{:S(2)}) collective-permute-start(f32[1,1664]{1,0:T(1,128)S(1)} %fusion.44), channel_id=1, source_target_pairs={{8,0},{12,4},{16,8},{20,12},{24,16},{28,20},{9,1},{13,5},{17,9},{2... | collective-permute-start | bytes 19976 | tf_op jit(solution)/shard_map/ppermute | solution.py:16
  94.4 3.5 %collective-permute-done.12 = f32[1,1664]{1,0:T(1,128)S(1)} collective-permute-done((f32[1,1664]{1,0:T(1,128)S(1)}, f32[1,1664]{1,0:T(1,128)S(1)}, u32[]{:S(2)}, u32[]{:S(2)}) %collective-permute-start.12) | collective-permute-done | bytes 6688 | tf_op jit(solution)/shard_map/ppermute | solution.py:16
  97.9 1.3 %collective-permute-start.13 = (f32[1,1664]{1,0:T(1,128)S(1)}, f32[1,1664]{1,0:T(1,128)S(1)}, u32[]{:S(2)}, u32[]{:S(2)}) collective-permute-start(f32[1,1664]{1,0:T(1,128)S(1)} %get-tuple-element.15), channel_id=1, source_target_pairs={{16,0},{20,4},{24,8},{28,12},{17,1},{21,5},{25,9},{29,13},{18,2},{... | collective-permute-start | bytes 19976 | tf_op jit(solution)/shard_map/ppermute | solution.py:16
  99.2 1.0 maximum_bitcast_fusion
  101.4 2.9 %collective-permute-done.13 = f32[1,1664]{1,0:T(1,128)S(1)} collective-permute-done((f32[1,1664]{1,0:T(1,128)S(1)}, f32[1,1664]{1,0:T(1,128)S(1)}, u32[]{:S(2)}, u32[]{:S(2)}) %collective-permute-start.13) | collective-permute-done | bytes 6688 | tf_op jit(solution)/shard_map/ppermute | solution.py:16
  104.3 0.9 fusion.14
  (80 shorter events, 7.0 us)
Async XLA Ops:
  0.6 44.0 %collective-permute-start.5 = (bf16[384,1536]{1,0:T(8,128)(2,1)}, bf16[384,1536]{1,0:T(8,128)(2,1)S(1)}, u32[]{:S(2)}, u32[]{:S(2)}) collective-permute-start(bf16[384,1536]{1,0:T(8,128)(2,1)} %param.14), channel_id=1, source_target_pairs={{0,2},{1,3},{2,0},{3,1},{4,6},{5,7},{6,4},{7,5},{8,10},{9,11},{10,... | collective-permute-start | bytes 3538952 | tf_op jit(solution)/shard_map/ppermute | solution.py:48
  3.7 54.2 %collective-permute-start.6 = (bf16[384,1536]{1,0:T(8,128)(2,1)}, bf16[384,1536]{1,0:T(8,128)(2,1)}, u32[]{:S(2)}, u32[]{:S(2)}) collective-permute-start(bf16[384,1536]{1,0:T(8,128)(2,1)} %param.14), channel_id=1, source_target_pairs={{0,1},{1,0},{2,3},{3,2},{4,5},{5,4},{6,7},{7,6},{8,9},{9,8},{10,11... | collective-permute-start | bytes 3538952 | tf_op jit(solution)/shard_map/ppermute | solution.py:51
  8.5 9.8 %copy-start.14 = (f32[128,1536]{1,0:T(8,128)}, f32[128,1536]{1,0:T(8,128)S(1)}, u32[]{:S(2)}) copy-start(f32[128,1536]{1,0:T(8,128)S(1)} %fusion.11) | copy-start | bytes 2359300
  9.3 11.4 %collective-permute-start.1 = (f32[1,1664]{1,0:T(1,128)S(1)}, f32[1,1664]{1,0:T(1,128)S(1)}, u32[]{:S(2)}, u32[]{:S(2)}) collective-permute-start(f32[1,1664]{1,0:T(1,128)S(1)} %concatenate.24), channel_id=1, source_target_pairs={{0,4},{4,8},{8,12},{12,16},{16,20},{20,24},{24,28},{1,5},{5,9},{9,... | collective-permute-start | bytes 19976 | tf_op jit(solution)/shard_map/ppermute | solution.py:16
  13.5 31.1 %collective-permute-start = (bf16[1,1536]{1,0:T(2,128)(2,1)S(1)}, bf16[1,1536]{1,0:T(2,128)(2,1)S(1)}, u32[]{:S(2)}, u32[]{:S(2)}) collective-permute-start(bf16[1,1536]{1,0:T(2,128)(2,1)S(1)} %get-tuple-element.13), channel_id=1, source_target_pairs={{0,4},{4,8},{8,12},{12,16},{16,20},{20,24},{24,28},{1,5},{5,9},{9,... | collective-permute-start | bytes 9224 | tf_op jit(solution)/shard_map/ppermute | solution.py:16
  16.9 38.3 %collective-permute-start.8 = (bf16[384,1536]{1,0:T(8,128)(2,1)}, bf16[384,1536]{1,0:T(8,128)(2,1)}, u32[]{:S(2)}, u32[]{:S(2)}) collective-permute-start(bf16[384,1536]{1,0:T(8,128)(2,1)} %param.15), channel_id=1, source_target_pairs={{0,2},{1,3},{2,0},{3,1},{4,6},{5,7},{6,4},{7,5},{8,10},{9,11},{10,... | collective-permute-start | bytes 3538952 | tf_op jit(solution)/shard_map/ppermute | solution.py:48
  21.4 5.9 %collective-permute-start.2 = (f32[1,1664]{1,0:T(1,128)S(1)}, f32[1,1664]{1,0:T(1,128)S(1)}, u32[]{:S(2)}, u32[]{:S(2)}) collective-permute-start(f32[1,1664]{1,0:T(1,128)S(1)} %fusion.41), channel_id=1, source_target_pairs={{0,8},{4,12},{8,16},{12,20},{16,24},{20,28},{1,9},{5,13},{9,17},{1... | collective-permute-start | bytes 19976 | tf_op jit(solution)/shard_map/ppermute | solution.py:16
  27.3 5.9 %collective-permute-start.3 = (f32[1,1664]{1,0:T(1,128)S(1)}, f32[1,1664]{1,0:T(1,128)S(1)}, u32[]{:S(2)}, u32[]{:S(2)}) collective-permute-start(f32[1,1664]{1,0:T(1,128)S(1)} %get-tuple-element.17), channel_id=1, source_target_pairs={{0,16},{4,20},{8,24},{12,28},{1,17},{5,21},{9,25},{13,29},{2,18},{... | collective-permute-start | bytes 19976 | tf_op jit(solution)/shard_map/ppermute | solution.py:16
  33.3 10.7 %copy-start.3 = (bf16[384,1536]{1,0:T(8,128)(2,1)S(1)}, bf16[384,1536]{1,0:T(8,128)(2,1)}, u32[]{:S(2)}) copy-start(bf16[384,1536]{1,0:T(8,128)(2,1)} %param.15) | copy-start | bytes 3538948
  33.3 11.2 %copy-start.13 = (bf16[1,320,1536]{2,1,0:T(8,128)(2,1)S(1)}, bf16[1,320,1536]{2,1,0:T(8,128)(2,1)}, u32[]{:S(2)}) copy-start(bf16[1,320,1536]{2,1,0:T(8,128)(2,1)} %param.8) | copy-start | bytes 2949124
  37.5 6.4 %collective-permute-start.4 = (f32[1,1537]{1,0:T(1,128)S(1)}, f32[1,1537]{1,0:T(1,128)S(1)}, u32[]{:S(2)}, u32[]{:S(2)}) collective-permute-start(f32[1,1537]{1,0:T(1,128)S(1)} %pad_maximum_fusion.4), channel_id=1, source_target_pairs={{4,0},{8,4},{12,8},{16,12},{20,16},{24,20},{28,24},{5,1},{9,5},{13... | collective-permute-start | bytes 18452 | tf_op jit(solution)/shard_map/ppermute | solution.py:16
  44.0 15.9 %collective-permute-start.9 = (bf16[384,1536]{1,0:T(8,128)(2,1)S(1)}, bf16[384,1536]{1,0:T(8,128)(2,1)S(1)}, u32[]{:S(2)}, u32[]{:S(2)}) collective-permute-start(bf16[384,1536]{1,0:T(8,128)(2,1)S(1)} %copy-done.3), channel_id=1, source_target_pairs={{0,1},{1,0},{2,3},{3,2},{4,5},{5,4},{6,7},{7,6},{8,9},{9,8},{10,11... | collective-permute-start | bytes 3538952 | tf_op jit(solution)/shard_map/ppermute | solution.py:51
  44.6 1.3 %copy-start.7 = (bf16[384,1536]{1,0:T(8,128)(2,1)S(1)}, bf16[384,1536]{1,0:T(8,128)(2,1)}, u32[]{:S(2)}) copy-start(bf16[384,1536]{1,0:T(8,128)(2,1)} %param.14) | copy-start | bytes 3538948
  46.6 17.5 %collective-permute-start.7 = (bf16[384,1536]{1,0:T(8,128)(2,1)S(1)}, bf16[384,1536]{1,0:T(8,128)(2,1)S(1)}, u32[]{:S(2)}, u32[]{:S(2)}) collective-permute-start(bf16[384,1536]{1,0:T(8,128)(2,1)S(1)} %collective-permute-done.5), channel_id=1, source_target_pairs={{0,1},{1,0},{2,3},{3,2},{4,5},{5,4},{6,7},{7,6},{8,9},{9,8},{10,11... | collective-permute-start | bytes 3538952 | tf_op jit(solution)/shard_map/ppermute | solution.py:51
  55.2 5.7 %collective-permute-start.10 = (bf16[384,1536]{1,0:T(8,128)(2,1)}, bf16[384,1536]{1,0:T(8,128)(2,1)S(1)}, u32[]{:S(2)}, u32[]{:S(2)}) collective-permute-start(bf16[384,1536]{1,0:T(8,128)(2,1)} %collective-permute-done.8), channel_id=1, source_target_pairs={{0,1},{1,0},{2,3},{3,2},{4,5},{5,4},{6,7},{7,6},{8,9},{9,8},{10,11... | collective-permute-start | bytes 3538952 | tf_op jit(solution)/shard_map/ppermute | solution.py:51
  59.9 1.0 copy-start.9
  60.9 1.1 %copy-start.11 = (bf16[384,1536]{1,0:T(8,128)(2,1)}, bf16[384,1536]{1,0:T(8,128)(2,1)S(1)}, u32[]{:S(2)}) copy-start(bf16[384,1536]{1,0:T(8,128)(2,1)S(1)} %collective-permute-done.10) | copy-start | bytes 3538948
  64.2 1.1 %copy-start.5 = (bf16[384,1536]{1,0:T(8,128)(2,1)}, bf16[384,1536]{1,0:T(8,128)(2,1)S(1)}, u32[]{:S(2)}) copy-start(bf16[384,1536]{1,0:T(8,128)(2,1)S(1)} %collective-permute-done.7) | copy-start | bytes 3538948
  65.3 1.3 %copy-start = (f32[322,1536]{1,0:T(8,128)}, f32[322,1536]{1,0:T(8,128)S(1)}, u32[]{:S(2)}) copy-start(f32[322,1536]{1,0:T(8,128)S(1)} %convolution_add_fusion.3) | copy-start | bytes 5935108
  70.0 2.2 %copy-start.1 = (f32[322,1536]{1,0:T(8,128)S(1)}, f32[322,1536]{1,0:T(8,128)}, u32[]{:S(2)}) copy-start(f32[322,1536]{1,0:T(8,128)} %copy-done) | copy-start | bytes 5935108
  74.2 1.3 %copy-start.8 = (bf16[384,1536]{1,0:T(8,128)(2,1)S(1)}, bf16[384,1536]{1,0:T(8,128)(2,1)}, u32[]{:S(2)}) copy-start(bf16[384,1536]{1,0:T(8,128)(2,1)} %param.14) | copy-start | bytes 3538948
  74.5 1.6 %copy-start.2 = (bf16[1,320,1536]{2,1,0:T(8,128)(2,1)S(1)}, bf16[1,320,1536]{2,1,0:T(8,128)(2,1)}, u32[]{:S(2)}) copy-start(bf16[1,320,1536]{2,1,0:T(8,128)(2,1)} %param.9) | copy-start | bytes 2949124
  77.4 4.2 %copy-start.4 = (bf16[384,1536]{1,0:T(8,128)(2,1)S(1)}, bf16[384,1536]{1,0:T(8,128)(2,1)}, u32[]{:S(2)}) copy-start(bf16[384,1536]{1,0:T(8,128)(2,1)} %param.15) | copy-start | bytes 3538948
  78.8 3.5 %copy-start.12 = (bf16[384,1536]{1,0:T(8,128)(2,1)S(1)}, bf16[384,1536]{1,0:T(8,128)(2,1)}, u32[]{:S(2)}) copy-start(bf16[384,1536]{1,0:T(8,128)(2,1)} %copy-done.11) | copy-start | bytes 3538948
  80.1 9.8 %collective-permute-start.11 = (f32[1,1664]{1,0:T(1,128)S(1)}, f32[1,1664]{1,0:T(1,128)S(1)}, u32[]{:S(2)}, u32[]{:S(2)}) collective-permute-start(f32[1,1664]{1,0:T(1,128)S(1)} %concatenate.31), channel_id=1, source_target_pairs={{4,0},{8,4},{12,8},{16,12},{20,16},{24,20},{28,24},{5,1},{9,5},{13... | collective-permute-start | bytes 19976 | tf_op jit(solution)/shard_map/ppermute | solution.py:16
  82.3 1.3 %copy-start.10 = (bf16[384,1536]{1,0:T(8,128)(2,1)S(1)}, bf16[384,1536]{1,0:T(8,128)(2,1)}, u32[]{:S(2)}) copy-start(bf16[384,1536]{1,0:T(8,128)(2,1)} %copy-done.9) | copy-start | bytes 3538948
  84.3 2.1 %copy-start.6 = (bf16[384,1536]{1,0:T(8,128)(2,1)S(1)}, bf16[384,1536]{1,0:T(8,128)(2,1)}, u32[]{:S(2)}) copy-start(bf16[384,1536]{1,0:T(8,128)(2,1)} %copy-done.5) | copy-start | bytes 3538948
  90.6 7.3 %collective-permute-start.12 = (f32[1,1664]{1,0:T(1,128)S(1)}, f32[1,1664]{1,0:T(1,128)S(1)}, u32[]{:S(2)}, u32[]{:S(2)}) collective-permute-start(f32[1,1664]{1,0:T(1,128)S(1)} %fusion.44), channel_id=1, source_target_pairs={{8,0},{12,4},{16,8},{20,12},{24,16},{28,20},{9,1},{13,5},{17,9},{2... | collective-permute-start | bytes 19976 | tf_op jit(solution)/shard_map/ppermute | solution.py:16
  97.9 6.4 %collective-permute-start.13 = (f32[1,1664]{1,0:T(1,128)S(1)}, f32[1,1664]{1,0:T(1,128)S(1)}, u32[]{:S(2)}, u32[]{:S(2)}) collective-permute-start(f32[1,1664]{1,0:T(1,128)S(1)} %get-tuple-element.15), channel_id=1, source_target_pairs={{16,0},{20,4},{24,8},{28,12},{17,1},{21,5},{25,9},{29,13},{18,2},{... | collective-permute-start | bytes 19976 | tf_op jit(solution)/shard_map/ppermute | solution.py:16

commit v19 on v16

--- a/solution.py
+++ b/solution.py
@@ -45,7 +45,9 @@
     index = [own]
     for k in range(1, size // 2):
         route = [(i, (i + 2 * k) % size) for i in range(size)]
-        pairs.append(lax.ppermute(blocks, axis, route))
+        first = lax.ppermute(blocks[0], axis, route)
+        later, _ = lax.optimization_barrier((blocks[1], first))
+        pairs.append((first, lax.ppermute(later, axis, route)))
         index.append((own - 2 * k) % size)
     swap = [(i, i ^ 1) for i in range(size)]
     partner = lax.ppermute(pairs, axis, swap)

time: 106 us -> 126 us (1.19)
  waiting for transfers between devices: 14.4 us -> 28.8 us
  matrix products: 25 us -> 34.3 us
  local copies, waits for them, and re-layouts: 14.2 us -> 11.4 us
    ppermute x2, waiting for transfers between devices: 8.07 us -> 21.8 us  [the longest x1 21.8 us: gather_blocks(): pairs.append((first, lax.ppermute(later, axis, route)))]
    dot_general x8, matrix products: 8.06 us -> 13.8 us  [split_dot(): term = jnp.dot(part, block, preferred_element_type=jnp.float32)]
    dot_general x4, matrix products: 4.12 us -> 7.94 us  [per_device(): lax.dot_general(key_grad, k_block, contract_last, preferred_element_type=...]
    unnamed x30 -> x18, local copies, waits for them, and re-layouts: 4.81 us -> 2.1 us
  transfers between devices with their start and end apart: 14 -> 14, of which waited for: 3 -> 3; matrix products, arithmetic and copies ran while one was open for 36% -> 37% of each run, Pallas kernels for 0% -> 0%
where the time goes in v19:
time: 126 us; the launch traced here: 125 us
  matrix products  34.3 us (27%)
  waiting for transfers between devices  28.8 us (23%)
  starting transfers between devices  23.6 us (19%)
  other arithmetic  16.8 us (13%)
  local copies, waits for them, and re-layouts  11.4 us (9%)
  between operations  10.5 us (8%)
    ppermute x1, waiting for transfers between devices, gather_blocks(): pairs.append((first, lax.ppermute(later, axis, route)))  21.8 us
    ppermute x8, starting transfers between devices, shifted(): return lax.ppermute(block, axis, route)  19.9 us
    dot_general x8, matrix products, split_dot(): term = jnp.dot(part, block, preferred_element_type=jnp.float32)  13.8 us
    dot_general x4, matrix products, per_device(): lax.dot_general(key_grad, k_block, contract_last, preferred_element_type=...  7.94 us
    ppermute x8, waiting for transfers between devices, shifted(): return lax.ppermute(block, axis, route)  7.03 us
    dot_general x4, matrix products, per_device(): lax.dot_general(query_grad, q_block, contract_last, preferred_element_typ...  4.15 us
    ppermute x1, starting transfers between devices, gather_blocks(): first = lax.ppermute(blocks[0], axis, route)  3.03 us
    reduce_sum x3, other arithmetic, unit_of(): scale = lax.rsqrt(jnp.sum(rows * rows, axis=1, keepdims=True) + norm_eps)  2.84 us
  transfers between devices with their start and end apart: 14, of which 3 were waited for; matrix products, arithmetic and copies ran while one was open for 37% of the time, Pallas kernels for 0%

profile of v19, /device:TPU:0, one launch (start us, length us, event | category | flops | bytes accessed | tf_op | source)
XLA Modules:
  0.0 125.4 jit_solution(14368363716116345787)
XLA Ops:
  0.6 3.0 %collective-permute-start.5 = (bf16[384,1536]{1,0:T(8,128)(2,1)}, bf16[384,1536]{1,0:T(8,128)(2,1)S(1)}, u32[]{:S(2)}, u32[]{:S(2)}) collective-permute-start(bf16[384,1536]{1,0:T(8,128)(2,1)} %param.14), channel_id=1, source_target_pairs={{0,2},{1,3},{2,0},{3,1},{4,6},{5,7},{6,4},{7,5},{8,10},{9,11},{10,... | collective-permute-start | bytes 3538952 | tf_op jit(solution)/shard_map/ppermute | solution.py:48
  4.3 0.7 bitcast_select_fusion
  5.0 0.7 fusion.64
  5.9 0.5 slice.113
  6.6 1.9 %fusion.14 = f32[128,1536]{1,0:T(8,128)S(1)} fusion(bf16[1,128,1536]{2,1,0:T(8,128)(2,1)} %param.10, f32[128]{0:T(128)S(1)} %bitcast_select_fusion, f32[128]{0:T(128)S(1)} %reduce.2), kind=kOutput, calls=%fused_computation.46 | convolution fusion | flops 302448640 | bytes 1180672 | tf_op jit(solution)/shard_map/dot_general | solution.py:128
  8.5 0.7 concatenate.24
  9.1 3.4 %collective-permute-start.1 = (f32[1,1664]{1,0:T(1,128)S(1)}, f32[1,1664]{1,0:T(1,128)S(1)}, u32[]{:S(2)}, u32[]{:S(2)}) collective-permute-start(f32[1,1664]{1,0:T(1,128)S(1)} %concatenate.24), channel_id=1, source_target_pairs={{0,4},{4,8},{8,12},{12,16},{16,20},{20,24},{24,28},{1,5},{5,9},{9,... | collective-permute-start | bytes 19976 | tf_op jit(solution)/shard_map/ppermute | solution.py:16
  12.5 0.8 slice_bitcast_fusion
  13.3 3.5 %collective-permute-start = (bf16[1,1536]{1,0:T(2,128)(2,1)S(1)}, bf16[1,1536]{1,0:T(2,128)(2,1)S(1)}, u32[]{:S(2)}, u32[]{:S(2)}) collective-permute-start(bf16[1,1536]{1,0:T(2,128)(2,1)S(1)} %get-tuple-element.15), channel_id=1, source_target_pairs={{0,4},{4,8},{8,12},{12,16},{16,20},{20,24},{24,28},{1,5},{5,9},{9,... | collective-permute-start | bytes 9224 | tf_op jit(solution)/shard_map/ppermute | solution.py:16
  16.9 0.8 fusion.32
  17.7 0.8 convert_reduce_fusion
  18.5 0.7 subtract_exponential_fusion
  20.0 0.7 fusion.42
  20.6 3.5 %collective-permute-start.2 = (f32[1,1664]{1,0:T(1,128)S(1)}, f32[1,1664]{1,0:T(1,128)S(1)}, u32[]{:S(2)}, u32[]{:S(2)}) collective-permute-start(f32[1,1664]{1,0:T(1,128)S(1)} %fusion.42), channel_id=1, source_target_pairs={{0,8},{4,12},{8,16},{12,20},{16,24},{20,28},{1,9},{5,13},{9,17},{1... | collective-permute-start | bytes 19976 | tf_op jit(solution)/shard_map/ppermute | solution.py:16
  24.3 0.5 slice.116
  25.5 0.5 slice.114
  26.7 4.0 %collective-permute-start.3 = (f32[1,1664]{1,0:T(1,128)S(1)}, f32[1,1664]{1,0:T(1,128)S(1)}, u32[]{:S(2)}, u32[]{:S(2)}) collective-permute-start(f32[1,1664]{1,0:T(1,128)S(1)} %get-tuple-element.19), channel_id=1, source_target_pairs={{0,16},{4,20},{8,24},{12,28},{1,17},{5,21},{9,25},{13,29},{2,18},{... | collective-permute-start | bytes 19976 | tf_op jit(solution)/shard_map/ppermute | solution.py:16
  30.7 0.6 fusion.67
  31.3 0.5 slice.115
  32.5 2.7 %fusion.5 = f32[320]{0:T(512)S(1)} fusion(bf16[1,320,1536]{2,1,0:T(8,128)(2,1)} %param.9, f32[1536]{0:T(1024)S(1)} %fusion.51, f32[320]{0:T(512)S(1)} %compare_convert_fusion, f32[128,1536]{1,0:T(8,128)S(1)} %fusion.14, f32[128]{0:T(128)S(1)} %get-tuple-element.29, s32[320]{0:T(512)S(1)} %get-tuple-element.25), kind=kOutput, calls=%fused_computation.27 | convolution fusion | flops 757866176 | bytes 1779968 | tf_op jit(solution)/shard_map/dot_general | solution.py:133
  35.1 0.5 slice.93
  35.7 0.6 pad_maximum_fusion.4
  36.2 1.5 %collective-permute-start.4 = (f32[1,1537]{1,0:T(1,128)S(1)}, f32[1,1537]{1,0:T(1,128)S(1)}, u32[]{:S(2)}, u32[]{:S(2)}) collective-permute-start(f32[1,1537]{1,0:T(1,128)S(1)} %pad_maximum_fusion.4), channel_id=1, source_target_pairs={{4,0},{8,4},{12,8},{16,12},{20,16},{24,20},{28,24},{5,1},{9,5},{13... | collective-permute-start | bytes 18452 | tf_op jit(solution)/shard_map/ppermute | solution.py:16
  40.2 2.4 %gather_fusion = f32[320]{0:T(512)S(1)} fusion(f32[128]{0:T(128)S(1)} %get-tuple-element.29, s32[1024]{0:T(1024)S(1)} %pad_clamp_fusion), kind=kCustom, calls=%fused_computation | custom fusion | bytes 3840 | tf_op jit(solution)/shard_map/gather | solution.py:136
  42.7 0.5 slice.128
  43.7 1.3 %pad_maximum_fusion.2 = bf16[322,1536]{1,0:T(8,128)(2,1)S(1)} fusion(bf16[1,1536]{1,0:T(2,128)(2,1)S(1)} %slice.174, bf16[1,1536]{1,0:T(2,128)(2,1)S(1)} %collective-permute-done, bf16[320,1536]{1,0:T(8,128)(2,1)} %bitcast.83), kind=kLoop, calls=%fused_computation.38 | loop fusion | flops 2967552 | bytes 1978368 | tf_op jit(solution)/shard_map/concatenate | solution.py:146
  45.1 0.7 fusion.27
  46.3 0.7 convolution_add_fusion.5
  47.0 2.0 %convolution_add_fusion.4 = f32[322,1536]{1,0:T(8,128)S(1)} fusion(f32[322,1536]{1,0:T(8,128)S(1)} %convolution_add_fusion.5, bf16[384,1536]{1,0:T(8,128)(2,1)} %collective-permute-done.6, bf16[322,1536]{1,0:T(8,128)(2,1)S(1)} %pad_maximum_fusion.2, s32[]{:T(128)S(6)} %select_n.163), kind=kOutput, calls=%fused_computation.5 | convolution fusion | flops 380341248 | bytes 5425156 | tf_op jit(solution)/shard_map/dot_general | solution.py:75
  49.0 21.8 %collective-permute-done.8 = bf16[384,1536]{1,0:T(8,128)(2,1)} collective-permute-done((bf16[384,1536]{1,0:T(8,128)(2,1)}, bf16[384,1536]{1,0:T(8,128)(2,1)}, u32[]{:S(2)}, u32[]{:S(2)}) %collective-permute-start.8) | collective-permute-done | bytes 1179680 | tf_op jit(solution)/shard_map/ppermute | solution.py:50
  70.8 3.2 %fusion.25 = f32[322,1536]{1,0:T(8,128)} fusion(bf16[384,1536]{1,0:T(8,128)(2,1)} %collective-permute-done.8, bf16[322,1536]{1,0:T(8,128)(2,1)S(1)} %pad_maximum_fusion.2, s32[]{:T(128)S(6)} %select_n.162), kind=kOutput, calls=%fused_computation.57 | convolution fusion | flops 379846656 | bytes 3409924 | tf_op jit(solution)/shard_map/dot_general | solution.py:75
  74.0 0.7 convolution_add_fusion.3
  75.1 0.8 multiply_reduce_fusion.5
  76.5 2.6 %convolution_add_fusion.2 = f32[322,1536]{1,0:T(8,128)S(1)} fusion(f32[322,1536]{1,0:T(8,128)} %fusion.25, bf16[384,1536]{1,0:T(8,128)(2,1)} %param.15, bf16[322,1536]{1,0:T(8,128)(2,1)S(1)} %pad_maximum_fusion.2, s32[]{:T(128)S(6)} %select_n.160), kind=kOutput, calls=%fused_computation.3 | convolution fusion | flops 380341248 | bytes 5388292 | tf_op jit(solution)/shard_map/dot_general | solution.py:75
  79.2 2.0 %convolution_add_fusion.1 = f32[322,1536]{1,0:T(8,128)S(1)} fusion(f32[322,1536]{1,0:T(8,128)S(1)} %convolution_add_fusion.2, bf16[384,1536]{1,0:T(8,128)(2,1)} %collective-permute-done.9, bf16[322,1536]{1,0:T(8,128)(2,1)S(1)} %pad_maximum_fusion.2, s32[]{:T(128)S(6)} %select_n.163), kind=kOutput, calls=%fused_computation.2 | convolution fusion | flops 380341248 | bytes 5425156 | tf_op jit(solution)/shard_map/dot_general | solution.py:75
  81.2 0.6 multiply_multiply_fusion
  81.8 2.0 %convolution_add_fusion = f32[322,1536]{1,0:T(8,128)S(1)} fusion(f32[322,1536]{1,0:T(8,128)S(1)} %convolution_add_fusion.1, bf16[384,1536]{1,0:T(8,128)(2,1)} %collective-permute-done.10, bf16[322,1536]{1,0:T(8,128)(2,1)S(1)} %pad_maximum_fusion.2, s32[]{:T(128)S(6)} %select_n.164), kind=kOutput, calls=%fused_computation.1 | convolution fusion | flops 380341248 | bytes 5425156 | tf_op jit(solution)/shard_map/dot_general | solution.py:75
  83.7 1.4 %multiply_reduce_fusion.3 = (f32[320]{0:T(512)S(1)}, f32[320,1536]{1,0:T(8,128)}) fusion(f32[322,1536]{1,0:T(8,128)S(1)} %convolution_add_fusion), kind=kLoop, calls=%fused_computation.24 | loop fusion | flops 982720 | bytes 3933440 | tf_op jit(solution)/shard_map/reduce_sum | solution.py:87
  85.2 0.6 multiply_reduce_fusion.6
  86.5 1.9 %slice_multiply_fusion.1 = f32[319,1536]{1,0:T(8,128)S(1)} fusion(f32[320,1536]{1,0:T(8,128)} %get-tuple-element.10, f32[319]{0:T(512)S(1)} %bitcast.84), kind=kLoop, calls=%fused_computation.16 | loop fusion | flops 489984 | bytes 3921148 | tf_op jit(solution)/shard_map/mul | solution.py:88
  88.6 0.6 multiply_reduce_fusion.2
  89.3 0.8 multiply_reduce_fusion
  91.0 0.9 copy-done.8
  91.9 0.7 fusion.68
  92.6 1.2 fusion.4
  94.9 0.7 concatenate.31
  95.6 1.5 %collective-permute-start.11 = (f32[1,1664]{1,0:T(1,128)S(1)}, f32[1,1664]{1,0:T(1,128)S(1)}, u32[]{:S(2)}, u32[]{:S(2)}) collective-permute-start(f32[1,1664]{1,0:T(1,128)S(1)} %concatenate.31), channel_id=1, source_target_pairs={{4,0},{8,4},{12,8},{16,12},{20,16},{24,20},{28,24},{5,1},{9,5},{13... | collective-permute-start | bytes 19976 | tf_op jit(solution)/shard_map/ppermute | solution.py:16
  97.1 2.0 %fusion.6 = bf16[320,384]{1,0:T(8,128)(2,1)S(1)} fusion(f32[320,384]{1,0:T(8,128)S(1)} %fusion.68, bf16[320,1536]{1,0:T(8,128)(2,1)S(1)} %subtract_convert_fusion, bf16[384,1536]{1,0:T(8,128)(2,1)} %param.15), kind=kOutput, calls=%fused_computation.32 | convolution fusion | flops 377733120 | bytes 2899968 | tf_op jit(solution)/shard_map/dot_general | solution.py:179
  99.1 2.0 %fusion.71 = f32[320,384]{1,0:T(8,128)S(1)} fusion(bf16[320,1536]{1,0:T(8,128)(2,1)S(1)} %subtract_convert_fusion, bf16[384,1536]{1,0:T(8,128)(2,1)} %collective-permute-done.10), kind=kOutput, calls=%fused_computation.152 | convolution fusion | flops 377487360 | bytes 2654208 | tf_op jit(solution)/shard_map/dot_general | solution.py:179
  101.0 2.0 %fusion.70 = f32[320,384]{1,0:T(8,128)S(1)} fusion(bf16[320,1536]{1,0:T(8,128)(2,1)S(1)} %subtract_convert_fusion, bf16[384,1536]{1,0:T(8,128)(2,1)} %collective-permute-done.9), kind=kOutput, calls=%fused_computation.151 | convolution fusion | flops 377487360 | bytes 2654208 | tf_op jit(solution)/shard_map/dot_general | solution.py:179
  103.0 2.1 %fusion.69 = f32[320,384]{1,0:T(8,128)S(1)} fusion(bf16[320,1536]{1,0:T(8,128)(2,1)S(1)} %subtract_convert_fusion, bf16[384,1536]{1,0:T(8,128)(2,1)} %collective-permute-done.8), kind=kOutput, calls=%fused_computation.150 | convolution fusion | flops 377487360 | bytes 2654208 | tf_op jit(solution)/shard_map/dot_general | solution.py:179
  105.1 0.7 fusion.9
  105.8 2.1 %fusion.8 = bf16[320,384]{1,0:T(8,128)(2,1)S(1)} fusion(f32[320,384]{1,0:T(8,128)S(1)} %fusion.70, bf16[320,1536]{1,0:T(8,128)(2,1)S(1)} %get-tuple-element.8, bf16[384,1536]{1,0:T(8,128)(2,1)} %collective-permute-done.6), kind=kOutput, calls=%fused_computation.34 | convolution fusion | flops 377733120 | bytes 2899968 | tf_op jit(solution)/shard_map/dot_general | solution.py:178
  107.9 0.7 fusion.7
  108.7 0.7 fusion.45
  109.3 1.3 %collective-permute-start.12 = (f32[1,1664]{1,0:T(1,128)S(1)}, f32[1,1664]{1,0:T(1,128)S(1)}, u32[]{:S(2)}, u32[]{:S(2)}) collective-permute-start(f32[1,1664]{1,0:T(1,128)S(1)} %fusion.45), channel_id=1, source_target_pairs={{8,0},{12,4},{16,8},{20,12},{24,16},{28,20},{9,1},{13,5},{17,9},{2... | collective-permute-start | bytes 19976 | tf_op jit(solution)/shard_map/ppermute | solution.py:16
  110.7 0.5 slice.132
  111.9 0.5 slice.130
  113.2 4.1 %collective-permute-done.12 = f32[1,1664]{1,0:T(1,128)S(1)} collective-permute-done((f32[1,1664]{1,0:T(1,128)S(1)}, f32[1,1664]{1,0:T(1,128)S(1)}, u32[]{:S(2)}, u32[]{:S(2)}) %collective-permute-start.12) | collective-permute-done | bytes 6688 | tf_op jit(solution)/shard_map/ppermute | solution.py:16
  117.3 1.3 %collective-permute-start.13 = (f32[1,1664]{1,0:T(1,128)S(1)}, f32[1,1664]{1,0:T(1,128)S(1)}, u32[]{:S(2)}, u32[]{:S(2)}) collective-permute-start(f32[1,1664]{1,0:T(1,128)S(1)} %get-tuple-element.17), channel_id=1, source_target_pairs={{16,0},{20,4},{24,8},{28,12},{17,1},{21,5},{25,9},{29,13},{18,2},{... | collective-permute-start | bytes 19976 | tf_op jit(solution)/shard_map/ppermute | solution.py:16
  118.6 1.0 maximum_bitcast_fusion
  119.6 0.5 slice.131
  120.8 2.9 %collective-permute-done.13 = f32[1,1664]{1,0:T(1,128)S(1)} collective-permute-done((f32[1,1664]{1,0:T(1,128)S(1)}, f32[1,1664]{1,0:T(1,128)S(1)}, u32[]{:S(2)}, u32[]{:S(2)}) %collective-permute-start.13) | collective-permute-done | bytes 6688 | tf_op jit(solution)/shard_map/ppermute | solution.py:16
  123.7 1.7 %fusion.3 = bf16[1,128,1536]{2,1,0:T(8,128)(2,1)} fusion(f32[128,1536]{1,0:T(8,128)S(1)} %fusion.4, f32[1536]{0:T(1024)S(1)} %fusion.50, f32[128]{0:T(128)S(1)} %get-tuple-element.28, f32[128]{0:T(128)S(1)} %bitcast_select_fusion, f32[128]{0:T(128)S(1)} %reduce.2), kind=kOutput, calls=%fused_computation.13 | convolution fusion | flops 302841856 | bytes 1187328 | tf_op jit(solution)/shard_map/dot_general | solution.py:167
  (67 shorter events, 4.8 us)
Async XLA Ops:
  0.6 42.6 %collective-permute-start.5 = (bf16[384,1536]{1,0:T(8,128)(2,1)}, bf16[384,1536]{1,0:T(8,128)(2,1)S(1)}, u32[]{:S(2)}, u32[]{:S(2)}) collective-permute-start(bf16[384,1536]{1,0:T(8,128)(2,1)} %param.14), channel_id=1, source_target_pairs={{0,2},{1,3},{2,0},{3,1},{4,6},{5,7},{6,4},{7,5},{8,10},{9,11},{10,... | collective-permute-start | bytes 3538952 | tf_op jit(solution)/shard_map/ppermute | solution.py:48
  3.7 43.3 %collective-permute-start.6 = (bf16[384,1536]{1,0:T(8,128)(2,1)}, bf16[384,1536]{1,0:T(8,128)(2,1)}, u32[]{:S(2)}, u32[]{:S(2)}) collective-permute-start(bf16[384,1536]{1,0:T(8,128)(2,1)} %param.14), channel_id=1, source_target_pairs={{0,1},{1,0},{2,3},{3,2},{4,5},{5,4},{6,7},{7,6},{8,9},{9,8},{10,11... | collective-permute-start | bytes 3538952 | tf_op jit(solution)/shard_map/ppermute | solution.py:53
  9.1 10.8 %collective-permute-start.1 = (f32[1,1664]{1,0:T(1,128)S(1)}, f32[1,1664]{1,0:T(1,128)S(1)}, u32[]{:S(2)}, u32[]{:S(2)}) collective-permute-start(f32[1,1664]{1,0:T(1,128)S(1)} %concatenate.24), channel_id=1, source_target_pairs={{0,4},{4,8},{8,12},{12,16},{16,20},{20,24},{24,28},{1,5},{5,9},{9,... | collective-permute-start | bytes 19976 | tf_op jit(solution)/shard_map/ppermute | solution.py:16
  13.3 30.4 %collective-permute-start = (bf16[1,1536]{1,0:T(2,128)(2,1)S(1)}, bf16[1,1536]{1,0:T(2,128)(2,1)S(1)}, u32[]{:S(2)}, u32[]{:S(2)}) collective-permute-start(bf16[1,1536]{1,0:T(2,128)(2,1)S(1)} %get-tuple-element.15), channel_id=1, source_target_pairs={{0,4},{4,8},{8,12},{12,16},{16,20},{20,24},{24,28},{1,5},{5,9},{9,... | collective-permute-start | bytes 9224 | tf_op jit(solution)/shard_map/ppermute | solution.py:16
  16.8 62.4 %collective-permute-start.9 = (bf16[384,1536]{1,0:T(8,128)(2,1)}, bf16[384,1536]{1,0:T(8,128)(2,1)}, u32[]{:S(2)}, u32[]{:S(2)}) collective-permute-start(bf16[384,1536]{1,0:T(8,128)(2,1)} %param.15), channel_id=1, source_target_pairs={{0,1},{1,0},{2,3},{3,2},{4,5},{5,4},{6,7},{7,6},{8,9},{9,8},{10,11... | collective-permute-start | bytes 3538952 | tf_op jit(solution)/shard_map/ppermute | solution.py:53
  20.6 6.0 %collective-permute-start.2 = (f32[1,1664]{1,0:T(1,128)S(1)}, f32[1,1664]{1,0:T(1,128)S(1)}, u32[]{:S(2)}, u32[]{:S(2)}) collective-permute-start(f32[1,1664]{1,0:T(1,128)S(1)} %fusion.42), channel_id=1, source_target_pairs={{0,8},{4,12},{8,16},{12,20},{16,24},{20,28},{1,9},{5,13},{9,17},{1... | collective-permute-start | bytes 19976 | tf_op jit(solution)/shard_map/ppermute | solution.py:16
  26.7 5.8 %collective-permute-start.3 = (f32[1,1664]{1,0:T(1,128)S(1)}, f32[1,1664]{1,0:T(1,128)S(1)}, u32[]{:S(2)}, u32[]{:S(2)}) collective-permute-start(f32[1,1664]{1,0:T(1,128)S(1)} %get-tuple-element.19), channel_id=1, source_target_pairs={{0,16},{4,20},{8,24},{12,28},{1,17},{5,21},{9,25},{13,29},{2,18},{... | collective-permute-start | bytes 19976 | tf_op jit(solution)/shard_map/ppermute | solution.py:16
  36.2 6.5 %collective-permute-start.4 = (f32[1,1537]{1,0:T(1,128)S(1)}, f32[1,1537]{1,0:T(1,128)S(1)}, u32[]{:S(2)}, u32[]{:S(2)}) collective-permute-start(f32[1,1537]{1,0:T(1,128)S(1)} %pad_maximum_fusion.4), channel_id=1, source_target_pairs={{4,0},{8,4},{12,8},{16,12},{20,16},{24,20},{28,24},{5,1},{9,5},{13... | collective-permute-start | bytes 18452 | tf_op jit(solution)/shard_map/ppermute | solution.py:16
  43.2 2.6 %copy-start.3 = (bf16[384,1536]{1,0:T(8,128)(2,1)}, bf16[384,1536]{1,0:T(8,128)(2,1)S(1)}, u32[]{:S(2)}) copy-start(bf16[384,1536]{1,0:T(8,128)(2,1)S(1)} %collective-permute-done.5) | copy-start | bytes 3538948
  43.2 27.5 %collective-permute-start.8 = (bf16[384,1536]{1,0:T(8,128)(2,1)}, bf16[384,1536]{1,0:T(8,128)(2,1)}, u32[]{:S(2)}, u32[]{:S(2)}) collective-permute-start(bf16[384,1536]{1,0:T(8,128)(2,1)} %param.15), channel_id=1, source_target_pairs={{0,2},{1,3},{2,0},{3,1},{4,6},{5,7},{6,4},{7,5},{8,10},{9,11},{10,... | collective-permute-start | bytes 3538952 | tf_op jit(solution)/shard_map/ppermute | solution.py:50
  45.0 1.3 %copy-start.7 = (bf16[384,1536]{1,0:T(8,128)(2,1)S(1)}, bf16[384,1536]{1,0:T(8,128)(2,1)}, u32[]{:S(2)}) copy-start(bf16[384,1536]{1,0:T(8,128)(2,1)} %param.14) | copy-start | bytes 3538948
  45.0 29.0 %collective-permute-start.7 = (bf16[384,1536]{1,0:T(8,128)(2,1)S(1)}, bf16[384,1536]{1,0:T(8,128)(2,1)S(1)}, u32[]{:S(2)}, u32[]{:S(2)}) collective-permute-start(bf16[384,1536]{1,0:T(8,128)(2,1)S(1)} %collective-permute-done.5), channel_id=1, source_target_pairs={{0,1},{1,0},{2,3},{3,2},{4,5},{5,4},{6,7},{7,6},{8,9},{9,8},{10,11... | collective-permute-start | bytes 3538952 | tf_op jit(solution)/shard_map/ppermute | solution.py:53
  70.8 11.0 %collective-permute-start.10 = (bf16[384,1536]{1,0:T(8,128)(2,1)}, bf16[384,1536]{1,0:T(8,128)(2,1)}, u32[]{:S(2)}, u32[]{:S(2)}) collective-permute-start(bf16[384,1536]{1,0:T(8,128)(2,1)} %collective-permute-done.8), channel_id=1, source_target_pairs={{0,1},{1,0},{2,3},{3,2},{4,5},{5,4},{6,7},{7,6},{8,9},{9,8},{10,11... | collective-permute-start | bytes 3538952 | tf_op jit(solution)/shard_map/ppermute | solution.py:53
  74.0 1.1 copy-start.5
  75.1 6.1 %copy-start = (f32[322,1536]{1,0:T(8,128)}, f32[322,1536]{1,0:T(8,128)S(1)}, u32[]{:S(2)}) copy-start(f32[322,1536]{1,0:T(8,128)S(1)} %convolution_add_fusion.3) | copy-start | bytes 5935108
  86.5 2.2 %copy-start.1 = (f32[322,1536]{1,0:T(8,128)S(1)}, f32[322,1536]{1,0:T(8,128)}, u32[]{:S(2)}) copy-start(f32[322,1536]{1,0:T(8,128)} %copy-done) | copy-start | bytes 5935108
  90.6 1.3 %copy-start.8 = (bf16[384,1536]{1,0:T(8,128)(2,1)S(1)}, bf16[384,1536]{1,0:T(8,128)(2,1)}, u32[]{:S(2)}) copy-start(bf16[384,1536]{1,0:T(8,128)(2,1)} %param.14) | copy-start | bytes 3538948
  91.0 1.6 %copy-start.2 = (bf16[1,320,1536]{2,1,0:T(8,128)(2,1)S(1)}, bf16[1,320,1536]{2,1,0:T(8,128)(2,1)}, u32[]{:S(2)}) copy-start(bf16[1,320,1536]{2,1,0:T(8,128)(2,1)} %param.9) | copy-start | bytes 2949124
  95.6 13.1 %collective-permute-start.11 = (f32[1,1664]{1,0:T(1,128)S(1)}, f32[1,1664]{1,0:T(1,128)S(1)}, u32[]{:S(2)}, u32[]{:S(2)}) collective-permute-start(f32[1,1664]{1,0:T(1,128)S(1)} %concatenate.31), channel_id=1, source_target_pairs={{4,0},{8,4},{12,8},{16,12},{20,16},{24,20},{28,24},{5,1},{9,5},{13... | collective-permute-start | bytes 19976 | tf_op jit(solution)/shard_map/ppermute | solution.py:16
  103.0 2.1 %copy-start.6 = (bf16[384,1536]{1,0:T(8,128)(2,1)S(1)}, bf16[384,1536]{1,0:T(8,128)(2,1)}, u32[]{:S(2)}) copy-start(bf16[384,1536]{1,0:T(8,128)(2,1)} %copy-done.5) | copy-start | bytes 3538948
  105.8 2.1 %copy-start.4 = (bf16[384,1536]{1,0:T(8,128)(2,1)S(1)}, bf16[384,1536]{1,0:T(8,128)(2,1)}, u32[]{:S(2)}) copy-start(bf16[384,1536]{1,0:T(8,128)(2,1)} %copy-done.3) | copy-start | bytes 3538948
  109.3 7.9 %collective-permute-start.12 = (f32[1,1664]{1,0:T(1,128)S(1)}, f32[1,1664]{1,0:T(1,128)S(1)}, u32[]{:S(2)}, u32[]{:S(2)}) collective-permute-start(f32[1,1664]{1,0:T(1,128)S(1)} %fusion.45), channel_id=1, source_target_pairs={{8,0},{12,4},{16,8},{20,12},{24,16},{28,20},{9,1},{13,5},{17,9},{2... | collective-permute-start | bytes 19976 | tf_op jit(solution)/shard_map/ppermute | solution.py:16
  117.3 6.4 %collective-permute-start.13 = (f32[1,1664]{1,0:T(1,128)S(1)}, f32[1,1664]{1,0:T(1,128)S(1)}, u32[]{:S(2)}, u32[]{:S(2)}) collective-permute-start(f32[1,1664]{1,0:T(1,128)S(1)} %get-tuple-element.17), channel_id=1, source_target_pairs={{16,0},{20,4},{24,8},{28,12},{17,1},{21,5},{25,9},{29,13},{18,2},{... | collective-permute-start | bytes 19976 | tf_op jit(solution)/shard_map/ppermute | solution.py:16

commit v20 on v16

--- a/solution.py
+++ b/solution.py
@@ -141,7 +141,8 @@
     prev_row = shifted(token_rows[token_count - 1 :], "seq", 1)
     next_row = from_next[:, :-1].astype(token_rows.dtype)
     next_cos_grad = from_next[:, -1:]
-    rows_ext = jnp.concatenate([token_rows, prev_row, next_row], axis=0)
+    spare = jnp.zeros((6, token_rows.shape[1]), token_rows.dtype)
+    rows_ext = jnp.concatenate([token_rows, prev_row, next_row, spare], axis=0)
     queries_ext = split_dot(rows_ext, query_blocks, index, width)
     keys_ext = split_dot(rows_ext, key_blocks, index, width)
     queries = queries_ext[:token_count]
@@ -149,7 +150,7 @@
     query_unit, query_scale = unit_of(queries)
     key_unit, key_scale = unit_of(key_rows)
     key_before, _ = unit_of(keys_ext[token_count : token_count + 1])
-    query_next, _ = unit_of(queries_ext[token_count + 1 :])
+    query_next, _ = unit_of(queries_ext[token_count + 1 : token_count + 2])
     key_prior = jnp.concatenate([key_before, key_unit[:-1]], axis=0)
     cosine = jnp.sum(query_unit * key_prior, axis=1)
     boundary_prob = jnp.where(later_rows, 0.5 * (1.0 - cosine), 1.0)

time: 106 us -> 108 us (1.019)
  matrix products: 25 us -> 27.4 us
  waiting for transfers between devices: 14.4 us -> 15.5 us
    dot_general x8, matrix products: 8.06 us -> 9.38 us  [split_dot(): term = jnp.dot(part, block, preferred_element_type=jnp.float32)]
    dot_general x4, matrix products: 4.05 us -> 5.32 us  [per_device(): lax.dot_general(query_grad, q_block, contract_last, preferred_element_typ...]
    unnamed x30 -> x26, local copies, waits for them, and re-layouts: 4.81 us -> 4.23 us
  transfers between devices with their start and end apart: 14 -> 14, of which waited for: 3 -> 3; matrix products, arithmetic and copies ran while one was open for 36% -> 38% of each run, Pallas kernels for 0% -> 0%
where the time goes in v20:
time: 108 us; the launch traced here: 107 us
  matrix products  27.4 us (25%)
  starting transfers between devices  24 us (22%)
  other arithmetic  16.5 us (15%)
  waiting for transfers between devices  15.5 us (14%)
  local copies, waits for them, and re-layouts  13.6 us (13%)
  between operations  10.5 us (10%)
    ppermute x8, starting transfers between devices, shifted(): return lax.ppermute(block, axis, route)  19.9 us
    dot_general x8, matrix products, split_dot(): term = jnp.dot(part, block, preferred_element_type=jnp.float32)  9.38 us
    ppermute x2, waiting for transfers between devices, gather_blocks(): pairs.append(lax.ppermute(blocks, axis, route))  9.08 us
    ppermute x8, waiting for transfers between devices, shifted(): return lax.ppermute(block, axis, route)  6.38 us
    dot_general x4, matrix products, per_device(): lax.dot_general(query_grad, q_block, contract_last, preferred_element_typ...  5.32 us
    unnamed x26, local copies, waits for them, and re-layouts  4.23 us
    dot_general x4, matrix products, per_device(): lax.dot_general(key_grad, k_block, contract_last, preferred_element_type=...  4.12 us
    ppermute x2, starting transfers between devices, gather_blocks(): pairs.append(lax.ppermute(blocks, axis, route))  3.6 us
  transfers between devices with their start and end apart: 14, of which 3 were waited for; matrix products, arithmetic and copies ran while one was open for 38% of the time, Pallas kernels for 0%

profile of v20, /device:TPU:0, one launch (start us, length us, event | category | flops | bytes accessed | tf_op | source)
XLA Modules:
  0.0 107.5 jit_solution(3673581057209632174)
XLA Ops:
  0.6 3.0 %collective-permute-start.5 = (bf16[384,1536]{1,0:T(8,128)(2,1)}, bf16[384,1536]{1,0:T(8,128)(2,1)}, u32[]{:S(2)}, u32[]{:S(2)}) collective-permute-start(bf16[384,1536]{1,0:T(8,128)(2,1)} %param.14), channel_id=1, source_target_pairs={{0,2},{1,3},{2,0},{3,1},{4,6},{5,7},{6,4},{7,5},{8,10},{9,11},{10,... | collective-permute-start | bytes 3538952 | tf_op jit(solution)/shard_map/ppermute | solution.py:48
  4.3 0.7 bitcast_select_fusion
  5.0 0.7 fusion.64
  5.9 0.5 slice.113
  6.6 1.9 %fusion.14 = f32[128,1536]{1,0:T(8,128)S(1)} fusion(bf16[1,128,1536]{2,1,0:T(8,128)(2,1)} %param.10, f32[128]{0:T(128)S(1)} %bitcast_select_fusion, f32[128]{0:T(128)S(1)} %reduce.2), kind=kOutput, calls=%fused_computation.46 | convolution fusion | flops 302448640 | bytes 1180672 | tf_op jit(solution)/shard_map/dot_general | solution.py:126
  8.5 0.7 concatenate.24
  9.1 3.4 %collective-permute-start.1 = (f32[1,1664]{1,0:T(1,128)S(1)}, f32[1,1664]{1,0:T(1,128)S(1)}, u32[]{:S(2)}, u32[]{:S(2)}) collective-permute-start(f32[1,1664]{1,0:T(1,128)S(1)} %concatenate.24), channel_id=1, source_target_pairs={{0,4},{4,8},{8,12},{12,16},{16,20},{20,24},{24,28},{1,5},{5,9},{9,... | collective-permute-start | bytes 19976 | tf_op jit(solution)/shard_map/ppermute | solution.py:16
  12.5 0.8 slice_bitcast_fusion
  13.3 3.5 %collective-permute-start = (bf16[1,1536]{1,0:T(2,128)(2,1)S(1)}, bf16[1,1536]{1,0:T(2,128)(2,1)S(1)}, u32[]{:S(2)}, u32[]{:S(2)}) collective-permute-start(bf16[1,1536]{1,0:T(2,128)(2,1)S(1)} %get-tuple-element.13), channel_id=1, source_target_pairs={{0,4},{4,8},{8,12},{12,16},{16,20},{20,24},{24,28},{1,5},{5,9},{9,... | collective-permute-start | bytes 9224 | tf_op jit(solution)/shard_map/ppermute | solution.py:16
  16.8 0.6 collective-permute-start.8
  17.4 0.8 fusion.32
  18.2 0.8 convert_reduce_fusion
  19.0 0.7 subtract_exponential_fusion
  20.5 0.7 fusion.42
  21.1 3.5 %collective-permute-start.2 = (f32[1,1664]{1,0:T(1,128)S(1)}, f32[1,1664]{1,0:T(1,128)S(1)}, u32[]{:S(2)}, u32[]{:S(2)}) collective-permute-start(f32[1,1664]{1,0:T(1,128)S(1)} %fusion.42), channel_id=1, source_target_pairs={{0,8},{4,12},{8,16},{12,20},{16,24},{20,28},{1,9},{5,13},{9,17},{1... | collective-permute-start | bytes 19976 | tf_op jit(solution)/shard_map/ppermute | solution.py:16
  24.7 0.5 slice.116
  25.9 0.5 slice.114
  27.1 4.0 %collective-permute-start.3 = (f32[1,1664]{1,0:T(1,128)S(1)}, f32[1,1664]{1,0:T(1,128)S(1)}, u32[]{:S(2)}, u32[]{:S(2)}) collective-permute-start(f32[1,1664]{1,0:T(1,128)S(1)} %get-tuple-element.17), channel_id=1, source_target_pairs={{0,16},{4,20},{8,24},{12,28},{1,17},{5,21},{9,25},{13,29},{2,18},{... | collective-permute-start | bytes 19976 | tf_op jit(solution)/shard_map/ppermute | solution.py:16
  31.2 0.6 fusion.67
  33.0 2.8 %fusion.5 = f32[320]{0:T(512)S(1)} fusion(bf16[1,320,1536]{2,1,0:T(8,128)(2,1)} %param.9, f32[1536]{0:T(1024)S(1)} %fusion.51, f32[320]{0:T(512)S(1)} %compare_convert_fusion, f32[128,1536]{1,0:T(8,128)S(1)} %fusion.14, f32[128]{0:T(128)S(1)} %get-tuple-element.27, s32[320]{0:T(512)S(1)} %get-tuple-element.23), kind=kOutput, calls=%fused_computation.27 | convolution fusion | flops 757866176 | bytes 1779968 | tf_op jit(solution)/shard_map/dot_general | solution.py:131
  35.8 0.5 slice.93
  36.3 0.6 pad_maximum_fusion.3
  36.9 1.5 %collective-permute-start.4 = (f32[1,1537]{1,0:T(1,128)S(1)}, f32[1,1537]{1,0:T(1,128)S(1)}, u32[]{:S(2)}, u32[]{:S(2)}) collective-permute-start(f32[1,1537]{1,0:T(1,128)S(1)} %pad_maximum_fusion.3), channel_id=1, source_target_pairs={{4,0},{8,4},{12,8},{16,12},{20,16},{24,20},{28,24},{5,1},{9,5},{13... | collective-permute-start | bytes 18452 | tf_op jit(solution)/shard_map/ppermute | solution.py:16
  40.9 2.4 %gather_fusion = f32[320]{0:T(512)S(1)} fusion(f32[128]{0:T(128)S(1)} %get-tuple-element.27, s32[1024]{0:T(1024)S(1)} %pad_clamp_fusion), kind=kCustom, calls=%fused_computation | custom fusion | bytes 3840 | tf_op jit(solution)/shard_map/gather | solution.py:134
  43.7 0.7 fusion.29
  44.4 0.7 fusion.27
  45.1 0.5 slice.128
  46.1 9.1 %collective-permute-done.8 = bf16[384,1536]{1,0:T(8,128)(2,1)} collective-permute-done((bf16[384,1536]{1,0:T(8,128)(2,1)}, bf16[384,1536]{1,0:T(8,128)(2,1)}, u32[]{:S(2)}, u32[]{:S(2)}) %collective-permute-start.8) | collective-permute-done | bytes 1179680 | tf_op jit(solution)/shard_map/ppermute | solution.py:48
  55.2 2.0 %convolution_add_fusion.5 = f32[328,1536]{1,0:T(8,128)S(1)} fusion(f32[328,1536]{1,0:T(8,128)S(1)} %fusion.29, bf16[384,1536]{1,0:T(8,128)(2,1)} %collective-permute-done.5, bf16[328,1536]{1,0:T(8,128)(2,1)S(1)} %maximum_maximum_fusion, s32[]{:T(128)S(6)} %select_n.162), kind=kOutput, calls=%fused_computation.6 | convolution fusion | flops 387428352 | bytes 5462020 | tf_op jit(solution)/shard_map/dot_general | solution.py:73
  57.2 2.0 %convolution_add_fusion.2 = f32[328,1536]{1,0:T(8,128)S(1)} fusion(f32[328,1536]{1,0:T(8,128)S(1)} %fusion.27, bf16[384,1536]{1,0:T(8,128)(2,1)} %collective-permute-done.8, bf16[328,1536]{1,0:T(8,128)(2,1)S(1)} %maximum_maximum_fusion, s32[]{:T(128)S(6)} %select_n.162), kind=kOutput, calls=%fused_computation.3 | convolution fusion | flops 387428352 | bytes 5462020 | tf_op jit(solution)/shard_map/dot_general | solution.py:73
  59.2 2.0 %convolution_add_fusion.4 = f32[328,1536]{1,0:T(8,128)S(1)} fusion(f32[328,1536]{1,0:T(8,128)S(1)} %convolution_add_fusion.5, bf16[384,1536]{1,0:T(8,128)(2,1)} %collective-permute-done.6, bf16[328,1536]{1,0:T(8,128)(2,1)S(1)} %maximum_maximum_fusion, s32[]{:T(128)S(6)} %select_n.163), kind=kOutput, calls=%fused_computation.5 | convolution fusion | flops 387428352 | bytes 5462020 | tf_op jit(solution)/shard_map/dot_general | solution.py:73
  61.2 0.7 convolution_add_fusion.1
  62.3 0.7 convolution_add_fusion
  63.4 0.6 multiply_reduce_fusion.6
  64.0 1.4 %multiply_reduce_fusion.3 = (f32[320]{0:T(512)S(1)}, f32[320,1536]{1,0:T(8,128)}) fusion(f32[328,1536]{1,0:T(8,128)S(1)} %convolution_add_fusion), kind=kLoop, calls=%fused_computation.24 | loop fusion | flops 982720 | bytes 3933440 | tf_op jit(solution)/shard_map/reduce_sum | solution.py:85
  65.5 0.7 convolution_add_fusion.3
  66.5 1.3 %copy-done = f32[328,1536]{1,0:T(8,128)} copy-done((f32[328,1536]{1,0:T(8,128)}, f32[328,1536]{1,0:T(8,128)S(1)}, u32[]{:S(2)}) %copy-start) | copy-done | bytes 2015256
  67.8 0.6 multiply_reduce_fusion.5
  69.8 1.4 %multiply_multiply_fusion = f32[1,1536]{1,0:T(1,128)S(1)} fusion(f32[328,1536]{1,0:T(8,128)} %copy-done, f32[]{:T(128)S(6)} %rsqrt.33, f32[]{:T(128)} %bitcast.15), kind=kLoop, calls=%fused_computation.100 | loop fusion | flops 3072 | bytes 12296 | tf_op jit(solution)/shard_map/mul | solution.py:173
  71.3 1.9 %slice_multiply_fusion.1 = f32[319,1536]{1,0:T(8,128)S(1)} fusion(f32[320,1536]{1,0:T(8,128)} %get-tuple-element.8, f32[319]{0:T(512)S(1)} %bitcast.84), kind=kLoop, calls=%fused_computation.16 | loop fusion | flops 489984 | bytes 3921148 | tf_op jit(solution)/shard_map/mul | solution.py:86
  73.4 0.6 multiply_reduce_fusion.2
  74.1 0.8 multiply_reduce_fusion
  75.8 0.9 copy-done.5
  76.7 0.7 fusion.68
  77.4 1.2 %fusion.4 = f32[128,1536]{1,0:T(8,128)S(1)} fusion(bf16[1,320,1536]{2,1,0:T(8,128)(2,1)S(1)} %copy-done.2, f32[320]{0:T(512)S(1)} %get-tuple-element.21, s32[320]{0:T(512)S(1)} %get-tuple-element.23), kind=kOutput, calls=%fused_computation.14 | convolution fusion | flops 755998720 | bytes 1772032 | tf_op jit(solution)/shard_map/dot_general | solution.py:159
  79.7 0.7 concatenate.31
  80.3 1.5 %collective-permute-start.11 = (f32[1,1664]{1,0:T(1,128)S(1)}, f32[1,1664]{1,0:T(1,128)S(1)}, u32[]{:S(2)}, u32[]{:S(2)}) collective-permute-start(f32[1,1664]{1,0:T(1,128)S(1)} %concatenate.31), channel_id=1, source_target_pairs={{4,0},{8,4},{12,8},{16,12},{20,16},{24,20},{28,24},{5,1},{9,5},{13... | collective-permute-start | bytes 19976 | tf_op jit(solution)/shard_map/ppermute | solution.py:16
  81.9 0.7 fusion.6
  82.6 0.7 fusion.71
  83.3 0.6 copy-done.9
  83.9 0.7 fusion.70
  84.6 2.1 %fusion.69 = f32[320,384]{1,0:T(8,128)S(1)} fusion(bf16[320,1536]{1,0:T(8,128)(2,1)S(1)} %subtract_convert_fusion, bf16[384,1536]{1,0:T(8,128)(2,1)} %collective-permute-done.8), kind=kOutput, calls=%fused_computation.150 | convolution fusion | flops 377487360 | bytes 2654208 | tf_op jit(solution)/shard_map/dot_general | solution.py:178
  86.6 0.7 fusion.9
  87.3 2.0 %fusion.8 = bf16[320,384]{1,0:T(8,128)(2,1)S(1)} fusion(f32[320,384]{1,0:T(8,128)S(1)} %fusion.70, bf16[320,1536]{1,0:T(8,128)(2,1)S(1)} %get-tuple-element.6, bf16[384,1536]{1,0:T(8,128)(2,1)} %collective-permute-done.6), kind=kOutput, calls=%fused_computation.34 | convolution fusion | flops 377733120 | bytes 2899968 | tf_op jit(solution)/shard_map/dot_general | solution.py:177
  89.3 2.0 %fusion.7 = bf16[320,384]{1,0:T(8,128)(2,1)S(1)} fusion(f32[320,384]{1,0:T(8,128)S(1)} %fusion.69, bf16[320,1536]{1,0:T(8,128)(2,1)S(1)} %get-tuple-element.6, bf16[384,1536]{1,0:T(8,128)(2,1)} %collective-permute-done.5), kind=kOutput, calls=%fused_computation.33 | convolution fusion | flops 377733120 | bytes 2899968 | tf_op jit(solution)/shard_map/dot_general | solution.py:177
  91.4 0.7 fusion.45
  92.0 1.3 %collective-permute-start.12 = (f32[1,1664]{1,0:T(1,128)S(1)}, f32[1,1664]{1,0:T(1,128)S(1)}, u32[]{:S(2)}, u32[]{:S(2)}) collective-permute-start(f32[1,1664]{1,0:T(1,128)S(1)} %fusion.45), channel_id=1, source_target_pairs={{8,0},{12,4},{16,8},{20,12},{24,16},{28,20},{9,1},{13,5},{17,9},{2... | collective-permute-start | bytes 19976 | tf_op jit(solution)/shard_map/ppermute | solution.py:16
  93.5 0.5 slice.132
  94.7 0.5 slice.130
  95.9 3.5 %collective-permute-done.12 = f32[1,1664]{1,0:T(1,128)S(1)} collective-permute-done((f32[1,1664]{1,0:T(1,128)S(1)}, f32[1,1664]{1,0:T(1,128)S(1)}, u32[]{:S(2)}, u32[]{:S(2)}) %collective-permute-start.12) | collective-permute-done | bytes 6688 | tf_op jit(solution)/shard_map/ppermute | solution.py:16
  99.4 1.3 %collective-permute-start.13 = (f32[1,1664]{1,0:T(1,128)S(1)}, f32[1,1664]{1,0:T(1,128)S(1)}, u32[]{:S(2)}, u32[]{:S(2)}) collective-permute-start(f32[1,1664]{1,0:T(1,128)S(1)} %get-tuple-element.15), channel_id=1, source_target_pairs={{16,0},{20,4},{24,8},{28,12},{17,1},{21,5},{25,9},{29,13},{18,2},{... | collective-permute-start | bytes 19976 | tf_op jit(solution)/shard_map/ppermute | solution.py:16
  100.7 1.0 maximum_bitcast_fusion
  102.9 2.9 %collective-permute-done.13 = f32[1,1664]{1,0:T(1,128)S(1)} collective-permute-done((f32[1,1664]{1,0:T(1,128)S(1)}, f32[1,1664]{1,0:T(1,128)S(1)}, u32[]{:S(2)}, u32[]{:S(2)}) %collective-permute-start.13) | collective-permute-done | bytes 6688 | tf_op jit(solution)/shard_map/ppermute | solution.py:16
  105.8 1.7 %fusion.3 = bf16[1,128,1536]{2,1,0:T(8,128)(2,1)} fusion(f32[128,1536]{1,0:T(8,128)S(1)} %fusion.4, f32[1536]{0:T(1024)S(1)} %fusion.50, f32[128]{0:T(128)S(1)} %get-tuple-element.26, f32[128]{0:T(128)S(1)} %bitcast_select_fusion, f32[128]{0:T(128)S(1)} %reduce.2), kind=kOutput, calls=%fused_computation.13 | convolution fusion | flops 302841856 | bytes 1187328 | tf_op jit(solution)/shard_map/dot_general | solution.py:166
  (77 shorter events, 6.2 us)
Async XLA Ops:
  0.6 45.0 %collective-permute-start.5 = (bf16[384,1536]{1,0:T(8,128)(2,1)}, bf16[384,1536]{1,0:T(8,128)(2,1)}, u32[]{:S(2)}, u32[]{:S(2)}) collective-permute-start(bf16[384,1536]{1,0:T(8,128)(2,1)} %param.14), channel_id=1, source_target_pairs={{0,2},{1,3},{2,0},{3,1},{4,6},{5,7},{6,4},{7,5},{8,10},{9,11},{10,... | collective-permute-start | bytes 3538952 | tf_op jit(solution)/shard_map/ppermute | solution.py:48
  3.7 55.5 %collective-permute-start.6 = (bf16[384,1536]{1,0:T(8,128)(2,1)}, bf16[384,1536]{1,0:T(8,128)(2,1)}, u32[]{:S(2)}, u32[]{:S(2)}) collective-permute-start(bf16[384,1536]{1,0:T(8,128)(2,1)} %param.14), channel_id=1, source_target_pairs={{0,1},{1,0},{2,3},{3,2},{4,5},{5,4},{6,7},{7,6},{8,9},{9,8},{10,11... | collective-permute-start | bytes 3538952 | tf_op jit(solution)/shard_map/ppermute | solution.py:51
  9.1 11.3 %collective-permute-start.1 = (f32[1,1664]{1,0:T(1,128)S(1)}, f32[1,1664]{1,0:T(1,128)S(1)}, u32[]{:S(2)}, u32[]{:S(2)}) collective-permute-start(f32[1,1664]{1,0:T(1,128)S(1)} %concatenate.24), channel_id=1, source_target_pairs={{0,4},{4,8},{8,12},{12,16},{16,20},{20,24},{24,28},{1,5},{5,9},{9,... | collective-permute-start | bytes 19976 | tf_op jit(solution)/shard_map/ppermute | solution.py:16
  13.3 30.1 %collective-permute-start = (bf16[1,1536]{1,0:T(2,128)(2,1)S(1)}, bf16[1,1536]{1,0:T(2,128)(2,1)S(1)}, u32[]{:S(2)}, u32[]{:S(2)}) collective-permute-start(bf16[1,1536]{1,0:T(2,128)(2,1)S(1)} %get-tuple-element.13), channel_id=1, source_target_pairs={{0,4},{4,8},{8,12},{12,16},{16,20},{20,24},{24,28},{1,5},{5,9},{9,... | collective-permute-start | bytes 9224 | tf_op jit(solution)/shard_map/ppermute | solution.py:16
  16.8 38.5 %collective-permute-start.8 = (bf16[384,1536]{1,0:T(8,128)(2,1)}, bf16[384,1536]{1,0:T(8,128)(2,1)}, u32[]{:S(2)}, u32[]{:S(2)}) collective-permute-start(bf16[384,1536]{1,0:T(8,128)(2,1)} %param.15), channel_id=1, source_target_pairs={{0,2},{1,3},{2,0},{3,1},{4,6},{5,7},{6,4},{7,5},{8,10},{9,11},{10,... | collective-permute-start | bytes 3538952 | tf_op jit(solution)/shard_map/ppermute | solution.py:48
  21.1 6.0 %collective-permute-start.2 = (f32[1,1664]{1,0:T(1,128)S(1)}, f32[1,1664]{1,0:T(1,128)S(1)}, u32[]{:S(2)}, u32[]{:S(2)}) collective-permute-start(f32[1,1664]{1,0:T(1,128)S(1)} %fusion.42), channel_id=1, source_target_pairs={{0,8},{4,12},{8,16},{12,20},{16,24},{20,28},{1,9},{5,13},{9,17},{1... | collective-permute-start | bytes 19976 | tf_op jit(solution)/shard_map/ppermute | solution.py:16
  27.1 5.8 %collective-permute-start.3 = (f32[1,1664]{1,0:T(1,128)S(1)}, f32[1,1664]{1,0:T(1,128)S(1)}, u32[]{:S(2)}, u32[]{:S(2)}) collective-permute-start(f32[1,1664]{1,0:T(1,128)S(1)} %get-tuple-element.17), channel_id=1, source_target_pairs={{0,16},{4,20},{8,24},{12,28},{1,17},{5,21},{9,25},{13,29},{2,18},{... | collective-permute-start | bytes 19976 | tf_op jit(solution)/shard_map/ppermute | solution.py:16
  32.9 10.5 %copy-start.3 = (bf16[384,1536]{1,0:T(8,128)(2,1)S(1)}, bf16[384,1536]{1,0:T(8,128)(2,1)}, u32[]{:S(2)}) copy-start(bf16[384,1536]{1,0:T(8,128)(2,1)} %param.15) | copy-start | bytes 3538948
  33.0 10.5 %copy-start.12 = (bf16[1,320,1536]{2,1,0:T(8,128)(2,1)S(1)}, bf16[1,320,1536]{2,1,0:T(8,128)(2,1)}, u32[]{:S(2)}) copy-start(bf16[1,320,1536]{2,1,0:T(8,128)(2,1)} %param.8) | copy-start | bytes 2949124
  36.9 6.5 %collective-permute-start.4 = (f32[1,1537]{1,0:T(1,128)S(1)}, f32[1,1537]{1,0:T(1,128)S(1)}, u32[]{:S(2)}, u32[]{:S(2)}) collective-permute-start(f32[1,1537]{1,0:T(1,128)S(1)} %pad_maximum_fusion.3), channel_id=1, source_target_pairs={{4,0},{8,4},{12,8},{16,12},{20,16},{24,20},{28,24},{5,1},{9,5},{13... | collective-permute-start | bytes 18452 | tf_op jit(solution)/shard_map/ppermute | solution.py:16
  40.9 2.9 %copy-start.4 = (bf16[384,1536]{1,0:T(8,128)(2,1)S(1)}, bf16[384,1536]{1,0:T(8,128)(2,1)}, u32[]{:S(2)}) copy-start(bf16[384,1536]{1,0:T(8,128)(2,1)} %param.14) | copy-start | bytes 3538948
  43.4 17.8 %collective-permute-start.9 = (bf16[384,1536]{1,0:T(8,128)(2,1)S(1)}, bf16[384,1536]{1,0:T(8,128)(2,1)S(1)}, u32[]{:S(2)}, u32[]{:S(2)}) collective-permute-start(bf16[384,1536]{1,0:T(8,128)(2,1)S(1)} %copy-done.3), channel_id=1, source_target_pairs={{0,1},{1,0},{2,3},{3,2},{4,5},{5,4},{6,7},{7,6},{8,9},{9,8},{10,11... | collective-permute-start | bytes 3538952 | tf_op jit(solution)/shard_map/ppermute | solution.py:51
  45.7 19.8 %collective-permute-start.7 = (bf16[384,1536]{1,0:T(8,128)(2,1)}, bf16[384,1536]{1,0:T(8,128)(2,1)S(1)}, u32[]{:S(2)}, u32[]{:S(2)}) collective-permute-start(bf16[384,1536]{1,0:T(8,128)(2,1)} %collective-permute-done.5), channel_id=1, source_target_pairs={{0,1},{1,0},{2,3},{3,2},{4,5},{5,4},{6,7},{7,6},{8,9},{9,8},{10,11... | collective-permute-start | bytes 3538952 | tf_op jit(solution)/shard_map/ppermute | solution.py:51
  55.2 7.1 %collective-permute-start.10 = (bf16[384,1536]{1,0:T(8,128)(2,1)}, bf16[384,1536]{1,0:T(8,128)(2,1)S(1)}, u32[]{:S(2)}, u32[]{:S(2)}) collective-permute-start(bf16[384,1536]{1,0:T(8,128)(2,1)} %collective-permute-done.8), channel_id=1, source_target_pairs={{0,1},{1,0},{2,3},{3,2},{4,5},{5,4},{6,7},{7,6},{8,9},{9,8},{10,11... | collective-permute-start | bytes 3538952 | tf_op jit(solution)/shard_map/ppermute | solution.py:51
  61.2 1.1 %copy-start.8 = (bf16[384,1536]{1,0:T(8,128)(2,1)}, bf16[384,1536]{1,0:T(8,128)(2,1)S(1)}, u32[]{:S(2)}) copy-start(bf16[384,1536]{1,0:T(8,128)(2,1)S(1)} %collective-permute-done.9) | copy-start | bytes 3538948
  62.3 1.1 %copy-start.10 = (bf16[384,1536]{1,0:T(8,128)(2,1)}, bf16[384,1536]{1,0:T(8,128)(2,1)S(1)}, u32[]{:S(2)}) copy-start(bf16[384,1536]{1,0:T(8,128)(2,1)S(1)} %collective-permute-done.10) | copy-start | bytes 3538948
  65.5 1.1 copy-start.6
  66.5 1.3 %copy-start = (f32[328,1536]{1,0:T(8,128)}, f32[328,1536]{1,0:T(8,128)S(1)}, u32[]{:S(2)}) copy-start(f32[328,1536]{1,0:T(8,128)S(1)} %convolution_add_fusion.3) | copy-start | bytes 6045700
  71.3 2.2 %copy-start.1 = (f32[328,1536]{1,0:T(8,128)S(1)}, f32[328,1536]{1,0:T(8,128)}, u32[]{:S(2)}) copy-start(f32[328,1536]{1,0:T(8,128)} %copy-done) | copy-start | bytes 6045700
  75.4 1.3 %copy-start.5 = (bf16[384,1536]{1,0:T(8,128)(2,1)S(1)}, bf16[384,1536]{1,0:T(8,128)(2,1)}, u32[]{:S(2)}) copy-start(bf16[384,1536]{1,0:T(8,128)(2,1)} %param.14) | copy-start | bytes 3538948
  75.7 1.6 %copy-start.2 = (bf16[1,320,1536]{2,1,0:T(8,128)(2,1)S(1)}, bf16[1,320,1536]{2,1,0:T(8,128)(2,1)}, u32[]{:S(2)}) copy-start(bf16[1,320,1536]{2,1,0:T(8,128)(2,1)} %param.9) | copy-start | bytes 2949124
  79.1 3.4 %copy-start.11 = (bf16[384,1536]{1,0:T(8,128)(2,1)S(1)}, bf16[384,1536]{1,0:T(8,128)(2,1)}, u32[]{:S(2)}) copy-start(bf16[384,1536]{1,0:T(8,128)(2,1)} %copy-done.10) | copy-start | bytes 3538948
  80.3 11.0 %collective-permute-start.11 = (f32[1,1664]{1,0:T(1,128)S(1)}, f32[1,1664]{1,0:T(1,128)S(1)}, u32[]{:S(2)}, u32[]{:S(2)}) collective-permute-start(f32[1,1664]{1,0:T(1,128)S(1)} %concatenate.31), channel_id=1, source_target_pairs={{4,0},{8,4},{12,8},{16,12},{20,16},{24,20},{28,24},{5,1},{9,5},{13... | collective-permute-start | bytes 19976 | tf_op jit(solution)/shard_map/ppermute | solution.py:16
  82.6 1.3 %copy-start.9 = (bf16[384,1536]{1,0:T(8,128)(2,1)S(1)}, bf16[384,1536]{1,0:T(8,128)(2,1)}, u32[]{:S(2)}) copy-start(bf16[384,1536]{1,0:T(8,128)(2,1)} %copy-done.8) | copy-start | bytes 3538948
  84.5 2.1 %copy-start.7 = (bf16[384,1536]{1,0:T(8,128)(2,1)S(1)}, bf16[384,1536]{1,0:T(8,128)(2,1)}, u32[]{:S(2)}) copy-start(bf16[384,1536]{1,0:T(8,128)(2,1)} %copy-done.6) | copy-start | bytes 3538948
  92.0 7.3 %collective-permute-start.12 = (f32[1,1664]{1,0:T(1,128)S(1)}, f32[1,1664]{1,0:T(1,128)S(1)}, u32[]{:S(2)}, u32[]{:S(2)}) collective-permute-start(f32[1,1664]{1,0:T(1,128)S(1)} %fusion.45), channel_id=1, source_target_pairs={{8,0},{12,4},{16,8},{20,12},{24,16},{28,20},{9,1},{13,5},{17,9},{2... | collective-permute-start | bytes 19976 | tf_op jit(solution)/shard_map/ppermute | solution.py:16
  99.4 6.4 %collective-permute-start.13 = (f32[1,1664]{1,0:T(1,128)S(1)}, f32[1,1664]{1,0:T(1,128)S(1)}, u32[]{:S(2)}, u32[]{:S(2)}) collective-permute-start(f32[1,1664]{1,0:T(1,128)S(1)} %get-tuple-element.15), channel_id=1, source_target_pairs={{16,0},{20,4},{24,8},{28,12},{17,1},{21,5},{25,9},{29,13},{18,2},{... | collective-permute-start | bytes 19976 | tf_op jit(solution)/shard_map/ppermute | solution.py:16

commit v21 on v16

--- a/solution.py
+++ b/solution.py
@@ -21,7 +21,7 @@
     return scales * unit_grad - scales * scales * scales * inner_prod * vectors
 
 
-def seq_scan(log_keep, vectors, axis, from_lower):
+def seq_scan(log_keep, vectors, axis, from_lower, held=None):
     size = lax.axis_size(axis)
     width = vectors.shape[-1]
     tail = jnp.zeros(vectors.shape[:-1] + (128,), vectors.dtype)
@@ -31,10 +31,14 @@
     step = 1
     while step < size:
         got = shifted(incl, axis, step if from_lower else -step)
+        if held is not None and step == 1:
+            got, held = lax.optimization_barrier((got, held))
         excl = jnp.where(is_vec, jnp.exp(excl[:, width:width + 1]) * got, got) + excl
         if 2 * step < size:
             incl = jnp.where(is_vec, jnp.exp(incl[:, width:width + 1]) * got, got) + incl
         step *= 2
+    if held is not None:
+        return excl[:, :width], held
     return excl[:, :width]
 
 
@@ -159,7 +163,9 @@
     back_vector = base_vector + jnp.dot(
         (owner_keep * rise * cosine)[None, :], grad_wide, precision=exact
     )
-    grad_in = seq_scan(last_log, back_vector, "seq", False)
+    grad_in, (key_rows, key_scale, query_unit, query_next) = seq_scan(
+        last_log, back_vector, "seq", False, (key_rows, key_scale, query_unit, query_next)
+    )
     reach_end = jnp.exp(running[slot_count - 1] - running)
     state_grad = (
         lax.dot_general(decay_table, slot_grad, contract_first, precision=exact)

time: 106 us -> 112 us (1.057)
  matrix products: 25 us -> 31.3 us
  other arithmetic: 16.5 us -> 18.6 us
  waiting for transfers between devices: 14.4 us -> 12.7 us
    dot_general x8, matrix products: 8.06 us -> 11.9 us  [split_dot(): term = jnp.dot(part, block, preferred_element_type=jnp.float32)]
    dot_general x4, matrix products: 4.05 us -> 6.82 us  [per_device(): lax.dot_general(query_grad, q_block, contract_last, preferred_element_typ...]
    concatenate x1, other arithmetic: 0.08 us -> 1.27 us  [per_device(): rows_ext = jnp.concatenate([token_rows, prev_row, next_row], axis=0)]
    reduce_sum x1, other arithmetic: 0.79 us -> 1.98 us  [per_device(): cosine = jnp.sum(query_unit * key_prior, axis=1)]
    unnamed x30 -> x28, local copies, waits for them, and re-layouts: 4.81 us -> 4.13 us
  transfers between devices with their start and end apart: 14 -> 14, of which waited for: 3 -> 2; matrix products, arithmetic and copies ran while one was open for 36% -> 45% of each run, Pallas kernels for 0% -> 0%
where the time goes in v21:
time: 112 us; the launch traced here: 110 us
  matrix products  31.3 us (28%)
  starting transfers between devices  24 us (21%)
  other arithmetic  18.6 us (17%)
  local copies, waits for them, and re-layouts  13.4 us (12%)
  waiting for transfers between devices  12.7 us (11%)
  between operations  10.5 us (9%)
    ppermute x8, starting transfers between devices, shifted(): return lax.ppermute(block, axis, route)  19.7 us
    dot_general x8, matrix products, split_dot(): term = jnp.dot(part, block, preferred_element_type=jnp.float32)  11.9 us
    ppermute x2, waiting for transfers between devices, gather_blocks(): pairs.append(lax.ppermute(blocks, axis, route))  7.44 us
    dot_general x4, matrix products, per_device(): lax.dot_general(query_grad, q_block, contract_last, preferred_element_typ...  6.82 us
    ppermute x8, waiting for transfers between devices, shifted(): return lax.ppermute(block, axis, route)  5.26 us
    unnamed x28, local copies, waits for them, and re-layouts  4.13 us
    dot_general x4, matrix products, per_device(): lax.dot_general(key_grad, k_block, contract_last, preferred_element_type=...  4.11 us
    ppermute x2, starting transfers between devices, gather_blocks(): pairs.append(lax.ppermute(blocks, axis, route))  3.6 us
  transfers between devices with their start and end apart: 14, of which 2 were waited for; matrix products, arithmetic and copies ran while one was open for 45% of the time, Pallas kernels for 0%

profile of v21, /device:TPU:0, one launch (start us, length us, event | category | flops | bytes accessed | tf_op | source)
XLA Modules:
  0.0 110.4 jit_solution(6973400424896591198)
XLA Ops:
  0.6 3.0 %collective-permute-start.8 = (bf16[384,1536]{1,0:T(8,128)(2,1)}, bf16[384,1536]{1,0:T(8,128)(2,1)S(1)}, u32[]{:S(2)}, u32[]{:S(2)}) collective-permute-start(bf16[384,1536]{1,0:T(8,128)(2,1)} %param.15), channel_id=1, source_target_pairs={{0,2},{1,3},{2,0},{3,1},{4,6},{5,7},{6,4},{7,5},{8,10},{9,11},{10,... | collective-permute-start | bytes 3538952 | tf_op jit(solution)/shard_map/ppermute | solution.py:52
  4.3 0.7 bitcast_select_fusion
  5.0 0.7 fusion.65
  5.9 0.5 slice.113
  6.6 1.9 %fusion.14 = f32[128,1536]{1,0:T(8,128)S(1)} fusion(bf16[1,128,1536]{2,1,0:T(8,128)(2,1)} %param.10, f32[128]{0:T(128)S(1)} %bitcast_select_fusion, f32[128]{0:T(128)S(1)} %reduce.2), kind=kOutput, calls=%fused_computation.46 | convolution fusion | flops 302448640 | bytes 1180672 | tf_op jit(solution)/shard_map/dot_general | solution.py:130
  8.5 0.7 concatenate.24
  9.1 3.4 %collective-permute-start.1 = (f32[1,1664]{1,0:T(1,128)S(1)}, f32[1,1664]{1,0:T(1,128)S(1)}, u32[]{:S(2)}, u32[]{:S(2)}) collective-permute-start(f32[1,1664]{1,0:T(1,128)S(1)} %concatenate.24), channel_id=1, source_target_pairs={{0,4},{4,8},{8,12},{12,16},{16,20},{20,24},{24,28},{1,5},{5,9},{9,... | collective-permute-start | bytes 19976 | tf_op jit(solution)/shard_map/ppermute | solution.py:16
  12.5 0.8 slice_bitcast_fusion
  13.3 3.5 %collective-permute-start = (bf16[1,1536]{1,0:T(2,128)(2,1)S(1)}, bf16[1,1536]{1,0:T(2,128)(2,1)S(1)}, u32[]{:S(2)}, u32[]{:S(2)}) collective-permute-start(bf16[1,1536]{1,0:T(2,128)(2,1)S(1)} %get-tuple-element.25), channel_id=1, source_target_pairs={{0,4},{4,8},{8,12},{12,16},{16,20},{20,24},{24,28},{1,5},{5,9},{9,... | collective-permute-start | bytes 9224 | tf_op jit(solution)/shard_map/ppermute | solution.py:16
  16.8 0.6 collective-permute-start.5
  17.4 0.8 fusion.32
  18.2 0.8 convert_reduce_fusion
  19.0 0.7 subtract_exponential_fusion
  20.5 0.7 fusion.42
  21.1 3.5 %collective-permute-start.2 = (f32[1,1664]{1,0:T(1,128)S(1)}, f32[1,1664]{1,0:T(1,128)S(1)}, u32[]{:S(2)}, u32[]{:S(2)}) collective-permute-start(f32[1,1664]{1,0:T(1,128)S(1)} %fusion.42), channel_id=1, source_target_pairs={{0,8},{4,12},{8,16},{12,20},{16,24},{20,28},{1,9},{5,13},{9,17},{1... | collective-permute-start | bytes 19976 | tf_op jit(solution)/shard_map/ppermute | solution.py:16
  24.7 0.5 slice.116
  25.9 0.5 slice.114
  27.1 4.0 %collective-permute-start.3 = (f32[1,1664]{1,0:T(1,128)S(1)}, f32[1,1664]{1,0:T(1,128)S(1)}, u32[]{:S(2)}, u32[]{:S(2)}) collective-permute-start(f32[1,1664]{1,0:T(1,128)S(1)} %get-tuple-element.29), channel_id=1, source_target_pairs={{0,16},{4,20},{8,24},{12,28},{1,17},{5,21},{9,25},{13,29},{2,18},{... | collective-permute-start | bytes 19976 | tf_op jit(solution)/shard_map/ppermute | solution.py:16
  31.2 0.6 fusion.69
  32.9 2.7 %fusion.5 = f32[320]{0:T(512)S(1)} fusion(bf16[1,320,1536]{2,1,0:T(8,128)(2,1)} %param.9, f32[1536]{0:T(1024)S(1)} %fusion.51, f32[320]{0:T(512)S(1)} %compare_convert_fusion, f32[128,1536]{1,0:T(8,128)S(1)} %fusion.14, f32[128]{0:T(128)S(1)} %get-tuple-element.39, s32[320]{0:T(512)S(1)} %get-tuple-element.36), kind=kOutput, calls=%fused_computation.27 | convolution fusion | flops 757866176 | bytes 1779968 | tf_op jit(solution)/shard_map/dot_general | solution.py:135
  36.1 0.6 pad_maximum_fusion.4
  36.7 1.3 %collective-permute-start.4 = (f32[1,1537]{1,0:T(1,128)S(1)}, f32[1,1537]{1,0:T(1,128)S(1)}, u32[]{:S(2)}, u32[]{:S(2)}) collective-permute-start(f32[1,1537]{1,0:T(1,128)S(1)} %pad_maximum_fusion.4), channel_id=1, source_target_pairs={{4,0},{8,4},{12,8},{16,12},{20,16},{24,20},{28,24},{5,1},{9,5},{13... | collective-permute-start | bytes 18452 | tf_op jit(solution)/shard_map/ppermute | solution.py:16
  40.5 2.4 %gather_fusion = f32[320]{0:T(512)S(1)} fusion(f32[128]{0:T(128)S(1)} %get-tuple-element.39, s32[1024]{0:T(1024)S(1)} %pad_clamp_fusion), kind=kCustom, calls=%fused_computation | custom fusion | bytes 3840 | tf_op jit(solution)/shard_map/gather | solution.py:138
  43.0 0.5 slice.129
  43.6 1.3 %pad_maximum_fusion.2 = bf16[322,1536]{1,0:T(8,128)(2,1)S(1)} fusion(bf16[1,1536]{1,0:T(2,128)(2,1)S(1)} %slice.171, bf16[1,1536]{1,0:T(2,128)(2,1)S(1)} %collective-permute-done, bf16[320,1536]{1,0:T(8,128)(2,1)} %bitcast.83), kind=kLoop, calls=%fused_computation.38 | loop fusion | flops 2967552 | bytes 1978368 | tf_op jit(solution)/shard_map/concatenate | solution.py:148
  44.9 0.7 fusion.25
  45.6 1.0 copy-done.6
  46.5 0.7 convolution_add_fusion.2
  47.2 0.6 collective-permute-start.10
  47.8 7.4 %collective-permute-done.5 = bf16[384,1536]{1,0:T(8,128)(2,1)} collective-permute-done((bf16[384,1536]{1,0:T(8,128)(2,1)}, bf16[384,1536]{1,0:T(8,128)(2,1)}, u32[]{:S(2)}, u32[]{:S(2)}) %collective-permute-start.5) | collective-permute-done | bytes 1179680 | tf_op jit(solution)/shard_map/ppermute | solution.py:52
  55.2 2.0 %fusion.27 = f32[322,1536]{1,0:T(8,128)S(1)} fusion(bf16[384,1536]{1,0:T(8,128)(2,1)} %collective-permute-done.5, bf16[322,1536]{1,0:T(8,128)(2,1)S(1)} %pad_maximum_fusion.2, s32[]{:T(128)S(6)} %select_n.162), kind=kOutput, calls=%fused_computation.59 | convolution fusion | flops 379846656 | bytes 3409924 | tf_op jit(solution)/shard_map/dot_general | solution.py:77
  57.3 2.0 %convolution_add_fusion.5 = f32[322,1536]{1,0:T(8,128)S(1)} fusion(f32[322,1536]{1,0:T(8,128)S(1)} %fusion.27, bf16[384,1536]{1,0:T(8,128)(2,1)} %param.14, bf16[322,1536]{1,0:T(8,128)(2,1)S(1)} %pad_maximum_fusion.2, s32[]{:T(128)S(6)} %select_n.160), kind=kOutput, calls=%fused_computation.6 | convolution fusion | flops 380341248 | bytes 5425156 | tf_op jit(solution)/shard_map/dot_general | solution.py:77
  59.2 2.0 %convolution_add_fusion.1 = f32[322,1536]{1,0:T(8,128)S(1)} fusion(f32[322,1536]{1,0:T(8,128)S(1)} %convolution_add_fusion.2, bf16[384,1536]{1,0:T(8,128)(2,1)} %collective-permute-done.9, bf16[322,1536]{1,0:T(8,128)(2,1)S(1)} %pad_maximum_fusion.2, s32[]{:T(128)S(6)} %select_n.163), kind=kOutput, calls=%fused_computation.2 | convolution fusion | flops 380341248 | bytes 5425156 | tf_op jit(solution)/shard_map/dot_general | solution.py:77
  61.2 2.0 %convolution_add_fusion.4 = f32[322,1536]{1,0:T(8,128)} fusion(f32[322,1536]{1,0:T(8,128)S(1)} %convolution_add_fusion.5, bf16[384,1536]{1,0:T(8,128)(2,1)S(1)} %collective-permute-done.6, bf16[322,1536]{1,0:T(8,128)(2,1)S(1)} %pad_maximum_fusion.2, s32[]{:T(128)S(6)} %select_n.163), kind=kOutput, calls=%fused_computation.5 | convolution fusion | flops 380341248 | bytes 5425156 | tf_op jit(solution)/shard_map/dot_general | solution.py:77
  63.3 0.7 convolution_add_fusion
  64.3 1.3 %copy-done.4 = f32[322,1536]{1,0:T(8,128)} copy-done((f32[322,1536]{1,0:T(8,128)}, f32[322,1536]{1,0:T(8,128)S(1)}, u32[]{:S(2)}) %copy-start.4) | copy-done | bytes 1978392
  65.6 0.6 multiply_reduce_fusion.6
  66.9 2.0 %multiply_reduce_fusion.3 = (f32[320]{0:T(512)S(1)}, f32[320,1536]{1,0:T(8,128)S(1)}) fusion(f32[322,1536]{1,0:T(8,128)} %copy-done.4), kind=kLoop, calls=%fused_computation.24 | loop fusion | flops 982720 | bytes 3933440 | tf_op jit(solution)/shard_map/reduce_sum | solution.py:89
  68.9 0.8 slice_multiply_fusion.4
  69.7 2.0 %convolution_add_fusion.3 = f32[322,1536]{1,0:T(8,128)S(1)} fusion(f32[322,1536]{1,0:T(8,128)S(1)} %copy-done.3, bf16[384,1536]{1,0:T(8,128)(2,1)} %collective-permute-done.7, bf16[322,1536]{1,0:T(8,128)(2,1)S(1)} %pad_maximum_fusion.2, s32[]{:T(128)S(6)} %select_n.164), kind=kOutput, calls=%fused_computation.4 | convolution fusion | flops 380341248 | bytes 5425156 | tf_op jit(solution)/shard_map/dot_general | solution.py:77
  71.7 0.8 multiply_reduce_fusion.5
  72.7 0.6 multiply_reduce_fusion.2
  73.4 2.0 %multiply_reduce_fusion.1 = (f32[320]{0:T(512)S(1)}, f32[320,1536]{1,0:T(8,128)}, bf16[320,1536]{1,0:T(8,128)(2,1)S(1)}) fusion(f32[319,1536]{1,0:T(8,128)S(1)} %slice_multiply_fusion.1, f32[1,1536]{1,0:T(1,128)S(1)} %slice_multiply_fusion.4, f32[320]{0:T(512)S(1)} %get-tuple-element.35, f32[322,1536]{1,0:T(8,128)S(1)} %convolution_add_fusion.3, ...), kind=kLoop, calls=%fused_computation.21 | loop fusion | flops 4423360 | bytes 6886400 | tf_op jit(solution)/shard_map/reduce_sum | solution.py:158
  76.4 0.7 concatenate.28
  77.1 1.5 %collective-permute-start.11 = (f32[1,1664]{1,0:T(1,128)S(1)}, f32[1,1664]{1,0:T(1,128)S(1)}, u32[]{:S(2)}, u32[]{:S(2)}) collective-permute-start(f32[1,1664]{1,0:T(1,128)S(1)} %concatenate.28), channel_id=1, source_target_pairs={{4,0},{8,4},{12,8},{16,12},{20,16},{24,20},{28,24},{5,1},{9,5},{13... | collective-permute-start | bytes 19976 | tf_op jit(solution)/shard_map/ppermute | solution.py:16
  79.2 0.9 slice_multiply_fusion.3
  80.1 2.1 %fusion.70 = f32[320,384]{1,0:T(8,128)S(1)} fusion(bf16[320,1536]{1,0:T(8,128)(2,1)S(1)} %get-tuple-element.18, bf16[384,1536]{1,0:T(8,128)(2,1)} %param.14), kind=kOutput, calls=%fused_computation.152 | convolution fusion | flops 377487360 | bytes 2654208 | tf_op jit(solution)/shard_map/dot_general | solution.py:182
  82.2 1.2 %fusion.4 = f32[128,1536]{1,0:T(8,128)S(1)} fusion(bf16[1,320,1536]{2,1,0:T(8,128)(2,1)S(1)} %copy-done.2, f32[320]{0:T(512)S(1)} %get-tuple-element.33, s32[320]{0:T(512)S(1)} %get-tuple-element.36), kind=kOutput, calls=%fused_computation.14 | convolution fusion | flops 755998720 | bytes 1772032 | tf_op jit(solution)/shard_map/dot_general | solution.py:162
  83.5 0.7 fusion.45
  84.1 1.3 %collective-permute-start.12 = (f32[1,1664]{1,0:T(1,128)S(1)}, f32[1,1664]{1,0:T(1,128)S(1)}, u32[]{:S(2)}, u32[]{:S(2)}) collective-permute-start(f32[1,1664]{1,0:T(1,128)S(1)} %fusion.45), channel_id=1, source_target_pairs={{8,0},{12,4},{16,8},{20,12},{24,16},{28,20},{9,1},{13,5},{17,9},{2... | collective-permute-start | bytes 19976 | tf_op jit(solution)/shard_map/ppermute | solution.py:16
  85.4 0.6 broadcast_multiply_fusion
  86.9 0.9 copy-done.7
  87.8 0.7 fusion.6
  88.5 0.6 copy-done.13
  89.1 0.7 fusion.73
  89.8 2.0 %fusion.72 = f32[320,384]{1,0:T(8,128)S(1)} fusion(bf16[320,1536]{1,0:T(8,128)(2,1)S(1)} %subtract_convert_fusion, bf16[384,1536]{1,0:T(8,128)(2,1)} %collective-permute-done.9), kind=kOutput, calls=%fused_computation.154 | convolution fusion | flops 377487360 | bytes 2654208 | tf_op jit(solution)/shard_map/dot_general | solution.py:183
  91.9 0.7 fusion.71
  92.6 2.1 %fusion.9 = bf16[320,384]{1,0:T(8,128)(2,1)S(1)} fusion(f32[320,384]{1,0:T(8,128)S(1)} %fusion.73, bf16[320,1536]{1,0:T(8,128)(2,1)S(1)} %get-tuple-element.18, bf16[384,1536]{1,0:T(8,128)(2,1)} %collective-permute-done.7), kind=kOutput, calls=%fused_computation.35 | convolution fusion | flops 377733120 | bytes 2899968 | tf_op jit(solution)/shard_map/dot_general | solution.py:182
  94.6 0.7 fusion.8
  95.3 2.0 %fusion.7 = bf16[320,384]{1,0:T(8,128)(2,1)S(1)} fusion(f32[320,384]{1,0:T(8,128)S(1)} %fusion.71, bf16[320,1536]{1,0:T(8,128)(2,1)S(1)} %get-tuple-element.18, bf16[384,1536]{1,0:T(8,128)(2,1)} %collective-permute-done.5), kind=kOutput, calls=%fused_computation.33 | convolution fusion | flops 377733120 | bytes 2899968 | tf_op jit(solution)/shard_map/dot_general | solution.py:182
  100.0 1.3 %collective-permute-start.13 = (f32[1,1664]{1,0:T(1,128)S(1)}, f32[1,1664]{1,0:T(1,128)S(1)}, u32[]{:S(2)}, u32[]{:S(2)}) collective-permute-start(f32[1,1664]{1,0:T(1,128)S(1)} %get-tuple-element.27), channel_id=1, source_target_pairs={{16,0},{20,4},{24,8},{28,12},{17,1},{21,5},{25,9},{29,13},{18,2},{... | collective-permute-start | bytes 19976 | tf_op jit(solution)/shard_map/ppermute | solution.py:16
  101.3 1.0 maximum_bitcast_fusion
  103.5 5.2 %collective-permute-done.13 = f32[1,1664]{1,0:T(1,128)S(1)} collective-permute-done((f32[1,1664]{1,0:T(1,128)S(1)}, f32[1,1664]{1,0:T(1,128)S(1)}, u32[]{:S(2)}, u32[]{:S(2)}) %collective-permute-start.13) | collective-permute-done | bytes 6688 | tf_op jit(solution)/shard_map/ppermute | solution.py:16
  108.8 1.7 %fusion.3 = bf16[1,128,1536]{2,1,0:T(8,128)(2,1)} fusion(f32[128,1536]{1,0:T(8,128)S(1)} %fusion.4, f32[1536]{0:T(1024)S(1)} %fusion.50, f32[128]{0:T(128)S(1)} %get-tuple-element.38, f32[128]{0:T(128)S(1)} %bitcast_select_fusion, f32[128]{0:T(128)S(1)} %reduce.2), kind=kOutput, calls=%fused_computation.13 | convolution fusion | flops 302841856 | bytes 1187328 | tf_op jit(solution)/shard_map/dot_general | solution.py:171
  (79 shorter events, 6.2 us)
Async XLA Ops:
  0.6 44.2 %collective-permute-start.8 = (bf16[384,1536]{1,0:T(8,128)(2,1)}, bf16[384,1536]{1,0:T(8,128)(2,1)S(1)}, u32[]{:S(2)}, u32[]{:S(2)}) collective-permute-start(bf16[384,1536]{1,0:T(8,128)(2,1)} %param.15), channel_id=1, source_target_pairs={{0,2},{1,3},{2,0},{3,1},{4,6},{5,7},{6,4},{7,5},{8,10},{9,11},{10,... | collective-permute-start | bytes 3538952 | tf_op jit(solution)/shard_map/ppermute | solution.py:52
  3.7 55.6 %collective-permute-start.9 = (bf16[384,1536]{1,0:T(8,128)(2,1)}, bf16[384,1536]{1,0:T(8,128)(2,1)}, u32[]{:S(2)}, u32[]{:S(2)}) collective-permute-start(bf16[384,1536]{1,0:T(8,128)(2,1)} %param.15), channel_id=1, source_target_pairs={{0,1},{1,0},{2,3},{3,2},{4,5},{5,4},{6,7},{7,6},{8,9},{9,8},{10,11... | collective-permute-start | bytes 3538952 | tf_op jit(solution)/shard_map/ppermute | solution.py:55
  9.1 11.3 %collective-permute-start.1 = (f32[1,1664]{1,0:T(1,128)S(1)}, f32[1,1664]{1,0:T(1,128)S(1)}, u32[]{:S(2)}, u32[]{:S(2)}) collective-permute-start(f32[1,1664]{1,0:T(1,128)S(1)} %concatenate.24), channel_id=1, source_target_pairs={{0,4},{4,8},{8,12},{12,16},{16,20},{20,24},{24,28},{1,5},{5,9},{9,... | collective-permute-start | bytes 19976 | tf_op jit(solution)/shard_map/ppermute | solution.py:16
  13.3 30.3 %collective-permute-start = (bf16[1,1536]{1,0:T(2,128)(2,1)S(1)}, bf16[1,1536]{1,0:T(2,128)(2,1)S(1)}, u32[]{:S(2)}, u32[]{:S(2)}) collective-permute-start(bf16[1,1536]{1,0:T(2,128)(2,1)S(1)} %get-tuple-element.25), channel_id=1, source_target_pairs={{0,4},{4,8},{8,12},{12,16},{16,20},{20,24},{24,28},{1,5},{5,9},{9,... | collective-permute-start | bytes 9224 | tf_op jit(solution)/shard_map/ppermute | solution.py:16
  16.8 38.5 %collective-permute-start.5 = (bf16[384,1536]{1,0:T(8,128)(2,1)}, bf16[384,1536]{1,0:T(8,128)(2,1)}, u32[]{:S(2)}, u32[]{:S(2)}) collective-permute-start(bf16[384,1536]{1,0:T(8,128)(2,1)} %param.14), channel_id=1, source_target_pairs={{0,2},{1,3},{2,0},{3,1},{4,6},{5,7},{6,4},{7,5},{8,10},{9,11},{10,... | collective-permute-start | bytes 3538952 | tf_op jit(solution)/shard_map/ppermute | solution.py:52
  21.1 6.0 %collective-permute-start.2 = (f32[1,1664]{1,0:T(1,128)S(1)}, f32[1,1664]{1,0:T(1,128)S(1)}, u32[]{:S(2)}, u32[]{:S(2)}) collective-permute-start(f32[1,1664]{1,0:T(1,128)S(1)} %fusion.42), channel_id=1, source_target_pairs={{0,8},{4,12},{8,16},{12,20},{16,24},{20,28},{1,9},{5,13},{9,17},{1... | collective-permute-start | bytes 19976 | tf_op jit(solution)/shard_map/ppermute | solution.py:16
  27.1 5.8 %collective-permute-start.3 = (f32[1,1664]{1,0:T(1,128)S(1)}, f32[1,1664]{1,0:T(1,128)S(1)}, u32[]{:S(2)}, u32[]{:S(2)}) collective-permute-start(f32[1,1664]{1,0:T(1,128)S(1)} %get-tuple-element.29), channel_id=1, source_target_pairs={{0,16},{4,20},{8,24},{12,28},{1,17},{5,21},{9,25},{13,29},{2,18},{... | collective-permute-start | bytes 19976 | tf_op jit(solution)/shard_map/ppermute | solution.py:16
  36.7 6.3 %collective-permute-start.4 = (f32[1,1537]{1,0:T(1,128)S(1)}, f32[1,1537]{1,0:T(1,128)S(1)}, u32[]{:S(2)}, u32[]{:S(2)}) collective-permute-start(f32[1,1537]{1,0:T(1,128)S(1)} %pad_maximum_fusion.4), channel_id=1, source_target_pairs={{4,0},{8,4},{12,8},{16,12},{20,16},{24,20},{28,24},{5,1},{9,5},{13... | collective-permute-start | bytes 18452 | tf_op jit(solution)/shard_map/ppermute | solution.py:16
  43.0 18.2 %collective-permute-start.6 = (bf16[384,1536]{1,0:T(8,128)(2,1)}, bf16[384,1536]{1,0:T(8,128)(2,1)S(1)}, u32[]{:S(2)}, u32[]{:S(2)}) collective-permute-start(bf16[384,1536]{1,0:T(8,128)(2,1)} %param.14), channel_id=1, source_target_pairs={{0,1},{1,0},{2,3},{3,2},{4,5},{5,4},{6,7},{7,6},{8,9},{9,8},{10,11... | collective-permute-start | bytes 3538952 | tf_op jit(solution)/shard_map/ppermute | solution.py:55
  44.8 1.7 %copy-start.6 = (bf16[384,1536]{1,0:T(8,128)(2,1)S(1)}, bf16[384,1536]{1,0:T(8,128)(2,1)}, u32[]{:S(2)}) copy-start(bf16[384,1536]{1,0:T(8,128)(2,1)} %param.15) | copy-start | bytes 3538948
  44.9 2.4 %copy-start.8 = (bf16[384,1536]{1,0:T(8,128)(2,1)}, bf16[384,1536]{1,0:T(8,128)(2,1)S(1)}, u32[]{:S(2)}) copy-start(bf16[384,1536]{1,0:T(8,128)(2,1)S(1)} %collective-permute-done.8) | copy-start | bytes 3538948
  47.2 16.0 %collective-permute-start.10 = (bf16[384,1536]{1,0:T(8,128)(2,1)S(1)}, bf16[384,1536]{1,0:T(8,128)(2,1)S(1)}, u32[]{:S(2)}, u32[]{:S(2)}) collective-permute-start(bf16[384,1536]{1,0:T(8,128)(2,1)S(1)} %collective-permute-done.8), channel_id=1, source_target_pairs={{0,1},{1,0},{2,3},{3,2},{4,5},{5,4},{6,7},{7,6},{8,9},{9,8},{10,11... | collective-permute-start | bytes 3538952 | tf_op jit(solution)/shard_map/ppermute | solution.py:55
  57.2 12.5 %collective-permute-start.7 = (bf16[384,1536]{1,0:T(8,128)(2,1)}, bf16[384,1536]{1,0:T(8,128)(2,1)}, u32[]{:S(2)}, u32[]{:S(2)}) collective-permute-start(bf16[384,1536]{1,0:T(8,128)(2,1)} %collective-permute-done.5), channel_id=1, source_target_pairs={{0,1},{1,0},{2,3},{3,2},{4,5},{5,4},{6,7},{7,6},{8,9},{9,8},{10,11... | collective-permute-start | bytes 3538952 | tf_op jit(solution)/shard_map/ppermute | solution.py:55
  61.2 2.0 %copy-start.10 = (bf16[384,1536]{1,0:T(8,128)(2,1)}, bf16[384,1536]{1,0:T(8,128)(2,1)S(1)}, u32[]{:S(2)}) copy-start(bf16[384,1536]{1,0:T(8,128)(2,1)S(1)} %collective-permute-done.6) | copy-start | bytes 3538948
  63.3 1.0 copy-start.12
  64.3 1.3 %copy-start.4 = (f32[322,1536]{1,0:T(8,128)}, f32[322,1536]{1,0:T(8,128)S(1)}, u32[]{:S(2)}) copy-start(f32[322,1536]{1,0:T(8,128)S(1)} %convolution_add_fusion) | copy-start | bytes 5935108
  66.9 2.8 %copy-start.3 = (f32[322,1536]{1,0:T(8,128)S(1)}, f32[322,1536]{1,0:T(8,128)}, u32[]{:S(2)}) copy-start(f32[322,1536]{1,0:T(8,128)} %convolution_add_fusion.4) | copy-start | bytes 5935108
  71.7 1.7 %copy-start = (f32[322,1536]{1,0:T(8,128)}, f32[322,1536]{1,0:T(8,128)S(1)}, u32[]{:S(2)}) copy-start(f32[322,1536]{1,0:T(8,128)S(1)} %convolution_add_fusion.3) | copy-start | bytes 5935108
  73.3 2.0 %copy-start.1 = (bf16[1,320,1536]{2,1,0:T(8,128)(2,1)S(1)}, bf16[1,320,1536]{2,1,0:T(8,128)(2,1)}, u32[]{:S(2)}) copy-start(bf16[1,320,1536]{2,1,0:T(8,128)(2,1)} %param.9) | copy-start | bytes 2949124
  77.1 6.4 %collective-permute-start.11 = (f32[1,1664]{1,0:T(1,128)S(1)}, f32[1,1664]{1,0:T(1,128)S(1)}, u32[]{:S(2)}, u32[]{:S(2)}) collective-permute-start(f32[1,1664]{1,0:T(1,128)S(1)} %concatenate.28), channel_id=1, source_target_pairs={{4,0},{8,4},{12,8},{16,12},{20,16},{24,20},{28,24},{5,1},{9,5},{13... | collective-permute-start | bytes 19976 | tf_op jit(solution)/shard_map/ppermute | solution.py:16
  79.2 3.0 %copy-start.2 = (bf16[1,320,1536]{2,1,0:T(8,128)(2,1)S(1)}, bf16[1,320,1536]{2,1,0:T(8,128)(2,1)}, u32[]{:S(2)}) copy-start(bf16[1,320,1536]{2,1,0:T(8,128)(2,1)} %param.9) | copy-start | bytes 2949124
  80.1 5.9 %copy-start.5 = (f32[320,1536]{1,0:T(8,128)S(1)}, f32[320,1536]{1,0:T(8,128)}, u32[]{:S(2)}) copy-start(f32[320,1536]{1,0:T(8,128)} %get-tuple-element.8) | copy-start | bytes 5898244
  84.1 15.8 %collective-permute-start.12 = (f32[1,1664]{1,0:T(1,128)S(1)}, f32[1,1664]{1,0:T(1,128)S(1)}, u32[]{:S(2)}, u32[]{:S(2)}) collective-permute-start(f32[1,1664]{1,0:T(1,128)S(1)} %fusion.45), channel_id=1, source_target_pairs={{8,0},{12,4},{16,8},{20,12},{24,16},{28,20},{9,1},{13,5},{17,9},{2... | collective-permute-start | bytes 19976 | tf_op jit(solution)/shard_map/ppermute | solution.py:16
  86.6 1.3 %copy-start.7 = (bf16[384,1536]{1,0:T(8,128)(2,1)S(1)}, bf16[384,1536]{1,0:T(8,128)(2,1)}, u32[]{:S(2)}) copy-start(bf16[384,1536]{1,0:T(8,128)(2,1)} %param.15) | copy-start | bytes 3538948
  87.8 1.3 %copy-start.13 = (bf16[384,1536]{1,0:T(8,128)(2,1)S(1)}, bf16[384,1536]{1,0:T(8,128)(2,1)}, u32[]{:S(2)}) copy-start(bf16[384,1536]{1,0:T(8,128)(2,1)} %copy-done.12) | copy-start | bytes 3538948
  89.8 2.1 %copy-start.9 = (bf16[384,1536]{1,0:T(8,128)(2,1)S(1)}, bf16[384,1536]{1,0:T(8,128)(2,1)}, u32[]{:S(2)}) copy-start(bf16[384,1536]{1,0:T(8,128)(2,1)} %copy-done.8) | copy-start | bytes 3538948
  92.6 2.1 %copy-start.11 = (bf16[384,1536]{1,0:T(8,128)(2,1)S(1)}, bf16[384,1536]{1,0:T(8,128)(2,1)}, u32[]{:S(2)}) copy-start(bf16[384,1536]{1,0:T(8,128)(2,1)} %copy-done.10) | copy-start | bytes 3538948
  100.0 8.8 %collective-permute-start.13 = (f32[1,1664]{1,0:T(1,128)S(1)}, f32[1,1664]{1,0:T(1,128)S(1)}, u32[]{:S(2)}, u32[]{:S(2)}) collective-permute-start(f32[1,1664]{1,0:T(1,128)S(1)} %get-tuple-element.27), channel_id=1, source_target_pairs={{16,0},{20,4},{24,8},{28,12},{17,1},{21,5},{25,9},{29,13},{18,2},{... | collective-permute-start | bytes 19976 | tf_op jit(solution)/shard_map/ppermute | solution.py:16

commit v22 on v16

--- a/solution.py
+++ b/solution.py
@@ -151,7 +151,12 @@
     key_before, _ = unit_of(keys_ext[token_count : token_count + 1])
     query_next, _ = unit_of(queries_ext[token_count + 1 :])
     key_prior = jnp.concatenate([key_before, key_unit[:-1]], axis=0)
-    cosine = jnp.sum(query_unit * key_prior, axis=1)
+    raw_prior = jnp.concatenate([keys_ext[token_count : token_count + 1], key_rows[:-1]], axis=0)
+    prior_sq = jnp.sum(raw_prior * raw_prior, axis=1)
+    query_sq = jnp.sum(queries * queries, axis=1)
+    cosine = (
+        jnp.sum(queries * raw_prior, axis=1) * lax.rsqrt(query_sq + norm_eps) * lax.rsqrt(prior_sq + norm_eps)
+    )
     boundary_prob = jnp.where(later_rows, 0.5 * (1.0 - cosine), 1.0)
     confidence = jnp.where(starts, boundary_prob, 1.0 - boundary_prob)
     weighted_grad = confidence[:, None] * grad_rows

time: 106 us -> 108 us (1.019)
  other arithmetic: 16.5 us -> 18.8 us
    reduce_sum x1, other arithmetic: 0.79 us -> 2.8 us  [per_device(): jnp.sum(queries * raw_prior, axis=1) * lax.rsqrt(query_sq + norm_eps)]
    concatenate x1, other arithmetic: 0.08 us -> 1.27 us  [per_device(): rows_ext = jnp.concatenate([token_rows, prev_row, next_row], axis=0)]
where the time goes in v22:
time: 108 us; the launch traced here: 107 us
  matrix products  24.8 us (23%)
  starting transfers between devices  24.1 us (22%)
  other arithmetic  18.8 us (17%)
  local copies, waits for them, and re-layouts  15.2 us (14%)
  waiting for transfers between devices  13.9 us (13%)
  between operations  10.5 us (10%)
    ppermute x8, starting transfers between devices, shifted(): return lax.ppermute(block, axis, route)  19.9 us
    dot_general x8, matrix products, split_dot(): term = jnp.dot(part, block, preferred_element_type=jnp.float32)  8.07 us
    ppermute x2, waiting for transfers between devices, gather_blocks(): pairs.append(lax.ppermute(blocks, axis, route))  7.55 us
    ppermute x8, waiting for transfers between devices, shifted(): return lax.ppermute(block, axis, route)  6.38 us
    unnamed x30, local copies, waits for them, and re-layouts  5.62 us
    dot_general x4, matrix products, per_device(): lax.dot_general(key_grad, k_block, contract_last, preferred_element_type=...  4.11 us
    dot_general x4, matrix products, per_device(): lax.dot_general(query_grad, q_block, contract_last, preferred_element_typ...  4.06 us
    ppermute x2, starting transfers between devices, gather_blocks(): pairs.append(lax.ppermute(blocks, axis, route))  3.6 us
  transfers between devices with their start and end apart: 14, of which 3 were waited for; matrix products, arithmetic and copies ran while one was open for 36% of the time, Pallas kernels for 0%

profile of v22, /device:TPU:0, one launch (start us, length us, event | category | flops | bytes accessed | tf_op | source)
XLA Modules:
  0.0 107.3 jit_solution(12830519002702087408)
XLA Ops:
  0.6 3.0 %collective-permute-start.5 = (bf16[384,1536]{1,0:T(8,128)(2,1)}, bf16[384,1536]{1,0:T(8,128)(2,1)S(1)}, u32[]{:S(2)}, u32[]{:S(2)}) collective-permute-start(bf16[384,1536]{1,0:T(8,128)(2,1)} %param.14), channel_id=1, source_target_pairs={{0,2},{1,3},{2,0},{3,1},{4,6},{5,7},{6,4},{7,5},{8,10},{9,11},{10,... | collective-permute-start | bytes 3538952 | tf_op jit(solution)/shard_map/ppermute | solution.py:48
  4.3 0.7 bitcast_select_fusion
  5.0 0.7 fusion.65
  5.9 0.5 slice.119
  6.6 1.9 %fusion.15 = f32[128,1536]{1,0:T(8,128)S(1)} fusion(bf16[1,128,1536]{2,1,0:T(8,128)(2,1)} %param.10, f32[128]{0:T(128)S(1)} %bitcast_select_fusion, f32[128]{0:T(128)S(1)} %reduce.2), kind=kOutput, calls=%fused_computation.48 | convolution fusion | flops 302448640 | bytes 1180672 | tf_op jit(solution)/shard_map/dot_general | solution.py:126
  8.5 0.7 concatenate.27
  9.1 3.4 %collective-permute-start.1 = (f32[1,1664]{1,0:T(1,128)S(1)}, f32[1,1664]{1,0:T(1,128)S(1)}, u32[]{:S(2)}, u32[]{:S(2)}) collective-permute-start(f32[1,1664]{1,0:T(1,128)S(1)} %concatenate.27), channel_id=1, source_target_pairs={{0,4},{4,8},{8,12},{12,16},{16,20},{20,24},{24,28},{1,5},{5,9},{9,... | collective-permute-start | bytes 19976 | tf_op jit(solution)/shard_map/ppermute | solution.py:16
  12.5 0.8 slice_bitcast_fusion
  13.3 3.5 %collective-permute-start = (bf16[1,1536]{1,0:T(2,128)(2,1)S(1)}, bf16[1,1536]{1,0:T(2,128)(2,1)S(1)}, u32[]{:S(2)}, u32[]{:S(2)}) collective-permute-start(bf16[1,1536]{1,0:T(2,128)(2,1)S(1)} %get-tuple-element.16), channel_id=1, source_target_pairs={{0,4},{4,8},{8,12},{12,16},{16,20},{20,24},{24,28},{1,5},{5,9},{9,... | collective-permute-start | bytes 9224 | tf_op jit(solution)/shard_map/ppermute | solution.py:16
  16.8 0.6 collective-permute-start.8
  17.4 0.8 fusion.33
  18.2 0.8 convert_reduce_fusion
  19.0 0.7 subtract_exponential_fusion
  20.5 0.7 fusion.43
  21.1 3.5 %collective-permute-start.2 = (f32[1,1664]{1,0:T(1,128)S(1)}, f32[1,1664]{1,0:T(1,128)S(1)}, u32[]{:S(2)}, u32[]{:S(2)}) collective-permute-start(f32[1,1664]{1,0:T(1,128)S(1)} %fusion.43), channel_id=1, source_target_pairs={{0,8},{4,12},{8,16},{12,20},{16,24},{20,28},{1,9},{5,13},{9,17},{1... | collective-permute-start | bytes 19976 | tf_op jit(solution)/shard_map/ppermute | solution.py:16
  24.7 0.5 slice.122
  25.9 0.5 slice.120
  27.1 4.0 %collective-permute-start.3 = (f32[1,1664]{1,0:T(1,128)S(1)}, f32[1,1664]{1,0:T(1,128)S(1)}, u32[]{:S(2)}, u32[]{:S(2)}) collective-permute-start(f32[1,1664]{1,0:T(1,128)S(1)} %get-tuple-element.22), channel_id=1, source_target_pairs={{0,16},{4,20},{8,24},{12,28},{1,17},{5,21},{9,25},{13,29},{2,18},{... | collective-permute-start | bytes 19976 | tf_op jit(solution)/shard_map/ppermute | solution.py:16
  31.2 0.6 fusion.68
  33.0 2.7 %fusion.6 = f32[320]{0:T(512)S(1)} fusion(bf16[1,320,1536]{2,1,0:T(8,128)(2,1)} %param.9, f32[1536]{0:T(1024)S(1)} %fusion.52, f32[320]{0:T(512)S(1)} %compare_convert_fusion, f32[128,1536]{1,0:T(8,128)S(1)} %fusion.15, f32[128]{0:T(128)S(1)} %get-tuple-element.30, s32[320]{0:T(512)S(1)} %get-tuple-element.28), kind=kOutput, calls=%fused_computation.29 | convolution fusion | flops 757866176 | bytes 1779968 | tf_op jit(solution)/shard_map/dot_general | solution.py:131
  36.2 0.6 pad_maximum_fusion.4
  36.8 1.5 %collective-permute-start.4 = (f32[1,1537]{1,0:T(1,128)S(1)}, f32[1,1537]{1,0:T(1,128)S(1)}, u32[]{:S(2)}, u32[]{:S(2)}) collective-permute-start(f32[1,1537]{1,0:T(1,128)S(1)} %pad_maximum_fusion.4), channel_id=1, source_target_pairs={{4,0},{8,4},{12,8},{16,12},{20,16},{24,20},{28,24},{5,1},{9,5},{13... | collective-permute-start | bytes 18452 | tf_op jit(solution)/shard_map/ppermute | solution.py:16
  40.8 2.4 %gather_fusion = f32[320]{0:T(512)S(1)} fusion(f32[128]{0:T(128)S(1)} %get-tuple-element.30, s32[1024]{0:T(1024)S(1)} %pad_clamp_fusion), kind=kCustom, calls=%fused_computation | custom fusion | bytes 3840 | tf_op jit(solution)/shard_map/gather | solution.py:134
  43.3 0.5 slice.135
  43.9 1.3 %pad_maximum_fusion.2 = bf16[322,1536]{1,0:T(8,128)(2,1)S(1)} fusion(bf16[1,1536]{1,0:T(2,128)(2,1)S(1)} %slice.184, bf16[1,1536]{1,0:T(2,128)(2,1)S(1)} %collective-permute-done, bf16[320,1536]{1,0:T(8,128)(2,1)} %bitcast.83), kind=kLoop, calls=%fused_computation.40 | loop fusion | flops 2967552 | bytes 1978368 | tf_op jit(solution)/shard_map/concatenate | solution.py:144
  45.2 0.7 fusion.28
  45.9 0.6 copy-done.9
  46.4 0.7 convolution_add_fusion.5
  47.1 0.6 collective-permute-start.7
  47.7 7.6 %collective-permute-done.8 = bf16[384,1536]{1,0:T(8,128)(2,1)} collective-permute-done((bf16[384,1536]{1,0:T(8,128)(2,1)}, bf16[384,1536]{1,0:T(8,128)(2,1)}, u32[]{:S(2)}, u32[]{:S(2)}) %collective-permute-start.8) | collective-permute-done | bytes 1179680 | tf_op jit(solution)/shard_map/ppermute | solution.py:48
  55.2 1.9 %fusion.26 = f32[322,1536]{1,0:T(8,128)S(1)} fusion(bf16[384,1536]{1,0:T(8,128)(2,1)} %collective-permute-done.8, bf16[322,1536]{1,0:T(8,128)(2,1)S(1)} %pad_maximum_fusion.2, s32[]{:T(128)S(6)} %select_n.162), kind=kOutput, calls=%fused_computation.59 | convolution fusion | flops 379846656 | bytes 3409924 | tf_op jit(solution)/shard_map/dot_general | solution.py:73
  57.2 0.7 convolution_add_fusion.2
  57.9 2.0 %convolution_add_fusion.4 = f32[322,1536]{1,0:T(8,128)S(1)} fusion(f32[322,1536]{1,0:T(8,128)S(1)} %convolution_add_fusion.5, bf16[384,1536]{1,0:T(8,128)(2,1)} %collective-permute-done.6, bf16[322,1536]{1,0:T(8,128)(2,1)S(1)} %pad_maximum_fusion.2, s32[]{:T(128)S(6)} %select_n.163), kind=kOutput, calls=%fused_computation.5 | convolution fusion | flops 380341248 | bytes 5425156 | tf_op jit(solution)/shard_map/dot_general | solution.py:73
  59.9 0.7 convolution_add_fusion.1
  61.0 0.7 convolution_add_fusion
  62.0 0.7 multiply_reduce_fusion.7
  62.7 1.5 %multiply_reduce_fusion.4 = (f32[320]{0:T(512)S(1)}, f32[320,1536]{1,0:T(8,128)}) fusion(f32[322,1536]{1,0:T(8,128)S(1)} %convolution_add_fusion), kind=kLoop, calls=%fused_computation.27 | loop fusion | flops 982720 | bytes 3933440 | tf_op jit(solution)/shard_map/reduce_sum | solution.py:85
  64.2 0.7 convolution_add_fusion.3
  65.2 1.3 %copy-done.2 = f32[322,1536]{1,0:T(8,128)} copy-done((f32[322,1536]{1,0:T(8,128)}, f32[322,1536]{1,0:T(8,128)S(1)}, u32[]{:S(2)}) %copy-start.2) | copy-done | bytes 1978392
  66.5 0.7 multiply_reduce_fusion.6
  68.5 1.9 %slice_multiply_fusion.1 = f32[319,1536]{1,0:T(8,128)S(1)} fusion(f32[320,1536]{1,0:T(8,128)} %get-tuple-element.11, f32[319]{0:T(512)S(1)} %bitcast.84), kind=kLoop, calls=%fused_computation.17 | loop fusion | flops 489984 | bytes 3921148 | tf_op jit(solution)/shard_map/mul | solution.py:86
  70.6 2.8 %multiply_reduce_fusion.1 = (f32[320]{0:T(512)S(1)}, f32[320]{0:T(512)S(1)}, f32[320]{0:T(512)S(1)}, f32[320]{0:T(512)S(1)}) fusion(f32[319,1536]{1,0:T(8,128)S(1)} %slice-done, f32[1,1536]{1,0:T(1,128)S(1)} %get-tuple-element.9, f32[322,1536]{1,0:T(8,128)} %copy-done.2, f32[319,1536]{1,0:T(8,128)S(1)} %slice_multiply_fusion.1, ...), kind=kLoop, calls=%fused_computation.22 | loop fusion | flops 5405440 | bytes 5904640 | tf_op jit(solution)/shard_map/reduce_sum | solution.py:158
  74.0 0.6 multiply_multiply_fusion
  75.0 1.2 %copy-done.1 = f32[322,1536]{1,0:T(8,128)S(1)} copy-done((f32[322,1536]{1,0:T(8,128)S(1)}, f32[322,1536]{1,0:T(8,128)}, u32[]{:S(2)}) %copy-start.1) | copy-done | bytes 1978392
  76.9 0.9 copy-done.10
  77.8 0.7 fusion.69
  78.5 1.2 %fusion.4 = f32[128,1536]{1,0:T(8,128)S(1)} fusion(bf16[1,320,1536]{2,1,0:T(8,128)(2,1)S(1)} %copy-done.4, f32[320]{0:T(512)S(1)} %get-tuple-element.21, s32[320]{0:T(512)S(1)} %get-tuple-element.28), kind=kOutput, calls=%fused_computation.14 | convolution fusion | flops 755998720 | bytes 1772032 | tf_op jit(solution)/shard_map/dot_general | solution.py:163
  80.8 0.7 concatenate.35
  81.5 1.5 %collective-permute-start.11 = (f32[1,1664]{1,0:T(1,128)S(1)}, f32[1,1664]{1,0:T(1,128)S(1)}, u32[]{:S(2)}, u32[]{:S(2)}) collective-permute-start(f32[1,1664]{1,0:T(1,128)S(1)} %concatenate.35), channel_id=1, source_target_pairs={{4,0},{8,4},{12,8},{16,12},{20,16},{24,20},{28,24},{5,1},{9,5},{13... | collective-permute-start | bytes 19976 | tf_op jit(solution)/shard_map/ppermute | solution.py:16
  83.0 0.7 fusion.7
  83.7 0.7 fusion.72
  84.4 0.6 copy-done.12
  85.0 0.7 fusion.71
  85.7 2.1 %fusion.70 = f32[320,384]{1,0:T(8,128)S(1)} fusion(bf16[320,1536]{1,0:T(8,128)(2,1)S(1)} %subtract_convert_fusion, bf16[384,1536]{1,0:T(8,128)(2,1)} %collective-permute-done.8), kind=kOutput, calls=%fused_computation.153 | convolution fusion | flops 377487360 | bytes 2654208 | tf_op jit(solution)/shard_map/dot_general | solution.py:182
  87.7 0.7 fusion.10
  88.4 2.0 %fusion.9 = bf16[320,384]{1,0:T(8,128)(2,1)S(1)} fusion(f32[320,384]{1,0:T(8,128)S(1)} %fusion.71, bf16[320,1536]{1,0:T(8,128)(2,1)S(1)} %get-tuple-element.6, bf16[384,1536]{1,0:T(8,128)(2,1)} %collective-permute-done.6), kind=kOutput, calls=%fused_computation.36 | convolution fusion | flops 377733120 | bytes 2899968 | tf_op jit(solution)/shard_map/dot_general | solution.py:181
  90.4 0.7 fusion.8
  91.2 0.7 fusion.46
  91.9 1.3 %collective-permute-start.12 = (f32[1,1664]{1,0:T(1,128)S(1)}, f32[1,1664]{1,0:T(1,128)S(1)}, u32[]{:S(2)}, u32[]{:S(2)}) collective-permute-start(f32[1,1664]{1,0:T(1,128)S(1)} %fusion.46), channel_id=1, source_target_pairs={{8,0},{12,4},{16,8},{20,12},{24,16},{28,20},{9,1},{13,5},{17,9},{2... | collective-permute-start | bytes 19976 | tf_op jit(solution)/shard_map/ppermute | solution.py:16
  95.7 3.5 %collective-permute-done.12 = f32[1,1664]{1,0:T(1,128)S(1)} collective-permute-done((f32[1,1664]{1,0:T(1,128)S(1)}, f32[1,1664]{1,0:T(1,128)S(1)}, u32[]{:S(2)}, u32[]{:S(2)}) %collective-permute-start.12) | collective-permute-done | bytes 6688 | tf_op jit(solution)/shard_map/ppermute | solution.py:16
  99.2 1.3 %collective-permute-start.13 = (f32[1,1664]{1,0:T(1,128)S(1)}, f32[1,1664]{1,0:T(1,128)S(1)}, u32[]{:S(2)}, u32[]{:S(2)}) collective-permute-start(f32[1,1664]{1,0:T(1,128)S(1)} %get-tuple-element.18), channel_id=1, source_target_pairs={{16,0},{20,4},{24,8},{28,12},{17,1},{21,5},{25,9},{29,13},{18,2},{... | collective-permute-start | bytes 19976 | tf_op jit(solution)/shard_map/ppermute | solution.py:16
  100.5 1.0 maximum_bitcast_fusion
  102.7 2.9 %collective-permute-done.13 = f32[1,1664]{1,0:T(1,128)S(1)} collective-permute-done((f32[1,1664]{1,0:T(1,128)S(1)}, f32[1,1664]{1,0:T(1,128)S(1)}, u32[]{:S(2)}, u32[]{:S(2)}) %collective-permute-start.13) | collective-permute-done | bytes 6688 | tf_op jit(solution)/shard_map/ppermute | solution.py:16
  105.7 1.7 %fusion.3 = bf16[1,128,1536]{2,1,0:T(8,128)(2,1)} fusion(f32[128,1536]{1,0:T(8,128)S(1)} %fusion.4, f32[1536]{0:T(1024)S(1)} %fusion.51, f32[128]{0:T(128)S(1)} %get-tuple-element.29, f32[128]{0:T(128)S(1)} %bitcast_select_fusion, f32[128]{0:T(128)S(1)} %reduce.2), kind=kOutput, calls=%fused_computation.13 | convolution fusion | flops 302841856 | bytes 1187328 | tf_op jit(solution)/shard_map/dot_general | solution.py:170
  (81 shorter events, 7.4 us)
Async XLA Ops:
  0.6 44.5 %collective-permute-start.5 = (bf16[384,1536]{1,0:T(8,128)(2,1)}, bf16[384,1536]{1,0:T(8,128)(2,1)S(1)}, u32[]{:S(2)}, u32[]{:S(2)}) collective-permute-start(bf16[384,1536]{1,0:T(8,128)(2,1)} %param.14), channel_id=1, source_target_pairs={{0,2},{1,3},{2,0},{3,1},{4,6},{5,7},{6,4},{7,5},{8,10},{9,11},{10,... | collective-permute-start | bytes 3538952 | tf_op jit(solution)/shard_map/ppermute | solution.py:48
  3.7 54.2 %collective-permute-start.6 = (bf16[384,1536]{1,0:T(8,128)(2,1)}, bf16[384,1536]{1,0:T(8,128)(2,1)}, u32[]{:S(2)}, u32[]{:S(2)}) collective-permute-start(bf16[384,1536]{1,0:T(8,128)(2,1)} %param.14), channel_id=1, source_target_pairs={{0,1},{1,0},{2,3},{3,2},{4,5},{5,4},{6,7},{7,6},{8,9},{9,8},{10,11... | collective-permute-start | bytes 3538952 | tf_op jit(solution)/shard_map/ppermute | solution.py:51
  9.1 11.3 %collective-permute-start.1 = (f32[1,1664]{1,0:T(1,128)S(1)}, f32[1,1664]{1,0:T(1,128)S(1)}, u32[]{:S(2)}, u32[]{:S(2)}) collective-permute-start(f32[1,1664]{1,0:T(1,128)S(1)} %concatenate.27), channel_id=1, source_target_pairs={{0,4},{4,8},{8,12},{12,16},{16,20},{20,24},{24,28},{1,5},{5,9},{9,... | collective-permute-start | bytes 19976 | tf_op jit(solution)/shard_map/ppermute | solution.py:16
  13.3 30.6 %collective-permute-start = (bf16[1,1536]{1,0:T(2,128)(2,1)S(1)}, bf16[1,1536]{1,0:T(2,128)(2,1)S(1)}, u32[]{:S(2)}, u32[]{:S(2)}) collective-permute-start(bf16[1,1536]{1,0:T(2,128)(2,1)S(1)} %get-tuple-element.16), channel_id=1, source_target_pairs={{0,4},{4,8},{8,12},{12,16},{16,20},{20,24},{24,28},{1,5},{5,9},{9,... | collective-permute-start | bytes 9224 | tf_op jit(solution)/shard_map/ppermute | solution.py:16
  16.8 38.5 %collective-permute-start.8 = (bf16[384,1536]{1,0:T(8,128)(2,1)}, bf16[384,1536]{1,0:T(8,128)(2,1)}, u32[]{:S(2)}, u32[]{:S(2)}) collective-permute-start(bf16[384,1536]{1,0:T(8,128)(2,1)} %param.15), channel_id=1, source_target_pairs={{0,2},{1,3},{2,0},{3,1},{4,6},{5,7},{6,4},{7,5},{8,10},{9,11},{10,... | collective-permute-start | bytes 3538952 | tf_op jit(solution)/shard_map/ppermute | solution.py:48
  21.1 6.0 %collective-permute-start.2 = (f32[1,1664]{1,0:T(1,128)S(1)}, f32[1,1664]{1,0:T(1,128)S(1)}, u32[]{:S(2)}, u32[]{:S(2)}) collective-permute-start(f32[1,1664]{1,0:T(1,128)S(1)} %fusion.43), channel_id=1, source_target_pairs={{0,8},{4,12},{8,16},{12,20},{16,24},{20,28},{1,9},{5,13},{9,17},{1... | collective-permute-start | bytes 19976 | tf_op jit(solution)/shard_map/ppermute | solution.py:16
  27.1 5.8 %collective-permute-start.3 = (f32[1,1664]{1,0:T(1,128)S(1)}, f32[1,1664]{1,0:T(1,128)S(1)}, u32[]{:S(2)}, u32[]{:S(2)}) collective-permute-start(f32[1,1664]{1,0:T(1,128)S(1)} %get-tuple-element.22), channel_id=1, source_target_pairs={{0,16},{4,20},{8,24},{12,28},{1,17},{5,21},{9,25},{13,29},{2,18},{... | collective-permute-start | bytes 19976 | tf_op jit(solution)/shard_map/ppermute | solution.py:16
  32.9 10.3 %copy-start.5 = (bf16[384,1536]{1,0:T(8,128)(2,1)S(1)}, bf16[384,1536]{1,0:T(8,128)(2,1)}, u32[]{:S(2)}) copy-start(bf16[384,1536]{1,0:T(8,128)(2,1)} %param.15) | copy-start | bytes 3538948
  36.8 6.5 %collective-permute-start.4 = (f32[1,1537]{1,0:T(1,128)S(1)}, f32[1,1537]{1,0:T(1,128)S(1)}, u32[]{:S(2)}, u32[]{:S(2)}) collective-permute-start(f32[1,1537]{1,0:T(1,128)S(1)} %pad_maximum_fusion.4), channel_id=1, source_target_pairs={{4,0},{8,4},{12,8},{16,12},{20,16},{24,20},{28,24},{5,1},{9,5},{13... | collective-permute-start | bytes 18452 | tf_op jit(solution)/shard_map/ppermute | solution.py:16
  43.3 16.6 %collective-permute-start.9 = (bf16[384,1536]{1,0:T(8,128)(2,1)S(1)}, bf16[384,1536]{1,0:T(8,128)(2,1)S(1)}, u32[]{:S(2)}, u32[]{:S(2)}) collective-permute-start(bf16[384,1536]{1,0:T(8,128)(2,1)S(1)} %copy-done.5), channel_id=1, source_target_pairs={{0,1},{1,0},{2,3},{3,2},{4,5},{5,4},{6,7},{7,6},{8,9},{9,8},{10,11... | collective-permute-start | bytes 3538952 | tf_op jit(solution)/shard_map/ppermute | solution.py:51
  45.1 1.3 %copy-start.9 = (bf16[384,1536]{1,0:T(8,128)(2,1)S(1)}, bf16[384,1536]{1,0:T(8,128)(2,1)}, u32[]{:S(2)}) copy-start(bf16[384,1536]{1,0:T(8,128)(2,1)} %param.14) | copy-start | bytes 3538948
  47.1 17.1 %collective-permute-start.7 = (bf16[384,1536]{1,0:T(8,128)(2,1)S(1)}, bf16[384,1536]{1,0:T(8,128)(2,1)S(1)}, u32[]{:S(2)}, u32[]{:S(2)}) collective-permute-start(bf16[384,1536]{1,0:T(8,128)(2,1)S(1)} %collective-permute-done.5), channel_id=1, source_target_pairs={{0,1},{1,0},{2,3},{3,2},{4,5},{5,4},{6,7},{7,6},{8,9},{9,8},{10,11... | collective-permute-start | bytes 3538952 | tf_op jit(solution)/shard_map/ppermute | solution.py:51
  55.2 5.8 %collective-permute-start.10 = (bf16[384,1536]{1,0:T(8,128)(2,1)}, bf16[384,1536]{1,0:T(8,128)(2,1)S(1)}, u32[]{:S(2)}, u32[]{:S(2)}) collective-permute-start(bf16[384,1536]{1,0:T(8,128)(2,1)} %collective-permute-done.8), channel_id=1, source_target_pairs={{0,1},{1,0},{2,3},{3,2},{4,5},{5,4},{6,7},{7,6},{8,9},{9,8},{10,11... | collective-permute-start | bytes 3538952 | tf_op jit(solution)/shard_map/ppermute | solution.py:51
  59.9 1.1 %copy-start.11 = (bf16[384,1536]{1,0:T(8,128)(2,1)}, bf16[384,1536]{1,0:T(8,128)(2,1)S(1)}, u32[]{:S(2)}) copy-start(bf16[384,1536]{1,0:T(8,128)(2,1)S(1)} %collective-permute-done.9) | copy-start | bytes 3538948
  61.0 1.0 copy-start.13
  62.0 6.4 %copy-start = (f32[322,1536]{1,0:T(8,128)}, f32[322,1536]{1,0:T(8,128)S(1)}, u32[]{:S(2)}) copy-start(f32[322,1536]{1,0:T(8,128)S(1)} %convolution_add_fusion) | copy-start | bytes 5935108
  64.2 1.0 copy-start.7
  65.2 1.3 %copy-start.2 = (f32[322,1536]{1,0:T(8,128)}, f32[322,1536]{1,0:T(8,128)S(1)}, u32[]{:S(2)}) copy-start(f32[322,1536]{1,0:T(8,128)S(1)} %convolution_add_fusion.3) | copy-start | bytes 5935108
  68.5 2.1 %slice-start = ((f32[322,1536]{1,0:T(8,128)}), f32[319,1536]{1,0:T(8,128)S(1)}, s32[]{:S(2)}) async-start(f32[322,1536]{1,0:T(8,128)} %copy-done), calls=%async_computation | async-start | bytes 3932160 | tf_op jit(solution)/shard_map/slice | solution.py:154
  70.6 2.9 %copy-start.3 = (f32[322,1536]{1,0:T(8,128)S(1)}, f32[322,1536]{1,0:T(8,128)}, u32[]{:S(2)}) copy-start(f32[322,1536]{1,0:T(8,128)} %copy-done.2) | copy-start | bytes 5935108
  74.7 1.6 %copy-start.1 = (f32[322,1536]{1,0:T(8,128)S(1)}, f32[322,1536]{1,0:T(8,128)}, u32[]{:S(2)}) copy-start(f32[322,1536]{1,0:T(8,128)} %copy-done) | copy-start | bytes 5935108
  76.5 1.3 %copy-start.10 = (bf16[384,1536]{1,0:T(8,128)(2,1)S(1)}, bf16[384,1536]{1,0:T(8,128)(2,1)}, u32[]{:S(2)}) copy-start(bf16[384,1536]{1,0:T(8,128)(2,1)} %param.14) | copy-start | bytes 3538948
  76.9 1.6 %copy-start.4 = (bf16[1,320,1536]{2,1,0:T(8,128)(2,1)S(1)}, bf16[1,320,1536]{2,1,0:T(8,128)(2,1)}, u32[]{:S(2)}) copy-start(bf16[1,320,1536]{2,1,0:T(8,128)(2,1)} %param.9) | copy-start | bytes 2949124
  78.5 4.5 %copy-start.6 = (bf16[384,1536]{1,0:T(8,128)(2,1)S(1)}, bf16[384,1536]{1,0:T(8,128)(2,1)}, u32[]{:S(2)}) copy-start(bf16[384,1536]{1,0:T(8,128)(2,1)} %param.15) | copy-start | bytes 3538948
  80.3 3.4 %copy-start.14 = (bf16[384,1536]{1,0:T(8,128)(2,1)S(1)}, bf16[384,1536]{1,0:T(8,128)(2,1)}, u32[]{:S(2)}) copy-start(bf16[384,1536]{1,0:T(8,128)(2,1)} %copy-done.13) | copy-start | bytes 3538948
  81.5 9.8 %collective-permute-start.11 = (f32[1,1664]{1,0:T(1,128)S(1)}, f32[1,1664]{1,0:T(1,128)S(1)}, u32[]{:S(2)}, u32[]{:S(2)}) collective-permute-start(f32[1,1664]{1,0:T(1,128)S(1)} %concatenate.35), channel_id=1, source_target_pairs={{4,0},{8,4},{12,8},{16,12},{20,16},{24,20},{28,24},{5,1},{9,5},{13... | collective-permute-start | bytes 19976 | tf_op jit(solution)/shard_map/ppermute | solution.py:16
  83.7 1.3 %copy-start.12 = (bf16[384,1536]{1,0:T(8,128)(2,1)S(1)}, bf16[384,1536]{1,0:T(8,128)(2,1)}, u32[]{:S(2)}) copy-start(bf16[384,1536]{1,0:T(8,128)(2,1)} %copy-done.11) | copy-start | bytes 3538948
  85.7 2.1 %copy-start.8 = (bf16[384,1536]{1,0:T(8,128)(2,1)S(1)}, bf16[384,1536]{1,0:T(8,128)(2,1)}, u32[]{:S(2)}) copy-start(bf16[384,1536]{1,0:T(8,128)(2,1)} %copy-done.7) | copy-start | bytes 3538948
  91.9 7.3 %collective-permute-start.12 = (f32[1,1664]{1,0:T(1,128)S(1)}, f32[1,1664]{1,0:T(1,128)S(1)}, u32[]{:S(2)}, u32[]{:S(2)}) collective-permute-start(f32[1,1664]{1,0:T(1,128)S(1)} %fusion.46), channel_id=1, source_target_pairs={{8,0},{12,4},{16,8},{20,12},{24,16},{28,20},{9,1},{13,5},{17,9},{2... | collective-permute-start | bytes 19976 | tf_op jit(solution)/shard_map/ppermute | solution.py:16
  99.2 6.4 %collective-permute-start.13 = (f32[1,1664]{1,0:T(1,128)S(1)}, f32[1,1664]{1,0:T(1,128)S(1)}, u32[]{:S(2)}, u32[]{:S(2)}) collective-permute-start(f32[1,1664]{1,0:T(1,128)S(1)} %get-tuple-element.18), channel_id=1, source_target_pairs={{16,0},{20,4},{24,8},{28,12},{17,1},{21,5},{25,9},{29,13},{18,2},{... | collective-permute-start | bytes 19976 | tf_op jit(solution)/shard_map/ppermute | solution.py:16

commit v23 on v18

--- a/solution.py
+++ b/solution.py
@@ -161,11 +161,10 @@
     )
     grad_in = seq_scan(last_log, back_vector, "seq", False)
     reach_end = jnp.exp(running[slot_count - 1] - running)
-    state_local = lax.optimization_barrier(
-        lax.dot_general(decay_table, slot_grad, contract_first, precision=exact)
-    )
-    state_grad = state_local + reach_end[:, None] * grad_in
-    segment_grad = (smoothing[:, None] * state_grad).astype(jnp.bfloat16)
+    local_part = lax.optimization_barrier(
+        smoothing[:, None] * lax.dot_general(decay_table, slot_grad, contract_first, precision=exact)
+    )
+    segment_grad = (local_part + (smoothing * reach_end)[:, None] * grad_in).astype(jnp.bfloat16)
     unit_q_grad = cos_grad[:, None] * key_prior
     prior_grad = cos_grad[:, None] * query_unit
     query_grad = normalize_grad(queries, query_scale, unit_q_grad).astype(jnp.bfloat16)

time: 106 us -> 106 us (level)
    mul x0 -> x1, other arithmetic: none -> 1.36 us  [per_device(): smoothing * reach_end]
where the time goes in v23:
time: 106 us; the launch traced here: 105 us
  matrix products  24.3 us (23%)
  starting transfers between devices  24.2 us (23%)
  other arithmetic  17.4 us (16%)
  local copies, waits for them, and re-layouts  15.1 us (14%)
  waiting for transfers between devices  13.6 us (13%)
  between operations  10.6 us (10%)
    ppermute x8, starting transfers between devices, shifted(): return lax.ppermute(block, axis, route)  20 us
    dot_general x8, matrix products, split_dot(): term = jnp.dot(part, block, preferred_element_type=jnp.float32)  8.06 us
    ppermute x2, waiting for transfers between devices, gather_blocks(): pairs.append(lax.ppermute(blocks, axis, route))  7.24 us
    ppermute x8, waiting for transfers between devices, shifted(): return lax.ppermute(block, axis, route)  6.38 us
    unnamed x30, local copies, waits for them, and re-layouts  5.67 us
    dot_general x4, matrix products, per_device(): lax.dot_general(key_grad, k_block, contract_last, preferred_element_type=...  4.13 us
    dot_general x4, matrix products, per_device(): lax.dot_general(query_grad, q_block, contract_last, preferred_element_typ...  4.05 us
    ppermute x2, starting transfers between devices, gather_blocks(): pairs.append(lax.ppermute(blocks, axis, route))  3.6 us
  transfers between devices with their start and end apart: 14, of which 3 were waited for; matrix products, arithmetic and copies ran while one was open for 36% of the time, Pallas kernels for 0%

profile of v23, /device:TPU:0, one launch (start us, length us, event | category | flops | bytes accessed | tf_op | source)
XLA Modules:
  0.0 105.2 jit_solution(6521020647922859595)
XLA Ops:
  0.6 3.0 %collective-permute-start.5 = (bf16[384,1536]{1,0:T(8,128)(2,1)}, bf16[384,1536]{1,0:T(8,128)(2,1)S(1)}, u32[]{:S(2)}, u32[]{:S(2)}) collective-permute-start(bf16[384,1536]{1,0:T(8,128)(2,1)} %param.14), channel_id=1, source_target_pairs={{0,2},{1,3},{2,0},{3,1},{4,6},{5,7},{6,4},{7,5},{8,10},{9,11},{10,... | collective-permute-start | bytes 3538952 | tf_op jit(solution)/shard_map/ppermute | solution.py:48
  4.3 0.7 fusion.62
  5.3 0.6 slice.113
  6.0 1.4 %exponential_multiply_fusion = (f32[128]{0:T(128)S(1)}, f32[128]{0:T(128)S(1)}, f32[128]{0:T(128)S(1)}) fusion(f32[128]{0:T(128)S(1)} %reduce.2, f32[]{:T(128)} %bitcast.9, s32[1,128]{1,0:T(1,128)} %param.13, s32[]{:T(128)} %bitcast.83), kind=kLoop, calls=%fused_computation.141 | loop fusion | flops 768 | bytes 2568 | tf_op jit(solution)/shard_map/mul | solution.py:167
  7.3 1.9 %fusion.11 = f32[128,1536]{1,0:T(8,128)S(1)} fusion(bf16[1,128,1536]{2,1,0:T(8,128)(2,1)} %param.10, f32[128]{0:T(128)S(1)} %get-tuple-element.5, f32[128]{0:T(128)S(1)} %reduce.2), kind=kOutput, calls=%fused_computation.43 | convolution fusion | flops 302448640 | bytes 1180672 | tf_op jit(solution)/shard_map/dot_general | solution.py:126
  9.2 0.9 copy-done.14
  10.1 0.7 concatenate.24
  10.8 3.4 %collective-permute-start.1 = (f32[1,1664]{1,0:T(1,128)S(1)}, f32[1,1664]{1,0:T(1,128)S(1)}, u32[]{:S(2)}, u32[]{:S(2)}) collective-permute-start(f32[1,1664]{1,0:T(1,128)S(1)} %concatenate.24), channel_id=1, source_target_pairs={{0,4},{4,8},{8,12},{12,16},{16,20},{20,24},{24,28},{1,5},{5,9},{9,... | collective-permute-start | bytes 19976 | tf_op jit(solution)/shard_map/ppermute | solution.py:16
  14.2 0.8 slice_bitcast_fusion
  15.0 3.5 %collective-permute-start = (bf16[1,1536]{1,0:T(2,128)(2,1)S(1)}, bf16[1,1536]{1,0:T(2,128)(2,1)S(1)}, u32[]{:S(2)}, u32[]{:S(2)}) collective-permute-start(bf16[1,1536]{1,0:T(2,128)(2,1)S(1)} %get-tuple-element.15), channel_id=1, source_target_pairs={{0,4},{4,8},{8,12},{12,16},{16,20},{20,24},{24,28},{1,5},{5,9},{9,... | collective-permute-start | bytes 9224 | tf_op jit(solution)/shard_map/ppermute | solution.py:16
  18.5 0.6 collective-permute-start.8
  19.0 0.8 fusion.30
  19.8 0.8 convert_reduce_fusion
  21.5 0.7 fusion.40
  22.2 3.5 %collective-permute-start.2 = (f32[1,1664]{1,0:T(1,128)S(1)}, f32[1,1664]{1,0:T(1,128)S(1)}, u32[]{:S(2)}, u32[]{:S(2)}) collective-permute-start(f32[1,1664]{1,0:T(1,128)S(1)} %fusion.40), channel_id=1, source_target_pairs={{0,8},{4,12},{8,16},{12,20},{16,24},{20,28},{1,9},{5,13},{9,17},{1... | collective-permute-start | bytes 19976 | tf_op jit(solution)/shard_map/ppermute | solution.py:16
  25.8 0.5 slice.116
  28.2 4.1 %collective-permute-start.3 = (f32[1,1664]{1,0:T(1,128)S(1)}, f32[1,1664]{1,0:T(1,128)S(1)}, u32[]{:S(2)}, u32[]{:S(2)}) collective-permute-start(f32[1,1664]{1,0:T(1,128)S(1)} %get-tuple-element.19), channel_id=1, source_target_pairs={{0,16},{4,20},{8,24},{12,28},{1,17},{5,21},{9,25},{13,29},{2,18},{... | collective-permute-start | bytes 19976 | tf_op jit(solution)/shard_map/ppermute | solution.py:16
  32.3 0.6 fusion.65
  32.9 0.5 slice.115
  34.2 3.0 %fusion.2 = f32[320]{0:T(512)S(1)} fusion(bf16[1,320,1536]{2,1,0:T(8,128)(2,1)} %param.9, f32[1536]{0:T(1024)S(1)} %fusion.49, f32[320]{0:T(512)S(1)} %compare_convert_fusion, f32[128,1536]{1,0:T(8,128)} %copy-done.14, f32[128]{0:T(128)S(1)} %get-tuple-element.32, s32[320]{0:T(512)S(1)} %get-tuple-element.25), kind=kOutput, calls=%fused_computation.24 | convolution fusion | flops 757866176 | bytes 1779968 | tf_op jit(solution)/shard_map/dot_general | solution.py:131
  37.2 0.5 slice.93
  37.7 0.7 pad_maximum_fusion.4
  38.4 1.5 %collective-permute-start.4 = (f32[1,1537]{1,0:T(1,128)S(1)}, f32[1,1537]{1,0:T(1,128)S(1)}, u32[]{:S(2)}, u32[]{:S(2)}) collective-permute-start(f32[1,1537]{1,0:T(1,128)S(1)} %pad_maximum_fusion.4), channel_id=1, source_target_pairs={{4,0},{8,4},{12,8},{16,12},{20,16},{24,20},{28,24},{5,1},{9,5},{13... | collective-permute-start | bytes 18452 | tf_op jit(solution)/shard_map/ppermute | solution.py:16
  42.3 2.4 %gather_fusion = f32[320]{0:T(512)S(1)} fusion(f32[128]{0:T(128)S(1)} %get-tuple-element.32, s32[1024]{0:T(1024)S(1)} %pad_clamp_fusion), kind=kCustom, calls=%fused_computation | custom fusion | bytes 3840 | tf_op jit(solution)/shard_map/gather | solution.py:134
  45.5 0.7 fusion.25
  46.2 0.6 copy-done.7
  46.7 0.7 convolution_add_fusion.5
  47.4 0.6 collective-permute-start.7
  48.0 7.2 %collective-permute-done.8 = bf16[384,1536]{1,0:T(8,128)(2,1)} collective-permute-done((bf16[384,1536]{1,0:T(8,128)(2,1)}, bf16[384,1536]{1,0:T(8,128)(2,1)}, u32[]{:S(2)}, u32[]{:S(2)}) %collective-permute-start.8) | collective-permute-done | bytes 1179680 | tf_op jit(solution)/shard_map/ppermute | solution.py:48
  55.2 1.9 %fusion.23 = f32[322,1536]{1,0:T(8,128)S(1)} fusion(bf16[384,1536]{1,0:T(8,128)(2,1)} %collective-permute-done.8, bf16[322,1536]{1,0:T(8,128)(2,1)S(1)} %pad_maximum_fusion.2, s32[]{:T(128)S(6)} %select_n.165), kind=kOutput, calls=%fused_computation.56 | convolution fusion | flops 379846656 | bytes 3409924 | tf_op jit(solution)/shard_map/dot_general | solution.py:73
  57.2 0.7 convolution_add_fusion.2
  57.9 2.0 %convolution_add_fusion.4 = f32[322,1536]{1,0:T(8,128)S(1)} fusion(f32[322,1536]{1,0:T(8,128)S(1)} %convolution_add_fusion.5, bf16[384,1536]{1,0:T(8,128)(2,1)} %collective-permute-done.6, bf16[322,1536]{1,0:T(8,128)(2,1)S(1)} %pad_maximum_fusion.2, s32[]{:T(128)S(6)} %select_n.166), kind=kOutput, calls=%fused_computation.5 | convolution fusion | flops 380341248 | bytes 5425156 | tf_op jit(solution)/shard_map/dot_general | solution.py:73
  59.9 0.7 convolution_add_fusion.1
  60.9 0.7 convolution_add_fusion
  62.0 0.7 multiply_reduce_fusion.6
  62.7 1.4 %multiply_reduce_fusion.3 = (f32[320]{0:T(512)S(1)}, f32[320,1536]{1,0:T(8,128)}) fusion(f32[322,1536]{1,0:T(8,128)S(1)} %convolution_add_fusion), kind=kLoop, calls=%fused_computation.21 | loop fusion | flops 982720 | bytes 3933440 | tf_op jit(solution)/shard_map/reduce_sum | solution.py:85
  64.2 0.7 convolution_add_fusion.3
  65.3 1.3 %copy-done = f32[322,1536]{1,0:T(8,128)} copy-done((f32[322,1536]{1,0:T(8,128)}, f32[322,1536]{1,0:T(8,128)S(1)}, u32[]{:S(2)}) %copy-start) | copy-done | bytes 1978392
  66.6 0.6 multiply_reduce_fusion.5
  68.7 1.4 %multiply_multiply_fusion = f32[1,1536]{1,0:T(1,128)S(1)} fusion(f32[322,1536]{1,0:T(8,128)} %copy-done, f32[]{:T(128)S(6)} %rsqrt.33, f32[]{:T(128)} %bitcast.15), kind=kLoop, calls=%fused_computation.99 | loop fusion | flops 3072 | bytes 12296 | tf_op jit(solution)/shard_map/mul | solution.py:171
  70.0 1.9 %slice_multiply_fusion.1 = f32[319,1536]{1,0:T(8,128)S(1)} fusion(f32[320,1536]{1,0:T(8,128)} %get-tuple-element.10, f32[319]{0:T(512)S(1)} %bitcast.85), kind=kLoop, calls=%fused_computation.13 | loop fusion | flops 489984 | bytes 3921148 | tf_op jit(solution)/shard_map/mul | solution.py:86
  72.2 0.6 multiply_reduce_fusion.2
  72.8 0.8 multiply_reduce_fusion
  74.5 0.9 copy-done.8
  75.4 0.7 fusion.66
  76.2 1.2 %fusion.1 = f32[128,1536]{1,0:T(8,128)S(1)} fusion(bf16[1,320,1536]{2,1,0:T(8,128)(2,1)S(1)} %copy-done.2, f32[320]{0:T(512)S(1)} %get-tuple-element.23, s32[320]{0:T(512)S(1)} %get-tuple-element.25), kind=kOutput, calls=%fused_computation.11 | convolution fusion | flops 755998720 | bytes 1772032 | tf_op jit(solution)/shard_map/dot_general | solution.py:158
  77.4 0.9 convolution_multiply_fusion
  79.4 0.7 concatenate.31
  80.1 1.5 %collective-permute-start.11 = (f32[1,1664]{1,0:T(1,128)S(1)}, f32[1,1664]{1,0:T(1,128)S(1)}, u32[]{:S(2)}, u32[]{:S(2)}) collective-permute-start(f32[1,1664]{1,0:T(1,128)S(1)} %concatenate.31), channel_id=1, source_target_pairs={{4,0},{8,4},{12,8},{16,12},{20,16},{24,20},{28,24},{5,1},{9,5},{13... | collective-permute-start | bytes 19976 | tf_op jit(solution)/shard_map/ppermute | solution.py:16
  81.6 0.7 fusion.3
  82.4 0.7 fusion.69
  83.0 0.6 copy-done.10
  83.6 0.7 fusion.68
  84.3 2.0 %fusion.67 = f32[320,384]{1,0:T(8,128)S(1)} fusion(bf16[320,1536]{1,0:T(8,128)(2,1)S(1)} %subtract_convert_fusion, bf16[384,1536]{1,0:T(8,128)(2,1)} %collective-permute-done.8), kind=kOutput, calls=%fused_computation.149 | convolution fusion | flops 377487360 | bytes 2654208 | tf_op jit(solution)/shard_map/dot_general | solution.py:176
  86.4 0.7 fusion.6
  87.1 2.0 %fusion.5 = bf16[320,384]{1,0:T(8,128)(2,1)S(1)} fusion(f32[320,384]{1,0:T(8,128)S(1)} %fusion.68, bf16[320,1536]{1,0:T(8,128)(2,1)S(1)} %get-tuple-element.8, bf16[384,1536]{1,0:T(8,128)(2,1)} %collective-permute-done.6), kind=kOutput, calls=%fused_computation.31 | convolution fusion | flops 377733120 | bytes 2899968 | tf_op jit(solution)/shard_map/dot_general | solution.py:175
  89.1 0.7 fusion.4
  89.9 0.7 fusion.43
  90.6 1.3 %collective-permute-start.12 = (f32[1,1664]{1,0:T(1,128)S(1)}, f32[1,1664]{1,0:T(1,128)S(1)}, u32[]{:S(2)}, u32[]{:S(2)}) collective-permute-start(f32[1,1664]{1,0:T(1,128)S(1)} %fusion.43), channel_id=1, source_target_pairs={{8,0},{12,4},{16,8},{20,12},{24,16},{28,20},{9,1},{13,5},{17,9},{2... | collective-permute-start | bytes 19976 | tf_op jit(solution)/shard_map/ppermute | solution.py:16
  94.4 3.5 %collective-permute-done.12 = f32[1,1664]{1,0:T(1,128)S(1)} collective-permute-done((f32[1,1664]{1,0:T(1,128)S(1)}, f32[1,1664]{1,0:T(1,128)S(1)}, u32[]{:S(2)}, u32[]{:S(2)}) %collective-permute-start.12) | collective-permute-done | bytes 6688 | tf_op jit(solution)/shard_map/ppermute | solution.py:16
  97.9 1.3 %collective-permute-start.13 = (f32[1,1664]{1,0:T(1,128)S(1)}, f32[1,1664]{1,0:T(1,128)S(1)}, u32[]{:S(2)}, u32[]{:S(2)}) collective-permute-start(f32[1,1664]{1,0:T(1,128)S(1)} %get-tuple-element.17), channel_id=1, source_target_pairs={{16,0},{20,4},{24,8},{28,12},{17,1},{21,5},{25,9},{29,13},{18,2},{... | collective-permute-start | bytes 19976 | tf_op jit(solution)/shard_map/ppermute | solution.py:16
  99.2 1.0 maximum_bitcast_fusion
  101.4 2.9 %collective-permute-done.13 = f32[1,1664]{1,0:T(1,128)S(1)} collective-permute-done((f32[1,1664]{1,0:T(1,128)S(1)}, f32[1,1664]{1,0:T(1,128)S(1)}, u32[]{:S(2)}, u32[]{:S(2)}) %collective-permute-start.13) | collective-permute-done | bytes 6688 | tf_op jit(solution)/shard_map/ppermute | solution.py:16
  104.4 0.9 fusion.14
  (79 shorter events, 7.0 us)
Async XLA Ops:
  0.6 44.9 %collective-permute-start.5 = (bf16[384,1536]{1,0:T(8,128)(2,1)}, bf16[384,1536]{1,0:T(8,128)(2,1)S(1)}, u32[]{:S(2)}, u32[]{:S(2)}) collective-permute-start(bf16[384,1536]{1,0:T(8,128)(2,1)} %param.14), channel_id=1, source_target_pairs={{0,2},{1,3},{2,0},{3,1},{4,6},{5,7},{6,4},{7,5},{8,10},{9,11},{10,... | collective-permute-start | bytes 3538952 | tf_op jit(solution)/shard_map/ppermute | solution.py:48
  3.7 54.2 %collective-permute-start.6 = (bf16[384,1536]{1,0:T(8,128)(2,1)}, bf16[384,1536]{1,0:T(8,128)(2,1)}, u32[]{:S(2)}, u32[]{:S(2)}) collective-permute-start(bf16[384,1536]{1,0:T(8,128)(2,1)} %param.14), channel_id=1, source_target_pairs={{0,1},{1,0},{2,3},{3,2},{4,5},{5,4},{6,7},{7,6},{8,9},{9,8},{10,11... | collective-permute-start | bytes 3538952 | tf_op jit(solution)/shard_map/ppermute | solution.py:51
  9.2 0.9 copy-start.14
  10.8 10.7 %collective-permute-start.1 = (f32[1,1664]{1,0:T(1,128)S(1)}, f32[1,1664]{1,0:T(1,128)S(1)}, u32[]{:S(2)}, u32[]{:S(2)}) collective-permute-start(f32[1,1664]{1,0:T(1,128)S(1)} %concatenate.24), channel_id=1, source_target_pairs={{0,4},{4,8},{8,12},{12,16},{16,20},{20,24},{24,28},{1,5},{5,9},{9,... | collective-permute-start | bytes 19976 | tf_op jit(solution)/shard_map/ppermute | solution.py:16
  15.0 30.4 %collective-permute-start = (bf16[1,1536]{1,0:T(2,128)(2,1)S(1)}, bf16[1,1536]{1,0:T(2,128)(2,1)S(1)}, u32[]{:S(2)}, u32[]{:S(2)}) collective-permute-start(bf16[1,1536]{1,0:T(2,128)(2,1)S(1)} %get-tuple-element.15), channel_id=1, source_target_pairs={{0,4},{4,8},{8,12},{12,16},{16,20},{20,24},{24,28},{1,5},{5,9},{9,... | collective-permute-start | bytes 9224 | tf_op jit(solution)/shard_map/ppermute | solution.py:16
  18.5 36.8 %collective-permute-start.8 = (bf16[384,1536]{1,0:T(8,128)(2,1)}, bf16[384,1536]{1,0:T(8,128)(2,1)}, u32[]{:S(2)}, u32[]{:S(2)}) collective-permute-start(bf16[384,1536]{1,0:T(8,128)(2,1)} %param.15), channel_id=1, source_target_pairs={{0,2},{1,3},{2,0},{3,1},{4,6},{5,7},{6,4},{7,5},{8,10},{9,11},{10,... | collective-permute-start | bytes 3538952 | tf_op jit(solution)/shard_map/ppermute | solution.py:48
  22.2 5.9 %collective-permute-start.2 = (f32[1,1664]{1,0:T(1,128)S(1)}, f32[1,1664]{1,0:T(1,128)S(1)}, u32[]{:S(2)}, u32[]{:S(2)}) collective-permute-start(f32[1,1664]{1,0:T(1,128)S(1)} %fusion.40), channel_id=1, source_target_pairs={{0,8},{4,12},{8,16},{12,20},{16,24},{20,28},{1,9},{5,13},{9,17},{1... | collective-permute-start | bytes 19976 | tf_op jit(solution)/shard_map/ppermute | solution.py:16
  28.2 5.9 %collective-permute-start.3 = (f32[1,1664]{1,0:T(1,128)S(1)}, f32[1,1664]{1,0:T(1,128)S(1)}, u32[]{:S(2)}, u32[]{:S(2)}) collective-permute-start(f32[1,1664]{1,0:T(1,128)S(1)} %get-tuple-element.19), channel_id=1, source_target_pairs={{0,16},{4,20},{8,24},{12,28},{1,17},{5,21},{9,25},{13,29},{2,18},{... | collective-permute-start | bytes 19976 | tf_op jit(solution)/shard_map/ppermute | solution.py:16
  34.1 10.7 %copy-start.3 = (bf16[384,1536]{1,0:T(8,128)(2,1)S(1)}, bf16[384,1536]{1,0:T(8,128)(2,1)}, u32[]{:S(2)}) copy-start(bf16[384,1536]{1,0:T(8,128)(2,1)} %param.15) | copy-start | bytes 3538948
  34.1 11.2 %copy-start.13 = (bf16[1,320,1536]{2,1,0:T(8,128)(2,1)S(1)}, bf16[1,320,1536]{2,1,0:T(8,128)(2,1)}, u32[]{:S(2)}) copy-start(bf16[1,320,1536]{2,1,0:T(8,128)(2,1)} %param.8) | copy-start | bytes 2949124
  38.4 6.4 %collective-permute-start.4 = (f32[1,1537]{1,0:T(1,128)S(1)}, f32[1,1537]{1,0:T(1,128)S(1)}, u32[]{:S(2)}, u32[]{:S(2)}) collective-permute-start(f32[1,1537]{1,0:T(1,128)S(1)} %pad_maximum_fusion.4), channel_id=1, source_target_pairs={{4,0},{8,4},{12,8},{16,12},{20,16},{24,20},{28,24},{5,1},{9,5},{13... | collective-permute-start | bytes 18452 | tf_op jit(solution)/shard_map/ppermute | solution.py:16
  44.8 15.1 %collective-permute-start.9 = (bf16[384,1536]{1,0:T(8,128)(2,1)S(1)}, bf16[384,1536]{1,0:T(8,128)(2,1)S(1)}, u32[]{:S(2)}, u32[]{:S(2)}) collective-permute-start(bf16[384,1536]{1,0:T(8,128)(2,1)S(1)} %copy-done.3), channel_id=1, source_target_pairs={{0,1},{1,0},{2,3},{3,2},{4,5},{5,4},{6,7},{7,6},{8,9},{9,8},{10,11... | collective-permute-start | bytes 3538952 | tf_op jit(solution)/shard_map/ppermute | solution.py:51
  45.5 1.3 %copy-start.7 = (bf16[384,1536]{1,0:T(8,128)(2,1)S(1)}, bf16[384,1536]{1,0:T(8,128)(2,1)}, u32[]{:S(2)}) copy-start(bf16[384,1536]{1,0:T(8,128)(2,1)} %param.14) | copy-start | bytes 3538948
  47.4 16.7 %collective-permute-start.7 = (bf16[384,1536]{1,0:T(8,128)(2,1)S(1)}, bf16[384,1536]{1,0:T(8,128)(2,1)S(1)}, u32[]{:S(2)}, u32[]{:S(2)}) collective-permute-start(bf16[384,1536]{1,0:T(8,128)(2,1)S(1)} %collective-permute-done.5), channel_id=1, source_target_pairs={{0,1},{1,0},{2,3},{3,2},{4,5},{5,4},{6,7},{7,6},{8,9},{9,8},{10,11... | collective-permute-start | bytes 3538952 | tf_op jit(solution)/shard_map/ppermute | solution.py:51
  55.2 5.7 %collective-permute-start.10 = (bf16[384,1536]{1,0:T(8,128)(2,1)}, bf16[384,1536]{1,0:T(8,128)(2,1)S(1)}, u32[]{:S(2)}, u32[]{:S(2)}) collective-permute-start(bf16[384,1536]{1,0:T(8,128)(2,1)} %collective-permute-done.8), channel_id=1, source_target_pairs={{0,1},{1,0},{2,3},{3,2},{4,5},{5,4},{6,7},{7,6},{8,9},{9,8},{10,11... | collective-permute-start | bytes 3538952 | tf_op jit(solution)/shard_map/ppermute | solution.py:51
  59.9 1.0 copy-start.9
  60.9 1.1 %copy-start.11 = (bf16[384,1536]{1,0:T(8,128)(2,1)}, bf16[384,1536]{1,0:T(8,128)(2,1)S(1)}, u32[]{:S(2)}) copy-start(bf16[384,1536]{1,0:T(8,128)(2,1)S(1)} %collective-permute-done.10) | copy-start | bytes 3538948
  64.2 1.1 %copy-start.5 = (bf16[384,1536]{1,0:T(8,128)(2,1)}, bf16[384,1536]{1,0:T(8,128)(2,1)S(1)}, u32[]{:S(2)}) copy-start(bf16[384,1536]{1,0:T(8,128)(2,1)S(1)} %collective-permute-done.7) | copy-start | bytes 3538948
  65.3 1.3 %copy-start = (f32[322,1536]{1,0:T(8,128)}, f32[322,1536]{1,0:T(8,128)S(1)}, u32[]{:S(2)}) copy-start(f32[322,1536]{1,0:T(8,128)S(1)} %convolution_add_fusion.3) | copy-start | bytes 5935108
  70.0 2.2 %copy-start.1 = (f32[322,1536]{1,0:T(8,128)S(1)}, f32[322,1536]{1,0:T(8,128)}, u32[]{:S(2)}) copy-start(f32[322,1536]{1,0:T(8,128)} %copy-done) | copy-start | bytes 5935108
  74.2 1.3 %copy-start.8 = (bf16[384,1536]{1,0:T(8,128)(2,1)S(1)}, bf16[384,1536]{1,0:T(8,128)(2,1)}, u32[]{:S(2)}) copy-start(bf16[384,1536]{1,0:T(8,128)(2,1)} %param.14) | copy-start | bytes 3538948
  74.5 1.6 %copy-start.2 = (bf16[1,320,1536]{2,1,0:T(8,128)(2,1)S(1)}, bf16[1,320,1536]{2,1,0:T(8,128)(2,1)}, u32[]{:S(2)}) copy-start(bf16[1,320,1536]{2,1,0:T(8,128)(2,1)} %param.9) | copy-start | bytes 2949124
  77.4 4.2 %copy-start.4 = (bf16[384,1536]{1,0:T(8,128)(2,1)S(1)}, bf16[384,1536]{1,0:T(8,128)(2,1)}, u32[]{:S(2)}) copy-start(bf16[384,1536]{1,0:T(8,128)(2,1)} %param.15) | copy-start | bytes 3538948
  78.8 3.5 %copy-start.12 = (bf16[384,1536]{1,0:T(8,128)(2,1)S(1)}, bf16[384,1536]{1,0:T(8,128)(2,1)}, u32[]{:S(2)}) copy-start(bf16[384,1536]{1,0:T(8,128)(2,1)} %copy-done.11) | copy-start | bytes 3538948
  80.1 9.8 %collective-permute-start.11 = (f32[1,1664]{1,0:T(1,128)S(1)}, f32[1,1664]{1,0:T(1,128)S(1)}, u32[]{:S(2)}, u32[]{:S(2)}) collective-permute-start(f32[1,1664]{1,0:T(1,128)S(1)} %concatenate.31), channel_id=1, source_target_pairs={{4,0},{8,4},{12,8},{16,12},{20,16},{24,20},{28,24},{5,1},{9,5},{13... | collective-permute-start | bytes 19976 | tf_op jit(solution)/shard_map/ppermute | solution.py:16
  82.3 1.3 %copy-start.10 = (bf16[384,1536]{1,0:T(8,128)(2,1)S(1)}, bf16[384,1536]{1,0:T(8,128)(2,1)}, u32[]{:S(2)}) copy-start(bf16[384,1536]{1,0:T(8,128)(2,1)} %copy-done.9) | copy-start | bytes 3538948
  84.3 2.1 %copy-start.6 = (bf16[384,1536]{1,0:T(8,128)(2,1)S(1)}, bf16[384,1536]{1,0:T(8,128)(2,1)}, u32[]{:S(2)}) copy-start(bf16[384,1536]{1,0:T(8,128)(2,1)} %copy-done.5) | copy-start | bytes 3538948
  90.6 7.3 %collective-permute-start.12 = (f32[1,1664]{1,0:T(1,128)S(1)}, f32[1,1664]{1,0:T(1,128)S(1)}, u32[]{:S(2)}, u32[]{:S(2)}) collective-permute-start(f32[1,1664]{1,0:T(1,128)S(1)} %fusion.43), channel_id=1, source_target_pairs={{8,0},{12,4},{16,8},{20,12},{24,16},{28,20},{9,1},{13,5},{17,9},{2... | collective-permute-start | bytes 19976 | tf_op jit(solution)/shard_map/ppermute | solution.py:16
  97.9 6.4 %collective-permute-start.13 = (f32[1,1664]{1,0:T(1,128)S(1)}, f32[1,1664]{1,0:T(1,128)S(1)}, u32[]{:S(2)}, u32[]{:S(2)}) collective-permute-start(f32[1,1664]{1,0:T(1,128)S(1)} %get-tuple-element.17), channel_id=1, source_target_pairs={{16,0},{20,4},{24,8},{28,12},{17,1},{21,5},{25,9},{29,13},{18,2},{... | collective-permute-start | bytes 19976 | tf_op jit(solution)/shard_map/ppermute | solution.py:16
